TPU v7x, 32 devices: a whole 2x2x4 slice. The times are simulated.
32 devices in a mesh: pages: 8 (over y, x, core), mp: 4 (over z).
Axes of the slice: x: 2, y: 2, z: 4, core: 2. Of those that a mesh axis runs over, the one named last changes fastest.
Arguments:
- hidden_in: bfloat16 [2048, 1280], P('pages'), may hold values from -240 to 240
- w_qkv: bfloat16 [3, 1280, 1280], P(None, None, 'mp'), may hold values from -0.15625 to 0.15625
- w_out: bfloat16 [1280, 1280], replicated, may hold values from -0.15625 to 0.15625
- w_gate_up: bfloat16 [2, 1280, 5120], P(None, None, 'mp'), may hold values from -0.15625 to 0.15625
- w_down: bfloat16 [5120, 1280], P('mp'), may hold values from -0.078125 to 0.078125
- scale_qk: float32 [1280], replicated, may hold values from 0.4 to 1.6
- scale_gate_up: float32 [2, 5120], P(None, 'mp'), may hold values from 0.5 to 2
- eigen_rates: float32 [2, 1280], replicated, may hold values from 0.1 to 1
- cache_keys: bfloat16 [32, 128, 1280], P('pages'), may hold values from -6 to 6
- cache_values: bfloat16 [32, 128, 1280], P('pages'), may hold values from -6 to 6
- page_table: int32 [32], replicated, may hold values from 0 to 31, as said below
- request_group: int32 [8, 4], replicated, may hold values from 0 to 7
- suffix_len: int32 [8, 4], replicated, may hold values from 1 to 253, as said below
Outputs:
- hidden_out: bfloat16 [2048, 1280], P(('pages', 'mp'))
Inputs may be any that keep to these rules, and one draw needn't show every extreme that they name: `suffix_len`: the 4 lengths of one index of pages sum to at least 153 and at most 256, and to exactly 256 for at least one index. `page_table`: A permutation of the pool pages; the 4 pool pages of one index of pages hold prefix pages of 4 different groups.
All inputs are finite; a program needn't handle non-finite values.
Results may differ from a plain program's by a relative error of at most 0.013.
Values may be sent and summed in bfloat16 or wider, within the bound.
No kernel may reach another device: no remote copies, remote signals or barrier semaphores. Data moves between devices by JAX's collectives and lax.ppermute only.
A program may use at most 128 MiB of HBM per device.

v0:
```python
import math

import jax
import jax.numpy as jnp
from jax import lax
from jax.sharding import PartitionSpec as P

HEADS = 20
GROUPS = 8


EPSILON = 1e-06


def rms_rows(values_in):
    return values_in * lax.rsqrt(jnp.mean(values_in * values_in, axis=-1, keepdims=True) + EPSILON)


def head_norm(values_in, scale_vec, head_count):
    row_count, model_width = values_in.shape
    per_head = values_in.reshape(row_count, head_count, model_width // head_count)
    normed = per_head * lax.rsqrt(jnp.mean(per_head * per_head, axis=-1, keepdims=True) + EPSILON)
    return normed.reshape(row_count, model_width) * scale_vec[None, :]


def rotate(values_in, position, head_count):
    row_count, model_width = values_in.shape
    head_dim = model_width // head_count
    half_dim = head_dim // 2
    frequency = jnp.exp(
        jnp.arange(half_dim).astype(jnp.float32) * (-2.0 * math.log(10000.0) / head_dim)
    )
    rotation = position.astype(jnp.float32)[:, None] * frequency[None, :]
    cosine_table = jnp.cos(rotation)[:, None, :]
    sine_table = jnp.sin(rotation)[:, None, :]
    per_head = values_in.reshape(row_count, head_count, head_dim)
    lower_half = per_head[:, :, :half_dim]
    upper_half = per_head[:, :, half_dim:]
    turned = jnp.concatenate(
        [
            lower_half * cosine_table - upper_half * sine_table,
            upper_half * cosine_table + lower_half * sine_table,
        ],
        axis=-1,
    )
    return turned.reshape(row_count, model_width)


def slot_tables(suffix_len, request_group, slot_count):
    end_slots = jnp.cumsum(suffix_len, axis=1)
    start_slots = end_slots - suffix_len
    slot_ids = jnp.arange(slot_count)
    inside = (slot_ids[None, None, :] >= start_slots[:, :, None]) & (
        slot_ids[None, None, :] < end_slots[:, :, None]
    )
    request_ids = jnp.arange(suffix_len.shape[1])
    slot_valid = jnp.any(inside, axis=1)
    request = jnp.sum(jnp.where(inside, request_ids[None, :, None], 0), axis=1)
    offset = slot_ids[None, :] - jnp.sum(jnp.where(inside, start_slots[:, :, None], 0), axis=1)
    group_id = jnp.where(
        slot_valid, jnp.sum(jnp.where(inside, request_group[:, :, None], 0), axis=1), -1
    )
    return (slot_valid, request, offset, group_id)


def prefix_block(query_block, group_block, prefix_keys, prefix_values, key_group, score_scale):
    row_count, model_width = query_block.shape
    head_dim = model_width // HEADS
    query_heads = query_block.reshape(row_count, HEADS, head_dim)
    key_heads = prefix_keys.reshape(-1, HEADS, head_dim)
    value_heads = prefix_values.reshape(-1, HEADS, head_dim)
    scores = (
        jnp.einsum("qhd,khd->qhk", query_heads, key_heads, preferred_element_type=jnp.float32)
        * score_scale
    )
    allowed = group_block[:, None] == key_group[None, :]
    weights = jnp.where(allowed[:, None, :], jnp.exp(scores), 0.0)
    weight_sum = jnp.sum(weights, axis=-1)
    summed = jnp.einsum(
        "qhk,khd->qhd",
        weights.astype(jnp.bfloat16),
        value_heads,
        preferred_element_type=jnp.float32,
    )
    return (summed.reshape(row_count, model_width), weight_sum)


def shards(
    hidden_in,
    w_qkv,
    w_out,
    w_gate_up,
    w_down,
    scale_qk,
    scale_gate_up,
    eigen_rates,
    cache_keys,
    cache_values,
    page_table,
    request_group,
    suffix_len,
):
    slot_count, model_width = hidden_in.shape
    head_dim = model_width // HEADS
    score_scale = 1.0 / math.sqrt(head_dim)
    mp_count = lax.axis_size("mp")
    mp_index = lax.axis_index("mp")
    own_rows = slot_count // mp_count
    row_first = mp_index * own_rows
    shard_index = lax.axis_index("pages")
    pages_here, page_len = (cache_keys.shape[0], cache_keys.shape[1])
    pool_pages = page_table.shape[0]
    prefix_pages = pool_pages // GROUPS
    slot_valid, request, offset, group_id = slot_tables(suffix_len, request_group, slot_count)
    live_shard = lax.dynamic_index_in_dim(slot_valid, shard_index, 0, keepdims=False)
    request_shard = lax.dynamic_index_in_dim(request, shard_index, 0, keepdims=False)
    offset_shard = lax.dynamic_index_in_dim(offset, shard_index, 0, keepdims=False)
    position_shard = prefix_pages * page_len + offset_shard
    live_own = lax.dynamic_slice_in_dim(live_shard, row_first, own_rows, 0)
    request_own = lax.dynamic_slice_in_dim(request_shard, row_first, own_rows, 0)
    offset_own = lax.dynamic_slice_in_dim(offset_shard, row_first, own_rows, 0)
    position_own = lax.dynamic_slice_in_dim(position_shard, row_first, own_rows, 0)
    state_in = rms_rows(hidden_in.astype(jnp.float32)).astype(jnp.bfloat16)
    projected = jnp.einsum(
        "sd,jdc->jsc", state_in, w_qkv, preferred_element_type=jnp.float32
    ).astype(jnp.bfloat16)
    columns = lax.all_gather(projected, "mp", axis=2, tiled=True)
    query_raw = lax.dynamic_slice_in_dim(columns[0], row_first, own_rows, 0)
    key_raw, value_rows = (columns[1], columns[2])
    queries = head_norm(
        rotate(query_raw.astype(jnp.float32), position_own, HEADS), scale_qk, HEADS
    ).astype(jnp.bfloat16)
    keys_new = head_norm(
        rotate(key_raw.astype(jnp.float32), position_shard, HEADS), scale_qk, HEADS
    ).astype(jnp.bfloat16)
    query_heads = queries.reshape(own_rows, HEADS, head_dim)
    scores = (
        jnp.einsum(
            "qhd,khd->hqk",
            query_heads,
            keys_new.reshape(slot_count, HEADS, head_dim),
            preferred_element_type=jnp.float32,
        )
        * score_scale
    )
    allowed = (
        (request_own[:, None] == request_shard[None, :])
        & (offset_shard[None, :] <= offset_own[:, None])
        & live_own[:, None]
        & live_shard[None, :]
    )
    weights = jnp.where(allowed[None], jnp.exp(scores), 0.0)
    suffix_total = jnp.sum(weights, axis=-1)
    suffix_sum = jnp.einsum(
        "hqk,khd->qhd",
        weights.astype(jnp.bfloat16),
        value_rows.reshape(slot_count, HEADS, head_dim),
        preferred_element_type=jnp.float32,
    )
    physical = shard_index * pages_here + jnp.arange(pages_here, dtype=jnp.int32)
    matches = page_table[:, None] == physical[None, :]
    logical = jnp.sum(
        jnp.where(matches, jnp.arange(pool_pages, dtype=jnp.int32)[:, None], 0), axis=0
    )
    key_group = jnp.repeat(logical // prefix_pages, page_len)
    prefix_keys = head_norm(
        cache_keys.reshape(pages_here * page_len, model_width).astype(jnp.float32), scale_qk, HEADS
    ).astype(jnp.bfloat16)
    prefix_values = cache_values.reshape(pages_here * page_len, model_width)
    gathered = lax.all_gather(queries, "pages", axis=0, tiled=True)
    gathered_group = lax.dynamic_slice_in_dim(group_id, row_first, own_rows, 1).reshape(-1)
    row_count = own_rows * lax.axis_size("pages")
    block_rows = row_count if row_count <= 512 else math.gcd(row_count, 512)

    def attend_block(block_first):
        query_block = lax.dynamic_slice_in_dim(gathered, block_first, block_rows, 0)
        group_block = lax.dynamic_slice_in_dim(gathered_group, block_first, block_rows, 0)
        return prefix_block(
            query_block, group_block, prefix_keys, prefix_values, key_group, score_scale
        )

    block_starts = jnp.arange(row_count // block_rows, dtype=jnp.int32) * block_rows
    summed, weight_sum = lax.map(attend_block, block_starts)
    prefix_sum, prefix_total = lax.psum_scatter(
        (summed.reshape(row_count, model_width), weight_sum.reshape(row_count, HEADS)),
        "pages",
        scatter_dimension=0,
        tiled=True,
    )
    denominator = suffix_total.T + prefix_total + (1.0 - live_own.astype(jnp.float32))[:, None]
    mixed = (suffix_sum + prefix_sum.reshape(own_rows, HEADS, head_dim)) / denominator[:, :, None]
    attention = mixed.reshape(own_rows, model_width).astype(jnp.bfloat16)
    projected_out = jnp.dot(
        lax.all_gather(attention, "mp", axis=0, tiled=True),
        w_out,
        preferred_element_type=jnp.float32,
    )
    residual_in = state_in.astype(jnp.float32)
    state_mid = rms_rows(
        residual_in + eigen_rates[0][None, :] * (rms_rows(projected_out) - residual_in)
    ).astype(jnp.bfloat16)
    state_own = lax.dynamic_slice_in_dim(state_mid, row_first, own_rows, 0)
    gate_up = jnp.einsum("sd,jdf->jsf", state_mid, w_gate_up, preferred_element_type=jnp.float32)
    hidden = (
        jax.nn.silu(scale_gate_up[0][None, :] * gate_up[0])
        * (scale_gate_up[1][None, :] * gate_up[1])
    ).astype(jnp.bfloat16)
    feed_sum = lax.psum_scatter(
        jnp.dot(hidden, w_down, preferred_element_type=jnp.float32),
        "mp",
        scatter_dimension=0,
        tiled=True,
    )
    middle = state_own.astype(jnp.float32)
    result = rms_rows(middle + eigen_rates[1][None, :] * (rms_rows(feed_sum) - middle))
    return (live_own.astype(jnp.float32)[:, None] * result).astype(jnp.bfloat16)


def solution(mesh):
    return jax.shard_map(
        shards,
        mesh=mesh,
        in_specs=(
            P("pages", None),
            P(None, None, "mp"),
            P(),
            P(None, None, "mp"),
            P("mp", None),
            P(),
            P(None, "mp"),
            P(),
            P("pages", None, None),
            P("pages", None, None),
            P(),
            P(),
            P(),
        ),
        out_specs=P(("pages", "mp"), None),
        check_vma=False,
    )
```

profile of v0, /device:TPU:2, one launch (start us, length us, event | category | flops | bytes accessed | tf_op | source)
XLA Modules:
  0.0 268.4 jit_solution(947115484770179296)
XLA Ops:
  6.5 1.4 fusion.9
  8.0 0.5 copy-done.9
  8.5 3.7 %fusion.22 = bf16[3,256,320]{1,2,0:T(8,128)(2,1)} fusion(bf16[3,1280,320]{1,2,0:T(8,128)(2,1)} %param.14, bf16[256,1280]{1,0:T(8,128)(2,1)} %param.13, f32[256]{0:T(256)S(1)} %add_rsqrt_fusion.5), kind=kOutput, calls=%fused_computation.40 | convolution fusion | flops 630374400 | bytes 3605504 | tf_op jit(solution)/shard_map/sd,jdc->jsc/dot_general | solution.py:124
  12.5 0.6 constant_dynamic-slice_fusion.1
  13.1 0.6 fusion.41
  14.0 43.2 %all-gather.3.cloned.1.call-done = bf16[3,256,1280]{1,2,0:T(8,128)(2,1)} async-done(((bf16[3,256,320]{1,2,0:T(8,128)(2,1)}), bf16[3,256,1280]{1,2,0:T(8,128)(2,1)}) %all-gather.3.cloned.1.call-update) | async-done | bytes 1966096 | tf_op jit(solution)/shard_map/all_gather | solution.py:127
  57.2 2.6 fusion.45
  60.0 0.9 fusion.46
  60.9 2.1 copy.56
  63.0 2.2 copy.57
  65.2 1.5 multiply_subtract_fusion
  66.7 0.5 multiply_reduce_fusion.4
  67.3 1.5 multiply_convert_fusion.4
  68.8 2.0 mul.353
  70.9 1.7 multiply_convert_fusion.7
  72.8 0.7 eq.64
  73.4 3.4 %copy.46 = f32[4,128,1280]{1,0,2:T(4,128)} copy(bf16[4,128,1280]{2,1,0:T(8,128)(2,1)} %param.21) | data formatting | bytes 3932160 | tf_op jit(solution)/shard_map/convert_element_type | solution.py:167
  76.9 4.1 %reshape.381 = f32[512,20,64]{0,2,1:T(8,128)} reshape(f32[4,128,1280]{1,0,2:T(4,128)} %copy.46) | data formatting | bytes 5242880 | tf_op jit(solution)/shard_map/convert_element_type | solution.py:167
  81.0 3.5 %copy.48 = bf16[4,128,1280]{1,0,2:T(4,128)(2,1)} copy(bf16[4,128,1280]{2,1,0:T(8,128)(2,1)} %param.22) | data formatting | bytes 2621440 | tf_op args[9]
  84.5 3.5 %reshape_reshape.4 = bf16[512,20,64]{0,2,1:T(8,128)(2,1)} reshape(bf16[4,128,1280]{1,0,2:T(4,128)(2,1)} %copy.48) | data formatting | bytes 2621440 | tf_op jit(solution)/shard_map/while/body/eval_jaxpr/reshape;reshape | solution.py:71
  88.1 2.3 multiply_reduce_fusion
  90.6 0.6 add_rsqrt_fusion
  91.4 4.7 %all-gather.5.cloned.1.call-done = bf16[512,1280]{1,0:T(8,128)(2,1)} async-done(((bf16[64,1280]{1,0:T(8,128)(2,1)}), bf16[512,1280]{1,0:T(8,128)(2,1)}) %all-gather.5.cloned.1.call-update) | async-done | bytes 1310736 | tf_op jit(solution)/shard_map/all_gather | solution.py:170
  96.1 2.5 copy.47
  98.6 12.5 %fusion = (f32[512,20]{0,1:T(8,128)}, f32[20,512,512]{2,1,0:T(8,128)}) fusion(pred[512,512]{0,1:T(8,128)(4,1)S(1)} %broadcast_compare_fusion, bf16[512,20,64]{0,2,1:T(8,128)(2,1)} %bitcast.85, f32[512,20,64]{0,2,1:T(8,128)} %reshape.381, f32[20,64]{1,0:T(8,128)S(1)} %mul.328, f32[512,20]{0,1:T(8,128)} %add_rsqrt_fusion), kind=kOutput, calls=%fused_computation.1 | convolution fusion | flops 688773120 | bytes 25252864 | tf_op jit(solution)/shard_map/while/body/eval_jaxpr/qhd,khd->qhk/dot_general | solution.py:73
  111.2 1.7 copy.54
  113.1 12.3 %fusion.2 = f32[20,512,64]{1,2,0:T(8,128)} fusion(bf16[512,20,64]{0,2,1:T(8,128)(2,1)} %reshape_reshape.4, f32[20,512,512]{2,1,0:T(8,128)} %get-tuple-element.56, pred[512,512]{0,1:T(8,128)(4,1)S(1)} %broadcast_compare_fusion), kind=kOutput, calls=%fused_computation.3 | convolution fusion | flops 686817280 | bytes 25165824 | tf_op jit(solution)/shard_map/while/body/eval_jaxpr/qhk,khd->qhd/dot_general | solution.py:79
  125.4 3.2 %copy.52 = f32[512,1280]{1,0:T(8,128)} copy(f32[512,1280]{0,1:T(8,128)} %bitcast.82) | data formatting | bytes 5242880
  128.8 0.8 dynamic-slice_bitcast_fusion.1
  129.6 0.6 fusion.44
  130.6 1.2 convert.4
  132.2 0.8 copy-done.3
  133.0 1.4 fusion.47
  134.4 12.2 %reduce-scatter.12.cloned.1.call-done = f32[64,20]{1,0:T(8,128)} async-done(((f32[512,20]{1,0:T(8,128)}), f32[64,20]{1,0:T(8,128)}) %reduce-scatter.12.cloned.1.call-update) | async-done | bytes 5136
  146.6 0.8 copy.55
  147.4 46.4 %reduce-scatter.10.cloned.1.call-done = f32[64,1280]{1,0:T(8,128)} async-done(((f32[512,1280]{1,0:T(8,128)}), f32[64,1280]{1,0:T(8,128)}) %reduce-scatter.10.cloned.1.call-update) | async-done | bytes 327696
  193.9 2.0 copy.53
  195.9 2.5 fusion.21
  198.4 1.1 copy.50
  199.6 17.9 %all_gather.11 = bf16[256,1280]{1,0:T(8,128)(2,1)S(1)} all-gather(bf16[64,1280]{1,0:T(8,128)(2,1)S(1)} %copy.50), channel_id=1, replica_groups=mesh['pages'=8,'mp'=4] {'mp'}, dimensions={0}, use_global_device_ids=true | all-gather | bytes 819200 | tf_op jit(solution)/shard_map/all_gather | solution.py:194
  217.5 1.1 multiply_reduce_fusion.2
  218.6 0.5 multiply_reduce_fusion.1
  219.5 5.0 %convolution_bitcast_fusion = f32[2,256,1280]{2,1,0:T(8,128)S(1)} fusion(bf16[2,1280,1280]{2,1,0:T(8,128)(2,1)} %param.16, bf16[256,1280]{1,0:T(8,128)(2,1)S(1)} %multiply_convert_fusion.2), kind=kOutput, calls=%fused_computation.7 | convolution fusion | flops 1677721600 | bytes 9830400 | tf_op jit(solution)/shard_map/sd,jdf->jsf/dot_general | solution.py:203
  224.6 2.3 fusion.23
  226.9 30.7 %reduce-scatter.8.cloned.1.call-done = f32[64,1280]{1,0:T(8,128)} async-done(((f32[256,1280]{1,0:T(8,128)}), f32[64,1280]{1,0:T(8,128)}) %reduce-scatter.8.cloned.1.call-update) | async-done | bytes 327696 | tf_op jit(solution)/shard_map/reduce_scatter | solution.py:208
  257.6 1.1 multiply_reduce_fusion.6
  258.7 1.3 multiply_reduce_fusion.5
  260.0 1.9 multiply_convert_fusion.6
  (87 shorter events, 3.0 us)
Async XLA Ops:
  6.5 210.9 %copy-start = (bf16[1280,1280]{1,0:T(8,128)(2,1)S(1)}, bf16[1280,1280]{1,0:T(8,128)(2,1)}, u32[]{:S(2)}) copy-start(bf16[1280,1280]{1,0:T(8,128)(2,1)} %param.15) | copy-start | bytes 9830404
  6.5 50.6 %all-gather.3.cloned.1.call-start = ((), (), s32[]{:S(2)}) async-start(), calls=%async_computation.3 | async-start | bytes 2457600 | tf_op jit(solution)/shard_map/all_gather | solution.py:127
  8.0 0.5 copy-start.9
  8.5 3.8 %copy-start.14 = (s32[8,4]{0,1:T(4,128)S(1)}, s32[8,4]{0,1:T(4,128)}, u32[]{:S(2)}) copy-start(s32[8,4]{0,1:T(4,128)} %param.25) | copy-start | bytes 388
  8.5 3.8 %copy-start.4 = (f32[1280]{0:T(1024)S(1)}, f32[1280]{0:T(1024)}, u32[]{:S(2)}) copy-start(f32[1280]{0:T(1024)} %param.18) | copy-start | bytes 15364
  8.5 3.9 %copy-start.19 = (s32[8,4]{0,1:T(4,128)S(1)}, s32[8,4]{0,1:T(4,128)}, u32[]{:S(2)}) copy-start(s32[8,4]{0,1:T(4,128)} %param.24) | copy-start | bytes 388
  12.2 83.9 %all-gather.5.cloned.1.call-start = ((), (), s32[]{:S(2)}) async-start(), calls=%async_computation.4 | async-start | bytes 1474560 | tf_op jit(solution)/shard_map/all_gather | solution.py:170
  12.4 47.4 %copy-start.17 = (f32[32]{0:T(128)}, f32[32]{0:T(128)S(1)}, u32[]{:S(2)}) copy-start(f32[32]{0:T(128)S(1)} %multiply_exponential_fusion) | copy-start | bytes 388
  12.5 47.3 %copy-start.6 = (s32[8,256]{1,0:T(8,128)}, s32[8,256]{1,0:T(8,128)S(1)}, u32[]{:S(2)}) copy-start(s32[8,256]{1,0:T(8,128)S(1)} %get-tuple-element.23) | copy-start | bytes 24580
  12.5 47.3 %copy-start.5 = (s32[8,256]{1,0:T(8,128)}, s32[8,256]{1,0:T(8,128)S(1)}, u32[]{:S(2)}) copy-start(s32[8,256]{1,0:T(8,128)S(1)} %iota_subtract_fusion) | copy-start | bytes 24580
  13.1 46.7 %copy-start.11 = (s32[1,256]{1,0:T(1,128)}, s32[1,256]{1,0:T(1,128)S(1)}, u32[]{:S(2)}) copy-start(s32[1,256]{1,0:T(1,128)S(1)} %get-tuple-element.61) | copy-start | bytes 3076
  72.5 74.1 %reduce-scatter.12.cloned.1.call-start = ((), (), s32[]{:S(2)}) async-start(), calls=%async_computation.7 | async-start | bytes 294912
  84.5 3.5 %copy-start.22 = (s32[32]{0:T(128)S(1)}, s32[32]{0:T(128)}, u32[]{:S(2)}) copy-start(s32[32]{0:T(128)} %param.23) | copy-start | bytes 388
  88.1 3.1 %copy-start.13 = (s32[512]{0:T(512)S(1)}, s32[512]{0:T(512)}, u32[]{:S(2)}) copy-start(s32[512]{0:T(512)} %eq.64) | copy-start | bytes 6148
  112.8 81.0 %reduce-scatter.10.cloned.1.call-start = ((), (), s32[]{:S(2)}) async-start(), calls=%async_computation.6 | async-start | bytes 2949120
  128.6 1.5 copy-start.7
  128.6 1.6 copy-start.8
  128.6 1.6 copy-start.12
  128.6 1.6 copy-start.16
  128.6 1.7 copy-start.15
  128.6 1.7 copy-start.18
  128.7 128.9 %reduce-scatter.8.cloned.1.call-start = ((), (), s32[]{:S(2)}) async-start(), calls=%async_computation.5 | async-start | bytes 1638400 | tf_op jit(solution)/shard_map/reduce_scatter | solution.py:208
  132.0 1.0 copy-start.3
  217.4 1.1 copy-start.1
  217.4 1.1 copy-start.10
  219.5 5.0 %copy-start.2 = (bf16[256,1280]{1,0:T(8,128)(2,1)}, bf16[256,1280]{1,0:T(8,128)(2,1)S(1)}, u32[]{:S(2)}) copy-start(bf16[256,1280]{1,0:T(8,128)(2,1)S(1)} %multiply_convert_fusion.2) | copy-start | bytes 1966084
  219.5 5.0 %copy-start.21 = (bf16[1280,1280]{1,0:T(8,128)(2,1)S(1)}, bf16[1280,1280]{1,0:T(8,128)(2,1)}, u32[]{:S(2)}) copy-start(bf16[1280,1280]{1,0:T(8,128)(2,1)} %param.17) | copy-start | bytes 9830404
  226.8 33.1 %copy-start.20 = (f32[64]{0:T(128)S(1)}, f32[64]{0:T(128)}, u32[]{:S(2)}) copy-start(f32[64]{0:T(128)} %get-tuple-element.36) | copy-start | bytes 772
Sparse Core Ops, SparseCore 0:
  12.3 44.7 all-gather.2
  72.7 23.4 all-gather.4
  113.0 33.6 reduce-scatter.11
  150.1 43.6 reduce-scatter.9
  227.0 30.5 reduce-scatter.7
where the time goes:
time: 271 us; the launch traced here: 268 us
  waiting for transfers between devices  137 us (51%)
  matrix products  40.8 us (15%)
  local copies, waits for them, and re-layouts  39.7 us (15%)
  other arithmetic  18.9 us (7%)
  blocking collectives  17.9 us (7%)
  between operations  13.5 us (5%)
    unnamed x7, waiting for transfers between devices  58.7 us
    all_gather x1, waiting for transfers between devices, shards(): columns = lax.all_gather(projected, 'mp', axis=2, tiled=True)  43.2 us
    reduce_scatter x1, waiting for transfers between devices, shards(): lax.psum_scatter(jnp.dot(hidden, w_down, preferred_element_type=jnp.float...  30.7 us
    all_gather x1, blocking collectives, shards(): lax.all_gather(attention, 'mp', axis=0, tiled=True)  17.9 us
    unnamed x53, local copies, waits for them, and re-layouts  16.9 us
    dot_general x1, matrix products, prefix_block(): jnp.einsum('qhd,khd->qhk', query_heads, key_heads, preferred_element_type...  12.5 us
    dot_general x1, matrix products, prefix_block(): jnp.einsum('qhk,khd->qhd', weights.astype(jnp.bfloat16), value_heads, pre...  12.3 us
    convert_element_type x2, local copies, waits for them, and re-layouts, shards(): cache_keys.reshape(pages_here * page_len, model_width).astype(jnp.float32)  7.59 us
  transfers between devices with their start and end apart: 5, of which 5 were waited for; matrix products, arithmetic and copies ran while one was open for 15% of the time, Pallas kernels for 0%

commit v1 on v0

--- a/solution.py
+++ b/solution.py
@@ -85,7 +85,7 @@
     return (summed.reshape(row_count, model_width), weight_sum)
 
 
-def shards(
+def shards_columns(
     hidden_in,
     w_qkv,
     w_out,
@@ -216,7 +216,145 @@
     return (live_own.astype(jnp.float32)[:, None] * result).astype(jnp.bfloat16)
 
 
+def shards_heads(
+    hidden_in,
+    w_qkv,
+    w_out,
+    w_gate_up,
+    w_down,
+    scale_qk,
+    scale_gate_up,
+    eigen_rates,
+    cache_keys,
+    cache_values,
+    page_table,
+    request_group,
+    suffix_len,
+):
+    slot_count, model_width = hidden_in.shape
+    head_dim = model_width // HEADS
+    score_scale = 1.0 / math.sqrt(head_dim)
+    mp_count = lax.axis_size("mp")
+    mp_index = lax.axis_index("mp")
+    local_heads = HEADS // mp_count
+    local_width = local_heads * head_dim
+    own_rows = slot_count // mp_count
+    row_first = mp_index * own_rows
+    shard_index = lax.axis_index("pages")
+    pages_here, page_len = (cache_keys.shape[0], cache_keys.shape[1])
+    pool_pages = page_table.shape[0]
+    prefix_pages = pool_pages // GROUPS
+    slot_valid, request, offset, group_id = slot_tables(suffix_len, request_group, slot_count)
+    live_shard = lax.dynamic_index_in_dim(slot_valid, shard_index, 0, keepdims=False)
+    request_shard = lax.dynamic_index_in_dim(request, shard_index, 0, keepdims=False)
+    offset_shard = lax.dynamic_index_in_dim(offset, shard_index, 0, keepdims=False)
+    position_shard = prefix_pages * page_len + offset_shard
+    live_own = lax.dynamic_slice_in_dim(live_shard, row_first, own_rows, 0)
+    scale_local = lax.dynamic_slice_in_dim(scale_qk, mp_index * local_width, local_width, 0)
+    state_in = rms_rows(hidden_in.astype(jnp.float32)).astype(jnp.bfloat16)
+    projected = jnp.einsum(
+        "sd,jdc->jsc", state_in, w_qkv, preferred_element_type=jnp.float32
+    ).astype(jnp.bfloat16)
+    queries = head_norm(
+        rotate(projected[0].astype(jnp.float32), position_shard, local_heads), scale_local, local_heads
+    ).astype(jnp.bfloat16)
+    keys_new = head_norm(
+        rotate(projected[1].astype(jnp.float32), position_shard, local_heads), scale_local, local_heads
+    ).astype(jnp.bfloat16)
+    value_rows = projected[2]
+    gathered = lax.all_gather(queries, "pages", axis=0, tiled=True)
+    scores = (
+        jnp.einsum(
+            "qhd,khd->hqk",
+            queries.reshape(slot_count, local_heads, head_dim),
+            keys_new.reshape(slot_count, local_heads, head_dim),
+            preferred_element_type=jnp.float32,
+        )
+        * score_scale
+    )
+    allowed = (
+        (request_shard[:, None] == request_shard[None, :])
+        & (offset_shard[None, :] <= offset_shard[:, None])
+        & live_shard[:, None]
+        & live_shard[None, :]
+    )
+    weights = jnp.where(allowed[None], jnp.exp(scores), 0.0)
+    suffix_total = jnp.sum(weights, axis=-1)
+    suffix_sum = jnp.einsum(
+        "hqk,khd->qhd",
+        weights.astype(jnp.bfloat16),
+        value_rows.reshape(slot_count, local_heads, head_dim),
+        preferred_element_type=jnp.float32,
+    )
+    physical = shard_index * pages_here + jnp.arange(pages_here, dtype=jnp.int32)
+    matches = page_table[:, None] == physical[None, :]
+    logical = jnp.sum(
+        jnp.where(matches, jnp.arange(pool_pages, dtype=jnp.int32)[:, None], 0), axis=0
+    )
+    key_group = jnp.repeat(logical // prefix_pages, page_len)
+    cache_local = lax.dynamic_slice_in_dim(cache_keys, mp_index * local_width, local_width, 2)
+    prefix_keys = head_norm(
+        cache_local.reshape(pages_here * page_len, local_width).astype(jnp.float32),
+        scale_local,
+        local_heads,
+    ).astype(jnp.bfloat16)
+    prefix_values = lax.dynamic_slice_in_dim(
+        cache_values, mp_index * local_width, local_width, 2
+    ).reshape(pages_here * page_len, local_width)
+    gathered_group = group_id.reshape(-1)
+    row_count = gathered.shape[0]
+    query_heads = gathered.reshape(row_count, local_heads, head_dim)
+    key_heads = prefix_keys.reshape(-1, local_heads, head_dim)
+    value_heads = prefix_values.reshape(-1, local_heads, head_dim)
+    prefix_scores = (
+        jnp.einsum("qhd,khd->qhk", query_heads, key_heads, preferred_element_type=jnp.float32)
+        * score_scale
+    )
+    prefix_allowed = gathered_group[:, None] == key_group[None, :]
+    prefix_weights = jnp.where(prefix_allowed[:, None, :], jnp.exp(prefix_scores), 0.0)
+    weight_sum = jnp.sum(prefix_weights, axis=-1)
+    summed = jnp.einsum(
+        "qhk,khd->qhd",
+        prefix_weights.astype(jnp.bfloat16),
+        value_heads,
+        preferred_element_type=jnp.float32,
+    )
+    prefix_sum, prefix_total = lax.psum_scatter(
+        (summed.reshape(row_count, local_width), weight_sum),
+        "pages",
+        scatter_dimension=0,
+        tiled=True,
+    )
+    denominator = suffix_total.T + prefix_total + (1.0 - live_shard.astype(jnp.float32))[:, None]
+    mixed = (suffix_sum + prefix_sum.reshape(slot_count, local_heads, head_dim)) / denominator[
+        :, :, None
+    ]
+    attention_local = mixed.reshape(slot_count, local_width).astype(jnp.bfloat16)
+    attention = lax.all_gather(attention_local, "mp", axis=1, tiled=True)
+    projected_out = jnp.dot(attention, w_out, preferred_element_type=jnp.float32)
+    residual_in = state_in.astype(jnp.float32)
+    state_mid = rms_rows(
+        residual_in + eigen_rates[0][None, :] * (rms_rows(projected_out) - residual_in)
+    ).astype(jnp.bfloat16)
+    state_own = lax.dynamic_slice_in_dim(state_mid, row_first, own_rows, 0)
+    gate_up = jnp.einsum("sd,jdf->jsf", state_mid, w_gate_up, preferred_element_type=jnp.float32)
+    hidden = (
+        jax.nn.silu(scale_gate_up[0][None, :] * gate_up[0])
+        * (scale_gate_up[1][None, :] * gate_up[1])
+    ).astype(jnp.bfloat16)
+    feed_sum = lax.psum_scatter(
+        jnp.dot(hidden, w_down, preferred_element_type=jnp.float32),
+        "mp",
+        scatter_dimension=0,
+        tiled=True,
+    )
+    middle = state_own.astype(jnp.float32)
+    result = rms_rows(middle + eigen_rates[1][None, :] * (rms_rows(feed_sum) - middle))
+    return (live_own.astype(jnp.float32)[:, None] * result).astype(jnp.bfloat16)
+
+
 def solution(mesh):
+    shards = shards_heads if HEADS % mesh.shape["mp"] == 0 else shards_columns
     return jax.shard_map(
         shards,
         mesh=mesh,

time: 271 us -> 207 us (0.76)
  waiting for transfers between devices: 137 us -> 105 us
  local copies, waits for them, and re-layouts: 39.7 us -> 14.4 us
  matrix products: 40.8 us -> 36.4 us
    reduce_scatter x1 -> x3, waiting for transfers between devices: 30.7 us -> 94.3 us  [the longest x2 63.7 us: shards_heads(): lax.psum_scatter((summed.reshape(row_count, local_width), weight_sum), 'p...]
    unnamed x7 -> x4, waiting for transfers between devices: 58.7 us -> 0.07 us
    all_gather x2 -> x1, waiting for transfers between devices: 47.9 us -> 10.4 us  [shards_heads(): gathered = lax.all_gather(queries, 'pages', axis=0, tiled=True)]
    unnamed x53 -> x20, local copies, waits for them, and re-layouts: 16.9 us -> 2.24 us
    convert_element_type x3 -> x2, local copies, waits for them, and re-layouts: 8.71 us -> 4.28 us  [shards_heads(): cache_local.reshape(pages_here * page_len, local_width).astype(jnp.float32)]
    dot_general x8, matrix products: 40.8 us -> 36.4 us  [the longest x1 12.5 us: shards_heads(): jnp.einsum('qhk,khd->qhd', prefix_weights.astype(jnp.bfloat16), value_hea...]
    dynamic_slice x3 -> x4, local copies, waits for them, and re-layouts: 0.77 us -> 5.14 us  [the longest x1 2.43 us: shards_heads(): lax.dynamic_slice_in_dim(cache_keys, mp_index * local_width, local_width, 2)]
    convert_element_type x6, other arithmetic: 7.33 us -> 4.19 us  [the longest x2 2 us: shards_heads(): return (live_own.astype(jnp.float32)[:, None] * result).astype(jnp.bfloat16)]
  transfers between devices with their start and end apart: 5 -> 4, of which waited for: 5 -> 4; matrix products, arithmetic and copies ran while one was open for 15% -> 16% of each run, Pallas kernels for 0% -> 0%
where the time goes in v1:
time: 207 us; the launch traced here: 205 us
  waiting for transfers between devices  105 us (51%)
  matrix products  36.4 us (18%)
  blocking collectives  18.1 us (9%)
  other arithmetic  17.5 us (8%)
  local copies, waits for them, and re-layouts  14.4 us (7%)
  between operations  13.4 us (6%)
    reduce_scatter x2, waiting for transfers between devices, shards_heads(): lax.psum_scatter((summed.reshape(row_count, local_width), weight_sum), 'p...  63.7 us
    reduce_scatter x1, waiting for transfers between devices, shards_heads(): lax.psum_scatter(jnp.dot(hidden, w_down, preferred_element_type=jnp.float...  30.6 us
    all_gather x1, blocking collectives, shards_heads(): attention = lax.all_gather(attention_local, 'mp', axis=1, tiled=True)  18.1 us
    dot_general x1, matrix products, shards_heads(): jnp.einsum('qhk,khd->qhd', prefix_weights.astype(jnp.bfloat16), value_hea...  12.5 us
    dot_general x1, matrix products, shards_heads(): jnp.einsum('qhd,khd->qhk', query_heads, key_heads, preferred_element_type...  11.8 us
    all_gather x1, waiting for transfers between devices, shards_heads(): gathered = lax.all_gather(queries, 'pages', axis=0, tiled=True)  10.4 us
    convert_element_type x2, local copies, waits for them, and re-layouts, shards_heads(): cache_local.reshape(pages_here * page_len, local_width).astype(jnp.float32)  4.28 us
    reduce_sum x4, other arithmetic, rms_rows(): jnp.mean(values_in * values_in, axis=-1, keepdims=True) + EPSILON  4.16 us
  transfers between devices with their start and end apart: 4, of which 4 were waited for; matrix products, arithmetic and copies ran while one was open for 16% of the time, Pallas kernels for 0%

profile of v1, /device:TPU:2, one launch (start us, length us, event | category | flops | bytes accessed | tf_op | source)
XLA Modules:
  0.0 204.7 jit_solution(12084083910439738020)
XLA Ops:
  6.6 0.9 reduce_window_sum.11
  7.4 0.8 sub.37
  8.2 0.8 select_reduce_fusion.2
  9.0 1.3 fusion.9
  10.3 2.8 %fusion.16 = bf16[3,256,320]{1,2,0:T(8,128)(2,1)S(1)} fusion(bf16[3,1280,320]{1,2,0:T(8,128)(2,1)} %param.14, bf16[256,1280]{1,0:T(8,128)(2,1)} %param.13, f32[256]{0:T(256)S(1)} %add_rsqrt_fusion.5), kind=kOutput, calls=%fused_computation.29 | convolution fusion | flops 630374400 | bytes 3605504 | tf_op jit(solution)/shard_map/sd,jdc->jsc/dot_general | solution.py:255
  13.2 0.7 fusion.46
  13.9 0.2 multiply_cosine_fusion
  14.1 0.7 multiply_subtract_fusion
  14.9 0.8 fusion.33
  15.7 0.8 dynamic_slice.33
  16.4 1.7 fusion.30
  18.2 0.0 reduce-scatter.6.cloned.1.call-start
  18.3 0.1 mul.315
  18.3 0.1 fusion.44
  18.4 2.4 %constant_dynamic-slice_fusion = (bf16[4,128,320]{2,1,0:T(8,128)(2,1)}, bf16[4,128,320]{2,1,0:T(8,128)(2,1)}) fusion(bf16[4,128,1280]{2,1,0:T(8,128)(2,1)} %param.21, s32[]{:T(128)S(6)} %select_n.65, bf16[4,128,1280]{2,1,0:T(8,128)(2,1)} %param.22), kind=kLoop, calls=%fused_computation.90 | loop fusion | bytes 1310724 | tf_op jit(solution)/shard_map/dynamic_slice | solution.py:295
  20.9 1.9 copy.39
  22.8 2.1 %copy.35 = f32[4,128,320]{1,0,2:T(4,128)} copy(bf16[4,128,320]{1,2,0:T(8,128)(2,1)} %copy.39) | data formatting | bytes 983040 | tf_op jit(solution)/shard_map/convert_element_type | solution.py:297
  24.9 2.2 %reshape.336 = f32[512,5,64]{0,2,1:T(8,128)} reshape(f32[4,128,320]{1,0,2:T(4,128)} %copy.35) | data formatting | bytes 1310720 | tf_op jit(solution)/shard_map/convert_element_type | solution.py:297
  27.1 1.9 copy.33
  29.0 1.9 reshape_reshape.3
  30.9 0.2 select_reduce_fusion.3
  31.0 1.2 multiply_reduce_fusion.2
  32.2 0.1 broadcast_bitcast_fusion
  32.3 1.6 broadcast_compare_fusion
  33.9 10.4 %all-gather.2.cloned.1.call-done = bf16[2048,320]{0,1:T(8,128)(2,1)} async-done(((bf16[256,320]{0,1:T(8,128)(2,1)}), bf16[2048,320]{0,1:T(8,128)(2,1)}) %all-gather.2.cloned.1.call-update) | async-done | bytes 1310736 | tf_op jit(solution)/shard_map/all_gather | solution.py:265
  44.3 11.8 %fusion = (f32[2048,5]{0,1:T(8,128)}, f32[5,512,2048]{2,1,0:T(8,128)}) fusion(pred[2048,512]{0,1:T(8,128)(4,1)} %broadcast_compare_fusion, bf16[2048,5,64]{0,2,1:T(8,128)(2,1)} %bitcast.93, f32[512,5,64]{0,2,1:T(8,128)} %reshape.336, f32[5,64]{1,0:T(8,128)S(1)} %mul.315, f32[512,5]{0,1:T(8,128)S(1)} %add_rsqrt_fusion), kind=kOutput, calls=%fused_computation.1 | convolution fusion | flops 687298560 | bytes 24038656 | tf_op jit(solution)/shard_map/qhd,khd->qhk/dot_general | solution.py:310
  56.1 0.0 reduce-scatter.4.cloned.1.call-start
  56.2 12.5 %fusion.2 = f32[5,64,2048]{2,1,0:T(8,128)} fusion(bf16[512,5,64]{0,2,1:T(8,128)(2,1)} %reshape_reshape.3, f32[5,512,2048]{2,1,0:T(8,128)} %get-tuple-element.24, pred[2048,512]{0,1:T(8,128)(4,1)} %broadcast_compare_fusion), kind=kOutput, calls=%fused_computation.3 | convolution fusion | flops 686817280 | bytes 24969216 | tf_op jit(solution)/shard_map/qhk,khd->qhd/dot_general | solution.py:316
  68.7 0.0 reduce-scatter.8.cloned.1.call-start
  68.7 1.0 multiply_reduce_fusion.5
  69.8 0.2 and_and_fusion
  70.0 2.4 %fusion.47 = (f32[5,256]{1,0:T(8,128)S(1)}, bf16[5,256,256]{1,2,0:T(8,128)(2,1)}) fusion(f32[256,5,32]{0,2,1:T(8,128)} %get-tuple-element.16, f32[256,5,32]{0,2,1:T(8,128)S(1)} %get-tuple-element.15, f32[256,5]{0,1:T(8,128)S(1)} %add_rsqrt_fusion.1, f32[5,64]{1,0:T(8,128)S(1)} %mul.315, f32[256,5,64]{0,2,1:T(8,128)} %fusion.33, ...), kind=kOutput, calls=%fused_computation.115 | convolution fusion | flops 43744000 | bytes 1387776 | tf_op jit(solution)/shard_map/qhd,khd->hqk/dot_general | solution.py:267
  72.4 17.0 %reduce-scatter.6.cloned.1.call-done = f32[256,5]{0,1:T(8,128)} async-done(((f32[2048,5]{0,1:T(8,128)}), f32[256,5]{0,1:T(8,128)}) %reduce-scatter.6.cloned.1.call-update) | async-done | bytes 5136 | tf_op jit(solution)/shard_map/reduce_scatter | solution.py:322
  89.4 0.7 fusion.37
  90.1 46.7 %reduce-scatter.4.cloned.1.call-done = f32[256,320]{0,1:T(8,128)} async-done(((f32[2048,320]{0,1:T(8,128)}), f32[256,320]{0,1:T(8,128)}) %reduce-scatter.4.cloned.1.call-update) | async-done | bytes 327696 | tf_op jit(solution)/shard_map/reduce_scatter | solution.py:322
  136.8 1.6 fusion.19
  138.4 18.1 %all_gather.7 = bf16[256,1280]{0,1:T(8,128)(2,1)S(1)} all-gather(bf16[256,320]{0,1:T(8,128)(2,1)S(1)} %bitcast.87), channel_id=1, replica_groups=mesh['pages'=8,'mp'=4] {'mp'}, dimensions={1}, use_global_device_ids=true | all-gather | bytes 819200 | tf_op jit(solution)/shard_map/all_gather | solution.py:333
  156.5 1.1 multiply_reduce_fusion.1
  157.7 0.5 multiply_reduce_fusion
  158.2 0.4 multiply_convert_fusion
  158.6 1.9 convolution_bitcast_fusion
  160.5 0.3 copy-done.5
  160.8 2.3 %fusion.20 = f32[256,1280]{1,0:T(8,128)} fusion(bf16[1280,1280]{1,0:T(8,128)(2,1)S(1)} %copy-done.5, f32[2,256,1280]{2,1,0:T(8,128)S(1)} %convolution_bitcast_fusion, f32[1280]{0:T(1024)S(1)} %get-tuple-element.8, f32[1280]{0:T(1024)S(1)} %get-tuple-element.7), kind=kOutput, calls=%fused_computation.34 | convolution fusion | flops 841482240 | bytes 7219200 | tf_op jit(solution)/shard_map/dot_general | solution.py:346
  163.1 0.1 fusion.39
  163.2 30.6 %reduce-scatter.8.cloned.1.call-done = f32[64,1280]{1,0:T(8,128)} async-done(((f32[256,1280]{1,0:T(8,128)}), f32[64,1280]{1,0:T(8,128)}) %reduce-scatter.8.cloned.1.call-update) | async-done | bytes 327696 | tf_op jit(solution)/shard_map/reduce_scatter | solution.py:345
  193.8 1.1 multiply_reduce_fusion.4
  194.9 1.3 multiply_reduce_fusion.3
  196.3 1.9 multiply_convert_fusion.3
  (45 shorter events, 0.4 us)
Async XLA Ops:
  6.5 150.0 %copy-start = (bf16[1280,1280]{1,0:T(8,128)(2,1)S(1)}, bf16[1280,1280]{1,0:T(8,128)(2,1)}, u32[]{:S(2)}) copy-start(bf16[1280,1280]{1,0:T(8,128)(2,1)} %param.15) | copy-start | bytes 9830404
  6.5 37.8 %all-gather.2.cloned.1.call-start = ((), (), s32[]{:S(2)}) async-start(), calls=%async_computation.3 | async-start | bytes 1474560 | tf_op jit(solution)/shard_map/all_gather | solution.py:265
  18.2 71.2 %reduce-scatter.6.cloned.1.call-start = ((), (), s32[]{:S(2)}) async-start(), calls=%async_computation.5 | async-start | bytes 73728 | tf_op jit(solution)/shard_map/reduce_scatter | solution.py:322
  24.9 6.0 %copy-start.6 = (s32[32]{0:T(128)S(1)}, s32[32]{0:T(128)}, u32[]{:S(2)}) copy-start(s32[32]{0:T(128)} %param.23) | copy-start | bytes 388
  56.1 80.7 %reduce-scatter.4.cloned.1.call-start = ((), (), s32[]{:S(2)}) async-start(), calls=%async_computation.4 | async-start | bytes 2949120 | tf_op jit(solution)/shard_map/reduce_scatter | solution.py:322
  68.6 1.1 copy-start.3
  68.6 1.1 copy-start.4
  68.7 125.2 %reduce-scatter.8.cloned.1.call-start = ((), (), s32[]{:S(2)}) async-start(), calls=%async_computation.6 | async-start | bytes 1638400 | tf_op jit(solution)/shard_map/reduce_scatter | solution.py:345
  136.8 21.8 %slice-start = ((s8[6553600]{0:T(1024)(128)(4,1)}), s8[4194304]{0:T(1024)(128)(4,1)S(1)}, s32[]{:S(2)}) async-start(s8[6553600]{0:T(1024)(128)(4,1)} %bitcast.82), calls=%async_computation.7 | async-start | bytes 8388608
  156.5 1.1 copy-start.1
  156.5 2.1 %slice-start.1 = ((s8[6553600]{0:T(1024)(128)(4,1)}), s8[2359296]{0:T(1024)(128)(4,1)S(1)}, s32[]{:S(2)}) async-start(s8[6553600]{0:T(1024)(128)(4,1)} %bitcast.82), calls=%async_computation.8 | async-start | bytes 4718592
  158.6 1.9 copy-start.2
  158.6 2.2 %copy-start.5 = (bf16[1280,1280]{1,0:T(8,128)(2,1)S(1)}, bf16[1280,1280]{1,0:T(8,128)(2,1)}, u32[]{:S(2)}) copy-start(bf16[1280,1280]{1,0:T(8,128)(2,1)} %param.17) | copy-start | bytes 9830404
Sparse Core Ops, SparseCore 0:
  18.3 25.9 all-gather.1
  56.2 33.1 reduce-scatter.5
  93.1 43.6 reduce-scatter.3
  163.2 30.5 reduce-scatter.7

commit v2 on v1

--- a/solution.py
+++ b/solution.py
@@ -319,12 +319,14 @@
         value_heads,
         preferred_element_type=jnp.float32,
     )
-    prefix_sum, prefix_total = lax.psum_scatter(
-        (summed.reshape(row_count, local_width), weight_sum),
+    prefix_both = lax.psum_scatter(
+        jnp.concatenate([summed.reshape(row_count, local_width), weight_sum], axis=1),
         "pages",
         scatter_dimension=0,
         tiled=True,
     )
+    prefix_sum = prefix_both[:, :local_width]
+    prefix_total = prefix_both[:, local_width:]
     denominator = suffix_total.T + prefix_total + (1.0 - live_shard.astype(jnp.float32))[:, None]
     mixed = (suffix_sum + prefix_sum.reshape(slot_count, local_heads, head_dim)) / denominator[
         :, :, None

time: 207 us -> 183 us (0.88)
  waiting for transfers between devices: 105 us -> 81.3 us
  matrix products: 36.4 us -> 32.3 us
  other arithmetic: 17.5 us -> 20.4 us
    reduce_scatter x2 -> x1, waiting for transfers between devices: 63.7 us -> 40.3 us  [shards_heads(): lax.psum_scatter(jnp.concatenate([summed.reshape(row_count, local_width),...]
    dot_general x1, matrix products: 12.5 us -> 8.89 us  [shards_heads(): jnp.einsum('qhk,khd->qhd', prefix_weights.astype(jnp.bfloat16), value_hea...]
  transfers between devices with their start and end apart: 4 -> 3, of which waited for: 4 -> 3; matrix products, arithmetic and copies ran while one was open for 16% -> 11% of each run, Pallas kernels for 0% -> 0%
where the time goes in v2:
time: 183 us; the launch traced here: 181 us
  waiting for transfers between devices  81.3 us (44%)
  matrix products  32.3 us (18%)
  other arithmetic  20.4 us (11%)
  blocking collectives  18.1 us (10%)
  local copies, waits for them, and re-layouts  15.5 us (8%)
  between operations  13.4 us (7%)
    reduce_scatter x1, waiting for transfers between devices, shards_heads(): lax.psum_scatter(jnp.concatenate([summed.reshape(row_count, local_width),...  40.3 us
    reduce_scatter x1, waiting for transfers between devices, shards_heads(): lax.psum_scatter(jnp.dot(hidden, w_down, preferred_element_type=jnp.float...  30.7 us
    all_gather x1, blocking collectives, shards_heads(): attention = lax.all_gather(attention_local, 'mp', axis=1, tiled=True)  18.1 us
    dot_general x1, matrix products, shards_heads(): jnp.einsum('qhd,khd->qhk', query_heads, key_heads, preferred_element_type...  11.3 us
    all_gather x1, waiting for transfers between devices, shards_heads(): gathered = lax.all_gather(queries, 'pages', axis=0, tiled=True)  10.3 us
    dot_general x1, matrix products, shards_heads(): jnp.einsum('qhk,khd->qhd', prefix_weights.astype(jnp.bfloat16), value_hea...  8.89 us
    convert_element_type x2, local copies, waits for them, and re-layouts, shards_heads(): cache_local.reshape(pages_here * page_len, local_width).astype(jnp.float32)  4.29 us
    reduce_sum x4, other arithmetic, rms_rows(): jnp.mean(values_in * values_in, axis=-1, keepdims=True) + EPSILON  4.16 us
  transfers between devices with their start and end apart: 3, of which 3 were waited for; matrix products, arithmetic and copies ran while one was open for 11% of the time, Pallas kernels for 0%

profile of v2, /device:TPU:2, one launch (start us, length us, event | category | flops | bytes accessed | tf_op | source)
XLA Modules:
  0.0 181.0 jit_solution(1924879757704601773)
XLA Ops:
  6.5 0.9 reduce_window_sum.11
  7.4 0.8 sub.37
  8.2 1.3 fusion.9
  9.5 2.8 %fusion.16 = bf16[3,256,320]{1,2,0:T(8,128)(2,1)S(1)} fusion(bf16[3,1280,320]{1,2,0:T(8,128)(2,1)} %param.14, bf16[256,1280]{1,0:T(8,128)(2,1)} %param.13, f32[256]{0:T(256)S(1)} %add_rsqrt_fusion.5), kind=kOutput, calls=%fused_computation.30 | convolution fusion | flops 630374400 | bytes 3605504 | tf_op jit(solution)/shard_map/sd,jdc->jsc/dot_general | solution.py:255
  12.4 0.7 fusion.46
  13.1 0.7 convert.5
  13.8 0.1 select_reduce_fusion.2
  14.0 0.2 multiply_cosine_fusion
  14.2 1.7 multiply_subtract_fusion
  15.9 0.8 fusion.33
  16.7 0.8 dynamic_slice.33
  17.5 1.7 fusion.30
  19.2 0.0 reduce-scatter.3.cloned.1.call-start
  19.3 0.1 mul.315
  19.4 0.1 fusion.44
  19.5 2.5 %constant_dynamic-slice_fusion = (bf16[4,128,320]{2,1,0:T(8,128)(2,1)}, bf16[4,128,320]{2,1,0:T(8,128)(2,1)}) fusion(bf16[4,128,1280]{2,1,0:T(8,128)(2,1)} %param.21, s32[]{:T(128)S(6)} %select_n.65, bf16[4,128,1280]{2,1,0:T(8,128)(2,1)} %param.22), kind=kLoop, calls=%fused_computation.91 | loop fusion | bytes 1310724 | tf_op jit(solution)/shard_map/dynamic_slice | solution.py:295
  21.9 1.9 %copy.39 = bf16[4,128,320]{1,2,0:T(8,128)(2,1)} copy(bf16[4,128,320]{2,1,0:T(8,128)(2,1)} %get-tuple-element.31) | data formatting | bytes 655360
  23.8 2.1 %copy.35 = f32[4,128,320]{1,0,2:T(4,128)} copy(bf16[4,128,320]{1,2,0:T(8,128)(2,1)} %copy.39) | data formatting | bytes 983040 | tf_op jit(solution)/shard_map/convert_element_type | solution.py:297
  25.9 2.2 %reshape.336 = f32[512,5,64]{0,2,1:T(8,128)} reshape(f32[4,128,320]{1,0,2:T(4,128)} %copy.35) | data formatting | bytes 1310720 | tf_op jit(solution)/shard_map/convert_element_type | solution.py:297
  28.1 2.0 %copy.33 = bf16[4,128,320]{1,0,2:T(4,128)(2,1)} copy(bf16[4,128,320]{2,1,0:T(8,128)(2,1)} %get-tuple-element.32) | data formatting | bytes 655360 | tf_op jit(solution)/shard_map/dynamic_slice | solution.py:301
  30.1 1.8 %reshape_reshape.3 = bf16[512,5,64]{0,2,1:T(8,128)(2,1)} reshape(bf16[4,128,320]{1,0,2:T(4,128)(2,1)} %copy.33) | data formatting | bytes 655360 | tf_op jit(solution)/shard_map/reshape;reshape | solution.py:308
  31.9 0.2 select_reduce_fusion.3
  32.1 1.2 multiply_reduce_fusion.2
  33.3 0.1 broadcast_bitcast_fusion
  33.4 1.7 broadcast_compare_fusion
  35.0 10.3 %all-gather.2.cloned.1.call-done = bf16[2048,320]{0,1:T(8,128)(2,1)} async-done(((bf16[256,320]{0,1:T(8,128)(2,1)}), bf16[2048,320]{0,1:T(8,128)(2,1)}) %all-gather.2.cloned.1.call-update) | async-done | bytes 1310736 | tf_op jit(solution)/shard_map/all_gather | solution.py:265
  45.3 11.3 %fusion = (f32[2048,5]{0,1:T(8,128)S(1)}, f32[5,512,2048]{2,1,0:T(8,128)}) fusion(pred[2048,512]{0,1:T(8,128)(4,1)} %broadcast_compare_fusion, bf16[2048,5,64]{0,2,1:T(8,128)(2,1)} %bitcast.92, f32[512,5,64]{0,2,1:T(8,128)} %reshape.336, f32[5,64]{1,0:T(8,128)S(1)} %mul.315, f32[512,5]{0,1:T(8,128)S(1)} %add_rsqrt_fusion), kind=kOutput, calls=%fused_computation.1 | convolution fusion | flops 687298560 | bytes 24038656 | tf_op jit(solution)/shard_map/qhd,khd->qhk/dot_general | solution.py:310
  56.6 8.9 %fusion.2 = f32[5,64,2048]{2,1,0:T(8,128)S(1)} fusion(bf16[512,5,64]{0,2,1:T(8,128)(2,1)S(1)} %copy-done.4, f32[5,512,2048]{2,1,0:T(8,128)} %get-tuple-element.24, pred[2048,512]{0,1:T(8,128)(4,1)S(1)} %copy-done.3), kind=kOutput, calls=%fused_computation.3 | convolution fusion | flops 686817280 | bytes 24969216 | tf_op jit(solution)/shard_map/qhk,khd->qhd/dot_general | solution.py:316
  65.5 1.8 %pad_maximum_fusion = f32[2048,325]{0,1:T(8,128)} fusion(f32[2048,5]{0,1:T(8,128)S(1)} %get-tuple-element.23, f32[2048,320]{0,1:T(8,128)S(1)} %bitcast.82), kind=kLoop, calls=%fused_computation.8 | loop fusion | flops 665600 | bytes 5324800 | tf_op jit(solution)/shard_map/concatenate | solution.py:323
  67.4 1.0 multiply_reduce_fusion.5
  68.5 0.2 and_and_fusion
  68.7 2.5 %fusion.47 = (f32[5,256]{1,0:T(8,128)S(1)}, bf16[5,256,256]{1,2,0:T(8,128)(2,1)}) fusion(f32[256,5,32]{0,2,1:T(8,128)} %get-tuple-element.16, f32[256,5,32]{0,2,1:T(8,128)S(1)} %get-tuple-element.15, f32[256,5]{0,1:T(8,128)S(1)} %add_rsqrt_fusion.1, f32[5,64]{1,0:T(8,128)S(1)} %mul.315, f32[256,5,64]{0,2,1:T(8,128)} %fusion.33, ...), kind=kOutput, calls=%fused_computation.116 | convolution fusion | flops 43744000 | bytes 1387776 | tf_op jit(solution)/shard_map/qhd,khd->hqk/dot_general | solution.py:267
  71.1 40.3 %reduce-scatter.3.cloned.1.call-done = f32[256,325]{0,1:T(8,128)} async-done(((f32[2048,325]{0,1:T(8,128)}), f32[256,325]{0,1:T(8,128)}) %reduce-scatter.3.cloned.1.call-update) | async-done | bytes 332816 | tf_op jit(solution)/shard_map/reduce_scatter | solution.py:322
  111.5 1.0 slice.67
  112.5 0.7 fusion.37
  113.2 1.6 fusion.19
  114.7 18.1 %all_gather.7 = bf16[256,1280]{0,1:T(8,128)(2,1)S(1)} all-gather(bf16[256,320]{0,1:T(8,128)(2,1)S(1)} %bitcast.86), channel_id=1, replica_groups=mesh['pages'=8,'mp'=4] {'mp'}, dimensions={1}, use_global_device_ids=true | all-gather | bytes 819200 | tf_op jit(solution)/shard_map/all_gather | solution.py:335
  132.8 1.1 multiply_reduce_fusion.1
  134.0 0.5 multiply_reduce_fusion
  134.5 0.4 multiply_convert_fusion
  134.9 1.9 %convolution_bitcast_fusion = f32[2,256,1280]{2,1,0:T(8,128)S(1)} fusion(bf16[2,1280,1280]{2,1,0:T(8,128)(2,1)S(1)} %bitcast.81, bf16[256,1280]{1,0:T(8,128)(2,1)S(1)} %multiply_convert_fusion), kind=kOutput, calls=%fused_computation.7 | convolution fusion | flops 1677721600 | bytes 9830400 | tf_op jit(solution)/shard_map/sd,jdf->jsf/dot_general | solution.py:342
  136.8 0.3 copy-done.8
  137.1 2.3 %fusion.20 = f32[256,1280]{1,0:T(8,128)} fusion(bf16[1280,1280]{1,0:T(8,128)(2,1)S(1)} %copy-done.8, f32[2,256,1280]{2,1,0:T(8,128)S(1)} %convolution_bitcast_fusion, f32[1280]{0:T(1024)S(1)} %get-tuple-element.8, f32[1280]{0:T(1024)S(1)} %get-tuple-element.7), kind=kOutput, calls=%fused_computation.35 | convolution fusion | flops 841482240 | bytes 7219200 | tf_op jit(solution)/shard_map/dot_general | solution.py:348
  139.4 0.1 fusion.39
  139.5 30.7 %reduce-scatter.5.cloned.1.call-done = f32[64,1280]{1,0:T(8,128)} async-done(((f32[256,1280]{1,0:T(8,128)}), f32[64,1280]{1,0:T(8,128)}) %reduce-scatter.5.cloned.1.call-update) | async-done | bytes 327696 | tf_op jit(solution)/shard_map/reduce_scatter | solution.py:347
  170.2 1.1 multiply_reduce_fusion.4
  171.3 1.3 multiply_reduce_fusion.3
  172.6 1.9 %multiply_convert_fusion.3 = bf16[64,1280]{1,0:T(8,128)(2,1)} fusion(f32[64,1280]{1,0:T(8,128)} %reduce-scatter.5.cloned.1.call-done, f32[64]{0:T(128)S(1)} %add_rsqrt_fusion.6, f32[64]{0:T(128)S(1)} %add_rsqrt_fusion.7, f32[1280]{0:T(1024)S(1)} %get-tuple-element.5, f32[64]{0:T(128)S(1)} %fusion.39, bf16[256,1280]{1,0:T(8,128)(2,1)} %copy-done.2, ...), kind=kLoop, calls=%fused_computation.52 | loop fusion | flops 655360 | bytes 661252 | tf_op jit(solution)/shard_map/convert_element_type | solution.py:355
  (50 shorter events, 0.4 us)
Async XLA Ops:
  6.5 126.3 %copy-start = (bf16[1280,1280]{1,0:T(8,128)(2,1)S(1)}, bf16[1280,1280]{1,0:T(8,128)(2,1)}, u32[]{:S(2)}) copy-start(bf16[1280,1280]{1,0:T(8,128)(2,1)} %param.15) | copy-start | bytes 9830404
  6.5 38.8 %all-gather.2.cloned.1.call-start = ((), (), s32[]{:S(2)}) async-start(), calls=%async_computation.2 | async-start | bytes 1474560 | tf_op jit(solution)/shard_map/all_gather | solution.py:265
  12.4 1.4 copy-start.7
  19.2 92.2 %reduce-scatter.3.cloned.1.call-start = ((), (), s32[]{:S(2)}) async-start(), calls=%async_computation.3 | async-start | bytes 3022848 | tf_op jit(solution)/shard_map/reduce_scatter | solution.py:322
  25.9 6.0 %copy-start.9 = (s32[32]{0:T(128)S(1)}, s32[32]{0:T(128)}, u32[]{:S(2)}) copy-start(s32[32]{0:T(128)} %param.23) | copy-start | bytes 388
  45.3 11.3 %copy-start.3 = (pred[2048,512]{0,1:T(8,128)(4,1)S(1)}, pred[2048,512]{0,1:T(8,128)(4,1)}, u32[]{:S(2)}) copy-start(pred[2048,512]{0,1:T(8,128)(4,1)} %broadcast_compare_fusion) | copy-start | bytes 3145732
  45.3 11.3 %copy-start.4 = (bf16[512,5,64]{0,2,1:T(8,128)(2,1)S(1)}, bf16[512,5,64]{0,2,1:T(8,128)(2,1)}, u32[]{:S(2)}) copy-start(bf16[512,5,64]{0,2,1:T(8,128)(2,1)} %reshape_reshape.3) | copy-start | bytes 983044
  67.3 1.1 copy-start.5
  67.3 1.1 copy-start.6
  67.3 102.8 %reduce-scatter.5.cloned.1.call-start = ((), (), s32[]{:S(2)}) async-start(), calls=%async_computation.4 | async-start | bytes 1638400 | tf_op jit(solution)/shard_map/reduce_scatter | solution.py:347
  113.2 21.7 %slice-start = ((s8[6553600]{0:T(1024)(128)(4,1)}), s8[4194304]{0:T(1024)(128)(4,1)S(1)}, s32[]{:S(2)}) async-start(s8[6553600]{0:T(1024)(128)(4,1)} %bitcast.80), calls=%async_computation.5 | async-start | bytes 8388608
  132.8 1.1 copy-start.1
  132.8 2.1 %slice-start.1 = ((s8[6553600]{0:T(1024)(128)(4,1)}), s8[2359296]{0:T(1024)(128)(4,1)S(1)}, s32[]{:S(2)}) async-start(s8[6553600]{0:T(1024)(128)(4,1)} %bitcast.80), calls=%async_computation.6 | async-start | bytes 4718592
  134.9 1.9 %copy-start.2 = (bf16[256,1280]{1,0:T(8,128)(2,1)}, bf16[256,1280]{1,0:T(8,128)(2,1)S(1)}, u32[]{:S(2)}) copy-start(bf16[256,1280]{1,0:T(8,128)(2,1)S(1)} %multiply_convert_fusion) | copy-start | bytes 1966084
  134.9 2.2 %copy-start.8 = (bf16[1280,1280]{1,0:T(8,128)(2,1)S(1)}, bf16[1280,1280]{1,0:T(8,128)(2,1)}, u32[]{:S(2)}) copy-start(bf16[1280,1280]{1,0:T(8,128)(2,1)} %param.17) | copy-start | bytes 9830404
Sparse Core Ops, SparseCore 0:
  19.3 25.9 all-gather.1
  67.5 43.9 reduce-scatter.2
  139.5 30.5 reduce-scatter.4

commit v3 on v2

--- a/solution.py
+++ b/solution.py
@@ -320,11 +320,13 @@
         preferred_element_type=jnp.float32,
     )
     prefix_both = lax.psum_scatter(
-        jnp.concatenate([summed.reshape(row_count, local_width), weight_sum], axis=1),
+        jnp.concatenate([summed.reshape(row_count, local_width), weight_sum], axis=1).astype(
+            jnp.bfloat16
+        ),
         "pages",
         scatter_dimension=0,
         tiled=True,
-    )
+    ).astype(jnp.float32)
     prefix_sum = prefix_both[:, :local_width]
     prefix_total = prefix_both[:, local_width:]
     denominator = suffix_total.T + prefix_total + (1.0 - live_shard.astype(jnp.float32))[:, None]
@@ -345,11 +347,11 @@
         * (scale_gate_up[1][None, :] * gate_up[1])
     ).astype(jnp.bfloat16)
     feed_sum = lax.psum_scatter(
-        jnp.dot(hidden, w_down, preferred_element_type=jnp.float32),
+        jnp.dot(hidden, w_down, preferred_element_type=jnp.float32).astype(jnp.bfloat16),
         "mp",
         scatter_dimension=0,
         tiled=True,
-    )
+    ).astype(jnp.float32)
     middle = state_own.astype(jnp.float32)
     result = rms_rows(middle + eigen_rates[1][None, :] * (rms_rows(feed_sum) - middle))
     return (live_own.astype(jnp.float32)[:, None] * result).astype(jnp.bfloat16)

time: 183 us -> 166 us (0.907)
  waiting for transfers between devices: 81.3 us -> 65.5 us
    reduce_scatter x1, waiting for transfers between devices: 30.7 us -> 21.6 us  [shards_heads(): lax.psum_scatter(jnp.dot(hidden, w_down, preferred_element_type=jnp.float...]
    reduce_scatter x1, waiting for transfers between devices: 40.3 us -> 33.6 us  [shards_heads(): lax.psum_scatter(jnp.concatenate([summed.reshape(row_count, local_width),...]
  transfers between devices with their start and end apart: 3 -> 3, of which waited for: 3 -> 3; matrix products, arithmetic and copies ran while one was open for 11% -> 12% of each run, Pallas kernels for 0% -> 0%
where the time goes in v3:
time: 166 us; the launch traced here: 164 us
  waiting for transfers between devices  65.5 us (39%)
  matrix products  32.3 us (19%)
  other arithmetic  18.8 us (11%)
  blocking collectives  18.1 us (11%)
  local copies, waits for them, and re-layouts  15.4 us (9%)
  between operations  13.4 us (8%)
    reduce_scatter x1, waiting for transfers between devices, shards_heads(): lax.psum_scatter(jnp.concatenate([summed.reshape(row_count, local_width),...  33.6 us
    reduce_scatter x1, waiting for transfers between devices, shards_heads(): lax.psum_scatter(jnp.dot(hidden, w_down, preferred_element_type=jnp.float...  21.6 us
    all_gather x1, blocking collectives, shards_heads(): attention = lax.all_gather(attention_local, 'mp', axis=1, tiled=True)  18.1 us
    dot_general x1, matrix products, shards_heads(): jnp.einsum('qhd,khd->qhk', query_heads, key_heads, preferred_element_type...  11.3 us
    all_gather x1, waiting for transfers between devices, shards_heads(): gathered = lax.all_gather(queries, 'pages', axis=0, tiled=True)  10.3 us
    dot_general x1, matrix products, shards_heads(): jnp.einsum('qhk,khd->qhd', prefix_weights.astype(jnp.bfloat16), value_hea...  9.11 us
    convert_element_type x2, local copies, waits for them, and re-layouts, shards_heads(): cache_local.reshape(pages_here * page_len, local_width).astype(jnp.float32)  4.29 us
    reduce_sum x4, other arithmetic, rms_rows(): jnp.mean(values_in * values_in, axis=-1, keepdims=True) + EPSILON  4.26 us
  transfers between devices with their start and end apart: 3, of which 3 were waited for; matrix products, arithmetic and copies ran while one was open for 12% of the time, Pallas kernels for 0%

profile of v3, /device:TPU:2, one launch (start us, length us, event | category | flops | bytes accessed | tf_op | source)
XLA Modules:
  0.0 163.7 jit_solution(5608173497659891775)
XLA Ops:
  6.6 1.4 fusion.12
  8.0 0.7 reduce_window_sum.11
  8.7 0.7 sub.37
  9.4 0.8 select_reduce_fusion.2
  10.2 2.8 %fusion.19 = bf16[3,256,320]{1,2,0:T(8,128)(2,1)S(1)} fusion(bf16[3,1280,320]{1,2,0:T(8,128)(2,1)} %param.14, bf16[256,1280]{1,0:T(8,128)(2,1)} %param.13, f32[256]{0:T(256)S(1)} %add_rsqrt_fusion.5), kind=kOutput, calls=%fused_computation.32 | convolution fusion | flops 630374400 | bytes 3605504 | tf_op jit(solution)/shard_map/sd,jdc->jsc/dot_general | solution.py:255
  13.0 0.7 fusion.49
  13.8 0.2 multiply_cosine_fusion
  14.0 0.7 multiply_subtract_fusion
  14.8 0.8 fusion.36
  15.5 0.8 dynamic_slice.33
  16.3 1.7 %fusion.33 = bf16[256,320]{0,1:T(8,128)(2,1)} fusion(f32[256,5,64]{0,2,1:T(8,128)} %fusion.36, f32[320]{0:T(512)S(1)} %dynamic_slice.33), kind=kLoop, calls=%fused_computation.55 | loop fusion | flops 163840 | bytes 492800 | tf_op jit(solution)/shard_map/convert_element_type | solution.py:260
  18.1 0.0 reduce-scatter.3.cloned.1.call-start
  18.1 0.1 mul.315
  18.2 0.1 fusion.47
  18.3 2.5 %constant_dynamic-slice_fusion = (bf16[4,128,320]{2,1,0:T(8,128)(2,1)}, bf16[4,128,320]{2,1,0:T(8,128)(2,1)}) fusion(bf16[4,128,1280]{2,1,0:T(8,128)(2,1)} %param.21, s32[]{:T(128)S(6)} %select_n.65, bf16[4,128,1280]{2,1,0:T(8,128)(2,1)} %param.22), kind=kLoop, calls=%fused_computation.94 | loop fusion | bytes 1310724 | tf_op jit(solution)/shard_map/dynamic_slice | solution.py:295
  20.8 1.9 %copy.39 = bf16[4,128,320]{1,2,0:T(8,128)(2,1)} copy(bf16[4,128,320]{2,1,0:T(8,128)(2,1)} %get-tuple-element.31) | data formatting | bytes 655360
  22.7 2.1 %copy.35 = f32[4,128,320]{1,0,2:T(4,128)} copy(bf16[4,128,320]{1,2,0:T(8,128)(2,1)} %copy.39) | data formatting | bytes 983040 | tf_op jit(solution)/shard_map/convert_element_type | solution.py:297
  24.8 2.2 %reshape.337 = f32[512,5,64]{0,2,1:T(8,128)} reshape(f32[4,128,320]{1,0,2:T(4,128)} %copy.35) | data formatting | bytes 1310720 | tf_op jit(solution)/shard_map/convert_element_type | solution.py:297
  27.0 2.0 %copy.33 = bf16[4,128,320]{1,0,2:T(4,128)(2,1)} copy(bf16[4,128,320]{2,1,0:T(8,128)(2,1)} %get-tuple-element.32) | data formatting | bytes 655360 | tf_op jit(solution)/shard_map/dynamic_slice | solution.py:301
  28.9 1.8 %reshape_reshape.3 = bf16[512,5,64]{0,2,1:T(8,128)(2,1)} reshape(bf16[4,128,320]{1,0,2:T(4,128)(2,1)} %copy.33) | data formatting | bytes 655360 | tf_op jit(solution)/shard_map/reshape;reshape | solution.py:308
  30.8 0.2 select_reduce_fusion.3
  30.9 1.2 multiply_reduce_fusion.2
  32.1 0.1 broadcast_bitcast_fusion
  32.2 1.7 %broadcast_compare_fusion = pred[2048,512]{0,1:T(8,128)(4,1)} fusion(s32[2048]{0:T(1024)S(1)} %bitcast.90, s32[512]{0:T(512)S(1)} %broadcast_bitcast_fusion), kind=kLoop, calls=%fused_computation.10 | loop fusion | flops 1048576 | bytes 1058816 | tf_op jit(solution)/shard_map/eq | solution.py:313
  33.9 10.3 %all-gather.2.cloned.1.call-done = bf16[2048,320]{0,1:T(8,128)(2,1)} async-done(((bf16[256,320]{0,1:T(8,128)(2,1)}), bf16[2048,320]{0,1:T(8,128)(2,1)}) %all-gather.2.cloned.1.call-update) | async-done | bytes 1310736 | tf_op jit(solution)/shard_map/all_gather | solution.py:265
  44.2 11.3 %fusion = (bf16[2048,5]{0,1:T(8,128)(2,1)S(1)}, f32[5,512,2048]{2,1,0:T(8,128)}) fusion(pred[2048,512]{0,1:T(8,128)(4,1)} %broadcast_compare_fusion, bf16[2048,5,64]{0,2,1:T(8,128)(2,1)} %bitcast.94, f32[512,5,64]{0,2,1:T(8,128)} %reshape.337, f32[5,64]{1,0:T(8,128)S(1)} %mul.315, f32[512,5]{0,1:T(8,128)S(1)} %add_rsqrt_fusion), kind=kOutput, calls=%fused_computation.1 | convolution fusion | flops 687298560 | bytes 24018176 | tf_op jit(solution)/shard_map/qhd,khd->qhk/dot_general | solution.py:310
  55.5 9.1 %fusion.7 = bf16[5,64,2048]{2,1,0:T(8,128)(2,1)S(1)} fusion(bf16[512,5,64]{0,2,1:T(8,128)(2,1)S(1)} %copy-done.4, f32[5,512,2048]{2,1,0:T(8,128)} %get-tuple-element.24, pred[2048,512]{0,1:T(8,128)(4,1)S(1)} %copy-done.3), kind=kOutput, calls=%fused_computation.8 | convolution fusion | flops 687472640 | bytes 23658496 | tf_op jit(solution)/shard_map/qhk,khd->qhd/dot_general | solution.py:316
  64.6 1.2 pad_maximum_fusion
  65.8 0.0 reduce-scatter.5.cloned.1.call-start
  65.9 1.0 multiply_reduce_fusion.4
  66.9 0.2 and_and_fusion
  67.1 2.5 %fusion.50 = (f32[5,256]{1,0:T(8,128)S(1)}, bf16[5,256,256]{1,2,0:T(8,128)(2,1)}) fusion(f32[256,5,32]{0,2,1:T(8,128)} %get-tuple-element.16, f32[256,5,32]{0,2,1:T(8,128)S(1)} %get-tuple-element.15, f32[256,5]{0,1:T(8,128)S(1)} %add_rsqrt_fusion.1, f32[5,64]{1,0:T(8,128)S(1)} %mul.315, f32[256,5,64]{0,2,1:T(8,128)} %fusion.36, ...), kind=kOutput, calls=%fused_computation.119 | convolution fusion | flops 43744000 | bytes 1387776 | tf_op jit(solution)/shard_map/qhd,khd->hqk/dot_general | solution.py:267
  69.6 33.6 %reduce-scatter.3.cloned.1.call-done = bf16[256,325]{0,1:T(8,128)(2,1)} async-done(((bf16[2048,325]{0,1:T(8,128)(2,1)}), bf16[256,325]{0,1:T(8,128)(2,1)}) %reduce-scatter.3.cloned.1.call-update) | async-done | bytes 166416 | tf_op jit(solution)/shard_map/reduce_scatter | solution.py:322
  103.2 0.9 convert_element_type.140
  104.1 0.9 slice.67
  105.1 1.6 fusion.22
  106.7 18.1 %all_gather.7 = bf16[256,1280]{0,1:T(8,128)(2,1)S(1)} all-gather(bf16[256,320]{0,1:T(8,128)(2,1)S(1)} %bitcast.88), channel_id=1, replica_groups=mesh['pages'=8,'mp'=4] {'mp'}, dimensions={1}, use_global_device_ids=true | all-gather | bytes 819200 | tf_op jit(solution)/shard_map/all_gather | solution.py:337
  124.8 1.1 multiply_reduce_fusion.1
  125.9 0.5 multiply_reduce_fusion
  126.4 0.4 multiply_convert_fusion
  126.9 1.9 %convolution_bitcast_fusion = f32[2,256,1280]{2,1,0:T(8,128)S(1)} fusion(bf16[2,1280,1280]{2,1,0:T(8,128)(2,1)S(1)} %bitcast.83, bf16[256,1280]{1,0:T(8,128)(2,1)S(1)} %multiply_convert_fusion), kind=kOutput, calls=%fused_computation.7 | convolution fusion | flops 1677721600 | bytes 9830400 | tf_op jit(solution)/shard_map/sd,jdf->jsf/dot_general | solution.py:344
  128.8 0.3 copy-done.7
  129.0 2.1 %convolution_convert_fusion = bf16[256,1280]{1,0:T(8,128)(2,1)} fusion(bf16[1280,1280]{1,0:T(8,128)(2,1)S(1)} %copy-done.7, f32[2,256,1280]{2,1,0:T(8,128)S(1)} %convolution_bitcast_fusion, f32[1280]{0:T(1024)S(1)} %get-tuple-element.8, f32[1280]{0:T(1024)S(1)} %get-tuple-element.7), kind=kOutput, calls=%fused_computation.9 | convolution fusion | flops 841809920 | bytes 6563840 | tf_op jit(solution)/shard_map/dot_general | solution.py:350
  131.2 0.1 fusion.42
  131.2 21.6 %reduce-scatter.5.cloned.1.call-done = bf16[64,1280]{1,0:T(8,128)(2,1)} async-done(((bf16[256,1280]{1,0:T(8,128)(2,1)}), bf16[64,1280]{1,0:T(8,128)(2,1)}) %reduce-scatter.5.cloned.1.call-update) | async-done | bytes 163856 | tf_op jit(solution)/shard_map/reduce_scatter | solution.py:349
  152.8 1.0 fusion.31
  153.9 1.3 multiply_reduce_fusion.3
  155.2 1.9 %multiply_convert_fusion.3 = bf16[64,1280]{1,0:T(8,128)(2,1)} fusion(bf16[64,1280]{1,0:T(8,128)(2,1)} %reduce-scatter.5.cloned.1.call-done, f32[64]{0:T(128)S(1)} %add_rsqrt_fusion.6, f32[64]{0:T(128)S(1)} %add_rsqrt_fusion.7, f32[1280]{0:T(1024)S(1)} %get-tuple-element.5, f32[64]{0:T(128)S(1)} %fusion.42, bf16[256,1280]{1,0:T(8,128)(2,1)} %copy-done.2, ...), kind=kLoop, calls=%fused_computation.56 | loop fusion | flops 737280 | bytes 497412 | tf_op jit(solution)/shard_map/convert_element_type | solution.py:357
  (49 shorter events, 0.4 us)
Async XLA Ops:
  6.5 118.2 %copy-start = (bf16[1280,1280]{1,0:T(8,128)(2,1)S(1)}, bf16[1280,1280]{1,0:T(8,128)(2,1)}, u32[]{:S(2)}) copy-start(bf16[1280,1280]{1,0:T(8,128)(2,1)} %param.15) | copy-start | bytes 9830404
  6.5 37.6 %all-gather.2.cloned.1.call-start = ((), (), s32[]{:S(2)}) async-start(), calls=%async_computation.2 | async-start | bytes 1474560 | tf_op jit(solution)/shard_map/all_gather | solution.py:265
  18.1 85.1 %reduce-scatter.3.cloned.1.call-start = ((), (), s32[]{:S(2)}) async-start(), calls=%async_computation.3 | async-start | bytes 1511424 | tf_op jit(solution)/shard_map/reduce_scatter | solution.py:322
  24.8 6.0 %copy-start.8 = (s32[32]{0:T(128)S(1)}, s32[32]{0:T(128)}, u32[]{:S(2)}) copy-start(s32[32]{0:T(128)} %param.23) | copy-start | bytes 388
  44.2 11.3 %copy-start.3 = (pred[2048,512]{0,1:T(8,128)(4,1)S(1)}, pred[2048,512]{0,1:T(8,128)(4,1)}, u32[]{:S(2)}) copy-start(pred[2048,512]{0,1:T(8,128)(4,1)} %broadcast_compare_fusion) | copy-start | bytes 3145732
  44.2 11.3 %copy-start.4 = (bf16[512,5,64]{0,2,1:T(8,128)(2,1)S(1)}, bf16[512,5,64]{0,2,1:T(8,128)(2,1)}, u32[]{:S(2)}) copy-start(bf16[512,5,64]{0,2,1:T(8,128)(2,1)} %reshape_reshape.3) | copy-start | bytes 983044
  65.8 1.1 copy-start.5
  65.8 1.1 copy-start.6
  65.8 87.1 %reduce-scatter.5.cloned.1.call-start = ((), (), s32[]{:S(2)}) async-start(), calls=%async_computation.4 | async-start | bytes 819200 | tf_op jit(solution)/shard_map/reduce_scatter | solution.py:349
  105.1 21.8 %slice-start = ((s8[6553600]{0:T(1024)(128)(4,1)}), s8[4194304]{0:T(1024)(128)(4,1)S(1)}, s32[]{:S(2)}) async-start(s8[6553600]{0:T(1024)(128)(4,1)} %bitcast.82), calls=%async_computation.5 | async-start | bytes 8388608
  124.8 1.2 copy-start.1
  124.8 2.1 %slice-start.1 = ((s8[6553600]{0:T(1024)(128)(4,1)}), s8[2359296]{0:T(1024)(128)(4,1)S(1)}, s32[]{:S(2)}) async-start(s8[6553600]{0:T(1024)(128)(4,1)} %bitcast.82), calls=%async_computation.6 | async-start | bytes 4718592
  126.9 1.9 %copy-start.2 = (bf16[256,1280]{1,0:T(8,128)(2,1)}, bf16[256,1280]{1,0:T(8,128)(2,1)S(1)}, u32[]{:S(2)}) copy-start(bf16[256,1280]{1,0:T(8,128)(2,1)S(1)} %multiply_convert_fusion) | copy-start | bytes 1966084
  126.9 2.2 %copy-start.7 = (bf16[1280,1280]{1,0:T(8,128)(2,1)S(1)}, bf16[1280,1280]{1,0:T(8,128)(2,1)}, u32[]{:S(2)}) copy-start(bf16[1280,1280]{1,0:T(8,128)(2,1)} %param.17) | copy-start | bytes 9830404
Sparse Core Ops, SparseCore 0:
  18.2 25.9 all-gather.1
  65.9 37.2 reduce-scatter.2
  131.3 21.5 reduce-scatter.4

commit v4 on v3

--- a/solution.py
+++ b/solution.py
@@ -1,8 +1,10 @@
+import functools
 import math
 
 import jax
 import jax.numpy as jnp
 from jax import lax
+from jax.experimental import pallas as pl
 from jax.sharding import PartitionSpec as P
 
 HEADS = 20
@@ -83,6 +85,68 @@
         preferred_element_type=jnp.float32,
     )
     return (summed.reshape(row_count, model_width), weight_sum)
+
+
+def prefix_kernel(q_ref, k_ref, v_ref, rg_ref, kg_ref, num_ref, den_ref, *, heads, head_dim, scale):
+    queries = q_ref[...]
+    keys = k_ref[...]
+    values = v_ref[...]
+    row_count, width = queries.shape
+    allowed = rg_ref[...] == kg_ref[...]
+    column = lax.broadcasted_iota(jnp.int32, (1, width), 1)
+    lane = lax.broadcasted_iota(jnp.int32, (1, den_ref.shape[1]), 1)
+    numerator = jnp.zeros((row_count, width), jnp.float32)
+    denominator = jnp.zeros((row_count, den_ref.shape[1]), jnp.float32)
+    for head in range(heads):
+        in_head = (column >= head * head_dim) & (column < (head + 1) * head_dim)
+        head_keys = jnp.where(in_head, keys, jnp.zeros_like(keys))
+        scores = (
+            lax.dot_general(
+                queries,
+                head_keys,
+                (((1,), (1,)), ((), ())),
+                preferred_element_type=jnp.float32,
+            )
+            * scale
+        )
+        weights = jnp.where(allowed, jnp.exp(scores), 0.0)
+        denominator = jnp.where(lane == head, jnp.sum(weights, axis=1, keepdims=True), denominator)
+        summed = jnp.dot(weights.astype(jnp.bfloat16), values, preferred_element_type=jnp.float32)
+        numerator = jnp.where(in_head, summed, numerator)
+    num_ref[...] = numerator.astype(num_ref.dtype)
+    den_ref[...] = denominator.astype(den_ref.dtype)
+
+
+def prefix_attention(queries, keys, values, row_group, key_group, heads, head_dim, scale):
+    row_count, width = queries.shape
+    key_count = keys.shape[0]
+    block = math.gcd(row_count, 256)
+    den_width = 128
+    flops = 4 * row_count * key_count * width * heads
+    return pl.pallas_call(
+        functools.partial(prefix_kernel, heads=heads, head_dim=head_dim, scale=scale),
+        grid=(row_count // block,),
+        in_specs=[
+            pl.BlockSpec((block, width), lambda i: (i, 0)),
+            pl.BlockSpec((key_count, width), lambda i: (0, 0)),
+            pl.BlockSpec((key_count, width), lambda i: (0, 0)),
+            pl.BlockSpec((block, 1), lambda i: (i, 0)),
+            pl.BlockSpec((1, key_count), lambda i: (0, 0)),
+        ],
+        out_specs=[
+            pl.BlockSpec((block, width), lambda i: (i, 0)),
+            pl.BlockSpec((block, den_width), lambda i: (i, 0)),
+        ],
+        out_shape=[
+            jax.ShapeDtypeStruct((row_count, width), jnp.bfloat16),
+            jax.ShapeDtypeStruct((row_count, den_width), jnp.bfloat16),
+        ],
+        cost_estimate=pl.CostEstimate(
+            flops=flops,
+            transcendentals=row_count * key_count * heads,
+            bytes_accessed=2 * (row_count * width * 2 + 2 * key_count * width + row_count * den_width),
+        ),
+    )(queries, keys, values, row_group.reshape(row_count, 1), key_group.reshape(1, key_count))
 
 
 def shards_columns(
@@ -303,26 +367,18 @@
     ).reshape(pages_here * page_len, local_width)
     gathered_group = group_id.reshape(-1)
     row_count = gathered.shape[0]
-    query_heads = gathered.reshape(row_count, local_heads, head_dim)
-    key_heads = prefix_keys.reshape(-1, local_heads, head_dim)
-    value_heads = prefix_values.reshape(-1, local_heads, head_dim)
-    prefix_scores = (
-        jnp.einsum("qhd,khd->qhk", query_heads, key_heads, preferred_element_type=jnp.float32)
-        * score_scale
-    )
-    prefix_allowed = gathered_group[:, None] == key_group[None, :]
-    prefix_weights = jnp.where(prefix_allowed[:, None, :], jnp.exp(prefix_scores), 0.0)
-    weight_sum = jnp.sum(prefix_weights, axis=-1)
-    summed = jnp.einsum(
-        "qhk,khd->qhd",
-        prefix_weights.astype(jnp.bfloat16),
-        value_heads,
-        preferred_element_type=jnp.float32,
+    prefix_num, prefix_den = prefix_attention(
+        gathered,
+        prefix_keys,
+        prefix_values,
+        gathered_group,
+        key_group,
+        local_heads,
+        head_dim,
+        score_scale,
     )
     prefix_both = lax.psum_scatter(
-        jnp.concatenate([summed.reshape(row_count, local_width), weight_sum], axis=1).astype(
-            jnp.bfloat16
-        ),
+        jnp.concatenate([prefix_num, prefix_den[:, :local_heads]], axis=1),
         "pages",
         scatter_dimension=0,
         tiled=True,

time: 166 us -> 176 us (1.060)
  matrix products: 32.3 us -> 12 us
  Pallas kernels: 0 us -> 19.4 us
  other arithmetic: 18.8 us -> 26.2 us
  local copies, waits for them, and re-layouts: 15.4 us -> 17.8 us
    dot_general x2 -> x0, matrix products: 20.4 us -> none  [the longest x1 11.3 us: shards_heads(): jnp.einsum('qhd,khd->qhk', query_heads, key_heads, preferred_element_type...]
    pallas_call x0 -> x1, Pallas kernels: none -> 19.4 us  [prefix_attention(): pl.pallas_call(functools.partial(prefix_kernel, heads=heads, head_dim=hea...]
    mul x0 -> x5, local copies, waits for them, and re-layouts: none -> 9.47 us  [the longest x3 5.05 us: head_norm(): per_head * lax.rsqrt(jnp.mean(per_head * per_head, axis=-1, keepdims=True...]
    dynamic_slice x2 -> x0, local copies, waits for them, and re-layouts: 4.41 us -> none  [the longest x1 2.46 us: shards_heads(): lax.dynamic_slice_in_dim(cache_keys, mp_index * local_width, local_width, 2)]
    convert_element_type x2 -> x0, local copies, waits for them, and re-layouts: 4.29 us -> none  [shards_heads(): cache_local.reshape(pages_here * page_len, local_width).astype(jnp.float32)]
    convert_element_type x1 -> x3, other arithmetic: 0.94 us -> 4.21 us  [the longest x1 2.34 us: shards_heads(): cache_local.reshape(pages_here * page_len, local_width).astype(jnp.float32)]
    mul x0 -> x1, other arithmetic: none -> 2.14 us  [head_norm(): per_head * per_head]
    concatenate x1, other arithmetic: 1.17 us -> 3.05 us  [shards_heads(): jnp.concatenate([prefix_num, prefix_den[:, :local_heads]], axis=1)]
where the time goes in v4:
time: 176 us; the launch traced here: 174 us
  waiting for transfers between devices  66.9 us (38%)
  other arithmetic  26.2 us (15%)
  Pallas kernels  19.4 us (11%)
  blocking collectives  17.9 us (10%)
  local copies, waits for them, and re-layouts  17.8 us (10%)
  between operations  13.4 us (8%)
  matrix products  12 us (7%)
    reduce_scatter x1, waiting for transfers between devices, shards_heads(): lax.psum_scatter(jnp.concatenate([prefix_num, prefix_den[:, :local_heads]...  33.9 us
    reduce_scatter x1, waiting for transfers between devices, shards_heads(): lax.psum_scatter(jnp.dot(hidden, w_down, preferred_element_type=jnp.float...  21.6 us
    pallas_call x1, Pallas kernels, prefix_attention(): pl.pallas_call(functools.partial(prefix_kernel, heads=heads, head_dim=hea...  19.4 us
    all_gather x1, blocking collectives, shards_heads(): attention = lax.all_gather(attention_local, 'mp', axis=1, tiled=True)  17.9 us
    all_gather x1, waiting for transfers between devices, shards_heads(): gathered = lax.all_gather(queries, 'pages', axis=0, tiled=True)  11.3 us
    mul x3, local copies, waits for them, and re-layouts, head_norm(): per_head * lax.rsqrt(jnp.mean(per_head * per_head, axis=-1, keepdims=True...  5.05 us
    mul x2, local copies, waits for them, and re-layouts, head_norm(): per_head * per_head  4.42 us
    reduce_sum x4, other arithmetic, rms_rows(): jnp.mean(values_in * values_in, axis=-1, keepdims=True) + EPSILON  4.11 us
  transfers between devices with their start and end apart: 3, of which 3 were waited for; matrix products, arithmetic and copies ran while one was open for 12% of the time, Pallas kernels for 0%

profile of v4, /device:TPU:2, one launch (start us, length us, event | category | flops | bytes accessed | tf_op | source)
XLA Modules:
  0.0 173.6 jit_solution(10649476942592748762)
XLA Ops:
  6.6 0.9 reduce_window_sum.11
  7.4 0.8 sub.37
  8.2 0.8 select_reduce_fusion.2
  9.0 1.3 fusion.2
  10.3 2.8 %fusion.9 = bf16[3,256,320]{1,2,0:T(8,128)(2,1)S(1)} fusion(bf16[3,1280,320]{1,2,0:T(8,128)(2,1)} %param.14, bf16[256,1280]{1,0:T(8,128)(2,1)} %param.13, f32[256]{0:T(256)S(1)} %add_rsqrt_fusion.5), kind=kOutput, calls=%fused_computation.23 | convolution fusion | flops 630374400 | bytes 3605504 | tf_op jit(solution)/shard_map/sd,jdc->jsc/dot_general | solution.py:319
  13.2 0.7 fusion.36
  13.9 0.2 multiply_cosine_fusion
  14.1 0.7 multiply_subtract_fusion
  14.9 0.8 fusion.24
  15.7 1.9 %copy.51 = f32[256,320]{1,0:T(8,128)} copy(f32[256,320]{0,1:T(8,128)} %bitcast.75) | data formatting | bytes 655360 | tf_op jit(solution)/shard_map/mul | solution.py:24
  17.6 0.8 dynamic_slice.33
  18.3 1.7 multiply_convert_fusion.1
  20.1 2.1 %fusion.27 = f32[4,128,320]{2,1,0:T(8,128)} fusion(bf16[4,128,1280]{2,1,0:T(8,128)(2,1)} %param.21, s32[]{:T(128)S(6)} %select_n.64), kind=kLoop, calls=%fused_computation.61 | loop fusion | flops 327680 | bytes 983044 | tf_op jit(solution)/shard_map/mul | solution.py:24
  22.2 2.2 %copy.53 = f32[4,128,320]{1,0,2:T(4,128)} copy(f32[4,128,320]{2,1,0:T(8,128)} %fusion.27) | data formatting | bytes 1310720 | tf_op jit(solution)/shard_map/mul | solution.py:24
  24.5 2.2 %mul.328 = f32[512,5,64]{0,2,1:T(8,128)} reshape(f32[4,128,320]{1,0,2:T(4,128)} %copy.53) | data formatting | bytes 1310720 | tf_op jit(solution)/shard_map/mul | solution.py:24
  26.7 1.1 reduce_sum.122
  27.8 0.9 mul.329
  28.7 2.3 %copy.54 = f32[512,320]{1,0:T(8,128)} copy(f32[512,320]{0,1:T(8,128)} %bitcast.74) | data formatting | bytes 1310720 | tf_op jit(solution)/shard_map/mul | solution.py:24
  31.1 1.4 copy.62
  32.5 0.2 select_reduce_fusion.3
  32.7 2.3 %dynamic-slice_convert_fusion = (f32[4,128,320]{2,1,0:T(8,128)S(1)}, bf16[4,128,320]{2,1,0:T(8,128)(2,1)}) fusion(bf16[4,128,1280]{2,1,0:T(8,128)(2,1)} %param.21, s32[]{:T(128)S(6)} %select_n.64, bf16[4,128,1280]{2,1,0:T(8,128)(2,1)} %param.22), kind=kLoop, calls=%fused_computation.41 | loop fusion | flops 163840 | bytes 1638404 | tf_op jit(solution)/shard_map/convert_element_type | solution.py:361
  35.0 0.8 fusion.14.k_ref
  35.9 11.3 %all-gather.2.cloned.1.call-done.q_ref = bf16[2048,320]{1,0:T(8,128)(2,1)} async-done(((bf16[256,320]{1,0:T(8,128)(2,1)}), bf16[2048,320]{1,0:T(8,128)(2,1)}) %all-gather.2.cloned.1.call-update) | async-done | bytes 1310736 | tf_op jit(solution)/shard_map/all_gather | solution.py:329
  47.2 0.6 broadcast_in_dim.60
  47.9 19.4 %shard_map.127 = (bf16[2048,320]{1,0:T(8,128)(2,1)}, bf16[2048,128]{1,0:T(8,128)(2,1)}) custom-call(bf16[2048,320]{1,0:T(8,128)(2,1)} %all-gather.2.cloned.1.call-done.q_ref, bf16[512,320]{1,0:T(8,128)(2,1)} %fusion.14.k_ref, bf16[512,320]{1,0:T(8,128)(2,1)} %bitcast.80, s32[2048,1]{1,0:T(8,128)} %bitcast.76, s32[1,512]{1,0:T(1,128)} %bitcast.88), custom_call_target="tpu_custom_call" | custom-call | flops 6710886400 | bytes 3801088 | tf_op jit(solution)/shard_map/pallas_call | solution.py:126
  67.3 3.1 %pad_maximum_fusion = bf16[2048,325]{1,0:T(8,128)(2,1)} fusion(bf16[2048,5]{1,0:T(8,128)(2,1)} %bitcast.79, bf16[2048,320]{1,0:T(8,128)(2,1)} %get-tuple-element.7), kind=kLoop, calls=%fused_computation.6 | loop fusion | flops 2662400 | bytes 2662400 | tf_op jit(solution)/shard_map/concatenate | solution.py:381
  70.5 1.0 multiply_reduce_fusion.3
  71.5 0.2 and_and_fusion
  71.7 2.5 %fusion.37 = (f32[5,256]{1,0:T(8,128)S(1)}, bf16[5,256,256]{1,2,0:T(8,128)(2,1)}) fusion(f32[256,5,32]{0,2,1:T(8,128)} %get-tuple-element.20, f32[256,5,32]{0,2,1:T(8,128)S(1)} %get-tuple-element.19, f32[256,5]{0,1:T(8,128)S(1)} %add_rsqrt_fusion.1, f32[5,64]{1,0:T(8,128)S(1)} %mul.311, f32[256,5,64]{0,2,1:T(8,128)} %fusion.24, ...), kind=kOutput, calls=%fused_computation.105 | convolution fusion | flops 43744000 | bytes 1387776 | tf_op jit(solution)/shard_map/qhd,khd->hqk/dot_general | solution.py:331
  74.1 0.8 copy.57
  75.0 33.9 %reduce-scatter.3.cloned.1.call-done = bf16[256,325]{1,0:T(8,128)(2,1)} async-done(((bf16[2048,325]{1,0:T(8,128)(2,1)}), bf16[256,325]{1,0:T(8,128)(2,1)}) %reduce-scatter.3.cloned.1.call-update) | async-done | bytes 166416 | tf_op jit(solution)/shard_map/reduce_scatter | solution.py:380
  108.9 1.0 convert_element_type.137
  109.9 1.7 fusion.28
  111.6 1.0 copy.58
  112.6 0.8 slice.71
  113.4 1.9 %copy.56 = f32[256,320]{0,1:T(8,128)} copy(f32[256,320]{1,0:T(8,128)} %slice.71) | data formatting | bytes 655360 | tf_op jit(solution)/shard_map/slice | solution.py:386
  115.2 1.6 fusion.12
  116.9 17.9 %all_gather.7 = bf16[256,1280]{0,1:T(8,128)(2,1)S(1)} all-gather(bf16[256,320]{0,1:T(8,128)(2,1)S(1)} %bitcast.82), channel_id=1, replica_groups=mesh['pages'=8,'mp'=4] {'mp'}, dimensions={1}, use_global_device_ids=true | all-gather | bytes 819200 | tf_op jit(solution)/shard_map/all_gather | solution.py:393
  134.7 1.1 multiply_reduce_fusion.1
  135.9 0.5 multiply_reduce_fusion
  136.4 0.4 multiply_convert_fusion
  136.8 1.9 %convolution_bitcast_fusion = f32[2,256,1280]{2,1,0:T(8,128)S(1)} fusion(bf16[2,1280,1280]{2,1,0:T(8,128)(2,1)S(1)} %bitcast.73, bf16[256,1280]{1,0:T(8,128)(2,1)S(1)} %multiply_convert_fusion), kind=kOutput, calls=%fused_computation | convolution fusion | flops 1677721600 | bytes 9830400 | tf_op jit(solution)/shard_map/sd,jdf->jsf/dot_general | solution.py:400
  138.7 0.3 copy-done.7
  139.0 2.1 %convolution_convert_fusion = bf16[256,1280]{1,0:T(8,128)(2,1)} fusion(bf16[1280,1280]{1,0:T(8,128)(2,1)S(1)} %copy-done.7, f32[2,256,1280]{2,1,0:T(8,128)S(1)} %convolution_bitcast_fusion, f32[1280]{0:T(1024)S(1)} %get-tuple-element.12, f32[1280]{0:T(1024)S(1)} %get-tuple-element.11), kind=kOutput, calls=%fused_computation.1 | convolution fusion | flops 841809920 | bytes 6563840 | tf_op jit(solution)/shard_map/dot_general | solution.py:406
  141.2 21.6 %reduce-scatter.5.cloned.1.call-done = bf16[64,1280]{1,0:T(8,128)(2,1)} async-done(((bf16[256,1280]{1,0:T(8,128)(2,1)}), bf16[64,1280]{1,0:T(8,128)(2,1)}) %reduce-scatter.5.cloned.1.call-update) | async-done | bytes 163856 | tf_op jit(solution)/shard_map/reduce_scatter | solution.py:405
  162.8 1.0 fusion.23
  163.9 1.3 multiply_reduce_fusion.2
  165.2 1.9 %multiply_convert_fusion.2 = bf16[64,1280]{1,0:T(8,128)(2,1)} fusion(bf16[64,1280]{1,0:T(8,128)(2,1)} %reduce-scatter.5.cloned.1.call-done, f32[64]{0:T(128)S(1)} %add_rsqrt_fusion.6, f32[64]{0:T(128)S(1)} %add_rsqrt_fusion.7, f32[1280]{0:T(1024)S(1)} %get-tuple-element.9, f32[64]{0:T(128)S(1)} %fusion.31, bf16[256,1280]{1,0:T(8,128)(2,1)} %copy-done.2, ...), kind=kLoop, calls=%fused_computation.47 | loop fusion | flops 737280 | bytes 497412 | tf_op jit(solution)/shard_map/convert_element_type | solution.py:413
  (53 shorter events, 0.7 us)
Async XLA Ops:
  6.5 128.2 %copy-start = (bf16[1280,1280]{1,0:T(8,128)(2,1)S(1)}, bf16[1280,1280]{1,0:T(8,128)(2,1)}, u32[]{:S(2)}) copy-start(bf16[1280,1280]{1,0:T(8,128)(2,1)} %param.15) | copy-start | bytes 9830404
  6.5 40.7 %all-gather.2.cloned.1.call-start = ((), (), s32[]{:S(2)}) async-start(), calls=%async_computation.2 | async-start | bytes 1769472 | tf_op jit(solution)/shard_map/all_gather | solution.py:329
  20.1 88.8 %reduce-scatter.3.cloned.1.call-start = ((), (), s32[]{:S(2)}) async-start(), calls=%async_computation.3 | async-start | bytes 1769472 | tf_op jit(solution)/shard_map/reduce_scatter | solution.py:380
  28.7 3.7 %copy-start.8 = (s32[32]{0:T(128)S(1)}, s32[32]{0:T(128)}, u32[]{:S(2)}) copy-start(s32[32]{0:T(128)} %param.23) | copy-start | bytes 388
  32.5 2.5 %copy-start.3 = (f32[512,320]{1,0:T(8,128)S(1)}, f32[512,320]{1,0:T(8,128)}, u32[]{:S(2)}) copy-start(f32[512,320]{1,0:T(8,128)} %copy.54) | copy-start | bytes 1966084
  70.3 92.5 %reduce-scatter.5.cloned.1.call-start = ((), (), s32[]{:S(2)}) async-start(), calls=%async_computation.4 | async-start | bytes 819200 | tf_op jit(solution)/shard_map/reduce_scatter | solution.py:405
  71.4 3.5 %copy-start.5 = (f32[2,1280]{1,0:T(2,128)S(1)}, f32[2,1280]{1,0:T(2,128)}, u32[]{:S(2)}) copy-start(f32[2,1280]{1,0:T(2,128)} %param.20) | copy-start | bytes 30724
  71.5 3.5 %copy-start.6 = (f32[2,1280]{1,0:T(2,128)S(1)}, f32[2,1280]{1,0:T(2,128)}, u32[]{:S(2)}) copy-start(f32[2,1280]{1,0:T(2,128)} %param.19) | copy-start | bytes 30724
  108.9 3.7 %copy-start.4 = (bf16[256,325]{1,0:T(8,128)(2,1)S(1)}, bf16[256,325]{1,0:T(8,128)(2,1)}, u32[]{:S(2)}) copy-start(bf16[256,325]{1,0:T(8,128)(2,1)} %reduce-scatter.3.cloned.1.call-done) | copy-start | bytes 499204
  115.2 21.6 %slice-start = ((s8[6553600]{0:T(1024)(128)(4,1)}), s8[4194304]{0:T(1024)(128)(4,1)S(1)}, s32[]{:S(2)}) async-start(s8[6553600]{0:T(1024)(128)(4,1)} %bitcast.72), calls=%async_computation.5 | async-start | bytes 8388608
  134.7 1.1 copy-start.1
  134.7 2.1 %slice-start.1 = ((s8[6553600]{0:T(1024)(128)(4,1)}), s8[2359296]{0:T(1024)(128)(4,1)S(1)}, s32[]{:S(2)}) async-start(s8[6553600]{0:T(1024)(128)(4,1)} %bitcast.72), calls=%async_computation.6 | async-start | bytes 4718592
  136.8 1.9 %copy-start.2 = (bf16[256,1280]{1,0:T(8,128)(2,1)}, bf16[256,1280]{1,0:T(8,128)(2,1)S(1)}, u32[]{:S(2)}) copy-start(bf16[256,1280]{1,0:T(8,128)(2,1)S(1)} %multiply_convert_fusion) | copy-start | bytes 1966084
  136.8 2.2 %copy-start.7 = (bf16[1280,1280]{1,0:T(8,128)(2,1)S(1)}, bf16[1280,1280]{1,0:T(8,128)(2,1)}, u32[]{:S(2)}) copy-start(bf16[1280,1280]{1,0:T(8,128)(2,1)} %param.17) | copy-start | bytes 9830404
Sparse Core Ops, SparseCore 0:
  20.2 26.9 all-gather.1
  70.5 38.3 reduce-scatter.2
  141.2 21.5 reduce-scatter.4

commit v5 on v3

--- a/solution.py
+++ b/solution.py
@@ -262,7 +262,6 @@
         rotate(projected[1].astype(jnp.float32), position_shard, local_heads), scale_local, local_heads
     ).astype(jnp.bfloat16)
     value_rows = projected[2]
-    gathered = lax.all_gather(queries, "pages", axis=0, tiled=True)
     scores = (
         jnp.einsum(
             "qhd,khd->hqk",
@@ -301,32 +300,48 @@
     prefix_values = lax.dynamic_slice_in_dim(
         cache_values, mp_index * local_width, local_width, 2
     ).reshape(pages_here * page_len, local_width)
-    gathered_group = group_id.reshape(-1)
-    row_count = gathered.shape[0]
-    query_heads = gathered.reshape(row_count, local_heads, head_dim)
     key_heads = prefix_keys.reshape(-1, local_heads, head_dim)
     value_heads = prefix_values.reshape(-1, local_heads, head_dim)
-    prefix_scores = (
-        jnp.einsum("qhd,khd->qhk", query_heads, key_heads, preferred_element_type=jnp.float32)
-        * score_scale
-    )
-    prefix_allowed = gathered_group[:, None] == key_group[None, :]
-    prefix_weights = jnp.where(prefix_allowed[:, None, :], jnp.exp(prefix_scores), 0.0)
-    weight_sum = jnp.sum(prefix_weights, axis=-1)
-    summed = jnp.einsum(
-        "qhk,khd->qhd",
-        prefix_weights.astype(jnp.bfloat16),
-        value_heads,
-        preferred_element_type=jnp.float32,
-    )
-    prefix_both = lax.psum_scatter(
-        jnp.concatenate([summed.reshape(row_count, local_width), weight_sum], axis=1).astype(
-            jnp.bfloat16
-        ),
-        "pages",
-        scatter_dimension=0,
-        tiled=True,
-    ).astype(jnp.float32)
+    chunk_count = 2 if slot_count % 16 == 0 else 1
+    chunk_rows = slot_count // chunk_count
+    pages_count = lax.axis_size("pages")
+    gathered_all = lax.all_gather(queries, "pages", axis=0, tiled=True).reshape(
+        pages_count, slot_count, local_width
+    )
+    pieces = []
+    for chunk in range(chunk_count):
+        gathered = lax.slice_in_dim(
+            gathered_all, chunk * chunk_rows, (chunk + 1) * chunk_rows, axis=1
+        ).reshape(pages_count * chunk_rows, local_width)
+        gathered_group = lax.slice_in_dim(
+            group_id, chunk * chunk_rows, (chunk + 1) * chunk_rows, axis=1
+        ).reshape(-1)
+        row_count = gathered.shape[0]
+        query_heads = gathered.reshape(row_count, local_heads, head_dim)
+        prefix_scores = (
+            jnp.einsum("qhd,khd->qhk", query_heads, key_heads, preferred_element_type=jnp.float32)
+            * score_scale
+        )
+        prefix_allowed = gathered_group[:, None] == key_group[None, :]
+        prefix_weights = jnp.where(prefix_allowed[:, None, :], jnp.exp(prefix_scores), 0.0)
+        weight_sum = jnp.sum(prefix_weights, axis=-1)
+        summed = jnp.einsum(
+            "qhk,khd->qhd",
+            prefix_weights.astype(jnp.bfloat16),
+            value_heads,
+            preferred_element_type=jnp.float32,
+        )
+        pieces.append(
+            lax.psum_scatter(
+                jnp.concatenate([summed.reshape(row_count, local_width), weight_sum], axis=1).astype(
+                    jnp.bfloat16
+                ),
+                "pages",
+                scatter_dimension=0,
+                tiled=True,
+            )
+        )
+    prefix_both = jnp.concatenate(pieces, axis=0).astype(jnp.float32)
     prefix_sum = prefix_both[:, :local_width]
     prefix_total = prefix_both[:, local_width:]
     denominator = suffix_total.T + prefix_total + (1.0 - live_shard.astype(jnp.float32))[:, None]

time: 166 us -> 196 us (1.18)
  waiting for transfers between devices: 65.5 us -> 90.9 us
  local copies, waits for them, and re-layouts: 15.4 us -> 29.1 us
  matrix products: 32.3 us -> 23.7 us
    unnamed x3 -> x6, waiting for transfers between devices: 0.05 us -> 59.6 us
    reduce_scatter x1 -> x0, waiting for transfers between devices: 33.6 us -> none  [shards_heads(): lax.psum_scatter(jnp.concatenate([summed.reshape(row_count, local_width),...]
    unnamed x24 -> x36, local copies, waits for them, and re-layouts: 2.23 us -> 11.6 us
    dot_general x1 -> x2, matrix products: 9.11 us -> 4.12 us  [shards_heads(): jnp.einsum('qhk,khd->qhd', prefix_weights.astype(jnp.bfloat16), value_hea...]
    another operation x0 -> x2, local copies, waits for them, and re-layouts: none -> 4.21 us  [shards_heads(): query_heads = gathered.reshape(row_count, local_heads, head_dim)]
    dot_general x1 -> x2, matrix products: 11.3 us -> 8.99 us  [shards_heads(): jnp.einsum('qhd,khd->qhk', query_heads, key_heads, preferred_element_type...]
  transfers between devices with their start and end apart: 3 -> 4, of which waited for: 3 -> 4; matrix products, arithmetic and copies ran while one was open for 12% -> 16% of each run, Pallas kernels for 0% -> 0%
where the time goes in v5:
time: 196 us; the launch traced here: 194 us
  waiting for transfers between devices  90.9 us (46%)
  local copies, waits for them, and re-layouts  29.1 us (15%)
  matrix products  23.7 us (12%)
  other arithmetic  18.5 us (9%)
  blocking collectives  17.8 us (9%)
  between operations  13.5 us (7%)
    unnamed x6, waiting for transfers between devices  59.6 us
    reduce_scatter x1, waiting for transfers between devices, shards_heads(): lax.psum_scatter(jnp.dot(hidden, w_down, preferred_element_type=jnp.float...  21.9 us
    all_gather x1, blocking collectives, shards_heads(): attention = lax.all_gather(attention_local, 'mp', axis=1, tiled=True)  17.8 us
    unnamed x36, local copies, waits for them, and re-layouts  11.6 us
    all_gather x1, waiting for transfers between devices, shards_heads(): lax.all_gather(queries, 'pages', axis=0, tiled=True)  9.37 us
    dot_general x2, matrix products, shards_heads(): jnp.einsum('qhd,khd->qhk', query_heads, key_heads, preferred_element_type...  8.99 us
    convert_element_type x2, local copies, waits for them, and re-layouts, shards_heads(): cache_local.reshape(pages_here * page_len, local_width).astype(jnp.float32)  4.29 us
    reduce_sum x4, other arithmetic, rms_rows(): jnp.mean(values_in * values_in, axis=-1, keepdims=True) + EPSILON  4.26 us
  transfers between devices with their start and end apart: 4, of which 4 were waited for; matrix products, arithmetic and copies ran while one was open for 16% of the time, Pallas kernels for 0%

profile of v5, /device:TPU:2, one launch (start us, length us, event | category | flops | bytes accessed | tf_op | source)
XLA Modules:
  0.0 193.8 jit_solution(4700650253405030736)
XLA Ops:
  6.6 1.4 fusion.22
  8.0 0.7 reduce_window_sum.11
  8.7 0.7 sub.37
  9.4 0.8 select_reduce_fusion.2
  10.2 2.8 %fusion.29 = bf16[3,256,320]{1,2,0:T(8,128)(2,1)S(1)} fusion(bf16[3,1280,320]{1,2,0:T(8,128)(2,1)} %param.14, bf16[256,1280]{1,0:T(8,128)(2,1)} %param.13, f32[256]{0:T(256)S(1)} %add_rsqrt_fusion.5), kind=kOutput, calls=%fused_computation.38 | convolution fusion | flops 630374400 | bytes 3605504 | tf_op jit(solution)/shard_map/sd,jdc->jsc/dot_general | solution.py:255
  13.0 0.7 fusion.61
  14.0 0.7 multiply_subtract_fusion
  14.8 0.7 fusion.43
  15.5 0.8 dynamic_slice.33
  16.3 1.7 fusion.42
  18.2 2.5 %constant_dynamic-slice_fusion = (bf16[4,128,320]{2,1,0:T(8,128)(2,1)}, bf16[4,128,320]{2,1,0:T(8,128)(2,1)}) fusion(bf16[4,128,1280]{2,1,0:T(8,128)(2,1)} %param.21, s32[]{:T(128)S(6)} %select_n.61, bf16[4,128,1280]{2,1,0:T(8,128)(2,1)} %param.22), kind=kLoop, calls=%fused_computation.106 | loop fusion | bytes 1310724 | tf_op jit(solution)/shard_map/dynamic_slice | solution.py:294
  20.6 1.9 copy.56
  22.5 2.1 %copy.46 = f32[4,128,320]{1,0,2:T(4,128)} copy(bf16[4,128,320]{1,2,0:T(8,128)(2,1)} %copy.56) | data formatting | bytes 983040 | tf_op jit(solution)/shard_map/convert_element_type | solution.py:296
  24.6 2.2 %reshape.362 = f32[512,5,64]{0,2,1:T(8,128)} reshape(f32[4,128,320]{1,0,2:T(4,128)} %copy.46) | data formatting | bytes 1310720 | tf_op jit(solution)/shard_map/convert_element_type | solution.py:296
  26.8 1.9 copy.44
  28.7 1.8 reshape_reshape.9
  30.7 1.0 multiply_reduce_fusion.4
  31.9 1.2 multiply_reduce_fusion.2
  33.1 1.6 broadcast_compare_fusion.1
  34.8 9.4 %all-gather.2.cloned.1.call-done = bf16[2048,320]{0,1:T(8,128)(2,1)} async-done(((bf16[256,320]{0,1:T(8,128)(2,1)}), bf16[2048,320]{0,1:T(8,128)(2,1)}) %all-gather.2.cloned.1.call-update) | async-done | bytes 1310736 | tf_op jit(solution)/shard_map/all_gather | solution.py:308
  44.2 1.7 copy.57
  45.9 1.1 fusion.60
  47.0 2.1 %reshape_reshape.10 = bf16[1024,5,64]{0,2,1:T(8,128)(2,1)} reshape(bf16[8,128,320]{1,0,2:T(8,128)(2,1)} %get-tuple-element.12) | data formatting | bytes 1310720 | tf_op jit(solution)/shard_map/reshape;reshape | solution.py:320
  49.1 2.1 %reshape_reshape.11 = bf16[1024,5,64]{0,2,1:T(8,128)(2,1)} reshape(bf16[8,128,320]{1,0,2:T(8,128)(2,1)} %get-tuple-element.13) | data formatting | bytes 1310720 | tf_op jit(solution)/shard_map/reshape;reshape | solution.py:320
  51.2 4.5 %fusion = (bf16[1024,5]{0,1:T(8,128)(2,1)S(1)}, f32[5,512,1024]{2,1,0:T(8,128)S(1)}) fusion(pred[1024,512]{0,1:T(8,128)(4,1)} %get-tuple-element.25, bf16[1024,5,64]{0,2,1:T(8,128)(2,1)} %reshape_reshape.10, f32[512,5,64]{0,2,1:T(8,128)} %reshape.362, f32[5,64]{1,0:T(8,128)S(1)} %mul.316, f32[512,5]{0,1:T(8,128)S(1)} %add_rsqrt_fusion), kind=kOutput, calls=%fused_computation.2 | convolution fusion | flops 343895040 | bytes 12342528 | tf_op jit(solution)/shard_map/qhd,khd->qhk/dot_general | solution.py:322
  55.8 2.1 %fusion.16 = bf16[5,64,1024]{2,1,0:T(8,128)(2,1)S(1)} fusion(bf16[512,5,64]{0,2,1:T(8,128)(2,1)S(1)} %copy-done.5, f32[5,512,1024]{2,1,0:T(8,128)S(1)} %get-tuple-element.32, pred[1024,512]{0,1:T(8,128)(4,1)S(1)} %copy-done.4), kind=kOutput, calls=%fused_computation.23 | convolution fusion | flops 343736320 | bytes 11993088 | tf_op jit(solution)/shard_map/qhk,khd->qhd/dot_general | solution.py:328
  57.8 0.9 pad_maximum_fusion
  58.7 2.3 %copy.52 = bf16[1024,325]{1,0:T(8,128)(2,1)} copy(bf16[1024,325]{0,1:T(8,128)(2,1)} %pad_maximum_fusion) | data formatting | bytes 1331200
  61.2 4.5 %fusion.2 = (bf16[1024,5]{0,1:T(8,128)(2,1)S(1)}, f32[5,512,1024]{2,1,0:T(8,128)S(1)}) fusion(pred[1024,512]{0,1:T(8,128)(4,1)} %get-tuple-element.26, bf16[1024,5,64]{0,2,1:T(8,128)(2,1)} %reshape_reshape.11, f32[512,5,64]{0,2,1:T(8,128)} %reshape.362, f32[5,64]{1,0:T(8,128)S(1)} %mul.316, f32[512,5]{0,1:T(8,128)S(1)} %add_rsqrt_fusion), kind=kOutput, calls=%fused_computation.4 | convolution fusion | flops 343895040 | bytes 12342528 | tf_op jit(solution)/shard_map/qhd,khd->qhk/dot_general | solution.py:322
  65.8 2.1 %fusion.19 = bf16[5,64,1024]{2,1,0:T(8,128)(2,1)S(1)} fusion(bf16[512,5,64]{0,2,1:T(8,128)(2,1)S(1)} %copy-done.6, f32[5,512,1024]{2,1,0:T(8,128)S(1)} %get-tuple-element.30, pred[1024,512]{0,1:T(8,128)(4,1)S(1)} %copy-done.3), kind=kOutput, calls=%fused_computation.24 | convolution fusion | flops 343736320 | bytes 11993088 | tf_op jit(solution)/shard_map/qhk,khd->qhd/dot_general | solution.py:328
  67.8 0.9 pad_maximum_fusion.1
  68.8 2.3 %copy.54 = bf16[1024,325]{1,0:T(8,128)(2,1)} copy(bf16[1024,325]{0,1:T(8,128)(2,1)} %pad_maximum_fusion.1) | data formatting | bytes 1331200
  71.4 2.5 %fusion.62 = (f32[5,256]{1,0:T(8,128)S(1)}, bf16[5,256,256]{1,2,0:T(8,128)(2,1)}) fusion(f32[256,5,32]{0,2,1:T(8,128)} %get-tuple-element.18, f32[256,5,32]{0,2,1:T(8,128)S(1)} %get-tuple-element.17, f32[256,5]{0,1:T(8,128)S(1)} %add_rsqrt_fusion.1, f32[5,64]{1,0:T(8,128)S(1)} %mul.316, f32[256,5,64]{0,2,1:T(8,128)} %fusion.43, ...), kind=kOutput, calls=%fused_computation.134 | convolution fusion | flops 43744000 | bytes 1387776 | tf_op jit(solution)/shard_map/qhd,khd->hqk/dot_general | solution.py:266
  73.8 22.4 %reduce-scatter.10.cloned.1.call-done = bf16[128,325]{1,0:T(8,128)(2,1)} async-done(((bf16[1024,325]{1,0:T(8,128)(2,1)}), bf16[128,325]{1,0:T(8,128)(2,1)}) %reduce-scatter.10.cloned.1.call-update) | async-done | bytes 83216
  96.2 1.0 copy.53
  97.2 37.2 %reduce-scatter.12.cloned.1.call-done = bf16[128,325]{1,0:T(8,128)(2,1)} async-done(((bf16[1024,325]{1,0:T(8,128)(2,1)}), bf16[128,325]{1,0:T(8,128)(2,1)}) %reduce-scatter.12.cloned.1.call-update) | async-done | bytes 83216
  134.4 1.0 copy.55
  135.5 0.8 copy-done.7
  136.9 17.8 %all_gather.7 = bf16[256,1280]{0,1:T(8,128)(2,1)S(1)} all-gather(bf16[256,320]{0,1:T(8,128)(2,1)S(1)} %bitcast.115), channel_id=1, replica_groups=mesh['pages'=8,'mp'=4] {'mp'}, dimensions={1}, use_global_device_ids=true | all-gather | bytes 819200 | tf_op jit(solution)/shard_map/all_gather | solution.py:352
  154.7 1.1 multiply_reduce_fusion.1
  155.8 0.5 multiply_reduce_fusion
  156.3 0.4 multiply_convert_fusion
  156.8 1.9 convolution_bitcast_fusion
  158.9 2.1 %convolution_convert_fusion = bf16[256,1280]{1,0:T(8,128)(2,1)} fusion(bf16[1280,1280]{1,0:T(8,128)(2,1)S(1)} %copy-done.10, f32[2,256,1280]{2,1,0:T(8,128)S(1)} %convolution_bitcast_fusion, f32[1280]{0:T(1024)S(1)} %get-tuple-element.8, f32[1280]{0:T(1024)S(1)} %get-tuple-element.7), kind=kOutput, calls=%fused_computation.15 | convolution fusion | flops 841809920 | bytes 6563840 | tf_op jit(solution)/shard_map/dot_general | solution.py:365
  161.1 21.9 %reduce-scatter.8.cloned.1.call-done = bf16[64,1280]{1,0:T(8,128)(2,1)} async-done(((bf16[256,1280]{1,0:T(8,128)(2,1)}), bf16[64,1280]{1,0:T(8,128)(2,1)}) %reduce-scatter.8.cloned.1.call-update) | async-done | bytes 163856 | tf_op jit(solution)/shard_map/reduce_scatter | solution.py:364
  183.0 1.0 fusion.41
  184.1 1.3 multiply_reduce_fusion.3
  185.4 1.9 multiply_convert_fusion.2
  (71 shorter events, 2.4 us)
Async XLA Ops:
  6.5 148.1 %copy-start = (bf16[1280,1280]{1,0:T(8,128)(2,1)S(1)}, bf16[1280,1280]{1,0:T(8,128)(2,1)}, u32[]{:S(2)}) copy-start(bf16[1280,1280]{1,0:T(8,128)(2,1)} %param.15) | copy-start | bytes 9830404
  6.5 37.6 %all-gather.2.cloned.1.call-start = ((), (), s32[]{:S(2)}) async-start(), calls=%async_computation.3 | async-start | bytes 1474560 | tf_op jit(solution)/shard_map/all_gather | solution.py:308
  18.1 78.1 %reduce-scatter.10.cloned.1.call-start = ((), (), s32[]{:S(2)}) async-start(), calls=%async_computation.5 | async-start | bytes 884736
  24.6 7.0 %copy-start.8 = (f32[2,1280]{1,0:T(2,128)S(1)}, f32[2,1280]{1,0:T(2,128)}, u32[]{:S(2)}) copy-start(f32[2,1280]{1,0:T(2,128)} %param.19) | copy-start | bytes 30724
  24.6 7.1 %copy-start.11 = (s32[32]{0:T(128)S(1)}, s32[32]{0:T(128)}, u32[]{:S(2)}) copy-start(s32[32]{0:T(128)} %param.23) | copy-start | bytes 388
  51.2 4.5 %copy-start.4 = (pred[1024,512]{0,1:T(8,128)(4,1)S(1)}, pred[1024,512]{0,1:T(8,128)(4,1)}, u32[]{:S(2)}) copy-start(pred[1024,512]{0,1:T(8,128)(4,1)} %get-tuple-element.25) | copy-start | bytes 1572868
  51.2 4.5 %copy-start.5 = (bf16[512,5,64]{0,2,1:T(8,128)(2,1)S(1)}, bf16[512,5,64]{0,2,1:T(8,128)(2,1)}, u32[]{:S(2)}) copy-start(bf16[512,5,64]{0,2,1:T(8,128)(2,1)} %reshape_reshape.9) | copy-start | bytes 983044
  61.0 73.4 %reduce-scatter.12.cloned.1.call-start = ((), (), s32[]{:S(2)}) async-start(), calls=%async_computation.6 | async-start | bytes 884736
  61.2 4.5 %copy-start.3 = (pred[1024,512]{0,1:T(8,128)(4,1)S(1)}, pred[1024,512]{0,1:T(8,128)(4,1)}, u32[]{:S(2)}) copy-start(pred[1024,512]{0,1:T(8,128)(4,1)} %get-tuple-element.26) | copy-start | bytes 1572868
  61.2 4.5 %copy-start.6 = (bf16[512,5,64]{0,2,1:T(8,128)(2,1)S(1)}, bf16[512,5,64]{0,2,1:T(8,128)(2,1)}, u32[]{:S(2)}) copy-start(bf16[512,5,64]{0,2,1:T(8,128)(2,1)} %reshape_reshape.9) | copy-start | bytes 983044
  68.8 2.4 %copy-start.9 = (f32[2,1280]{1,0:T(2,128)S(1)}, f32[2,1280]{1,0:T(2,128)}, u32[]{:S(2)}) copy-start(f32[2,1280]{1,0:T(2,128)} %param.20) | copy-start | bytes 30724
  71.1 112.0 %reduce-scatter.8.cloned.1.call-start = ((), (), s32[]{:S(2)}) async-start(), calls=%async_computation.4 | async-start | bytes 819200 | tf_op jit(solution)/shard_map/reduce_scatter | solution.py:364
  135.4 0.9 copy-start.7
  135.4 1.2 copy-start.12
  136.6 20.1 %slice-start = ((s8[6553600]{0:T(1024)(128)(4,1)}), s8[4194304]{0:T(1024)(128)(4,1)S(1)}, s32[]{:S(2)}) async-start(s8[6553600]{0:T(1024)(128)(4,1)} %bitcast.106), calls=%async_computation.7 | async-start | bytes 8388608
  154.7 1.1 copy-start.1
  154.7 2.1 %slice-start.1 = ((s8[6553600]{0:T(1024)(128)(4,1)}), s8[2359296]{0:T(1024)(128)(4,1)S(1)}, s32[]{:S(2)}) async-start(s8[6553600]{0:T(1024)(128)(4,1)} %bitcast.106), calls=%async_computation.8 | async-start | bytes 4718592
  156.8 1.9 copy-start.2
  156.8 2.2 %copy-start.10 = (bf16[1280,1280]{1,0:T(8,128)(2,1)S(1)}, bf16[1280,1280]{1,0:T(8,128)(2,1)}, u32[]{:S(2)}) copy-start(bf16[1280,1280]{1,0:T(8,128)(2,1)} %param.17) | copy-start | bytes 9830404
Sparse Core Ops, SparseCore 0:
  18.2 25.9 all-gather.1
  61.1 35.0 reduce-scatter.9
  99.3 35.0 reduce-scatter.11
  161.2 21.8 reduce-scatter.7

commit v6 on v3

--- a/solution.py
+++ b/solution.py
@@ -319,14 +319,20 @@
         value_heads,
         preferred_element_type=jnp.float32,
     )
-    prefix_both = lax.psum_scatter(
+    pages_count = lax.axis_size("pages")
+    prefix_parts = lax.all_to_all(
         jnp.concatenate([summed.reshape(row_count, local_width), weight_sum], axis=1).astype(
             jnp.bfloat16
         ),
         "pages",
-        scatter_dimension=0,
+        0,
+        0,
         tiled=True,
-    ).astype(jnp.float32)
+    )
+    prefix_both = jnp.sum(
+        prefix_parts.reshape(pages_count, slot_count, local_width + local_heads).astype(jnp.float32),
+        axis=0,
+    )
     prefix_sum = prefix_both[:, :local_width]
     prefix_total = prefix_both[:, local_width:]
     denominator = suffix_total.T + prefix_total + (1.0 - live_shard.astype(jnp.float32))[:, None]

time: 166 us -> 150 us (0.904)
  waiting for transfers between devices: 65.5 us -> 45.2 us
  starting transfers between devices: 0.09 us -> 4.85 us
    reduce_scatter x1 -> x0, waiting for transfers between devices: 33.6 us -> none  [shards_heads(): lax.psum_scatter(jnp.concatenate([summed.reshape(row_count, local_width),...]
    all_to_all x0 -> x1, waiting for transfers between devices: none -> 13.4 us  [shards_heads(): lax.all_to_all(jnp.concatenate([summed.reshape(row_count, local_width), w...]
    all_to_all x0 -> x1, starting transfers between devices: none -> 4.84 us  [shards_heads(): lax.all_to_all(jnp.concatenate([summed.reshape(row_count, local_width), w...]
  transfers between devices with their start and end apart: 3 -> 3, of which waited for: 3 -> 3; matrix products, arithmetic and copies ran while one was open for 12% -> 13% of each run, Pallas kernels for 0% -> 0%
where the time goes in v6:
time: 150 us; the launch traced here: 148 us
  waiting for transfers between devices  45.2 us (30%)
  matrix products  31 us (21%)
  other arithmetic  19.5 us (13%)
  blocking collectives  18.4 us (12%)
  local copies, waits for them, and re-layouts  15.2 us (10%)
  between operations  13.7 us (9%)
  starting transfers between devices  4.85 us (3%)
    reduce_scatter x1, waiting for transfers between devices, shards_heads(): lax.psum_scatter(jnp.dot(hidden, w_down, preferred_element_type=jnp.float...  21.3 us
    all_gather x1, blocking collectives, shards_heads(): attention = lax.all_gather(attention_local, 'mp', axis=1, tiled=True)  18.4 us
    all_to_all x1, waiting for transfers between devices, shards_heads(): lax.all_to_all(jnp.concatenate([summed.reshape(row_count, local_width), w...  13.4 us
    dot_general x1, matrix products, shards_heads(): jnp.einsum('qhd,khd->qhk', query_heads, key_heads, preferred_element_type...  11.3 us
    all_gather x1, waiting for transfers between devices, shards_heads(): gathered = lax.all_gather(queries, 'pages', axis=0, tiled=True)  10.4 us
    dot_general x1, matrix products, shards_heads(): jnp.einsum('qhk,khd->qhd', prefix_weights.astype(jnp.bfloat16), value_hea...  9.11 us
    all_to_all x1, starting transfers between devices, shards_heads(): lax.all_to_all(jnp.concatenate([summed.reshape(row_count, local_width), w...  4.84 us
    convert_element_type x2, local copies, waits for them, and re-layouts, shards_heads(): cache_local.reshape(pages_here * page_len, local_width).astype(jnp.float32)  4.29 us
  transfers between devices with their start and end apart: 3, of which 3 were waited for; matrix products, arithmetic and copies ran while one was open for 13% of the time, Pallas kernels for 0%

profile of v6, /device:TPU:2, one launch (start us, length us, event | category | flops | bytes accessed | tf_op | source)
XLA Modules:
  0.0 147.8 jit_solution(3674346052247115668)
XLA Ops:
  6.6 1.4 fusion.12
  8.0 0.7 reduce_window_sum.11
  8.7 0.7 sub.37
  9.4 0.8 select_reduce_fusion.2
  10.2 2.8 %fusion.19 = bf16[3,256,320]{1,2,0:T(8,128)(2,1)S(1)} fusion(bf16[3,1280,320]{1,2,0:T(8,128)(2,1)} %param.14, bf16[256,1280]{1,0:T(8,128)(2,1)} %param.13, f32[256]{0:T(256)S(1)} %add_rsqrt_fusion.5), kind=kOutput, calls=%fused_computation.33 | convolution fusion | flops 630374400 | bytes 3605504 | tf_op jit(solution)/shard_map/sd,jdc->jsc/dot_general | solution.py:255
  13.0 0.7 fusion.49
  13.8 0.2 multiply_cosine_fusion
  14.0 0.7 multiply_subtract_fusion
  14.8 0.8 fusion.36
  15.5 0.8 dynamic_slice.33
  16.3 1.7 %fusion.33 = bf16[256,320]{0,1:T(8,128)(2,1)} fusion(f32[256,5,64]{0,2,1:T(8,128)} %fusion.36, f32[320]{0:T(512)S(1)} %dynamic_slice.33), kind=kLoop, calls=%fused_computation.56 | loop fusion | flops 163840 | bytes 492800 | tf_op jit(solution)/shard_map/convert_element_type | solution.py:260
  18.1 0.1 mul.315
  18.2 0.1 fusion.47
  18.3 2.5 %constant_dynamic-slice_fusion = (bf16[4,128,320]{2,1,0:T(8,128)(2,1)}, bf16[4,128,320]{2,1,0:T(8,128)(2,1)}) fusion(bf16[4,128,1280]{2,1,0:T(8,128)(2,1)} %param.21, s32[]{:T(128)S(6)} %select_n.65, bf16[4,128,1280]{2,1,0:T(8,128)(2,1)} %param.22), kind=kLoop, calls=%fused_computation.95 | loop fusion | bytes 1310724 | tf_op jit(solution)/shard_map/dynamic_slice | solution.py:295
  20.7 1.9 %copy.60 = bf16[4,128,320]{1,2,0:T(8,128)(2,1)} copy(bf16[4,128,320]{2,1,0:T(8,128)(2,1)} %get-tuple-element.31) | data formatting | bytes 655360
  22.6 2.1 %copy.54 = f32[4,128,320]{1,0,2:T(4,128)} copy(bf16[4,128,320]{1,2,0:T(8,128)(2,1)} %copy.60) | data formatting | bytes 983040 | tf_op jit(solution)/shard_map/convert_element_type | solution.py:297
  24.7 2.2 %reshape.342 = f32[512,5,64]{0,2,1:T(8,128)} reshape(f32[4,128,320]{1,0,2:T(4,128)} %copy.54) | data formatting | bytes 1310720 | tf_op jit(solution)/shard_map/convert_element_type | solution.py:297
  26.9 2.0 %copy.52 = bf16[4,128,320]{1,0,2:T(4,128)(2,1)} copy(bf16[4,128,320]{2,1,0:T(8,128)(2,1)} %get-tuple-element.32) | data formatting | bytes 655360 | tf_op jit(solution)/shard_map/dynamic_slice | solution.py:301
  28.9 1.8 %reshape_reshape.3 = bf16[512,5,64]{0,2,1:T(8,128)(2,1)} reshape(bf16[4,128,320]{1,0,2:T(4,128)(2,1)} %copy.52) | data formatting | bytes 655360 | tf_op jit(solution)/shard_map/reshape;reshape | solution.py:308
  30.7 0.2 select_reduce_fusion.3
  30.9 1.2 multiply_reduce_fusion.2
  32.1 0.1 broadcast_bitcast_fusion
  32.1 1.7 %broadcast_compare_fusion = pred[2048,512]{0,1:T(8,128)(4,1)} fusion(s32[2048]{0:T(1024)S(1)} %bitcast.96, s32[512]{0:T(512)S(1)} %broadcast_bitcast_fusion), kind=kLoop, calls=%fused_computation.11 | loop fusion | flops 1048576 | bytes 1058816 | tf_op jit(solution)/shard_map/eq | solution.py:313
  33.8 10.4 %all-gather.2.cloned.1.call-done = bf16[2048,320]{0,1:T(8,128)(2,1)} async-done(((bf16[256,320]{0,1:T(8,128)(2,1)}), bf16[2048,320]{0,1:T(8,128)(2,1)}) %all-gather.2.cloned.1.call-update) | async-done | bytes 1310736 | tf_op jit(solution)/shard_map/all_gather | solution.py:265
  44.2 11.3 %fusion = (bf16[2048,5]{0,1:T(8,128)(2,1)S(1)}, f32[5,512,2048]{2,1,0:T(8,128)}) fusion(pred[2048,512]{0,1:T(8,128)(4,1)} %broadcast_compare_fusion, bf16[2048,5,64]{0,2,1:T(8,128)(2,1)} %bitcast.100, f32[512,5,64]{0,2,1:T(8,128)} %reshape.342, f32[5,64]{1,0:T(8,128)S(1)} %mul.315, f32[512,5]{0,1:T(8,128)S(1)} %add_rsqrt_fusion), kind=kOutput, calls=%fused_computation.1 | convolution fusion | flops 687298560 | bytes 24018176 | tf_op jit(solution)/shard_map/qhd,khd->qhk/dot_general | solution.py:310
  55.5 9.1 %fusion.7 = bf16[5,64,2048]{2,1,0:T(8,128)(2,1)S(1)} fusion(bf16[512,5,64]{0,2,1:T(8,128)(2,1)S(1)} %copy-done.4, f32[5,512,2048]{2,1,0:T(8,128)} %get-tuple-element.24, pred[2048,512]{0,1:T(8,128)(4,1)S(1)} %copy-done.3), kind=kOutput, calls=%fused_computation.8 | convolution fusion | flops 687472640 | bytes 23658496 | tf_op jit(solution)/shard_map/qhk,khd->qhd/dot_general | solution.py:316
  64.6 0.4 copy.62
  65.0 0.3 copy.56
  65.3 1.2 pad_maximum_fusion
  66.4 4.8 %all-to-all-start = ((bf16[8,256,325]{1,2,0:T(8,128)(2,1)}), bf16[8,256,325]{1,2,0:T(8,128)(2,1)}, u32[]{:S(2)}, u32[]{:S(2)}) async-start(bf16[8,256,325]{1,2,0:T(8,128)(2,1)} %pad_maximum_fusion), calls=%async_computation | async-start | bytes 2686976 | tf_op jit(solution)/shard_map/all_to_all | solution.py:323
  71.3 1.0 multiply_reduce_fusion.4
  72.4 0.2 and_and_fusion
  72.6 2.5 %fusion.50 = (f32[5,256]{1,0:T(8,128)S(1)}, bf16[5,256,256]{1,2,0:T(8,128)(2,1)}) fusion(f32[256,5,32]{0,2,1:T(8,128)} %get-tuple-element.16, f32[256,5,32]{0,2,1:T(8,128)S(1)} %get-tuple-element.15, f32[256,5]{0,1:T(8,128)S(1)} %add_rsqrt_fusion.1, f32[5,64]{1,0:T(8,128)S(1)} %mul.315, f32[256,5,64]{0,2,1:T(8,128)} %fusion.36, ...), kind=kOutput, calls=%fused_computation.120 | convolution fusion | flops 43744000 | bytes 1387776 | tf_op jit(solution)/shard_map/qhd,khd->hqk/dot_general | solution.py:267
  75.0 13.4 %all-to-all-done = bf16[8,256,325]{1,2,0:T(8,128)(2,1)} async-done(((bf16[8,256,325]{1,2,0:T(8,128)(2,1)}), bf16[8,256,325]{1,2,0:T(8,128)(2,1)}, u32[]{:S(2)}, u32[]{:S(2)}) %all-to-all-start) | async-done | bytes 1331232 | tf_op jit(solution)/shard_map/all_to_all | solution.py:323
  88.5 1.6 %convert_reduce_fusion = f32[256,325]{0,1:T(8,128)S(1)} fusion(bf16[8,256,325]{1,2,0:T(8,128)(2,1)} %all-to-all-done), kind=kLoop, calls=%fused_computation.9 | loop fusion | flops 1248000 | bytes 1664000 | tf_op jit(solution)/shard_map/reduce_sum | solution.py:332
  90.2 0.2 fusion.22
  90.4 18.4 %all_gather.7 = bf16[256,1280]{0,1:T(8,128)(2,1)S(1)} all-gather(bf16[256,320]{0,1:T(8,128)(2,1)S(1)} %bitcast.93), channel_id=1, replica_groups=mesh['pages'=8,'mp'=4] {'mp'}, dimensions={1}, use_global_device_ids=true | all-gather | bytes 819200 | tf_op jit(solution)/shard_map/all_gather | solution.py:343
  108.9 1.1 multiply_reduce_fusion.1
  110.0 0.5 multiply_reduce_fusion
  110.5 0.4 multiply_convert_fusion
  111.0 1.9 %convolution_bitcast_fusion = f32[2,256,1280]{2,1,0:T(8,128)S(1)} fusion(bf16[2,1280,1280]{2,1,0:T(8,128)(2,1)S(1)} %bitcast.87, bf16[256,1280]{1,0:T(8,128)(2,1)S(1)} %multiply_convert_fusion), kind=kOutput, calls=%fused_computation.7 | convolution fusion | flops 1677721600 | bytes 9830400 | tf_op jit(solution)/shard_map/sd,jdf->jsf/dot_general | solution.py:350
  112.9 0.3 copy-done.8
  113.1 2.1 %convolution_convert_fusion = bf16[256,1280]{1,0:T(8,128)(2,1)} fusion(bf16[1280,1280]{1,0:T(8,128)(2,1)S(1)} %copy-done.8, f32[2,256,1280]{2,1,0:T(8,128)S(1)} %convolution_bitcast_fusion, f32[1280]{0:T(1024)S(1)} %get-tuple-element.8, f32[1280]{0:T(1024)S(1)} %get-tuple-element.7), kind=kOutput, calls=%fused_computation.10 | convolution fusion | flops 841809920 | bytes 6563840 | tf_op jit(solution)/shard_map/dot_general | solution.py:356
  115.3 0.1 fusion.42
  115.3 21.3 %reduce-scatter.2.cloned.1.call-done = bf16[64,1280]{1,0:T(8,128)(2,1)} async-done(((bf16[256,1280]{1,0:T(8,128)(2,1)}), bf16[64,1280]{1,0:T(8,128)(2,1)}) %reduce-scatter.2.cloned.1.call-update) | async-done | bytes 163856 | tf_op jit(solution)/shard_map/reduce_scatter | solution.py:355
  136.7 1.0 fusion.31
  137.8 1.3 multiply_reduce_fusion.3
  139.0 1.9 %multiply_convert_fusion.3 = bf16[64,1280]{1,0:T(8,128)(2,1)} fusion(bf16[64,1280]{1,0:T(8,128)(2,1)} %reduce-scatter.2.cloned.1.call-done, f32[64]{0:T(128)S(1)} %add_rsqrt_fusion.6, f32[64]{0:T(128)S(1)} %add_rsqrt_fusion.7, f32[1280]{0:T(1024)S(1)} %get-tuple-element.5, f32[64]{0:T(128)S(1)} %fusion.42, bf16[256,1280]{1,0:T(8,128)(2,1)} %copy-done.2, ...), kind=kLoop, calls=%fused_computation.57 | loop fusion | flops 737280 | bytes 497412 | tf_op jit(solution)/shard_map/convert_element_type | solution.py:363
  (54 shorter events, 0.4 us)
Async XLA Ops:
  6.5 102.3 %copy-start = (bf16[1280,1280]{1,0:T(8,128)(2,1)S(1)}, bf16[1280,1280]{1,0:T(8,128)(2,1)}, u32[]{:S(2)}) copy-start(bf16[1280,1280]{1,0:T(8,128)(2,1)} %param.15) | copy-start | bytes 9830404
  6.5 37.6 %all-gather.2.cloned.1.call-start = ((), (), s32[]{:S(2)}) async-start(), calls=%async_computation.2 | async-start | bytes 1474560 | tf_op jit(solution)/shard_map/all_gather | solution.py:265
  24.7 6.0 %copy-start.9 = (s32[32]{0:T(128)S(1)}, s32[32]{0:T(128)}, u32[]{:S(2)}) copy-start(s32[32]{0:T(128)} %param.23) | copy-start | bytes 388
  44.2 11.3 %copy-start.3 = (pred[2048,512]{0,1:T(8,128)(4,1)S(1)}, pred[2048,512]{0,1:T(8,128)(4,1)}, u32[]{:S(2)}) copy-start(pred[2048,512]{0,1:T(8,128)(4,1)} %broadcast_compare_fusion) | copy-start | bytes 3145732
  44.2 11.3 %copy-start.4 = (bf16[512,5,64]{0,2,1:T(8,128)(2,1)S(1)}, bf16[512,5,64]{0,2,1:T(8,128)(2,1)}, u32[]{:S(2)}) copy-start(bf16[512,5,64]{0,2,1:T(8,128)(2,1)} %reshape_reshape.3) | copy-start | bytes 983044
  66.4 5.8 %copy-start.6 = (f32[2,1280]{1,0:T(2,128)S(1)}, f32[2,1280]{1,0:T(2,128)}, u32[]{:S(2)}) copy-start(f32[2,1280]{1,0:T(2,128)} %param.19) | copy-start | bytes 30724
  66.4 5.9 %copy-start.7 = (f32[2,1280]{1,0:T(2,128)S(1)}, f32[2,1280]{1,0:T(2,128)}, u32[]{:S(2)}) copy-start(f32[2,1280]{1,0:T(2,128)} %param.20) | copy-start | bytes 30724
  66.4 22.0 %all-to-all-start = ((bf16[8,256,325]{1,2,0:T(8,128)(2,1)}), bf16[8,256,325]{1,2,0:T(8,128)(2,1)}, u32[]{:S(2)}, u32[]{:S(2)}) async-start(bf16[8,256,325]{1,2,0:T(8,128)(2,1)} %pad_maximum_fusion), calls=%async_computation | async-start | bytes 2686976 | tf_op jit(solution)/shard_map/all_to_all | solution.py:323
  71.3 65.4 %reduce-scatter.2.cloned.1.call-start = ((), (), s32[]{:S(2)}) async-start(), calls=%async_computation.3 | async-start | bytes 819200 | tf_op jit(solution)/shard_map/reduce_scatter | solution.py:355
  75.0 15.1 %copy-start.5 = (bf16[1,256,320]{1,2,0:T(8,128)(2,1)S(1)}, bf16[1,256,320]{1,2,0:T(8,128)(2,1)}, u32[]{:S(2)}) copy-start(bf16[1,256,320]{1,2,0:T(8,128)(2,1)} %get-tuple-element.14) | copy-start | bytes 491524
  88.5 1.7 %copy-start.10 = (bf16[5,256,256]{1,2,0:T(8,128)(2,1)S(1)}, bf16[5,256,256]{1,2,0:T(8,128)(2,1)}, u32[]{:S(2)}) copy-start(bf16[5,256,256]{1,2,0:T(8,128)(2,1)} %get-tuple-element.26) | copy-start | bytes 1966084
  90.1 20.8 %slice-start = ((s8[6553600]{0:T(1024)(128)(4,1)}), s8[4194304]{0:T(1024)(128)(4,1)S(1)}, s32[]{:S(2)}) async-start(s8[6553600]{0:T(1024)(128)(4,1)} %bitcast.86), calls=%async_computation.4 | async-start | bytes 8388608
  108.9 1.2 copy-start.1
  108.9 2.1 %slice-start.1 = ((s8[6553600]{0:T(1024)(128)(4,1)}), s8[2359296]{0:T(1024)(128)(4,1)S(1)}, s32[]{:S(2)}) async-start(s8[6553600]{0:T(1024)(128)(4,1)} %bitcast.86), calls=%async_computation.5 | async-start | bytes 4718592
  111.0 1.9 %copy-start.2 = (bf16[256,1280]{1,0:T(8,128)(2,1)}, bf16[256,1280]{1,0:T(8,128)(2,1)S(1)}, u32[]{:S(2)}) copy-start(bf16[256,1280]{1,0:T(8,128)(2,1)S(1)} %multiply_convert_fusion) | copy-start | bytes 1966084
  111.0 2.2 %copy-start.8 = (bf16[1280,1280]{1,0:T(8,128)(2,1)S(1)}, bf16[1280,1280]{1,0:T(8,128)(2,1)}, u32[]{:S(2)}) copy-start(bf16[1280,1280]{1,0:T(8,128)(2,1)} %param.17) | copy-start | bytes 9830404
Sparse Core Ops, SparseCore 0:
  18.2 25.9 all-gather.1
  115.4 21.2 reduce-scatter.1

commit v7 on v6

--- a/solution.py
+++ b/solution.py
@@ -340,7 +340,10 @@
         :, :, None
     ]
     attention_local = mixed.reshape(slot_count, local_width).astype(jnp.bfloat16)
-    attention = lax.all_gather(attention_local, "mp", axis=1, tiled=True)
+    attention_parts = lax.all_to_all(
+        jnp.tile(attention_local, (mp_count, 1)), "mp", 0, 0, tiled=True
+    ).reshape(mp_count, slot_count, local_width)
+    attention = jnp.transpose(attention_parts, (1, 0, 2)).reshape(slot_count, model_width)
     projected_out = jnp.dot(attention, w_out, preferred_element_type=jnp.float32)
     residual_in = state_in.astype(jnp.float32)
     state_mid = rms_rows(
@@ -352,12 +355,16 @@
         jax.nn.silu(scale_gate_up[0][None, :] * gate_up[0])
         * (scale_gate_up[1][None, :] * gate_up[1])
     ).astype(jnp.bfloat16)
-    feed_sum = lax.psum_scatter(
+    feed_parts = lax.all_to_all(
         jnp.dot(hidden, w_down, preferred_element_type=jnp.float32).astype(jnp.bfloat16),
         "mp",
-        scatter_dimension=0,
+        0,
+        0,
         tiled=True,
-    ).astype(jnp.float32)
+    )
+    feed_sum = jnp.sum(
+        feed_parts.reshape(mp_count, own_rows, model_width).astype(jnp.float32), axis=0
+    )
     middle = state_own.astype(jnp.float32)
     result = rms_rows(middle + eigen_rates[1][None, :] * (rms_rows(feed_sum) - middle))
     return (live_own.astype(jnp.float32)[:, None] * result).astype(jnp.bfloat16)

time: 150 us -> 155 us (1.033)
  blocking collectives: 18.4 us -> 0 us
  waiting for transfers between devices: 45.2 us -> 58.3 us
  starting transfers between devices: 4.85 us -> 13.5 us
  matrix products: 31 us -> 35.3 us
  other arithmetic: 19.5 us -> 17.8 us
    all_to_all x0 -> x2, waiting for transfers between devices: none -> 34.3 us  [the longest x1 17.5 us: shards_heads(): lax.all_to_all(jnp.tile(attention_local, (mp_count, 1)), 'mp', 0, 0, tile...]
    reduce_scatter x1 -> x0, waiting for transfers between devices: 21.3 us -> none  [shards_heads(): lax.psum_scatter(jnp.dot(hidden, w_down, preferred_element_type=jnp.float...]
    all_gather x1 -> x0, blocking collectives: 18.4 us -> none  [shards_heads(): attention = lax.all_gather(attention_local, 'mp', axis=1, tiled=True)]
    all_to_all x0 -> x2, starting transfers between devices: none -> 8.75 us  [the longest x1 4.6 us: shards_heads(): lax.all_to_all(jnp.tile(attention_local, (mp_count, 1)), 'mp', 0, 0, tile...]
    dot_general x1, matrix products: 1.85 us -> 5 us  [shards_heads(): jnp.einsum('sd,jdf->jsf', state_mid, w_gate_up, preferred_element_type=jn...]
    reduce_sum x4, other arithmetic: 4.26 us -> 2.32 us  [rms_rows(): jnp.mean(values_in * values_in, axis=-1, keepdims=True) + EPSILON]
  transfers between devices with their start and end apart: 3 -> 4, of which waited for: 3 -> 4; matrix products, arithmetic and copies ran while one was open for 13% -> 13% of each run, Pallas kernels for 0% -> 0%
where the time goes in v7:
time: 155 us; the launch traced here: 154 us
  waiting for transfers between devices  58.3 us (38%)
  matrix products  35.3 us (23%)
  other arithmetic  17.8 us (11%)
  local copies, waits for them, and re-layouts  15.8 us (10%)
  between operations  13.7 us (9%)
  starting transfers between devices  13.5 us (9%)
    all_to_all x1, waiting for transfers between devices, shards_heads(): lax.all_to_all(jnp.tile(attention_local, (mp_count, 1)), 'mp', 0, 0, tile...  17.5 us
    all_to_all x1, waiting for transfers between devices, shards_heads(): lax.all_to_all(jnp.dot(hidden, w_down, preferred_element_type=jnp.float32...  16.8 us
    all_to_all x1, waiting for transfers between devices, shards_heads(): lax.all_to_all(jnp.concatenate([summed.reshape(row_count, local_width), w...  13.5 us
    dot_general x1, matrix products, shards_heads(): jnp.einsum('qhd,khd->qhk', query_heads, key_heads, preferred_element_type...  11.3 us
    all_gather x1, waiting for transfers between devices, shards_heads(): gathered = lax.all_gather(queries, 'pages', axis=0, tiled=True)  10.4 us
    dot_general x1, matrix products, shards_heads(): jnp.einsum('qhk,khd->qhd', prefix_weights.astype(jnp.bfloat16), value_hea...  9.11 us
    dot_general x1, matrix products, shards_heads(): jnp.einsum('sd,jdf->jsf', state_mid, w_gate_up, preferred_element_type=jn...  5 us
    all_to_all x1, starting transfers between devices, shards_heads(): lax.all_to_all(jnp.concatenate([summed.reshape(row_count, local_width), w...  4.71 us
  transfers between devices with their start and end apart: 4, of which 4 were waited for; matrix products, arithmetic and copies ran while one was open for 13% of the time, Pallas kernels for 0%

profile of v7, /device:TPU:2, one launch (start us, length us, event | category | flops | bytes accessed | tf_op | source)
XLA Modules:
  0.0 154.3 jit_solution(7879048635106829990)
XLA Ops:
  6.6 1.4 fusion.12
  8.0 0.7 reduce_window_sum.11
  8.7 0.7 sub.37
  9.4 0.8 select_reduce_fusion.2
  10.2 2.8 %fusion.19 = bf16[3,256,320]{1,2,0:T(8,128)(2,1)S(1)} fusion(bf16[3,1280,320]{1,2,0:T(8,128)(2,1)} %param.14, bf16[256,1280]{1,0:T(8,128)(2,1)} %param.13, f32[256]{0:T(256)S(1)} %add_rsqrt_fusion.5), kind=kOutput, calls=%fused_computation.34 | convolution fusion | flops 630374400 | bytes 3605504 | tf_op jit(solution)/shard_map/sd,jdc->jsc/dot_general | solution.py:255
  13.0 0.7 fusion.48
  13.8 0.2 multiply_cosine_fusion
  14.0 0.7 multiply_subtract_fusion
  14.8 0.8 fusion.35
  15.5 0.8 dynamic_slice.33
  16.3 1.7 %fusion.32 = bf16[256,320]{0,1:T(8,128)(2,1)} fusion(f32[256,5,64]{0,2,1:T(8,128)} %fusion.35, f32[320]{0:T(512)S(1)} %dynamic_slice.33), kind=kLoop, calls=%fused_computation.54 | loop fusion | flops 163840 | bytes 492800 | tf_op jit(solution)/shard_map/convert_element_type | solution.py:260
  18.3 2.5 %constant_dynamic-slice_fusion = (bf16[4,128,320]{2,1,0:T(8,128)(2,1)}, bf16[4,128,320]{2,1,0:T(8,128)(2,1)}) fusion(bf16[4,128,1280]{2,1,0:T(8,128)(2,1)} %param.21, s32[]{:T(128)S(6)} %select_n.65, bf16[4,128,1280]{2,1,0:T(8,128)(2,1)} %param.22), kind=kLoop, calls=%fused_computation.94 | loop fusion | bytes 1310724 | tf_op jit(solution)/shard_map/dynamic_slice | solution.py:295
  20.7 1.9 %copy.61 = bf16[4,128,320]{1,2,0:T(8,128)(2,1)} copy(bf16[4,128,320]{2,1,0:T(8,128)(2,1)} %get-tuple-element.31) | data formatting | bytes 655360
  22.6 2.1 %copy.55 = f32[4,128,320]{1,0,2:T(4,128)} copy(bf16[4,128,320]{1,2,0:T(8,128)(2,1)} %copy.61) | data formatting | bytes 983040 | tf_op jit(solution)/shard_map/convert_element_type | solution.py:297
  24.7 2.2 %reshape.363 = f32[512,5,64]{0,2,1:T(8,128)} reshape(f32[4,128,320]{1,0,2:T(4,128)} %copy.55) | data formatting | bytes 1310720 | tf_op jit(solution)/shard_map/convert_element_type | solution.py:297
  26.9 2.0 %copy.53 = bf16[4,128,320]{1,0,2:T(4,128)(2,1)} copy(bf16[4,128,320]{2,1,0:T(8,128)(2,1)} %get-tuple-element.32) | data formatting | bytes 655360 | tf_op jit(solution)/shard_map/dynamic_slice | solution.py:301
  28.9 1.8 %reshape_reshape.3 = bf16[512,5,64]{0,2,1:T(8,128)(2,1)} reshape(bf16[4,128,320]{1,0,2:T(4,128)(2,1)} %copy.53) | data formatting | bytes 655360 | tf_op jit(solution)/shard_map/reshape;reshape | solution.py:308
  30.7 0.2 select_reduce_fusion.3
  30.9 1.2 multiply_reduce_fusion.2
  32.1 1.7 %broadcast_compare_fusion = pred[2048,512]{0,1:T(8,128)(4,1)} fusion(s32[2048]{0:T(1024)S(1)} %bitcast.99, s32[512]{0:T(512)S(1)} %broadcast_bitcast_fusion), kind=kLoop, calls=%fused_computation.11 | loop fusion | flops 1048576 | bytes 1058816 | tf_op jit(solution)/shard_map/eq | solution.py:313
  33.8 10.4 %all-gather.2.cloned.1.call-done = bf16[2048,320]{0,1:T(8,128)(2,1)} async-done(((bf16[256,320]{0,1:T(8,128)(2,1)}), bf16[2048,320]{0,1:T(8,128)(2,1)}) %all-gather.2.cloned.1.call-update) | async-done | bytes 1310736 | tf_op jit(solution)/shard_map/all_gather | solution.py:265
  44.2 11.3 %fusion = (bf16[2048,5]{0,1:T(8,128)(2,1)S(1)}, f32[5,512,2048]{2,1,0:T(8,128)}) fusion(pred[2048,512]{0,1:T(8,128)(4,1)} %broadcast_compare_fusion, bf16[2048,5,64]{0,2,1:T(8,128)(2,1)} %bitcast.103, f32[512,5,64]{0,2,1:T(8,128)} %reshape.363, f32[5,64]{1,0:T(8,128)S(1)} %mul.315, f32[512,5]{0,1:T(8,128)S(1)} %add_rsqrt_fusion), kind=kOutput, calls=%fused_computation.1 | convolution fusion | flops 687298560 | bytes 24018176 | tf_op jit(solution)/shard_map/qhd,khd->qhk/dot_general | solution.py:310
  55.5 9.1 %fusion.7 = bf16[5,64,2048]{2,1,0:T(8,128)(2,1)S(1)} fusion(bf16[512,5,64]{0,2,1:T(8,128)(2,1)S(1)} %copy-done.5, f32[5,512,2048]{2,1,0:T(8,128)} %get-tuple-element.24, pred[2048,512]{0,1:T(8,128)(4,1)S(1)} %copy-done.4), kind=kOutput, calls=%fused_computation.8 | convolution fusion | flops 687472640 | bytes 23658496 | tf_op jit(solution)/shard_map/qhk,khd->qhd/dot_general | solution.py:316
  64.6 0.4 copy.63
  65.0 0.3 copy.57
  65.3 1.2 pad_maximum_fusion
  66.4 4.7 %all-to-all-start = ((bf16[8,256,325]{1,2,0:T(8,128)(2,1)}), bf16[8,256,325]{1,2,0:T(8,128)(2,1)}, u32[]{:S(2)}, u32[]{:S(2)}) async-start(bf16[8,256,325]{1,2,0:T(8,128)(2,1)} %pad_maximum_fusion), calls=%async_computation | async-start | bytes 2686976 | tf_op jit(solution)/shard_map/all_to_all | solution.py:323
  71.2 1.0 multiply_reduce_fusion.5
  72.2 0.2 and_and_fusion
  72.3 2.5 %fusion.49 = (f32[5,256]{1,0:T(8,128)S(1)}, bf16[5,256,256]{1,2,0:T(8,128)(2,1)}) fusion(f32[256,5,32]{0,2,1:T(8,128)} %get-tuple-element.16, f32[256,5,32]{0,2,1:T(8,128)S(1)} %get-tuple-element.15, f32[256,5]{0,1:T(8,128)S(1)} %add_rsqrt_fusion.1, f32[5,64]{1,0:T(8,128)S(1)} %mul.315, f32[256,5,64]{0,2,1:T(8,128)} %fusion.35, ...), kind=kOutput, calls=%fused_computation.119 | convolution fusion | flops 43744000 | bytes 1387776 | tf_op jit(solution)/shard_map/qhd,khd->hqk/dot_general | solution.py:267
  74.8 13.5 %all-to-all-done = bf16[8,256,325]{1,2,0:T(8,128)(2,1)} async-done(((bf16[8,256,325]{1,2,0:T(8,128)(2,1)}), bf16[8,256,325]{1,2,0:T(8,128)(2,1)}, u32[]{:S(2)}, u32[]{:S(2)}) %all-to-all-start) | async-done | bytes 1331232 | tf_op jit(solution)/shard_map/all_to_all | solution.py:323
  88.3 1.6 %convert_reduce_fusion = f32[256,325]{0,1:T(8,128)S(1)} fusion(bf16[8,256,325]{1,2,0:T(8,128)(2,1)} %all-to-all-done), kind=kLoop, calls=%fused_computation.9 | loop fusion | flops 1248000 | bytes 1664000 | tf_op jit(solution)/shard_map/reduce_sum | solution.py:332
  90.0 0.2 fusion.22
  90.3 0.9 tile.2
  91.2 4.6 %all-to-all-start.1 = ((bf16[4,256,320]{1,2,0:T(8,128)(2,1)}), bf16[4,256,320]{1,2,0:T(8,128)(2,1)}, u32[]{:S(2)}, u32[]{:S(2)}) async-start(bf16[4,256,320]{1,2,0:T(8,128)(2,1)} %tile.2), calls=%async_computation.1 | async-start | bytes 1310720 | tf_op jit(solution)/shard_map/all_to_all | solution.py:343
  95.9 17.5 %all-to-all-done.1 = bf16[4,256,320]{1,2,0:T(8,128)(2,1)} async-done(((bf16[4,256,320]{1,2,0:T(8,128)(2,1)}), bf16[4,256,320]{1,2,0:T(8,128)(2,1)}, u32[]{:S(2)}, u32[]{:S(2)}) %all-to-all-start.1) | async-done | bytes 655392 | tf_op jit(solution)/shard_map/all_to_all | solution.py:343
  113.4 2.3 %multiply_reduce_fusion.1 = (f32[256]{0:T(256)S(1)}, f32[256,1280]{1,0:T(8,128)S(1)}) fusion(bf16[256,1280]{0,1:T(8,128)(2,1)} %bitcast.21, bf16[1280,1280]{1,0:T(8,128)(2,1)S(1)} %copy-done), kind=kOutput, calls=%fused_computation.32 | convolution fusion | flops 839515904 | bytes 5243904 | tf_op jit(solution)/shard_map/dot_general | solution.py:347
  115.7 0.5 multiply_reduce_fusion
  116.2 0.4 multiply_convert_fusion
  116.7 5.0 %convolution_bitcast_fusion = f32[2,256,1280]{2,1,0:T(8,128)S(1)} fusion(bf16[2,1280,1280]{2,1,0:T(8,128)(2,1)} %param.16, bf16[256,1280]{1,0:T(8,128)(2,1)S(1)} %multiply_convert_fusion), kind=kOutput, calls=%fused_computation.7 | convolution fusion | flops 1677721600 | bytes 9830400 | tf_op jit(solution)/shard_map/sd,jdf->jsf/dot_general | solution.py:353
  121.7 2.1 %convolution_convert_fusion = bf16[256,1280]{1,0:T(8,128)(2,1)} fusion(bf16[1280,1280]{1,0:T(8,128)(2,1)S(1)} %copy-done.9, f32[2,256,1280]{2,1,0:T(8,128)S(1)} %convolution_bitcast_fusion, f32[1280]{0:T(1024)S(1)} %get-tuple-element.8, f32[1280]{0:T(1024)S(1)} %get-tuple-element.7), kind=kOutput, calls=%fused_computation.10 | convolution fusion | flops 841809920 | bytes 6563840 | tf_op jit(solution)/shard_map/dot_general | solution.py:359
  123.8 4.2 %all-to-all-start.2 = ((bf16[4,64,1280]{2,1,0:T(8,128)(2,1)}), bf16[4,64,1280]{2,1,0:T(8,128)(2,1)}, u32[]{:S(2)}, u32[]{:S(2)}) async-start(bf16[4,64,1280]{2,1,0:T(8,128)(2,1)} %bitcast.92), calls=%async_computation.2 | async-start | bytes 1310720 | tf_op jit(solution)/shard_map/all_to_all | solution.py:358
  128.0 0.1 fusion.41
  128.0 16.8 %all-to-all-done.2 = bf16[4,64,1280]{2,1,0:T(8,128)(2,1)} async-done(((bf16[4,64,1280]{2,1,0:T(8,128)(2,1)}), bf16[4,64,1280]{2,1,0:T(8,128)(2,1)}, u32[]{:S(2)}, u32[]{:S(2)}) %all-to-all-start.2) | async-done | bytes 655392 | tf_op jit(solution)/shard_map/all_to_all | solution.py:358
  144.8 1.3 convert_reduce_fusion.1
  146.1 0.1 multiply_reduce_fusion.4
  146.3 0.3 multiply_reduce_fusion.3
  146.5 0.9 multiply_convert_fusion.3
  (53 shorter events, 0.6 us)
Async XLA Ops:
  6.5 106.9 %copy-start = (bf16[1280,1280]{1,0:T(8,128)(2,1)S(1)}, bf16[1280,1280]{1,0:T(8,128)(2,1)}, u32[]{:S(2)}) copy-start(bf16[1280,1280]{1,0:T(8,128)(2,1)} %param.15) | copy-start | bytes 9830404
  6.5 37.6 %all-gather.2.cloned.1.call-start = ((), (), s32[]{:S(2)}) async-start(), calls=%async_computation.3 | async-start | bytes 1474560 | tf_op jit(solution)/shard_map/all_gather | solution.py:265
  24.7 6.0 %copy-start.10 = (s32[32]{0:T(128)S(1)}, s32[32]{0:T(128)}, u32[]{:S(2)}) copy-start(s32[32]{0:T(128)} %param.23) | copy-start | bytes 388
  44.2 11.3 %copy-start.4 = (pred[2048,512]{0,1:T(8,128)(4,1)S(1)}, pred[2048,512]{0,1:T(8,128)(4,1)}, u32[]{:S(2)}) copy-start(pred[2048,512]{0,1:T(8,128)(4,1)} %broadcast_compare_fusion) | copy-start | bytes 3145732
  44.2 11.3 %copy-start.5 = (bf16[512,5,64]{0,2,1:T(8,128)(2,1)S(1)}, bf16[512,5,64]{0,2,1:T(8,128)(2,1)}, u32[]{:S(2)}) copy-start(bf16[512,5,64]{0,2,1:T(8,128)(2,1)} %reshape_reshape.3) | copy-start | bytes 983044
  66.4 21.9 %all-to-all-start = ((bf16[8,256,325]{1,2,0:T(8,128)(2,1)}), bf16[8,256,325]{1,2,0:T(8,128)(2,1)}, u32[]{:S(2)}, u32[]{:S(2)}) async-start(bf16[8,256,325]{1,2,0:T(8,128)(2,1)} %pad_maximum_fusion), calls=%async_computation | async-start | bytes 2686976 | tf_op jit(solution)/shard_map/all_to_all | solution.py:323
  74.8 15.2 %copy-start.6 = (bf16[1,256,320]{1,2,0:T(8,128)(2,1)S(1)}, bf16[1,256,320]{1,2,0:T(8,128)(2,1)}, u32[]{:S(2)}) copy-start(bf16[1,256,320]{1,2,0:T(8,128)(2,1)} %get-tuple-element.14) | copy-start | bytes 491524
  88.3 1.7 %copy-start.11 = (bf16[5,256,256]{1,2,0:T(8,128)(2,1)S(1)}, bf16[5,256,256]{1,2,0:T(8,128)(2,1)}, u32[]{:S(2)}) copy-start(bf16[5,256,256]{1,2,0:T(8,128)(2,1)} %get-tuple-element.26) | copy-start | bytes 1966084
  90.3 5.5 %copy-start.7 = (f32[2,1280]{1,0:T(2,128)S(1)}, f32[2,1280]{1,0:T(2,128)}, u32[]{:S(2)}) copy-start(f32[2,1280]{1,0:T(2,128)} %param.19) | copy-start | bytes 30724
  90.3 5.5 %copy-start.8 = (f32[2,1280]{1,0:T(2,128)S(1)}, f32[2,1280]{1,0:T(2,128)}, u32[]{:S(2)}) copy-start(f32[2,1280]{1,0:T(2,128)} %param.20) | copy-start | bytes 30724
  91.2 22.2 %all-to-all-start.1 = ((bf16[4,256,320]{1,2,0:T(8,128)(2,1)}), bf16[4,256,320]{1,2,0:T(8,128)(2,1)}, u32[]{:S(2)}, u32[]{:S(2)}) async-start(bf16[4,256,320]{1,2,0:T(8,128)(2,1)} %tile.2), calls=%async_computation.1 | async-start | bytes 1310720 | tf_op jit(solution)/shard_map/all_to_all | solution.py:343
  113.4 2.3 %copy-start.1 = (bf16[256,1280]{1,0:T(8,128)(2,1)S(1)}, bf16[256,1280]{1,0:T(8,128)(2,1)}, u32[]{:S(2)}) copy-start(bf16[256,1280]{1,0:T(8,128)(2,1)} %param.13) | copy-start | bytes 1966084
  116.6 5.0 %copy-start.2 = (bf16[256,1280]{1,0:T(8,128)(2,1)}, bf16[256,1280]{1,0:T(8,128)(2,1)S(1)}, u32[]{:S(2)}) copy-start(bf16[256,1280]{1,0:T(8,128)(2,1)S(1)} %multiply_convert_fusion) | copy-start | bytes 1966084
  116.6 5.0 %copy-start.9 = (bf16[1280,1280]{1,0:T(8,128)(2,1)S(1)}, bf16[1280,1280]{1,0:T(8,128)(2,1)}, u32[]{:S(2)}) copy-start(bf16[1280,1280]{1,0:T(8,128)(2,1)} %param.17) | copy-start | bytes 9830404
  123.8 21.1 %all-to-all-start.2 = ((bf16[4,64,1280]{2,1,0:T(8,128)(2,1)}), bf16[4,64,1280]{2,1,0:T(8,128)(2,1)}, u32[]{:S(2)}, u32[]{:S(2)}) async-start(bf16[4,64,1280]{2,1,0:T(8,128)(2,1)} %bitcast.92), calls=%async_computation.2 | async-start | bytes 1310720 | tf_op jit(solution)/shard_map/all_to_all | solution.py:358
  144.8 1.4 copy-start.3
Sparse Core Ops, SparseCore 0:
  18.2 25.9 all-gather.1

commit v8 on v7

--- a/solution.py
+++ b/solution.py
@@ -301,29 +301,41 @@
     prefix_values = lax.dynamic_slice_in_dim(
         cache_values, mp_index * local_width, local_width, 2
     ).reshape(pages_here * page_len, local_width)
-    gathered_group = group_id.reshape(-1)
-    row_count = gathered.shape[0]
-    query_heads = gathered.reshape(row_count, local_heads, head_dim)
+    all_groups = group_id.reshape(-1)
     key_heads = prefix_keys.reshape(-1, local_heads, head_dim)
     value_heads = prefix_values.reshape(-1, local_heads, head_dim)
-    prefix_scores = (
-        jnp.einsum("qhd,khd->qhk", query_heads, key_heads, preferred_element_type=jnp.float32)
-        * score_scale
-    )
-    prefix_allowed = gathered_group[:, None] == key_group[None, :]
-    prefix_weights = jnp.where(prefix_allowed[:, None, :], jnp.exp(prefix_scores), 0.0)
-    weight_sum = jnp.sum(prefix_weights, axis=-1)
-    summed = jnp.einsum(
-        "qhk,khd->qhd",
-        prefix_weights.astype(jnp.bfloat16),
-        value_heads,
-        preferred_element_type=jnp.float32,
-    )
+    total_rows = gathered.shape[0]
+    chunk_count = 2 if total_rows % 16 == 0 else 1
+    row_count = total_rows // chunk_count
+    pieces = []
+    for chunk in range(chunk_count):
+        query_heads = lax.slice_in_dim(
+            gathered, chunk * row_count, (chunk + 1) * row_count, axis=0
+        ).reshape(row_count, local_heads, head_dim)
+        gathered_group = lax.slice_in_dim(
+            all_groups, chunk * row_count, (chunk + 1) * row_count, axis=0
+        )
+        prefix_scores = (
+            jnp.einsum("qhd,khd->qhk", query_heads, key_heads, preferred_element_type=jnp.float32)
+            * score_scale
+        )
+        prefix_allowed = gathered_group[:, None] == key_group[None, :]
+        prefix_weights = jnp.where(prefix_allowed[:, None, :], jnp.exp(prefix_scores), 0.0)
+        weight_sum = jnp.sum(prefix_weights, axis=-1)
+        summed = jnp.einsum(
+            "qhk,khd->qhd",
+            prefix_weights.astype(jnp.bfloat16),
+            value_heads,
+            preferred_element_type=jnp.float32,
+        )
+        pieces.append(
+            jnp.concatenate([summed.reshape(row_count, local_width), weight_sum], axis=1).astype(
+                jnp.bfloat16
+            )
+        )
     pages_count = lax.axis_size("pages")
     prefix_parts = lax.all_to_all(
-        jnp.concatenate([summed.reshape(row_count, local_width), weight_sum], axis=1).astype(
-            jnp.bfloat16
-        ),
+        jnp.concatenate(pieces, axis=0),
         "pages",
         0,
         0,
@@ -340,10 +352,7 @@
         :, :, None
     ]
     attention_local = mixed.reshape(slot_count, local_width).astype(jnp.bfloat16)
-    attention_parts = lax.all_to_all(
-        jnp.tile(attention_local, (mp_count, 1)), "mp", 0, 0, tiled=True
-    ).reshape(mp_count, slot_count, local_width)
-    attention = jnp.transpose(attention_parts, (1, 0, 2)).reshape(slot_count, model_width)
+    attention = lax.all_gather(attention_local, "mp", axis=1, tiled=True)
     projected_out = jnp.dot(attention, w_out, preferred_element_type=jnp.float32)
     residual_in = state_in.astype(jnp.float32)
     state_mid = rms_rows(

time: 155 us -> 137 us (0.88)
  waiting for transfers between devices: 58.3 us -> 39.2 us
  blocking collectives: 0 us -> 18.3 us
  matrix products: 35.3 us -> 20.9 us
  starting transfers between devices: 13.5 us -> 8.99 us
  local copies, waits for them, and re-layouts: 15.8 us -> 18 us
    all_gather x0 -> x1, blocking collectives: none -> 18.3 us  [shards_heads(): attention = lax.all_gather(attention_local, 'mp', axis=1, tiled=True)]
    all_to_all x2 -> x1, waiting for transfers between devices: 31.1 us -> 13.4 us  [shards_heads(): lax.all_to_all(jnp.concatenate(pieces, axis=0), 'pages', 0, 0, tiled=True)]
    dot_general x1 -> x2, matrix products: 11.3 us -> 5.97 us  [shards_heads(): jnp.einsum('qhd,khd->qhk', query_heads, key_heads, preferred_element_type...]
    dot_general x1 -> x2, matrix products: 9.11 us -> 4.29 us  [shards_heads(): jnp.einsum('qhk,khd->qhd', prefix_weights.astype(jnp.bfloat16), value_hea...]
    all_to_all x2 -> x1, starting transfers between devices: 9.31 us -> 4.84 us  [shards_heads(): lax.all_to_all(jnp.concatenate(pieces, axis=0), 'pages', 0, 0, tiled=True)]
    dot_general x1, matrix products: 5 us -> 1.85 us  [shards_heads(): jnp.einsum('sd,jdf->jsf', state_mid, w_gate_up, preferred_element_type=jn...]
  transfers between devices with their start and end apart: 4 -> 3, of which waited for: 4 -> 3; matrix products, arithmetic and copies ran while one was open for 13% -> 14% of each run, Pallas kernels for 0% -> 0%
where the time goes in v8:
time: 137 us; the launch traced here: 136 us
  waiting for transfers between devices  39.2 us (29%)
  matrix products  20.9 us (15%)
  blocking collectives  18.3 us (13%)
  local copies, waits for them, and re-layouts  18 us (13%)
  other arithmetic  16.7 us (12%)
  between operations  13.8 us (10%)
  starting transfers between devices  8.99 us (7%)
    all_gather x1, blocking collectives, shards_heads(): attention = lax.all_gather(attention_local, 'mp', axis=1, tiled=True)  18.3 us
    all_to_all x1, waiting for transfers between devices, shards_heads(): lax.all_to_all(jnp.dot(hidden, w_down, preferred_element_type=jnp.float32...  15.4 us
    all_to_all x1, waiting for transfers between devices, shards_heads(): lax.all_to_all(jnp.concatenate(pieces, axis=0), 'pages', 0, 0, tiled=True)  13.4 us
    all_gather x1, waiting for transfers between devices, shards_heads(): gathered = lax.all_gather(queries, 'pages', axis=0, tiled=True)  10.4 us
    dot_general x2, matrix products, shards_heads(): jnp.einsum('qhd,khd->qhk', query_heads, key_heads, preferred_element_type...  5.97 us
    all_to_all x1, starting transfers between devices, shards_heads(): lax.all_to_all(jnp.concatenate(pieces, axis=0), 'pages', 0, 0, tiled=True)  4.84 us
    convert_element_type x2, local copies, waits for them, and re-layouts, shards_heads(): cache_local.reshape(pages_here * page_len, local_width).astype(jnp.float32)  4.3 us
    dot_general x2, matrix products, shards_heads(): jnp.einsum('qhk,khd->qhd', prefix_weights.astype(jnp.bfloat16), value_hea...  4.29 us
  transfers between devices with their start and end apart: 3, of which 3 were waited for; matrix products, arithmetic and copies ran while one was open for 14% of the time, Pallas kernels for 0%

profile of v8, /device:TPU:2, one launch (start us, length us, event | category | flops | bytes accessed | tf_op | source)
XLA Modules:
  0.0 135.7 jit_solution(497276679531172989)
XLA Ops:
  6.6 1.4 %fusion.22 = f32[256]{0:T(256)S(1)} fusion(bf16[256,1280]{1,0:T(8,128)(2,1)} %param.13), kind=kLoop, calls=%fused_computation.28 | loop fusion | flops 982784 | bytes 656384 | tf_op jit(solution)/shard_map/reduce_sum | solution.py:16
  8.0 0.7 reduce_window_sum.11
  8.7 0.7 sub.37
  9.4 0.8 select_reduce_fusion.2
  10.2 2.8 %fusion.29 = bf16[3,256,320]{1,2,0:T(8,128)(2,1)S(1)} fusion(bf16[3,1280,320]{1,2,0:T(8,128)(2,1)} %param.14, bf16[256,1280]{1,0:T(8,128)(2,1)} %param.13, f32[256]{0:T(256)S(1)} %add_rsqrt_fusion.5), kind=kOutput, calls=%fused_computation.42 | convolution fusion | flops 630374400 | bytes 3605504 | tf_op jit(solution)/shard_map/sd,jdc->jsc/dot_general | solution.py:255
  13.0 0.7 fusion.60
  13.8 0.2 multiply_cosine_fusion
  14.0 0.7 multiply_subtract_fusion
  14.8 0.8 fusion.42
  15.5 0.8 dynamic_slice.33
  16.3 1.7 %fusion.41 = bf16[256,320]{0,1:T(8,128)(2,1)} fusion(f32[256,5,64]{0,2,1:T(8,128)} %fusion.42, f32[320]{0:T(512)S(1)} %dynamic_slice.33), kind=kLoop, calls=%fused_computation.63 | loop fusion | flops 163840 | bytes 492800 | tf_op jit(solution)/shard_map/convert_element_type | solution.py:260
  18.3 2.4 %constant_dynamic-slice_fusion = (bf16[4,128,320]{2,1,0:T(8,128)(2,1)}, bf16[4,128,320]{2,1,0:T(8,128)(2,1)}) fusion(bf16[4,128,1280]{2,1,0:T(8,128)(2,1)} %param.21, s32[]{:T(128)S(6)} %select_n.61, bf16[4,128,1280]{2,1,0:T(8,128)(2,1)} %param.22), kind=kLoop, calls=%fused_computation.105 | loop fusion | bytes 1310724 | tf_op jit(solution)/shard_map/dynamic_slice | solution.py:295
  20.7 1.9 %copy.63 = bf16[4,128,320]{1,2,0:T(8,128)(2,1)} copy(bf16[4,128,320]{2,1,0:T(8,128)(2,1)} %get-tuple-element.39) | data formatting | bytes 655360
  22.6 2.1 %copy.56 = f32[4,128,320]{1,0,2:T(4,128)} copy(bf16[4,128,320]{1,2,0:T(8,128)(2,1)} %copy.63) | data formatting | bytes 983040 | tf_op jit(solution)/shard_map/convert_element_type | solution.py:297
  24.7 2.2 %reshape.379 = f32[512,5,64]{0,2,1:T(8,128)} reshape(f32[4,128,320]{1,0,2:T(4,128)} %copy.56) | data formatting | bytes 1310720 | tf_op jit(solution)/shard_map/convert_element_type | solution.py:297
  26.9 1.9 %copy.54 = bf16[4,128,320]{1,0,2:T(4,128)(2,1)} copy(bf16[4,128,320]{2,1,0:T(8,128)(2,1)} %get-tuple-element.40) | data formatting | bytes 655360 | tf_op jit(solution)/shard_map/dynamic_slice | solution.py:301
  28.9 1.8 %reshape_reshape.3 = bf16[512,5,64]{0,2,1:T(8,128)(2,1)} reshape(bf16[4,128,320]{1,0,2:T(4,128)(2,1)} %copy.54) | data formatting | bytes 655360 | tf_op jit(solution)/shard_map/reshape;reshape | solution.py:306
  30.7 0.2 select_reduce_fusion.3
  30.9 1.2 multiply_reduce_fusion.2
  32.2 1.6 %broadcast_compare_fusion.1 = (pred[1024,512]{0,1:T(8,128)(4,1)}, pred[1024,512]{0,1:T(8,128)(4,1)}) fusion(s32[1024]{0:T(1024)S(1)} %bitcast.121, s32[512]{0:T(512)S(1)} %broadcast_bitcast_fusion, s32[1024]{0:T(1024)S(1)} %bitcast.122), kind=kLoop, calls=%fused_computation.48 | loop fusion | flops 1048576 | bytes 1058816 | tf_op jit(solution)/shard_map/eq | solution.py:322
  33.8 10.4 %all-gather.2.cloned.1.call-done = bf16[2048,320]{0,1:T(8,128)(2,1)} async-done(((bf16[256,320]{0,1:T(8,128)(2,1)}), bf16[2048,320]{0,1:T(8,128)(2,1)}) %all-gather.2.cloned.1.call-update) | async-done | bytes 1310736 | tf_op jit(solution)/shard_map/all_gather | solution.py:265
  44.2 1.5 %fusion.59 = (bf16[1024,320]{0,1:T(8,128)(2,1)S(1)}, bf16[1024,320]{0,1:T(8,128)(2,1)S(1)}) fusion(bf16[2048,320]{0,1:T(8,128)(2,1)} %all-gather.2.cloned.1.call-done), kind=kLoop, calls=%fused_computation.131 | loop fusion | bytes 2621440 | tf_op jit(solution)/shard_map/slice | solution.py:312
  45.7 0.1 copy-done.6
  45.8 3.0 %fusion = (bf16[1024,5]{0,1:T(8,128)(2,1)S(1)}, f32[5,512,1024]{2,1,0:T(8,128)S(1)}) fusion(pred[1024,512]{0,1:T(8,128)(4,1)S(1)} %copy-done.6, bf16[1024,5,64]{0,2,1:T(8,128)(2,1)S(1)} %bitcast.112, f32[512,5,64]{0,2,1:T(8,128)S(1)} %copy-done.4, f32[5,64]{1,0:T(8,128)S(1)} %mul.316, f32[512,5]{0,1:T(8,128)S(1)} %add_rsqrt_fusion), kind=kOutput, calls=%fused_computation.2 | convolution fusion | flops 343895040 | bytes 12342528 | tf_op jit(solution)/shard_map/qhd,khd->qhk/dot_general | solution.py:319
  48.8 2.1 %fusion.16 = bf16[5,64,1024]{2,1,0:T(8,128)(2,1)S(1)} fusion(bf16[512,5,64]{0,2,1:T(8,128)(2,1)S(1)} %copy-done.7, f32[5,512,1024]{2,1,0:T(8,128)S(1)} %get-tuple-element.32, pred[1024,512]{0,1:T(8,128)(4,1)S(1)} %copy-done.6), kind=kOutput, calls=%fused_computation.24 | convolution fusion | flops 343736320 | bytes 11993088 | tf_op jit(solution)/shard_map/qhk,khd->qhd/dot_general | solution.py:325
  50.9 3.0 %fusion.2 = (bf16[1024,5]{0,1:T(8,128)(2,1)S(1)}, f32[5,512,1024]{2,1,0:T(8,128)S(1)}) fusion(pred[1024,512]{0,1:T(8,128)(4,1)S(1)} %copy-done.5, bf16[1024,5,64]{0,2,1:T(8,128)(2,1)S(1)} %bitcast.111, f32[512,5,64]{0,2,1:T(8,128)S(1)} %copy-done.4, f32[5,64]{1,0:T(8,128)S(1)} %mul.316, f32[512,5]{0,1:T(8,128)S(1)} %add_rsqrt_fusion), kind=kOutput, calls=%fused_computation.4 | convolution fusion | flops 343895040 | bytes 12342528 | tf_op jit(solution)/shard_map/qhd,khd->qhk/dot_general | solution.py:319
  53.9 2.2 %fusion.19 = bf16[5,64,1024]{2,1,0:T(8,128)(2,1)S(1)} fusion(bf16[512,5,64]{0,2,1:T(8,128)(2,1)S(1)} %copy-done.7, f32[5,512,1024]{2,1,0:T(8,128)S(1)} %get-tuple-element.30, pred[1024,512]{0,1:T(8,128)(4,1)S(1)} %copy-done.5), kind=kOutput, calls=%fused_computation.25 | convolution fusion | flops 343736320 | bytes 11993088 | tf_op jit(solution)/shard_map/qhk,khd->qhd/dot_general | solution.py:325
  56.2 0.4 copy.66
  56.7 1.4 copy.59
  58.1 4.8 %all-to-all-start = ((bf16[8,256,325]{1,2,0:T(8,128)(2,1)}), bf16[8,256,325]{1,2,0:T(8,128)(2,1)}, u32[]{:S(2)}, u32[]{:S(2)}) async-start(bf16[8,256,325]{1,2,0:T(8,128)(2,1)} %copy.59), calls=%async_computation | async-start | bytes 2686976 | tf_op jit(solution)/shard_map/all_to_all | solution.py:337
  63.0 1.0 multiply_reduce_fusion.5
  64.0 0.2 and_and_fusion
  64.2 2.5 %fusion.61 = (f32[5,256]{1,0:T(8,128)S(1)}, bf16[5,256,256]{1,2,0:T(8,128)(2,1)}) fusion(f32[256,5,32]{0,2,1:T(8,128)} %get-tuple-element.18, f32[256,5,32]{0,2,1:T(8,128)S(1)} %get-tuple-element.17, f32[256,5]{0,1:T(8,128)S(1)} %add_rsqrt_fusion.1, f32[5,64]{1,0:T(8,128)S(1)} %mul.316, f32[256,5,64]{0,2,1:T(8,128)} %fusion.42, ...), kind=kOutput, calls=%fused_computation.133 | convolution fusion | flops 43744000 | bytes 1387776 | tf_op jit(solution)/shard_map/qhd,khd->hqk/dot_general | solution.py:267
  66.7 13.4 %all-to-all-done = bf16[8,256,325]{1,2,0:T(8,128)(2,1)} async-done(((bf16[8,256,325]{1,2,0:T(8,128)(2,1)}), bf16[8,256,325]{1,2,0:T(8,128)(2,1)}, u32[]{:S(2)}, u32[]{:S(2)}) %all-to-all-start) | async-done | bytes 1331232 | tf_op jit(solution)/shard_map/all_to_all | solution.py:337
  80.1 1.6 %convert_reduce_fusion = f32[256,325]{0,1:T(8,128)S(1)} fusion(bf16[8,256,325]{1,2,0:T(8,128)(2,1)} %all-to-all-done), kind=kLoop, calls=%fused_computation.15 | loop fusion | flops 1248000 | bytes 1664000 | tf_op jit(solution)/shard_map/reduce_sum | solution.py:344
  81.8 0.2 fusion.32
  82.1 18.3 %all_gather.7 = bf16[256,1280]{0,1:T(8,128)(2,1)S(1)} all-gather(bf16[256,320]{0,1:T(8,128)(2,1)S(1)} %bitcast.119), channel_id=1, replica_groups=mesh['pages'=8,'mp'=4] {'mp'}, dimensions={1}, use_global_device_ids=true | all-gather | bytes 819200 | tf_op jit(solution)/shard_map/all_gather | solution.py:355
  100.3 1.1 multiply_reduce_fusion.1
  101.5 0.5 multiply_reduce_fusion
  102.0 0.4 multiply_convert_fusion
  102.4 1.9 %convolution_bitcast_fusion = f32[2,256,1280]{2,1,0:T(8,128)S(1)} fusion(bf16[2,1280,1280]{2,1,0:T(8,128)(2,1)S(1)} %bitcast.108, bf16[256,1280]{1,0:T(8,128)(2,1)S(1)} %multiply_convert_fusion), kind=kOutput, calls=%fused_computation.14 | convolution fusion | flops 1677721600 | bytes 9830400 | tf_op jit(solution)/shard_map/sd,jdf->jsf/dot_general | solution.py:362
  104.3 0.3 copy-done.11
  104.6 2.1 %convolution_convert_fusion = bf16[256,1280]{1,0:T(8,128)(2,1)} fusion(bf16[1280,1280]{1,0:T(8,128)(2,1)S(1)} %copy-done.11, f32[2,256,1280]{2,1,0:T(8,128)S(1)} %convolution_bitcast_fusion, f32[1280]{0:T(1024)S(1)} %get-tuple-element.8, f32[1280]{0:T(1024)S(1)} %get-tuple-element.7), kind=kOutput, calls=%fused_computation.16 | convolution fusion | flops 841809920 | bytes 6563840 | tf_op jit(solution)/shard_map/dot_general | solution.py:368
  106.7 4.2 %all-to-all-start.1 = ((bf16[4,64,1280]{2,1,0:T(8,128)(2,1)}), bf16[4,64,1280]{2,1,0:T(8,128)(2,1)}, u32[]{:S(2)}, u32[]{:S(2)}) async-start(bf16[4,64,1280]{2,1,0:T(8,128)(2,1)} %bitcast.113), calls=%async_computation.1 | async-start | bytes 1310720 | tf_op jit(solution)/shard_map/all_to_all | solution.py:367
  111.0 15.4 %all-to-all-done.1 = bf16[4,64,1280]{2,1,0:T(8,128)(2,1)} async-done(((bf16[4,64,1280]{2,1,0:T(8,128)(2,1)}), bf16[4,64,1280]{2,1,0:T(8,128)(2,1)}, u32[]{:S(2)}, u32[]{:S(2)}) %all-to-all-start.1) | async-done | bytes 655392 | tf_op jit(solution)/shard_map/all_to_all | solution.py:367
  126.3 1.3 convert_reduce_fusion.1
  127.7 0.3 multiply_reduce_fusion.3
  128.0 0.9 multiply_convert_fusion.2
  (66 shorter events, 1.0 us)
Async XLA Ops:
  6.5 93.8 %copy-start = (bf16[1280,1280]{1,0:T(8,128)(2,1)S(1)}, bf16[1280,1280]{1,0:T(8,128)(2,1)}, u32[]{:S(2)}) copy-start(bf16[1280,1280]{1,0:T(8,128)(2,1)} %param.15) | copy-start | bytes 9830404
  6.5 37.6 %all-gather.2.cloned.1.call-start = ((), (), s32[]{:S(2)}) async-start(), calls=%async_computation.2 | async-start | bytes 1474560 | tf_op jit(solution)/shard_map/all_gather | solution.py:265
  24.7 6.0 %copy-start.12 = (s32[32]{0:T(128)S(1)}, s32[32]{0:T(128)}, u32[]{:S(2)}) copy-start(s32[32]{0:T(128)} %param.23) | copy-start | bytes 388
  44.2 1.5 %copy-start.4 = (f32[512,5,64]{0,2,1:T(8,128)S(1)}, f32[512,5,64]{0,2,1:T(8,128)}, u32[]{:S(2)}) copy-start(f32[512,5,64]{0,2,1:T(8,128)} %reshape.379) | copy-start | bytes 1966084
  44.2 1.6 %copy-start.6 = (pred[1024,512]{0,1:T(8,128)(4,1)S(1)}, pred[1024,512]{0,1:T(8,128)(4,1)}, u32[]{:S(2)}) copy-start(pred[1024,512]{0,1:T(8,128)(4,1)} %get-tuple-element.25) | copy-start | bytes 1572868
  45.8 3.0 %copy-start.7 = (bf16[512,5,64]{0,2,1:T(8,128)(2,1)S(1)}, bf16[512,5,64]{0,2,1:T(8,128)(2,1)}, u32[]{:S(2)}) copy-start(bf16[512,5,64]{0,2,1:T(8,128)(2,1)} %reshape_reshape.3) | copy-start | bytes 983044
  48.8 2.1 %copy-start.5 = (pred[1024,512]{0,1:T(8,128)(4,1)S(1)}, pred[1024,512]{0,1:T(8,128)(4,1)}, u32[]{:S(2)}) copy-start(pred[1024,512]{0,1:T(8,128)(4,1)} %get-tuple-element.26) | copy-start | bytes 1572868
  58.1 5.8 %copy-start.9 = (f32[2,1280]{1,0:T(2,128)S(1)}, f32[2,1280]{1,0:T(2,128)}, u32[]{:S(2)}) copy-start(f32[2,1280]{1,0:T(2,128)} %param.19) | copy-start | bytes 30724
  58.1 5.9 %copy-start.10 = (f32[2,1280]{1,0:T(2,128)S(1)}, f32[2,1280]{1,0:T(2,128)}, u32[]{:S(2)}) copy-start(f32[2,1280]{1,0:T(2,128)} %param.20) | copy-start | bytes 30724
  58.1 22.0 %all-to-all-start = ((bf16[8,256,325]{1,2,0:T(8,128)(2,1)}), bf16[8,256,325]{1,2,0:T(8,128)(2,1)}, u32[]{:S(2)}, u32[]{:S(2)}) async-start(bf16[8,256,325]{1,2,0:T(8,128)(2,1)} %copy.59), calls=%async_computation | async-start | bytes 2686976 | tf_op jit(solution)/shard_map/all_to_all | solution.py:337
  66.7 15.1 %copy-start.8 = (bf16[1,256,320]{1,2,0:T(8,128)(2,1)S(1)}, bf16[1,256,320]{1,2,0:T(8,128)(2,1)}, u32[]{:S(2)}) copy-start(bf16[1,256,320]{1,2,0:T(8,128)(2,1)} %get-tuple-element.16) | copy-start | bytes 491524
  80.1 1.7 %copy-start.13 = (bf16[5,256,256]{1,2,0:T(8,128)(2,1)S(1)}, bf16[5,256,256]{1,2,0:T(8,128)(2,1)}, u32[]{:S(2)}) copy-start(bf16[5,256,256]{1,2,0:T(8,128)(2,1)} %get-tuple-element.34) | copy-start | bytes 1966084
  81.8 20.6 %slice-start = ((s8[6553600]{0:T(1024)(128)(4,1)}), s8[4194304]{0:T(1024)(128)(4,1)S(1)}, s32[]{:S(2)}) async-start(s8[6553600]{0:T(1024)(128)(4,1)} %bitcast.107), calls=%async_computation.3 | async-start | bytes 8388608
  100.3 1.1 copy-start.1
  100.3 2.1 %slice-start.1 = ((s8[6553600]{0:T(1024)(128)(4,1)}), s8[2359296]{0:T(1024)(128)(4,1)S(1)}, s32[]{:S(2)}) async-start(s8[6553600]{0:T(1024)(128)(4,1)} %bitcast.107), calls=%async_computation.4 | async-start | bytes 4718592
  102.4 1.9 %copy-start.2 = (bf16[256,1280]{1,0:T(8,128)(2,1)}, bf16[256,1280]{1,0:T(8,128)(2,1)S(1)}, u32[]{:S(2)}) copy-start(bf16[256,1280]{1,0:T(8,128)(2,1)S(1)} %multiply_convert_fusion) | copy-start | bytes 1966084
  102.4 2.2 %copy-start.11 = (bf16[1280,1280]{1,0:T(8,128)(2,1)S(1)}, bf16[1280,1280]{1,0:T(8,128)(2,1)}, u32[]{:S(2)}) copy-start(bf16[1280,1280]{1,0:T(8,128)(2,1)} %param.17) | copy-start | bytes 9830404
  106.7 19.6 %all-to-all-start.1 = ((bf16[4,64,1280]{2,1,0:T(8,128)(2,1)}), bf16[4,64,1280]{2,1,0:T(8,128)(2,1)}, u32[]{:S(2)}, u32[]{:S(2)}) async-start(bf16[4,64,1280]{2,1,0:T(8,128)(2,1)} %bitcast.113), calls=%async_computation.1 | async-start | bytes 1310720 | tf_op jit(solution)/shard_map/all_to_all | solution.py:367
  126.3 1.4 %copy-start.3 = (bf16[256,1280]{1,0:T(8,128)(2,1)S(1)}, bf16[256,1280]{1,0:T(8,128)(2,1)}, u32[]{:S(2)}) copy-start(bf16[256,1280]{1,0:T(8,128)(2,1)} %copy-done.2) | copy-start | bytes 1966084
Sparse Core Ops, SparseCore 0:
  18.2 25.9 all-gather.1

commit v9 on v8

--- a/solution.py
+++ b/solution.py
@@ -352,8 +352,23 @@
         :, :, None
     ]
     attention_local = mixed.reshape(slot_count, local_width).astype(jnp.bfloat16)
-    attention = lax.all_gather(attention_local, "mp", axis=1, tiled=True)
-    projected_out = jnp.dot(attention, w_out, preferred_element_type=jnp.float32)
+    projected_out = jnp.dot(
+        attention_local,
+        lax.dynamic_slice_in_dim(w_out, mp_index * local_width, local_width, 0),
+        preferred_element_type=jnp.float32,
+    )
+    for shift in range(1, mp_count):
+        arrived = lax.ppermute(
+            attention_local,
+            "mp",
+            [(source, (source + shift) % mp_count) for source in range(mp_count)],
+        )
+        origin = (mp_index + mp_count - shift) % mp_count
+        projected_out = projected_out + jnp.dot(
+            arrived,
+            lax.dynamic_slice_in_dim(w_out, origin * local_width, local_width, 0),
+            preferred_element_type=jnp.float32,
+        )
     residual_in = state_in.astype(jnp.float32)
     state_mid = rms_rows(
         residual_in + eigen_rates[0][None, :] * (rms_rows(projected_out) - residual_in)

time: 137 us -> 139 us (1.015)
  blocking collectives: 18.3 us -> 0 us
  waiting for transfers between devices: 39.2 us -> 52.8 us
  starting transfers between devices: 8.99 us -> 15.4 us
    all_gather x1 -> x0, blocking collectives: 18.3 us -> none  [shards_heads(): attention = lax.all_gather(attention_local, 'mp', axis=1, tiled=True)]
    ppermute x0 -> x3, waiting for transfers between devices: none -> 11.6 us  [shards_heads(): lax.ppermute(attention_local, 'mp', [(source, (source + shift) % mp_count...]
    ppermute x0 -> x3, starting transfers between devices: none -> 4.48 us  [shards_heads(): lax.ppermute(attention_local, 'mp', [(source, (source + shift) % mp_count...]
    all_to_all x1, waiting for transfers between devices: 15.4 us -> 17.4 us  [shards_heads(): lax.all_to_all(jnp.dot(hidden, w_down, preferred_element_type=jnp.float32...]
    all_to_all x1, starting transfers between devices: 4.16 us -> 6.12 us  [shards_heads(): lax.all_to_all(jnp.dot(hidden, w_down, preferred_element_type=jnp.float32...]
  transfers between devices with their start and end apart: 3 -> 6, of which waited for: 3 -> 5; matrix products, arithmetic and copies ran while one was open for 14% -> 15% of each run, Pallas kernels for 0% -> 0%
where the time goes in v9:
time: 139 us
  waiting for transfers between devices  52.8 us (38%)
  matrix products  22 us (16%)
  local copies, waits for them, and re-layouts  18 us (13%)
  other arithmetic  16.6 us (12%)
  starting transfers between devices  15.4 us (11%)
  between operations  13.8 us (10%)
    all_to_all x1, waiting for transfers between devices, shards_heads(): lax.all_to_all(jnp.dot(hidden, w_down, preferred_element_type=jnp.float32...  17.4 us
    all_to_all x1, waiting for transfers between devices, shards_heads(): lax.all_to_all(jnp.concatenate(pieces, axis=0), 'pages', 0, 0, tiled=True)  13.4 us
    ppermute x3, waiting for transfers between devices, shards_heads(): lax.ppermute(attention_local, 'mp', [(source, (source + shift) % mp_count...  11.6 us
    all_gather x1, waiting for transfers between devices, shards_heads(): gathered = lax.all_gather(queries, 'pages', axis=0, tiled=True)  10.4 us
    all_to_all x1, starting transfers between devices, shards_heads(): lax.all_to_all(jnp.dot(hidden, w_down, preferred_element_type=jnp.float32...  6.12 us
    dot_general x2, matrix products, shards_heads(): jnp.einsum('qhd,khd->qhk', query_heads, key_heads, preferred_element_type...  5.97 us
    all_to_all x1, starting transfers between devices, shards_heads(): lax.all_to_all(jnp.concatenate(pieces, axis=0), 'pages', 0, 0, tiled=True)  4.84 us
    ppermute x3, starting transfers between devices, shards_heads(): lax.ppermute(attention_local, 'mp', [(source, (source + shift) % mp_count...  4.48 us
  transfers between devices with their start and end apart: 6, of which 5 were waited for; matrix products, arithmetic and copies ran while one was open for 15% of the time, Pallas kernels for 0%

profile of v9, /device:TPU:2, one launch (start us, length us, event | category | flops | bytes accessed | tf_op | source)
XLA Modules:
  0.0 138.6 jit_solution(16886169698035163530)
XLA Ops:
  6.6 1.4 %fusion.23 = f32[256]{0:T(256)S(1)} fusion(bf16[256,1280]{1,0:T(8,128)(2,1)} %param.13), kind=kLoop, calls=%fused_computation.31 | loop fusion | flops 982784 | bytes 656384 | tf_op jit(solution)/shard_map/reduce_sum | solution.py:16
  8.0 0.7 reduce_window_sum.11
  8.7 0.7 sub.46
  9.4 0.8 select_reduce_fusion.2
  10.2 2.8 %fusion.30 = bf16[3,256,320]{1,2,0:T(8,128)(2,1)S(1)} fusion(bf16[3,1280,320]{1,2,0:T(8,128)(2,1)} %param.14, bf16[256,1280]{1,0:T(8,128)(2,1)} %param.13, f32[256]{0:T(256)S(1)} %add_rsqrt_fusion.5), kind=kOutput, calls=%fused_computation.45 | convolution fusion | flops 630374400 | bytes 3605504 | tf_op jit(solution)/shard_map/sd,jdc->jsc/dot_general | solution.py:255
  13.0 0.7 fusion.71
  14.0 0.7 multiply_subtract_fusion
  14.8 0.8 fusion.49
  15.5 0.8 dynamic_slice.45
  16.3 1.7 %fusion.48 = bf16[256,320]{0,1:T(8,128)(2,1)} fusion(f32[256,5,64]{0,2,1:T(8,128)} %fusion.49, f32[320]{0:T(512)S(1)} %dynamic_slice.45), kind=kLoop, calls=%fused_computation.72 | loop fusion | flops 163840 | bytes 492800 | tf_op jit(solution)/shard_map/convert_element_type | solution.py:260
  18.3 2.4 %constant_dynamic-slice_fusion = (bf16[4,128,320]{2,1,0:T(8,128)(2,1)}, bf16[4,128,320]{2,1,0:T(8,128)(2,1)}) fusion(bf16[4,128,1280]{2,1,0:T(8,128)(2,1)} %param.21, s32[]{:T(128)S(6)} %select_n.86, bf16[4,128,1280]{2,1,0:T(8,128)(2,1)} %param.22), kind=kLoop, calls=%fused_computation.115 | loop fusion | bytes 1310724 | tf_op jit(solution)/shard_map/dynamic_slice | solution.py:295
  20.7 1.9 %copy.63 = bf16[4,128,320]{1,2,0:T(8,128)(2,1)} copy(bf16[4,128,320]{2,1,0:T(8,128)(2,1)} %get-tuple-element.39) | data formatting | bytes 655360
  22.6 2.1 %copy.56 = f32[4,128,320]{1,0,2:T(4,128)} copy(bf16[4,128,320]{1,2,0:T(8,128)(2,1)} %copy.63) | data formatting | bytes 983040 | tf_op jit(solution)/shard_map/convert_element_type | solution.py:297
  24.7 2.2 %reshape.379 = f32[512,5,64]{0,2,1:T(8,128)} reshape(f32[4,128,320]{1,0,2:T(4,128)} %copy.56) | data formatting | bytes 1310720 | tf_op jit(solution)/shard_map/convert_element_type | solution.py:297
  26.9 1.9 %copy.54 = bf16[4,128,320]{1,0,2:T(4,128)(2,1)} copy(bf16[4,128,320]{2,1,0:T(8,128)(2,1)} %get-tuple-element.40) | data formatting | bytes 655360 | tf_op jit(solution)/shard_map/dynamic_slice | solution.py:301
  28.9 1.8 %reshape_reshape.3 = bf16[512,5,64]{0,2,1:T(8,128)(2,1)} reshape(bf16[4,128,320]{1,0,2:T(4,128)(2,1)} %copy.54) | data formatting | bytes 655360 | tf_op jit(solution)/shard_map/reshape;reshape | solution.py:306
  30.9 1.2 multiply_reduce_fusion.2
  32.2 1.6 %broadcast_compare_fusion.1 = (pred[1024,512]{0,1:T(8,128)(4,1)}, pred[1024,512]{0,1:T(8,128)(4,1)}) fusion(s32[1024]{0:T(1024)S(1)} %bitcast.126, s32[512]{0:T(512)S(1)} %broadcast_bitcast_fusion, s32[1024]{0:T(1024)S(1)} %bitcast.127), kind=kLoop, calls=%fused_computation.51 | loop fusion | flops 1048576 | bytes 1058816 | tf_op jit(solution)/shard_map/eq | solution.py:322
  33.8 10.4 %all-gather.2.cloned.1.call-done = bf16[2048,320]{0,1:T(8,128)(2,1)} async-done(((bf16[256,320]{0,1:T(8,128)(2,1)}), bf16[2048,320]{0,1:T(8,128)(2,1)}) %all-gather.2.cloned.1.call-update) | async-done | bytes 1310736 | tf_op jit(solution)/shard_map/all_gather | solution.py:265
  44.2 1.5 %fusion.70 = (bf16[1024,320]{0,1:T(8,128)(2,1)S(1)}, bf16[1024,320]{0,1:T(8,128)(2,1)S(1)}) fusion(bf16[2048,320]{0,1:T(8,128)(2,1)} %all-gather.2.cloned.1.call-done), kind=kLoop, calls=%fused_computation.144 | loop fusion | bytes 2621440 | tf_op jit(solution)/shard_map/slice | solution.py:312
  45.8 3.0 %fusion = (bf16[1024,5]{0,1:T(8,128)(2,1)S(1)}, f32[5,512,1024]{2,1,0:T(8,128)S(1)}) fusion(pred[1024,512]{0,1:T(8,128)(4,1)S(1)} %copy-done.6, bf16[1024,5,64]{0,2,1:T(8,128)(2,1)S(1)} %bitcast.114, f32[512,5,64]{0,2,1:T(8,128)S(1)} %copy-done.4, f32[5,64]{1,0:T(8,128)S(1)} %mul.326, f32[512,5]{0,1:T(8,128)S(1)} %add_rsqrt_fusion), kind=kOutput, calls=%fused_computation.2 | convolution fusion | flops 343895040 | bytes 12342528 | tf_op jit(solution)/shard_map/qhd,khd->qhk/dot_general | solution.py:319
  48.8 2.1 %fusion.17 = bf16[5,64,1024]{2,1,0:T(8,128)(2,1)S(1)} fusion(bf16[512,5,64]{0,2,1:T(8,128)(2,1)S(1)} %copy-done.7, f32[5,512,1024]{2,1,0:T(8,128)S(1)} %get-tuple-element.32, pred[1024,512]{0,1:T(8,128)(4,1)S(1)} %copy-done.6), kind=kOutput, calls=%fused_computation.27 | convolution fusion | flops 343736320 | bytes 11993088 | tf_op jit(solution)/shard_map/qhk,khd->qhd/dot_general | solution.py:325
  50.9 3.0 %fusion.2 = (bf16[1024,5]{0,1:T(8,128)(2,1)S(1)}, f32[5,512,1024]{2,1,0:T(8,128)S(1)}) fusion(pred[1024,512]{0,1:T(8,128)(4,1)S(1)} %copy-done.5, bf16[1024,5,64]{0,2,1:T(8,128)(2,1)S(1)} %bitcast.113, f32[512,5,64]{0,2,1:T(8,128)S(1)} %copy-done.4, f32[5,64]{1,0:T(8,128)S(1)} %mul.326, f32[512,5]{0,1:T(8,128)S(1)} %add_rsqrt_fusion), kind=kOutput, calls=%fused_computation.4 | convolution fusion | flops 343895040 | bytes 12342528 | tf_op jit(solution)/shard_map/qhd,khd->qhk/dot_general | solution.py:319
  53.9 2.2 %fusion.20 = bf16[5,64,1024]{2,1,0:T(8,128)(2,1)S(1)} fusion(bf16[512,5,64]{0,2,1:T(8,128)(2,1)S(1)} %copy-done.7, f32[5,512,1024]{2,1,0:T(8,128)S(1)} %get-tuple-element.30, pred[1024,512]{0,1:T(8,128)(4,1)S(1)} %copy-done.5), kind=kOutput, calls=%fused_computation.28 | convolution fusion | flops 343736320 | bytes 11993088 | tf_op jit(solution)/shard_map/qhk,khd->qhd/dot_general | solution.py:325
  56.2 0.4 copy.66
  56.7 1.4 copy.59
  58.1 4.8 %all-to-all-start = ((bf16[8,256,325]{1,2,0:T(8,128)(2,1)}), bf16[8,256,325]{1,2,0:T(8,128)(2,1)}, u32[]{:S(2)}, u32[]{:S(2)}) async-start(bf16[8,256,325]{1,2,0:T(8,128)(2,1)} %copy.59), calls=%async_computation | async-start | bytes 2686976 | tf_op jit(solution)/shard_map/all_to_all | solution.py:337
  63.0 1.0 multiply_reduce_fusion.5
  64.2 2.5 %fusion.72 = (f32[5,256]{1,0:T(8,128)S(1)}, bf16[5,256,256]{1,2,0:T(8,128)(2,1)}) fusion(f32[256,5,32]{0,2,1:T(8,128)} %get-tuple-element.18, f32[256,5,32]{0,2,1:T(8,128)S(1)} %get-tuple-element.17, f32[256,5]{0,1:T(8,128)S(1)} %add_rsqrt_fusion.1, f32[5,64]{1,0:T(8,128)S(1)} %mul.326, f32[256,5,64]{0,2,1:T(8,128)} %fusion.49, ...), kind=kOutput, calls=%fused_computation.146 | convolution fusion | flops 43744000 | bytes 1387776 | tf_op jit(solution)/shard_map/qhd,khd->hqk/dot_general | solution.py:267
  66.7 13.4 %all-to-all-done = bf16[8,256,325]{1,2,0:T(8,128)(2,1)} async-done(((bf16[8,256,325]{1,2,0:T(8,128)(2,1)}), bf16[8,256,325]{1,2,0:T(8,128)(2,1)}, u32[]{:S(2)}, u32[]{:S(2)}) %all-to-all-start) | async-done | bytes 1331232 | tf_op jit(solution)/shard_map/all_to_all | solution.py:337
  80.1 1.6 %convert_reduce_fusion = f32[256,325]{0,1:T(8,128)S(1)} fusion(bf16[8,256,325]{1,2,0:T(8,128)(2,1)} %all-to-all-done), kind=kLoop, calls=%fused_computation.18 | loop fusion | flops 1248000 | bytes 1664000 | tf_op jit(solution)/shard_map/reduce_sum | solution.py:344
  82.0 3.4 %collective-permute-start.2 = (bf16[256,320]{0,1:T(8,128)(2,1)S(1)}, bf16[256,320]{0,1:T(8,128)(2,1)S(1)}, u32[]{:S(2)}, u32[]{:S(2)}) collective-permute-start(bf16[256,320]{0,1:T(8,128)(2,1)S(1)} %bitcast.121), channel_id=1, source_target_pairs={{0,3},{1,0},{2,1},{3,2},{4,7},{5,4},{6,5},{7,6},{8,11},{9,8},{10,9... | collective-permute-start | bytes 491528 | tf_op jit(solution)/shard_map/ppermute | solution.py:361
  85.4 1.1 collective-permute-start
  86.5 0.5 fusion.38
  87.1 10.2 %collective-permute-done = bf16[256,320]{0,1:T(8,128)(2,1)S(1)} collective-permute-done((bf16[256,320]{0,1:T(8,128)(2,1)S(1)}, bf16[256,320]{0,1:T(8,128)(2,1)S(1)}, u32[]{:S(2)}, u32[]{:S(2)}) %collective-permute-start) | collective-permute-done | bytes 163872 | tf_op jit(solution)/shard_map/ppermute | solution.py:361
  97.2 0.5 convolution_add_fusion.1
  97.8 0.5 fusion.34
  98.3 1.4 collective-permute-done.1
  99.7 0.7 multiply_reduce_fusion.1
  100.4 0.5 multiply_reduce_fusion
  100.9 0.4 multiply_convert_fusion
  101.4 1.9 %convolution_bitcast_fusion = f32[2,256,1280]{2,1,0:T(8,128)S(1)} fusion(bf16[2,1280,1280]{2,1,0:T(8,128)(2,1)S(1)} %bitcast.110, bf16[256,1280]{1,0:T(8,128)(2,1)S(1)} %multiply_convert_fusion), kind=kOutput, calls=%fused_computation.14 | convolution fusion | flops 1677721600 | bytes 9830400 | tf_op jit(solution)/shard_map/sd,jdf->jsf/dot_general | solution.py:377
  103.2 0.3 copy-done.11
  103.5 2.1 %convolution_convert_fusion = bf16[256,1280]{1,0:T(8,128)(2,1)} fusion(bf16[1280,1280]{1,0:T(8,128)(2,1)S(1)} %copy-done.11, f32[2,256,1280]{2,1,0:T(8,128)S(1)} %convolution_bitcast_fusion, f32[1280]{0:T(1024)S(1)} %get-tuple-element.8, f32[1280]{0:T(1024)S(1)} %get-tuple-element.7), kind=kOutput, calls=%fused_computation.19 | convolution fusion | flops 841809920 | bytes 6563840 | tf_op jit(solution)/shard_map/dot_general | solution.py:383
  105.6 6.1 %all-to-all-start.1 = ((bf16[4,64,1280]{2,1,0:T(8,128)(2,1)}), bf16[4,64,1280]{2,1,0:T(8,128)(2,1)}, u32[]{:S(2)}, u32[]{:S(2)}) async-start(bf16[4,64,1280]{2,1,0:T(8,128)(2,1)} %bitcast.115), calls=%async_computation.1 | async-start | bytes 1310720 | tf_op jit(solution)/shard_map/all_to_all | solution.py:382
  111.8 17.4 %all-to-all-done.1 = bf16[4,64,1280]{2,1,0:T(8,128)(2,1)} async-done(((bf16[4,64,1280]{2,1,0:T(8,128)(2,1)}), bf16[4,64,1280]{2,1,0:T(8,128)(2,1)}, u32[]{:S(2)}, u32[]{:S(2)}) %all-to-all-start.1) | async-done | bytes 655392 | tf_op jit(solution)/shard_map/all_to_all | solution.py:382
  129.2 1.3 convert_reduce_fusion.1
  130.9 0.9 multiply_convert_fusion.2
  (74 shorter events, 2.3 us)
Async XLA Ops:
  6.5 80.0 %copy-start = (bf16[1280,1280]{1,0:T(8,128)(2,1)S(1)}, bf16[1280,1280]{1,0:T(8,128)(2,1)}, u32[]{:S(2)}) copy-start(bf16[1280,1280]{1,0:T(8,128)(2,1)} %param.15) | copy-start | bytes 9830404
  6.5 37.6 %all-gather.2.cloned.1.call-start = ((), (), s32[]{:S(2)}) async-start(), calls=%async_computation.2 | async-start | bytes 1474560 | tf_op jit(solution)/shard_map/all_gather | solution.py:265
  24.7 6.0 %copy-start.12 = (s32[32]{0:T(128)S(1)}, s32[32]{0:T(128)}, u32[]{:S(2)}) copy-start(s32[32]{0:T(128)} %param.23) | copy-start | bytes 388
  44.2 1.5 %copy-start.4 = (f32[512,5,64]{0,2,1:T(8,128)S(1)}, f32[512,5,64]{0,2,1:T(8,128)}, u32[]{:S(2)}) copy-start(f32[512,5,64]{0,2,1:T(8,128)} %reshape.379) | copy-start | bytes 1966084
  44.2 1.6 %copy-start.6 = (pred[1024,512]{0,1:T(8,128)(4,1)S(1)}, pred[1024,512]{0,1:T(8,128)(4,1)}, u32[]{:S(2)}) copy-start(pred[1024,512]{0,1:T(8,128)(4,1)} %get-tuple-element.25) | copy-start | bytes 1572868
  45.8 3.0 %copy-start.7 = (bf16[512,5,64]{0,2,1:T(8,128)(2,1)S(1)}, bf16[512,5,64]{0,2,1:T(8,128)(2,1)}, u32[]{:S(2)}) copy-start(bf16[512,5,64]{0,2,1:T(8,128)(2,1)} %reshape_reshape.3) | copy-start | bytes 983044
  48.8 2.1 %copy-start.5 = (pred[1024,512]{0,1:T(8,128)(4,1)S(1)}, pred[1024,512]{0,1:T(8,128)(4,1)}, u32[]{:S(2)}) copy-start(pred[1024,512]{0,1:T(8,128)(4,1)} %get-tuple-element.26) | copy-start | bytes 1572868
  58.1 5.8 %copy-start.9 = (f32[2,1280]{1,0:T(2,128)S(1)}, f32[2,1280]{1,0:T(2,128)}, u32[]{:S(2)}) copy-start(f32[2,1280]{1,0:T(2,128)} %param.19) | copy-start | bytes 30724
  58.1 5.9 %copy-start.10 = (f32[2,1280]{1,0:T(2,128)S(1)}, f32[2,1280]{1,0:T(2,128)}, u32[]{:S(2)}) copy-start(f32[2,1280]{1,0:T(2,128)} %param.20) | copy-start | bytes 30724
  58.1 22.0 %all-to-all-start = ((bf16[8,256,325]{1,2,0:T(8,128)(2,1)}), bf16[8,256,325]{1,2,0:T(8,128)(2,1)}, u32[]{:S(2)}, u32[]{:S(2)}) async-start(bf16[8,256,325]{1,2,0:T(8,128)(2,1)} %copy.59), calls=%async_computation | async-start | bytes 2686976 | tf_op jit(solution)/shard_map/all_to_all | solution.py:337
  66.7 15.1 %copy-start.8 = (bf16[1,256,320]{1,2,0:T(8,128)(2,1)S(1)}, bf16[1,256,320]{1,2,0:T(8,128)(2,1)}, u32[]{:S(2)}) copy-start(bf16[1,256,320]{1,2,0:T(8,128)(2,1)} %get-tuple-element.16) | copy-start | bytes 491524
  80.1 1.7 %copy-start.13 = (bf16[5,256,256]{1,2,0:T(8,128)(2,1)S(1)}, bf16[5,256,256]{1,2,0:T(8,128)(2,1)}, u32[]{:S(2)}) copy-start(bf16[5,256,256]{1,2,0:T(8,128)(2,1)} %get-tuple-element.34) | copy-start | bytes 1966084
  82.0 15.7 %collective-permute-start.2 = (bf16[256,320]{0,1:T(8,128)(2,1)S(1)}, bf16[256,320]{0,1:T(8,128)(2,1)S(1)}, u32[]{:S(2)}, u32[]{:S(2)}) collective-permute-start(bf16[256,320]{0,1:T(8,128)(2,1)S(1)} %bitcast.121), channel_id=1, source_target_pairs={{0,3},{1,0},{2,1},{3,2},{4,7},{5,4},{6,5},{7,6},{8,11},{9,8},{10,9... | collective-permute-start | bytes 491528 | tf_op jit(solution)/shard_map/ppermute | solution.py:361
  85.4 14.3 %collective-permute-start.1 = (bf16[256,320]{0,1:T(8,128)(2,1)S(1)}, bf16[256,320]{0,1:T(8,128)(2,1)S(1)}, u32[]{:S(2)}, u32[]{:S(2)}) collective-permute-start(bf16[256,320]{0,1:T(8,128)(2,1)S(1)} %bitcast.122), channel_id=1, source_target_pairs={{0,2},{1,3},{2,0},{3,1},{4,6},{5,7},{6,4},{7,5},{8,10},{9,11},{10,... | collective-permute-start | bytes 491528 | tf_op jit(solution)/shard_map/ppermute | solution.py:361
  85.4 11.8 %collective-permute-start = (bf16[256,320]{0,1:T(8,128)(2,1)S(1)}, bf16[256,320]{0,1:T(8,128)(2,1)S(1)}, u32[]{:S(2)}, u32[]{:S(2)}) collective-permute-start(bf16[256,320]{0,1:T(8,128)(2,1)S(1)} %bitcast.123), channel_id=1, source_target_pairs={{0,1},{1,2},{2,3},{3,0},{4,5},{5,6},{6,7},{7,4},{8,9},{9,10},{10,1... | collective-permute-start | bytes 491528 | tf_op jit(solution)/shard_map/ppermute | solution.py:361
  97.8 3.5 %slice-start = ((s8[6553600]{0:T(1024)(128)(4,1)}), s8[4194304]{0:T(1024)(128)(4,1)S(1)}, s32[]{:S(2)}) async-start(s8[6553600]{0:T(1024)(128)(4,1)} %bitcast.109), calls=%async_computation.3 | async-start | bytes 8388608
  98.3 2.1 %copy-start.1 = (bf16[256,1280]{1,0:T(8,128)(2,1)S(1)}, bf16[256,1280]{1,0:T(8,128)(2,1)}, u32[]{:S(2)}) copy-start(bf16[256,1280]{1,0:T(8,128)(2,1)} %param.13) | copy-start | bytes 1966084
  98.3 3.0 %slice-start.1 = ((s8[6553600]{0:T(1024)(128)(4,1)}), s8[2359296]{0:T(1024)(128)(4,1)S(1)}, s32[]{:S(2)}) async-start(s8[6553600]{0:T(1024)(128)(4,1)} %bitcast.109), calls=%async_computation.4 | async-start | bytes 4718592
  101.3 1.9 %copy-start.2 = (bf16[256,1280]{1,0:T(8,128)(2,1)}, bf16[256,1280]{1,0:T(8,128)(2,1)S(1)}, u32[]{:S(2)}) copy-start(bf16[256,1280]{1,0:T(8,128)(2,1)S(1)} %multiply_convert_fusion) | copy-start | bytes 1966084
  101.4 2.2 %copy-start.11 = (bf16[1280,1280]{1,0:T(8,128)(2,1)S(1)}, bf16[1280,1280]{1,0:T(8,128)(2,1)}, u32[]{:S(2)}) copy-start(bf16[1280,1280]{1,0:T(8,128)(2,1)} %param.17) | copy-start | bytes 9830404
  105.6 23.6 %all-to-all-start.1 = ((bf16[4,64,1280]{2,1,0:T(8,128)(2,1)}), bf16[4,64,1280]{2,1,0:T(8,128)(2,1)}, u32[]{:S(2)}, u32[]{:S(2)}) async-start(bf16[4,64,1280]{2,1,0:T(8,128)(2,1)} %bitcast.115), calls=%async_computation.1 | async-start | bytes 1310720 | tf_op jit(solution)/shard_map/all_to_all | solution.py:382
  129.2 1.4 %copy-start.3 = (bf16[256,1280]{1,0:T(8,128)(2,1)S(1)}, bf16[256,1280]{1,0:T(8,128)(2,1)}, u32[]{:S(2)}) copy-start(bf16[256,1280]{1,0:T(8,128)(2,1)} %copy-done.2) | copy-start | bytes 1966084
Sparse Core Ops, SparseCore 0:
  18.2 25.9 all-gather.1

commit v10 on v8

--- a/solution.py
+++ b/solution.py
@@ -262,7 +262,9 @@
         rotate(projected[1].astype(jnp.float32), position_shard, local_heads), scale_local, local_heads
     ).astype(jnp.bfloat16)
     value_rows = projected[2]
-    gathered = lax.all_gather(queries, "pages", axis=0, tiled=True)
+    gathered = lax.all_to_all(
+        jnp.tile(queries, (lax.axis_size("pages"), 1)), "pages", 0, 0, tiled=True
+    )
     scores = (
         jnp.einsum(
             "qhd,khd->hqk",

time: 137 us -> 131 us (0.956)
  between operations: 13.8 us -> 0.44 us
  local copies, waits for them, and re-layouts: 18 us -> 28.3 us
  waiting for transfers between devices: 39.2 us -> 30 us
  starting transfers between devices: 8.99 us -> 14.2 us
    all_gather x1 -> x0, waiting for transfers between devices: 10.4 us -> none  [shards_heads(): gathered = lax.all_gather(queries, 'pages', axis=0, tiled=True)]
    reshape x0 -> x2, local copies, waits for them, and re-layouts: none -> 4.79 us  [shards_heads(): query_heads = lax.slice_in_dim(gathered, chunk * row_count, (chunk + 1) *...]
    slice x1 -> x3, local copies, waits for them, and re-layouts: 1.47 us -> 6.05 us  [shards_heads(): lax.slice_in_dim(gathered, chunk * row_count, (chunk + 1) * row_count, ax...]
    all_to_all x0 -> x1, starting transfers between devices: none -> 4.25 us  [shards_heads(): lax.all_to_all(jnp.tile(queries, (lax.axis_size('pages'), 1)), 'pages', 0...]
    dot_general x2, matrix products: 5.97 us -> 7.48 us  [shards_heads(): jnp.einsum('qhd,khd->qhk', query_heads, key_heads, preferred_element_type...]
    unnamed x37 -> x39, local copies, waits for them, and re-layouts: 2.8 us -> 2.66 us
  transfers between devices with their start and end apart: 3 -> 3, of which waited for: 3 -> 3; matrix products, arithmetic and copies ran while one was open for 14% -> 15% of each run, Pallas kernels for 0% -> 0%
where the time goes in v10:
time: 131 us; the launch traced here: 130 us
  waiting for transfers between devices  30 us (23%)
  local copies, waits for them, and re-layouts  28.3 us (22%)
  matrix products  22.2 us (17%)
  blocking collectives  19.2 us (15%)
  other arithmetic  16 us (12%)
  starting transfers between devices  14.2 us (11%)
    all_gather x1, blocking collectives, shards_heads(): attention = lax.all_gather(attention_local, 'mp', axis=1, tiled=True)  19.2 us
    all_to_all x1, waiting for transfers between devices, shards_heads(): lax.all_to_all(jnp.dot(hidden, w_down, preferred_element_type=jnp.float32...  15.4 us
    all_to_all x1, waiting for transfers between devices, shards_heads(): lax.all_to_all(jnp.concatenate(pieces, axis=0), 'pages', 0, 0, tiled=True)  13.4 us
    dot_general x2, matrix products, shards_heads(): jnp.einsum('qhd,khd->qhk', query_heads, key_heads, preferred_element_type...  7.48 us
    slice x3, local copies, waits for them, and re-layouts, shards_heads(): lax.slice_in_dim(gathered, chunk * row_count, (chunk + 1) * row_count, ax...  6.05 us
    all_to_all x1, starting transfers between devices, shards_heads(): lax.all_to_all(jnp.concatenate(pieces, axis=0), 'pages', 0, 0, tiled=True)  5.8 us
    reshape x2, local copies, waits for them, and re-layouts, shards_heads(): query_heads = lax.slice_in_dim(gathered, chunk * row_count, (chunk + 1) *...  4.79 us
    convert_element_type x2, local copies, waits for them, and re-layouts, shards_heads(): cache_local.reshape(pages_here * page_len, local_width).astype(jnp.float32)  4.26 us
  transfers between devices with their start and end apart: 3, of which 3 were waited for; matrix products, arithmetic and copies ran while one was open for 15% of the time, Pallas kernels for 0%

profile of v10, /device:TPU:2, one launch (start us, length us, event | category | flops | bytes accessed | tf_op | source)
XLA Modules:
  0.0 130.3 jit_solution(9782373340213448304)
XLA Ops:
  0.0 1.4 %fusion.22 = f32[256]{0:T(256)S(1)} fusion(bf16[256,1280]{1,0:T(8,128)(2,1)} %param.13), kind=kLoop, calls=%fused_computation.28 | loop fusion | flops 982784 | bytes 656384 | tf_op jit(solution)/shard_map/reduce_sum | solution.py:16
  1.5 0.7 reduce_window_sum.11
  2.2 0.7 sub.37
  2.9 0.8 select_reduce_fusion.2
  3.7 2.8 %fusion.29 = bf16[3,256,320]{1,2,0:T(8,128)(2,1)S(1)} fusion(bf16[3,1280,320]{1,2,0:T(8,128)(2,1)} %param.14, bf16[256,1280]{1,0:T(8,128)(2,1)} %param.13, f32[256]{0:T(256)S(1)} %add_rsqrt_fusion.5), kind=kOutput, calls=%fused_computation.42 | convolution fusion | flops 630374400 | bytes 3605504 | tf_op jit(solution)/shard_map/sd,jdc->jsc/dot_general | solution.py:255
  6.5 0.7 fusion.60
  7.5 0.7 multiply_subtract_fusion
  8.3 0.8 fusion.42
  9.0 0.8 dynamic_slice.33
  9.8 1.1 fusion.41
  10.9 1.2 tile.2
  12.0 4.3 %all-to-all-start = ((bf16[8,256,320]{1,2,0:T(8,128)(2,1)}), bf16[8,256,320]{1,2,0:T(8,128)(2,1)}, u32[]{:S(2)}, u32[]{:S(2)}) async-start(bf16[8,256,320]{1,2,0:T(8,128)(2,1)} %tile.2), calls=%async_computation | async-start | bytes 2621440 | tf_op jit(solution)/shard_map/all_to_all | solution.py:265
  16.4 2.4 %constant_dynamic-slice_fusion = (bf16[4,128,320]{2,1,0:T(8,128)(2,1)}, bf16[4,128,320]{2,1,0:T(8,128)(2,1)}) fusion(bf16[4,128,1280]{2,1,0:T(8,128)(2,1)} %param.21, s32[]{:T(128)S(6)} %select_n.61, bf16[4,128,1280]{2,1,0:T(8,128)(2,1)} %param.22), kind=kLoop, calls=%fused_computation.105 | loop fusion | bytes 1310724 | tf_op jit(solution)/shard_map/dynamic_slice | solution.py:297
  19.1 1.9 %copy.71 = bf16[4,128,320]{1,2,0:T(8,128)(2,1)} copy(bf16[4,128,320]{2,1,0:T(8,128)(2,1)} %get-tuple-element.39) | data formatting | bytes 655360
  21.0 2.1 %copy.62 = f32[4,128,320]{1,0,2:T(4,128)} copy(bf16[4,128,320]{1,2,0:T(8,128)(2,1)} %copy.71) | data formatting | bytes 983040 | tf_op jit(solution)/shard_map/convert_element_type | solution.py:299
  23.1 2.2 %reshape.412 = f32[512,5,64]{0,2,1:T(8,128)} reshape(f32[4,128,320]{1,0,2:T(4,128)} %copy.62) | data formatting | bytes 1310720 | tf_op jit(solution)/shard_map/convert_element_type | solution.py:299
  25.3 1.9 %copy.60 = bf16[4,128,320]{1,0,2:T(4,128)(2,1)} copy(bf16[4,128,320]{2,1,0:T(8,128)(2,1)} %get-tuple-element.40) | data formatting | bytes 655360 | tf_op jit(solution)/shard_map/dynamic_slice | solution.py:303
  27.2 1.8 %reshape_reshape.3 = bf16[512,5,64]{0,2,1:T(8,128)(2,1)} reshape(bf16[4,128,320]{1,0,2:T(4,128)(2,1)} %copy.60) | data formatting | bytes 655360 | tf_op jit(solution)/shard_map/reshape;reshape | solution.py:308
  29.0 1.2 multiply_reduce_fusion.2
  30.3 1.6 %broadcast_compare_fusion.1 = (pred[1024,512]{0,1:T(8,128)(4,1)}, pred[1024,512]{0,1:T(8,128)(4,1)}) fusion(s32[1024]{0:T(1024)S(1)} %bitcast.121, s32[512]{0:T(512)S(1)} %broadcast_bitcast_fusion, s32[1024]{0:T(1024)S(1)} %bitcast.122), kind=kLoop, calls=%fused_computation.48 | loop fusion | flops 1048576 | bytes 1058816 | tf_op jit(solution)/shard_map/eq | solution.py:324
  31.9 1.2 all-to-all-done
  33.1 2.2 %fusion.59 = (bf16[4,256,320]{1,2,0:T(8,128)(2,1)S(1)}, bf16[4,256,320]{1,2,0:T(8,128)(2,1)}) fusion(bf16[8,256,320]{1,2,0:T(8,128)(2,1)} %all-to-all-done), kind=kLoop, calls=%fused_computation.131 | loop fusion | bytes 2621440 | tf_op jit(solution)/shard_map/slice | solution.py:314
  35.3 1.4 %copy.63 = bf16[4,256,320]{1,0,2:T(4,128)(2,1)} copy(bf16[4,256,320]{1,2,0:T(8,128)(2,1)S(1)} %get-tuple-element.12) | data formatting | bytes 1310720 | tf_op jit(solution)/shard_map/slice | solution.py:314
  36.7 2.4 %reshape.404 = bf16[1024,5,64]{0,2,1:T(8,128)(2,1)} reshape(bf16[4,256,320]{1,0,2:T(4,128)(2,1)} %copy.63) | data formatting | bytes 1310720 | tf_op jit(solution)/shard_map/reshape | solution.py:316
  39.1 2.4 %copy.65 = bf16[4,256,320]{1,0,2:T(4,128)(2,1)} copy(bf16[4,256,320]{1,2,0:T(8,128)(2,1)} %get-tuple-element.13) | data formatting | bytes 1310720 | tf_op jit(solution)/shard_map/slice | solution.py:314
  41.5 2.4 %reshape.406 = bf16[1024,5,64]{0,2,1:T(8,128)(2,1)} reshape(bf16[4,256,320]{1,0,2:T(4,128)(2,1)} %copy.65) | data formatting | bytes 1310720 | tf_op jit(solution)/shard_map/reshape | solution.py:316
  43.9 4.5 %fusion.2 = (bf16[1024,5]{0,1:T(8,128)(2,1)S(1)}, f32[5,512,1024]{2,1,0:T(8,128)S(1)}) fusion(pred[1024,512]{0,1:T(8,128)(4,1)} %get-tuple-element.26, bf16[1024,5,64]{0,2,1:T(8,128)(2,1)} %reshape.406, f32[512,5,64]{0,2,1:T(8,128)} %reshape.412, f32[5,64]{1,0:T(8,128)S(1)} %mul.324, f32[512,5]{0,1:T(8,128)S(1)} %add_rsqrt_fusion), kind=kOutput, calls=%fused_computation.4 | convolution fusion | flops 343895040 | bytes 12342528 | tf_op jit(solution)/shard_map/qhd,khd->qhk/dot_general | solution.py:321
  48.5 2.1 %fusion.19 = bf16[5,64,1024]{2,1,0:T(8,128)(2,1)S(1)} fusion(bf16[512,5,64]{0,2,1:T(8,128)(2,1)S(1)} %copy-done.8, f32[5,512,1024]{2,1,0:T(8,128)S(1)} %get-tuple-element.30, pred[1024,512]{0,1:T(8,128)(4,1)S(1)} %copy-done.7), kind=kOutput, calls=%fused_computation.25 | convolution fusion | flops 343736320 | bytes 11993088 | tf_op jit(solution)/shard_map/qhk,khd->qhd/dot_general | solution.py:327
  50.6 3.0 %fusion = (bf16[1024,5]{0,1:T(8,128)(2,1)S(1)}, f32[5,512,1024]{2,1,0:T(8,128)S(1)}) fusion(pred[1024,512]{0,1:T(8,128)(4,1)S(1)} %copy-done.6, bf16[1024,5,64]{0,2,1:T(8,128)(2,1)S(1)} %copy-done.5, f32[512,5,64]{0,2,1:T(8,128)S(1)} %copy-done.4, f32[5,64]{1,0:T(8,128)S(1)} %mul.324, f32[512,5]{0,1:T(8,128)S(1)} %add_rsqrt_fusion), kind=kOutput, calls=%fused_computation.2 | convolution fusion | flops 343895040 | bytes 12342528 | tf_op jit(solution)/shard_map/qhd,khd->qhk/dot_general | solution.py:321
  53.6 2.1 %fusion.16 = bf16[5,64,1024]{2,1,0:T(8,128)(2,1)S(1)} fusion(bf16[512,5,64]{0,2,1:T(8,128)(2,1)S(1)} %copy-done.8, f32[5,512,1024]{2,1,0:T(8,128)S(1)} %get-tuple-element.32, pred[1024,512]{0,1:T(8,128)(4,1)S(1)} %copy-done.6), kind=kOutput, calls=%fused_computation.24 | convolution fusion | flops 343736320 | bytes 11993088 | tf_op jit(solution)/shard_map/qhk,khd->qhd/dot_general | solution.py:327
  55.8 0.4 copy.74
  56.3 1.4 %copy.67 = bf16[8,256,325]{1,2,0:T(8,128)(2,1)} copy(bf16[8,256,325]{1,0,2:T(8,128)(2,1)S(1)} %slice_bitcast_fusion) | data formatting | bytes 2662400 | tf_op jit(solution)/shard_map/all_to_all | solution.py:339
  57.6 5.8 %all-to-all-start.1 = ((bf16[8,256,325]{1,2,0:T(8,128)(2,1)}), bf16[8,256,325]{1,2,0:T(8,128)(2,1)}, u32[]{:S(2)}, u32[]{:S(2)}) async-start(bf16[8,256,325]{1,2,0:T(8,128)(2,1)} %copy.67), calls=%async_computation.1 | async-start | bytes 2686976 | tf_op jit(solution)/shard_map/all_to_all | solution.py:339
  63.4 1.0 multiply_reduce_fusion.5
  64.7 2.5 %fusion.61 = (f32[5,256]{1,0:T(8,128)S(1)}, bf16[5,256,256]{1,2,0:T(8,128)(2,1)}) fusion(f32[256,5,32]{0,2,1:T(8,128)} %get-tuple-element.18, f32[256,5,32]{0,2,1:T(8,128)S(1)} %get-tuple-element.17, f32[256,5]{0,1:T(8,128)S(1)} %add_rsqrt_fusion.1, f32[5,64]{1,0:T(8,128)S(1)} %mul.324, f32[256,5,64]{0,2,1:T(8,128)} %fusion.42, ...), kind=kOutput, calls=%fused_computation.133 | convolution fusion | flops 43744000 | bytes 1387776 | tf_op jit(solution)/shard_map/qhd,khd->hqk/dot_general | solution.py:269
  67.2 13.4 %all-to-all-done.1 = bf16[8,256,325]{1,2,0:T(8,128)(2,1)} async-done(((bf16[8,256,325]{1,2,0:T(8,128)(2,1)}), bf16[8,256,325]{1,2,0:T(8,128)(2,1)}, u32[]{:S(2)}, u32[]{:S(2)}) %all-to-all-start.1) | async-done | bytes 1331232 | tf_op jit(solution)/shard_map/all_to_all | solution.py:339
  80.6 1.6 %convert_reduce_fusion = f32[256,325]{0,1:T(8,128)S(1)} fusion(bf16[8,256,325]{1,2,0:T(8,128)(2,1)} %all-to-all-done.1), kind=kLoop, calls=%fused_computation.15 | loop fusion | flops 1248000 | bytes 1664000 | tf_op jit(solution)/shard_map/reduce_sum | solution.py:346
  82.5 19.2 %all_gather.3 = bf16[256,1280]{0,1:T(8,128)(2,1)S(1)} all-gather(bf16[256,320]{0,1:T(8,128)(2,1)S(1)} %bitcast.119), channel_id=1, replica_groups=mesh['pages'=8,'mp'=4] {'mp'}, dimensions={1}, use_global_device_ids=true | all-gather | bytes 819200 | tf_op jit(solution)/shard_map/all_gather | solution.py:357
  101.7 1.1 multiply_reduce_fusion.1
  102.9 0.5 multiply_reduce_fusion
  103.4 0.4 multiply_convert_fusion
  103.9 1.9 %convolution_bitcast_fusion = f32[2,256,1280]{2,1,0:T(8,128)S(1)} fusion(bf16[2,1280,1280]{2,1,0:T(8,128)(2,1)S(1)} %bitcast.110, bf16[256,1280]{1,0:T(8,128)(2,1)S(1)} %multiply_convert_fusion), kind=kOutput, calls=%fused_computation.14 | convolution fusion | flops 1677721600 | bytes 9830400 | tf_op jit(solution)/shard_map/sd,jdf->jsf/dot_general | solution.py:364
  105.7 0.3 copy-done.12
  106.0 2.1 %convolution_convert_fusion = bf16[256,1280]{1,0:T(8,128)(2,1)} fusion(bf16[1280,1280]{1,0:T(8,128)(2,1)S(1)} %copy-done.12, f32[2,256,1280]{2,1,0:T(8,128)S(1)} %convolution_bitcast_fusion, f32[1280]{0:T(1024)S(1)} %get-tuple-element.8, f32[1280]{0:T(1024)S(1)} %get-tuple-element.7), kind=kOutput, calls=%fused_computation.16 | convolution fusion | flops 841809920 | bytes 6563840 | tf_op jit(solution)/shard_map/dot_general | solution.py:370
  108.1 4.2 %all-to-all-start.2 = ((bf16[4,64,1280]{2,1,0:T(8,128)(2,1)}), bf16[4,64,1280]{2,1,0:T(8,128)(2,1)}, u32[]{:S(2)}, u32[]{:S(2)}) async-start(bf16[4,64,1280]{2,1,0:T(8,128)(2,1)} %bitcast.113), calls=%async_computation.2 | async-start | bytes 1310720 | tf_op jit(solution)/shard_map/all_to_all | solution.py:369
  112.4 15.4 %all-to-all-done.2 = bf16[4,64,1280]{2,1,0:T(8,128)(2,1)} async-done(((bf16[4,64,1280]{2,1,0:T(8,128)(2,1)}), bf16[4,64,1280]{2,1,0:T(8,128)(2,1)}, u32[]{:S(2)}, u32[]{:S(2)}) %all-to-all-start.2) | async-done | bytes 655392 | tf_op jit(solution)/shard_map/all_to_all | solution.py:369
  127.7 1.3 convert_reduce_fusion.1
  129.4 0.9 multiply_convert_fusion.2
  (72 shorter events, 2.1 us)
Async XLA Ops:
  0.0 101.7 %copy-start = (bf16[1280,1280]{1,0:T(8,128)(2,1)S(1)}, bf16[1280,1280]{1,0:T(8,128)(2,1)}, u32[]{:S(2)}) copy-start(bf16[1280,1280]{1,0:T(8,128)(2,1)} %param.15) | copy-start | bytes 9830404
  12.0 21.1 %all-to-all-start = ((bf16[8,256,320]{1,2,0:T(8,128)(2,1)}), bf16[8,256,320]{1,2,0:T(8,128)(2,1)}, u32[]{:S(2)}, u32[]{:S(2)}) async-start(bf16[8,256,320]{1,2,0:T(8,128)(2,1)} %tile.2), calls=%async_computation | async-start | bytes 2621440 | tf_op jit(solution)/shard_map/all_to_all | solution.py:265
  16.3 2.5 %copy-start.13 = (s32[32]{0:T(128)S(1)}, s32[32]{0:T(128)}, u32[]{:S(2)}) copy-start(s32[32]{0:T(128)} %param.23) | copy-start | bytes 388
  43.9 4.5 %copy-start.7 = (pred[1024,512]{0,1:T(8,128)(4,1)S(1)}, pred[1024,512]{0,1:T(8,128)(4,1)}, u32[]{:S(2)}) copy-start(pred[1024,512]{0,1:T(8,128)(4,1)} %get-tuple-element.26) | copy-start | bytes 1572868
  43.9 4.5 %copy-start.8 = (bf16[512,5,64]{0,2,1:T(8,128)(2,1)S(1)}, bf16[512,5,64]{0,2,1:T(8,128)(2,1)}, u32[]{:S(2)}) copy-start(bf16[512,5,64]{0,2,1:T(8,128)(2,1)} %reshape_reshape.3) | copy-start | bytes 983044
  48.5 2.1 %copy-start.4 = (f32[512,5,64]{0,2,1:T(8,128)S(1)}, f32[512,5,64]{0,2,1:T(8,128)}, u32[]{:S(2)}) copy-start(f32[512,5,64]{0,2,1:T(8,128)} %reshape.412) | copy-start | bytes 1966084
  48.5 2.1 %copy-start.5 = (bf16[1024,5,64]{0,2,1:T(8,128)(2,1)S(1)}, bf16[1024,5,64]{0,2,1:T(8,128)(2,1)}, u32[]{:S(2)}) copy-start(bf16[1024,5,64]{0,2,1:T(8,128)(2,1)} %reshape.404) | copy-start | bytes 1966084
  48.5 2.1 %copy-start.6 = (pred[1024,512]{0,1:T(8,128)(4,1)S(1)}, pred[1024,512]{0,1:T(8,128)(4,1)}, u32[]{:S(2)}) copy-start(pred[1024,512]{0,1:T(8,128)(4,1)} %get-tuple-element.25) | copy-start | bytes 1572868
  57.6 6.8 %copy-start.10 = (f32[2,1280]{1,0:T(2,128)S(1)}, f32[2,1280]{1,0:T(2,128)}, u32[]{:S(2)}) copy-start(f32[2,1280]{1,0:T(2,128)} %param.19) | copy-start | bytes 30724
  57.6 6.8 %copy-start.11 = (f32[2,1280]{1,0:T(2,128)S(1)}, f32[2,1280]{1,0:T(2,128)}, u32[]{:S(2)}) copy-start(f32[2,1280]{1,0:T(2,128)} %param.20) | copy-start | bytes 30724
  57.6 23.0 %all-to-all-start.1 = ((bf16[8,256,325]{1,2,0:T(8,128)(2,1)}), bf16[8,256,325]{1,2,0:T(8,128)(2,1)}, u32[]{:S(2)}, u32[]{:S(2)}) async-start(bf16[8,256,325]{1,2,0:T(8,128)(2,1)} %copy.67), calls=%async_computation.1 | async-start | bytes 2686976 | tf_op jit(solution)/shard_map/all_to_all | solution.py:339
  67.2 15.1 %copy-start.9 = (bf16[1,256,320]{1,2,0:T(8,128)(2,1)S(1)}, bf16[1,256,320]{1,2,0:T(8,128)(2,1)}, u32[]{:S(2)}) copy-start(bf16[1,256,320]{1,2,0:T(8,128)(2,1)} %get-tuple-element.16) | copy-start | bytes 491524
  80.6 1.7 %copy-start.14 = (bf16[5,256,256]{1,2,0:T(8,128)(2,1)S(1)}, bf16[5,256,256]{1,2,0:T(8,128)(2,1)}, u32[]{:S(2)}) copy-start(bf16[5,256,256]{1,2,0:T(8,128)(2,1)} %get-tuple-element.34) | copy-start | bytes 1966084
  82.3 21.5 %slice-start = ((s8[6553600]{0:T(1024)(128)(4,1)}), s8[4194304]{0:T(1024)(128)(4,1)S(1)}, s32[]{:S(2)}) async-start(s8[6553600]{0:T(1024)(128)(4,1)} %bitcast.109), calls=%async_computation.3 | async-start | bytes 8388608
  101.7 1.1 copy-start.1
  101.7 2.1 %slice-start.1 = ((s8[6553600]{0:T(1024)(128)(4,1)}), s8[2359296]{0:T(1024)(128)(4,1)S(1)}, s32[]{:S(2)}) async-start(s8[6553600]{0:T(1024)(128)(4,1)} %bitcast.109), calls=%async_computation.4 | async-start | bytes 4718592
  103.8 1.9 %copy-start.2 = (bf16[256,1280]{1,0:T(8,128)(2,1)}, bf16[256,1280]{1,0:T(8,128)(2,1)S(1)}, u32[]{:S(2)}) copy-start(bf16[256,1280]{1,0:T(8,128)(2,1)S(1)} %multiply_convert_fusion) | copy-start | bytes 1966084
  103.8 2.2 %copy-start.12 = (bf16[1280,1280]{1,0:T(8,128)(2,1)S(1)}, bf16[1280,1280]{1,0:T(8,128)(2,1)}, u32[]{:S(2)}) copy-start(bf16[1280,1280]{1,0:T(8,128)(2,1)} %param.17) | copy-start | bytes 9830404
  108.1 19.6 %all-to-all-start.2 = ((bf16[4,64,1280]{2,1,0:T(8,128)(2,1)}), bf16[4,64,1280]{2,1,0:T(8,128)(2,1)}, u32[]{:S(2)}, u32[]{:S(2)}) async-start(bf16[4,64,1280]{2,1,0:T(8,128)(2,1)} %bitcast.113), calls=%async_computation.2 | async-start | bytes 1310720 | tf_op jit(solution)/shard_map/all_to_all | solution.py:369
  127.7 1.4 %copy-start.3 = (bf16[256,1280]{1,0:T(8,128)(2,1)S(1)}, bf16[256,1280]{1,0:T(8,128)(2,1)}, u32[]{:S(2)}) copy-start(bf16[256,1280]{1,0:T(8,128)(2,1)} %copy-done.2) | copy-start | bytes 1966084

commit v11 on v8

--- a/solution.py
+++ b/solution.py
@@ -262,7 +262,11 @@
         rotate(projected[1].astype(jnp.float32), position_shard, local_heads), scale_local, local_heads
     ).astype(jnp.bfloat16)
     value_rows = projected[2]
-    gathered = lax.all_gather(queries, "pages", axis=0, tiled=True)
+    pages_count = lax.axis_size("pages")
+    queries_t = jnp.transpose(queries.reshape(slot_count, local_heads, head_dim), (1, 2, 0))
+    gathered_t = lax.all_to_all(
+        jnp.tile(queries_t[None], (pages_count, 1, 1, 1)), "pages", 0, 3, tiled=True
+    ).reshape(local_heads, head_dim, pages_count * slot_count)
     scores = (
         jnp.einsum(
             "qhd,khd->hqk",
@@ -304,51 +308,46 @@
     all_groups = group_id.reshape(-1)
     key_heads = prefix_keys.reshape(-1, local_heads, head_dim)
     value_heads = prefix_values.reshape(-1, local_heads, head_dim)
-    total_rows = gathered.shape[0]
-    chunk_count = 2 if total_rows % 16 == 0 else 1
+    total_rows = gathered_t.shape[2]
+    chunk_count = 2 if total_rows % 256 == 0 else 1
     row_count = total_rows // chunk_count
     pieces = []
     for chunk in range(chunk_count):
-        query_heads = lax.slice_in_dim(
-            gathered, chunk * row_count, (chunk + 1) * row_count, axis=0
-        ).reshape(row_count, local_heads, head_dim)
+        query_chunk = lax.slice_in_dim(
+            gathered_t, chunk * row_count, (chunk + 1) * row_count, axis=2
+        )
         gathered_group = lax.slice_in_dim(
             all_groups, chunk * row_count, (chunk + 1) * row_count, axis=0
         )
         prefix_scores = (
-            jnp.einsum("qhd,khd->qhk", query_heads, key_heads, preferred_element_type=jnp.float32)
+            jnp.einsum("hdq,khd->hkq", query_chunk, key_heads, preferred_element_type=jnp.float32)
             * score_scale
         )
-        prefix_allowed = gathered_group[:, None] == key_group[None, :]
-        prefix_weights = jnp.where(prefix_allowed[:, None, :], jnp.exp(prefix_scores), 0.0)
-        weight_sum = jnp.sum(prefix_weights, axis=-1)
+        prefix_allowed = key_group[:, None] == gathered_group[None, :]
+        prefix_weights = jnp.where(prefix_allowed[None], jnp.exp(prefix_scores), 0.0)
+        weight_sum = jnp.sum(prefix_weights, axis=1)
         summed = jnp.einsum(
-            "qhk,khd->qhd",
+            "hkq,khd->hdq",
             prefix_weights.astype(jnp.bfloat16),
             value_heads,
             preferred_element_type=jnp.float32,
         )
         pieces.append(
-            jnp.concatenate([summed.reshape(row_count, local_width), weight_sum], axis=1).astype(
-                jnp.bfloat16
-            )
-        )
-    pages_count = lax.axis_size("pages")
+            jnp.concatenate([summed, weight_sum[:, None, :]], axis=1).astype(jnp.bfloat16)
+        )
     prefix_parts = lax.all_to_all(
-        jnp.concatenate(pieces, axis=0),
-        "pages",
-        0,
-        0,
-        tiled=True,
+        jnp.concatenate(pieces, axis=2), "pages", 2, 0, tiled=True
     )
     prefix_both = jnp.sum(
-        prefix_parts.reshape(pages_count, slot_count, local_width + local_heads).astype(jnp.float32),
+        prefix_parts.reshape(pages_count, local_heads, head_dim + 1, slot_count).astype(
+            jnp.float32
+        ),
         axis=0,
     )
-    prefix_sum = prefix_both[:, :local_width]
-    prefix_total = prefix_both[:, local_width:]
+    prefix_sum = jnp.transpose(prefix_both[:, :head_dim, :], (2, 0, 1))
+    prefix_total = prefix_both[:, head_dim, :].T
     denominator = suffix_total.T + prefix_total + (1.0 - live_shard.astype(jnp.float32))[:, None]
-    mixed = (suffix_sum + prefix_sum.reshape(slot_count, local_heads, head_dim)) / denominator[
+    mixed = (suffix_sum + prefix_sum) / denominator[
         :, :, None
     ]
     attention_local = mixed.reshape(slot_count, local_width).astype(jnp.bfloat16)

time: 137 us -> 160 us (1.17)
  local copies, waits for them, and re-layouts: 18 us -> 51.6 us
  between operations: 13.8 us -> 0.42 us
  waiting for transfers between devices: 39.2 us -> 29.8 us
  starting transfers between devices: 8.99 us -> 14.3 us
  other arithmetic: 16.7 us -> 20.2 us
  matrix products: 20.9 us -> 23.1 us
    unnamed x37 -> x41, local copies, waits for them, and re-layouts: 2.8 us -> 23.4 us
    all_gather x1 -> x0, waiting for transfers between devices: 10.4 us -> none  [shards_heads(): gathered = lax.all_gather(queries, 'pages', axis=0, tiled=True)]
    concatenate x0 -> x1, local copies, waits for them, and re-layouts: none -> 5.49 us  [shards_heads(): jnp.concatenate(pieces, axis=2)]
    all_to_all x1 -> x2, starting transfers between devices: 4.84 us -> 10.2 us  [the longest x1 5.79 us: shards_heads(): lax.all_to_all(jnp.concatenate(pieces, axis=2), 'pages', 2, 0, tiled=True)]
    reshape x0 -> x1, local copies, waits for them, and re-layouts: none -> 3.28 us  [shards_heads(): gathered_t = lax.all_to_all(jnp.tile(queries_t[None], (pages_count, 1, 1,...]
    reduce_sum x1, other arithmetic: 1.6 us -> 3.4 us  [shards_heads(): jnp.sum(prefix_parts.reshape(pages_count, local_heads, head_dim + 1, slot...]
    convert_element_type x1 -> x0, other arithmetic: 1.74 us -> none  [shards_heads(): queries = head_norm(rotate(projected[0].astype(jnp.float32), position_sha...]
    all_to_all x2 -> x1, local copies, waits for them, and re-layouts: 1.44 us -> 3.15 us  [shards_heads(): lax.all_to_all(jnp.tile(queries_t[None], (pages_count, 1, 1, 1)), 'pages'...]
  transfers between devices with their start and end apart: 3 -> 3, of which waited for: 3 -> 3; matrix products, arithmetic and copies ran while one was open for 14% -> 12% of each run, Pallas kernels for 0% -> 0%
where the time goes in v11:
time: 160 us; the launch traced here: 158 us
  local copies, waits for them, and re-layouts  51.6 us (32%)
  waiting for transfers between devices  29.8 us (19%)
  matrix products  23.1 us (14%)
  other arithmetic  20.2 us (13%)
  blocking collectives  18.8 us (12%)
  starting transfers between devices  14.3 us (9%)
    unnamed x41, local copies, waits for them, and re-layouts  23.4 us
    all_gather x1, blocking collectives, shards_heads(): attention = lax.all_gather(attention_local, 'mp', axis=1, tiled=True)  18.8 us
    all_to_all x1, waiting for transfers between devices, shards_heads(): lax.all_to_all(jnp.dot(hidden, w_down, preferred_element_type=jnp.float32...  15.4 us
    all_to_all x1, waiting for transfers between devices, shards_heads(): lax.all_to_all(jnp.concatenate(pieces, axis=2), 'pages', 2, 0, tiled=True)  13.2 us
    dot_general x2, matrix products, shards_heads(): jnp.einsum('hdq,khd->hkq', query_chunk, key_heads, preferred_element_type...  7.22 us
    all_to_all x1, starting transfers between devices, shards_heads(): lax.all_to_all(jnp.concatenate(pieces, axis=2), 'pages', 2, 0, tiled=True)  5.79 us
    concatenate x1, local copies, waits for them, and re-layouts, shards_heads(): jnp.concatenate(pieces, axis=2)  5.49 us
    all_to_all x1, starting transfers between devices, shards_heads(): lax.all_to_all(jnp.tile(queries_t[None], (pages_count, 1, 1, 1)), 'pages'...  4.39 us
  transfers between devices with their start and end apart: 3, of which 3 were waited for; matrix products, arithmetic and copies ran while one was open for 12% of the time, Pallas kernels for 0%

profile of v11, /device:TPU:2, one launch (start us, length us, event | category | flops | bytes accessed | tf_op | source)
XLA Modules:
  0.0 158.3 jit_solution(3462485716029536520)
XLA Ops:
  0.0 0.9 reduce_window_sum.11
  0.9 0.8 sub.37
  1.7 0.8 select_reduce_fusion.2
  2.5 1.3 fusion.22
  3.8 2.8 %fusion.29 = bf16[3,256,320]{1,2,0:T(8,128)(2,1)S(1)} fusion(bf16[3,1280,320]{1,2,0:T(8,128)(2,1)} %param.14, bf16[256,1280]{1,0:T(8,128)(2,1)} %param.13, f32[256]{0:T(256)S(1)} %add_rsqrt_fusion.5), kind=kOutput, calls=%fused_computation.41 | convolution fusion | flops 630374400 | bytes 3605504 | tf_op jit(solution)/shard_map/sd,jdc->jsc/dot_general | solution.py:255
  7.6 0.8 multiply_subtract_fusion
  9.1 0.8 dynamic_slice.33
  10.0 1.0 fusion.59
  11.0 1.2 tile.2
  12.2 4.4 %all-to-all-start = ((bf16[8,5,64,256]{3,2,1,0:T(8,128)(2,1)}), bf16[8,5,64,256]{3,2,1,0:T(8,128)(2,1)}, u32[]{:S(2)}, u32[]{:S(2)}) async-start(bf16[8,5,64,256]{3,2,1,0:T(8,128)(2,1)} %tile.2), calls=%async_computation | async-start | bytes 2621440 | tf_op jit(solution)/shard_map/all_to_all | solution.py:267
  16.7 2.4 %constant_dynamic-slice_fusion = (bf16[4,128,320]{2,1,0:T(8,128)(2,1)}, bf16[4,128,320]{2,1,0:T(8,128)(2,1)}) fusion(bf16[4,128,1280]{2,1,0:T(8,128)(2,1)} %param.21, s32[]{:T(128)S(6)} %select_n.61, bf16[4,128,1280]{2,1,0:T(8,128)(2,1)} %param.22), kind=kLoop, calls=%fused_computation.106 | loop fusion | bytes 1310724 | tf_op jit(solution)/shard_map/dynamic_slice | solution.py:299
  19.3 1.9 %copy.82 = bf16[4,128,320]{1,2,0:T(8,128)(2,1)} copy(bf16[4,128,320]{2,1,0:T(8,128)(2,1)} %get-tuple-element.37) | data formatting | bytes 655360
  21.2 2.1 %copy.74 = f32[4,128,320]{1,0,2:T(4,128)} copy(bf16[4,128,320]{1,2,0:T(8,128)(2,1)} %copy.82) | data formatting | bytes 983040 | tf_op jit(solution)/shard_map/convert_element_type | solution.py:301
  23.3 2.2 %reshape.373 = f32[512,5,64]{0,2,1:T(8,128)} reshape(f32[4,128,320]{1,0,2:T(4,128)} %copy.74) | data formatting | bytes 1310720 | tf_op jit(solution)/shard_map/convert_element_type | solution.py:301
  25.5 1.9 %copy.72 = bf16[4,128,320]{1,0,2:T(4,128)(2,1)} copy(bf16[4,128,320]{2,1,0:T(8,128)(2,1)} %get-tuple-element.38) | data formatting | bytes 655360 | tf_op jit(solution)/shard_map/dynamic_slice | solution.py:305
  27.4 1.8 %reshape_reshape.3 = bf16[512,5,64]{0,2,1:T(8,128)(2,1)} reshape(bf16[4,128,320]{1,0,2:T(4,128)(2,1)} %copy.72) | data formatting | bytes 655360 | tf_op jit(solution)/shard_map/reshape;reshape | solution.py:310
  29.2 1.2 multiply_reduce_fusion.2
  30.5 1.6 %broadcast_compare_fusion.1 = (pred[512,1024]{1,0:T(8,128)(4,1)}, pred[512,1024]{1,0:T(8,128)(4,1)}) fusion(s32[1024]{0:T(1024)S(1)} %bitcast.100, s32[512]{0:T(512)S(1)} %broadcast_bitcast_fusion, s32[1024]{0:T(1024)S(1)} %bitcast.101), kind=kLoop, calls=%fused_computation.47 | loop fusion | flops 1048576 | bytes 1058816 | tf_op jit(solution)/shard_map/eq | solution.py:326
  32.2 1.3 all-to-all-done
  33.4 3.2 %copy.75 = bf16[1,5,64,8,256]{4,3,2,1,0:T(8,128)(2,1)} copy(bf16[1,5,64,8,256]{4,2,1,3,0:T(8,128)(2,1)} %bitcast.13) | data formatting | bytes 2621440 | tf_op jit(solution)/shard_map/all_to_all | solution.py:267
  36.6 3.3 %reshape.369 = bf16[5,64,2048]{2,1,0:T(8,128)(2,1)} reshape(bf16[1,5,64,8,256]{4,3,2,1,0:T(8,128)(2,1)} %copy.75) | data formatting | bytes 2621440 | tf_op jit(solution)/shard_map/reshape | solution.py:269
  39.9 4.4 %fusion = (bf16[5,1024]{1,0:T(8,128)(2,1)S(1)}, f32[5,512,1024]{2,1,0:T(8,128)S(1)}) fusion(pred[512,1024]{1,0:T(8,128)(4,1)} %get-tuple-element.23, bf16[5,64,2048]{2,1,0:T(8,128)(2,1)} %reshape.369, f32[512,5,64]{0,2,1:T(8,128)} %reshape.373, f32[5,64]{1,0:T(8,128)S(1)} %mul.307, f32[512,5]{0,1:T(8,128)S(1)} %add_rsqrt_fusion), kind=kOutput, calls=%fused_computation.2 | convolution fusion | flops 343895040 | bytes 12342528 | tf_op jit(solution)/shard_map/hdq,khd->hkq/dot_general | solution.py:323
  44.3 2.8 %fusion.2 = (bf16[5,1024]{1,0:T(8,128)(2,1)S(1)}, f32[5,512,1024]{2,1,0:T(8,128)S(1)}) fusion(pred[512,1024]{1,0:T(8,128)(4,1)S(1)} %copy-done.7, bf16[5,64,2048]{2,1,0:T(8,128)(2,1)S(1)} %copy-done.6, f32[512,5,64]{0,2,1:T(8,128)S(1)} %copy-done.4, f32[5,64]{1,0:T(8,128)S(1)} %mul.307, f32[512,5]{0,1:T(8,128)S(1)} %add_rsqrt_fusion), kind=kOutput, calls=%fused_computation.4 | convolution fusion | flops 343895040 | bytes 12351488 | tf_op jit(solution)/shard_map/hdq,khd->hkq/dot_general | solution.py:323
  47.2 1.9 %fusion.16 = bf16[5,64,1024]{2,1,0:T(8,128)(2,1)S(1)} fusion(bf16[512,5,64]{0,2,1:T(8,128)(2,1)S(1)} %copy-done.9, f32[5,512,1024]{2,1,0:T(8,128)S(1)} %get-tuple-element.30, pred[512,1024]{1,0:T(8,128)(4,1)S(1)} %copy-done.8), kind=kOutput, calls=%fused_computation.25 | convolution fusion | flops 343736320 | bytes 11993088 | tf_op jit(solution)/shard_map/hkq,khd->hdq/dot_general | solution.py:329
  49.1 1.9 %fusion.19 = bf16[5,64,1024]{2,1,0:T(8,128)(2,1)S(1)} fusion(bf16[512,5,64]{0,2,1:T(8,128)(2,1)S(1)} %copy-done.9, f32[5,512,1024]{2,1,0:T(8,128)S(1)} %get-tuple-element.28, pred[512,1024]{1,0:T(8,128)(4,1)S(1)} %copy-done.7), kind=kOutput, calls=%fused_computation.26 | convolution fusion | flops 343736320 | bytes 11993088 | tf_op jit(solution)/shard_map/hkq,khd->hdq/dot_general | solution.py:329
  51.1 1.3 maximum_maximum_fusion
  52.4 5.5 %copy.78 = bf16[5,65,2048]{1,0,2:T(8,128)(2,1)} copy(bf16[5,65,2048]{2,1,0:T(8,128)(2,1)} %maximum_maximum_fusion) | data formatting | bytes 2662400 | tf_op jit(solution)/shard_map/concatenate | solution.py:339
  57.9 8.6 %reshape.382 = bf16[8,2,41600]{2,1,0:T(2,128)(2,1)} reshape(bf16[2048,5,65]{2,1,0:T(8,128)(2,1)} %bitcast.91) | data formatting | bytes 2662400
  66.5 5.8 %all-to-all-start.1 = ((bf16[8,2,41600]{2,1,0:T(2,128)(2,1)}), bf16[8,2,41600]{2,1,0:T(2,128)(2,1)}, u32[]{:S(2)}, u32[]{:S(2)}) async-start(bf16[8,2,41600]{2,1,0:T(2,128)(2,1)} %reshape.382), calls=%async_computation.1 | async-start | bytes 2662400 | tf_op jit(solution)/shard_map/all_to_all | solution.py:338
  72.3 1.0 multiply_reduce_fusion.5
  73.6 2.5 %fusion.62 = (f32[5,256]{1,0:T(8,128)S(1)}, bf16[5,256,256]{1,2,0:T(8,128)(2,1)}) fusion(f32[256,5,32]{0,2,1:T(8,128)} %get-tuple-element.16, f32[256,5,32]{0,2,1:T(8,128)} %get-tuple-element.15, f32[256,5]{0,1:T(8,128)S(1)} %add_rsqrt_fusion.1, f32[5,64]{1,0:T(8,128)S(1)} %mul.307, f32[256,5,32]{0,2,1:T(8,128)S(1)} %get-tuple-element.19, ...), kind=kOutput, calls=%fused_computation.134 | convolution fusion | flops 43907840 | bytes 1392896 | tf_op jit(solution)/shard_map/qhd,khd->hqk/dot_general | solution.py:271
  76.1 13.2 %all-to-all-done.1 = bf16[8,2,41600]{2,1,0:T(2,128)(2,1)} async-done(((bf16[8,2,41600]{2,1,0:T(2,128)(2,1)}), bf16[8,2,41600]{2,1,0:T(2,128)(2,1)}, u32[]{:S(2)}, u32[]{:S(2)}) %all-to-all-start.1) | async-done | bytes 1331232 | tf_op jit(solution)/shard_map/all_to_all | solution.py:338
  89.3 8.7 %reshape.383 = bf16[2048,5,65]{2,1,0:T(8,128)(2,1)} reshape(bf16[8,2,41600]{2,1,0:T(2,128)(2,1)} %all-to-all-done.1) | data formatting | bytes 2662400
  98.0 3.4 %convert_reduce_fusion = f32[5,65,256]{1,0,2:T(8,128)S(1)} fusion(bf16[5,65,8,256]{1,0,3,2:T(8,128)(2,1)} %bitcast.90), kind=kLoop, calls=%fused_computation.6 | loop fusion | flops 1248000 | bytes 1664000 | tf_op jit(solution)/shard_map/reduce_sum | solution.py:341
  101.4 1.0 copy-done.1
  102.4 1.4 slice.90
  103.8 1.6 copy.80
  105.3 2.2 %copy.83 = f32[5,64,256]{2,1,0:T(8,128)} copy(f32[5,64,256]{1,0,2:T(8,128)} %bitcast.94) | data formatting | bytes 655360
  107.5 1.6 fusion.32
  109.1 18.8 %all_gather.3 = bf16[256,1280]{0,1:T(8,128)(2,1)S(1)} all-gather(bf16[256,320]{0,1:T(8,128)(2,1)S(1)} %bitcast.98), channel_id=1, replica_groups=mesh['pages'=8,'mp'=4] {'mp'}, dimensions={1}, use_global_device_ids=true | all-gather | bytes 819200 | tf_op jit(solution)/shard_map/all_gather | solution.py:354
  128.0 1.1 multiply_reduce_fusion.1
  130.1 1.9 %convolution_bitcast_fusion = f32[2,256,1280]{2,1,0:T(8,128)S(1)} fusion(bf16[2,1280,1280]{2,1,0:T(8,128)(2,1)S(1)} %bitcast.93, bf16[256,1280]{1,0:T(8,128)(2,1)S(1)} %multiply_convert_fusion), kind=kOutput, calls=%fused_computation.15 | convolution fusion | flops 1677721600 | bytes 9830400 | tf_op jit(solution)/shard_map/sd,jdf->jsf/dot_general | solution.py:361
  132.3 2.1 %convolution_convert_fusion = bf16[256,1280]{1,0:T(8,128)(2,1)} fusion(bf16[1280,1280]{1,0:T(8,128)(2,1)S(1)} %copy-done.13, f32[2,256,1280]{2,1,0:T(8,128)S(1)} %convolution_bitcast_fusion, f32[1280]{0:T(1024)S(1)} %get-tuple-element.8, f32[1280]{0:T(1024)S(1)} %get-tuple-element.7), kind=kOutput, calls=%fused_computation.16 | convolution fusion | flops 841809920 | bytes 6563840 | tf_op jit(solution)/shard_map/dot_general | solution.py:367
  134.4 4.2 %all-to-all-start.2 = ((bf16[4,64,1280]{2,1,0:T(8,128)(2,1)}), bf16[4,64,1280]{2,1,0:T(8,128)(2,1)}, u32[]{:S(2)}, u32[]{:S(2)}) async-start(bf16[4,64,1280]{2,1,0:T(8,128)(2,1)} %bitcast.95), calls=%async_computation.2 | async-start | bytes 1310720 | tf_op jit(solution)/shard_map/all_to_all | solution.py:366
  138.6 15.4 %all-to-all-done.2 = bf16[4,64,1280]{2,1,0:T(8,128)(2,1)} async-done(((bf16[4,64,1280]{2,1,0:T(8,128)(2,1)}), bf16[4,64,1280]{2,1,0:T(8,128)(2,1)}, u32[]{:S(2)}, u32[]{:S(2)}) %all-to-all-start.2) | async-done | bytes 655392 | tf_op jit(solution)/shard_map/all_to_all | solution.py:366
  154.0 1.2 convert_reduce_fusion.1
  155.3 1.2 multiply_reduce_fusion.3
  156.5 1.8 %multiply_convert_fusion.2 = bf16[64,1280]{1,0:T(8,128)(2,1)} fusion(f32[64,1280]{1,0:T(8,128)S(1)} %convert_reduce_fusion.1, f32[64]{0:T(128)S(1)} %add_rsqrt_fusion.6, f32[64]{0:T(128)S(1)} %add_rsqrt_fusion.7, f32[1280]{0:T(1024)S(1)} %get-tuple-element.5, f32[64]{0:T(128)S(1)} %fusion.51, bf16[256,1280]{1,0:T(8,128)(2,1)} %copy-done.3, s32[]{:T(128)S(6)} %select_n.57), kind=kLoop, calls=%fused_computation.65 | loop fusion | flops 655360 | bytes 661252 | tf_op jit(solution)/shard_map/convert_element_type | solution.py:378
  (72 shorter events, 3.9 us)
Async XLA Ops:
  0.0 128.0 %copy-start = (bf16[1280,1280]{1,0:T(8,128)(2,1)S(1)}, bf16[1280,1280]{1,0:T(8,128)(2,1)}, u32[]{:S(2)}) copy-start(bf16[1280,1280]{1,0:T(8,128)(2,1)} %param.15) | copy-start | bytes 9830404
  8.4 0.7 copy-start.5
  12.2 6.9 %copy-start.14 = (s32[32]{0:T(128)S(1)}, s32[32]{0:T(128)}, u32[]{:S(2)}) copy-start(s32[32]{0:T(128)} %param.23) | copy-start | bytes 388
  12.2 21.2 %all-to-all-start = ((bf16[8,5,64,256]{3,2,1,0:T(8,128)(2,1)}), bf16[8,5,64,256]{3,2,1,0:T(8,128)(2,1)}, u32[]{:S(2)}, u32[]{:S(2)}) async-start(bf16[8,5,64,256]{3,2,1,0:T(8,128)(2,1)} %tile.2), calls=%async_computation | async-start | bytes 2621440 | tf_op jit(solution)/shard_map/all_to_all | solution.py:267
  39.9 4.4 %copy-start.4 = (f32[512,5,64]{0,2,1:T(8,128)S(1)}, f32[512,5,64]{0,2,1:T(8,128)}, u32[]{:S(2)}) copy-start(f32[512,5,64]{0,2,1:T(8,128)} %reshape.373) | copy-start | bytes 1966084
  39.9 4.4 %copy-start.6 = (bf16[5,64,2048]{2,1,0:T(8,128)(2,1)S(1)}, bf16[5,64,2048]{2,1,0:T(8,128)(2,1)}, u32[]{:S(2)}) copy-start(bf16[5,64,2048]{2,1,0:T(8,128)(2,1)} %reshape.369) | copy-start | bytes 3932164
  39.9 4.4 %copy-start.7 = (pred[512,1024]{1,0:T(8,128)(4,1)S(1)}, pred[512,1024]{1,0:T(8,128)(4,1)}, u32[]{:S(2)}) copy-start(pred[512,1024]{1,0:T(8,128)(4,1)} %get-tuple-element.24) | copy-start | bytes 1572868
  44.3 2.9 %copy-start.8 = (pred[512,1024]{1,0:T(8,128)(4,1)S(1)}, pred[512,1024]{1,0:T(8,128)(4,1)}, u32[]{:S(2)}) copy-start(pred[512,1024]{1,0:T(8,128)(4,1)} %get-tuple-element.23) | copy-start | bytes 1572868
  44.3 2.9 %copy-start.9 = (bf16[512,5,64]{0,2,1:T(8,128)(2,1)S(1)}, bf16[512,5,64]{0,2,1:T(8,128)(2,1)}, u32[]{:S(2)}) copy-start(bf16[512,5,64]{0,2,1:T(8,128)(2,1)} %reshape_reshape.3) | copy-start | bytes 983044
  66.5 6.9 %copy-start.11 = (f32[2,1280]{1,0:T(2,128)S(1)}, f32[2,1280]{1,0:T(2,128)}, u32[]{:S(2)}) copy-start(f32[2,1280]{1,0:T(2,128)} %param.20) | copy-start | bytes 30724
  66.5 6.9 %copy-start.12 = (f32[2,1280]{1,0:T(2,128)S(1)}, f32[2,1280]{1,0:T(2,128)}, u32[]{:S(2)}) copy-start(f32[2,1280]{1,0:T(2,128)} %param.19) | copy-start | bytes 30724
  66.5 22.8 %all-to-all-start.1 = ((bf16[8,2,41600]{2,1,0:T(2,128)(2,1)}), bf16[8,2,41600]{2,1,0:T(2,128)(2,1)}, u32[]{:S(2)}, u32[]{:S(2)}) async-start(bf16[8,2,41600]{2,1,0:T(2,128)(2,1)} %reshape.382), calls=%async_computation.1 | async-start | bytes 2662400 | tf_op jit(solution)/shard_map/all_to_all | solution.py:338
  101.4 1.0 copy-start.1
  103.8 3.8 %copy-start.10 = (bf16[1,256,320]{1,2,0:T(8,128)(2,1)S(1)}, bf16[1,256,320]{1,2,0:T(8,128)(2,1)}, u32[]{:S(2)}) copy-start(bf16[1,256,320]{1,2,0:T(8,128)(2,1)} %get-tuple-element.14) | copy-start | bytes 491524
  107.5 22.5 %slice-start = ((s8[6553600]{0:T(1024)(128)(4,1)}), s8[4194304]{0:T(1024)(128)(4,1)S(1)}, s32[]{:S(2)}) async-start(s8[6553600]{0:T(1024)(128)(4,1)} %bitcast.92), calls=%async_computation.3 | async-start | bytes 8388608
  128.0 1.2 copy-start.2
  128.0 2.1 %slice-start.1 = ((s8[6553600]{0:T(1024)(128)(4,1)}), s8[2359296]{0:T(1024)(128)(4,1)S(1)}, s32[]{:S(2)}) async-start(s8[6553600]{0:T(1024)(128)(4,1)} %bitcast.92), calls=%async_computation.4 | async-start | bytes 4718592
  130.1 1.9 %copy-start.3 = (bf16[256,1280]{1,0:T(8,128)(2,1)}, bf16[256,1280]{1,0:T(8,128)(2,1)S(1)}, u32[]{:S(2)}) copy-start(bf16[256,1280]{1,0:T(8,128)(2,1)S(1)} %multiply_convert_fusion) | copy-start | bytes 1966084
  130.1 2.2 %copy-start.13 = (bf16[1280,1280]{1,0:T(8,128)(2,1)S(1)}, bf16[1280,1280]{1,0:T(8,128)(2,1)}, u32[]{:S(2)}) copy-start(bf16[1280,1280]{1,0:T(8,128)(2,1)} %param.17) | copy-start | bytes 9830404
  134.4 19.6 %all-to-all-start.2 = ((bf16[4,64,1280]{2,1,0:T(8,128)(2,1)}), bf16[4,64,1280]{2,1,0:T(8,128)(2,1)}, u32[]{:S(2)}, u32[]{:S(2)}) async-start(bf16[4,64,1280]{2,1,0:T(8,128)(2,1)} %bitcast.95), calls=%async_computation.2 | async-start | bytes 1310720 | tf_op jit(solution)/shard_map/all_to_all | solution.py:366

commit v12 on v10

--- a/solution.py
+++ b/solution.py
@@ -303,41 +303,46 @@
     prefix_values = lax.dynamic_slice_in_dim(
         cache_values, mp_index * local_width, local_width, 2
     ).reshape(pages_here * page_len, local_width)
-    all_groups = group_id.reshape(-1)
+    pages_count = lax.axis_size("pages")
     key_heads = prefix_keys.reshape(-1, local_heads, head_dim)
     value_heads = prefix_values.reshape(-1, local_heads, head_dim)
-    total_rows = gathered.shape[0]
-    chunk_count = 2 if total_rows % 16 == 0 else 1
-    row_count = total_rows // chunk_count
+    gathered_heads = gathered.reshape(pages_count, slot_count, local_heads, head_dim)
+    chunk_count = 2 if pages_count % 2 == 0 else 1
+    chunk_pages = pages_count // chunk_count
     pieces = []
     for chunk in range(chunk_count):
-        query_heads = lax.slice_in_dim(
-            gathered, chunk * row_count, (chunk + 1) * row_count, axis=0
-        ).reshape(row_count, local_heads, head_dim)
-        gathered_group = lax.slice_in_dim(
-            all_groups, chunk * row_count, (chunk + 1) * row_count, axis=0
+        query_chunk = lax.slice_in_dim(
+            gathered_heads, chunk * chunk_pages, (chunk + 1) * chunk_pages, axis=0
+        )
+        group_chunk = lax.slice_in_dim(
+            group_id, chunk * chunk_pages, (chunk + 1) * chunk_pages, axis=0
         )
         prefix_scores = (
-            jnp.einsum("qhd,khd->qhk", query_heads, key_heads, preferred_element_type=jnp.float32)
+            jnp.einsum(
+                "pshd,khd->phks", query_chunk, key_heads, preferred_element_type=jnp.float32
+            )
             * score_scale
         )
-        prefix_allowed = gathered_group[:, None] == key_group[None, :]
-        prefix_weights = jnp.where(prefix_allowed[:, None, :], jnp.exp(prefix_scores), 0.0)
-        weight_sum = jnp.sum(prefix_weights, axis=-1)
+        prefix_allowed = key_group[None, :, None] == group_chunk[:, None, :]
+        prefix_weights = jnp.where(prefix_allowed[:, None], jnp.exp(prefix_scores), 0.0)
+        weight_sum = jnp.sum(prefix_weights, axis=2)
         summed = jnp.einsum(
-            "qhk,khd->qhd",
+            "phks,khd->pshd",
             prefix_weights.astype(jnp.bfloat16),
             value_heads,
             preferred_element_type=jnp.float32,
         )
         pieces.append(
-            jnp.concatenate([summed.reshape(row_count, local_width), weight_sum], axis=1).astype(
-                jnp.bfloat16
-            )
-        )
-    pages_count = lax.axis_size("pages")
+            jnp.concatenate(
+                [
+                    summed.reshape(chunk_pages, slot_count, local_width),
+                    jnp.transpose(weight_sum, (0, 2, 1)),
+                ],
+                axis=2,
+            ).astype(jnp.bfloat16)
+        )
     prefix_parts = lax.all_to_all(
-        jnp.concatenate(pieces, axis=0),
+        jnp.concatenate(pieces, axis=0).reshape(pages_count * slot_count, local_width + local_heads),
         "pages",
         0,
         0,

time: 131 us -> 119 us (0.908)
  local copies, waits for them, and re-layouts: 28.3 us -> 17.3 us
  matrix products: 22.2 us -> 20.3 us
    reshape x2 -> x0, local copies, waits for them, and re-layouts: 4.79 us -> none  [shards_heads(): query_heads = lax.slice_in_dim(gathered, chunk * row_count, (chunk + 1) *...]
    slice x3 -> x2, local copies, waits for them, and re-layouts: 6.05 us -> 1.47 us  [the longest x1 1.47 us: shards_heads(): lax.slice_in_dim(gathered_heads, chunk * chunk_pages, (chunk + 1) * chunk...]
    dot_general x4, matrix products: 11.6 us -> 9.66 us  [the longest x2 5.66 us: shards_heads(): jnp.einsum('pshd,khd->phks', query_chunk, key_heads, preferred_element_ty...]
    all_to_all x2 -> x0, local copies, waits for them, and re-layouts: 1.44 us -> none  [shards_heads(): lax.all_to_all(jnp.concatenate(pieces, axis=0), 'pages', 0, 0, tiled=True)]
    unnamed x39 -> x33, local copies, waits for them, and re-layouts: 2.66 us -> 2.4 us
  transfers between devices with their start and end apart: 3 -> 3, of which waited for: 3 -> 3; matrix products, arithmetic and copies ran while one was open for 15% -> 16% of each run, Pallas kernels for 0% -> 0%
where the time goes in v12:
time: 119 us; the launch traced here: 118 us
  waiting for transfers between devices  30 us (25%)
  matrix products  20.3 us (17%)
  blocking collectives  19 us (16%)
  local copies, waits for them, and re-layouts  17.3 us (15%)
  other arithmetic  17.1 us (14%)
  starting transfers between devices  14.3 us (12%)
    all_gather x1, blocking collectives, shards_heads(): attention = lax.all_gather(attention_local, 'mp', axis=1, tiled=True)  19 us
    all_to_all x1, waiting for transfers between devices, shards_heads(): lax.all_to_all(jnp.dot(hidden, w_down, preferred_element_type=jnp.float32...  15.4 us
    all_to_all x1, waiting for transfers between devices, shards_heads(): lax.all_to_all(jnp.concatenate(pieces, axis=0).reshape(pages_count * slot...  13.4 us
    all_to_all x1, starting transfers between devices, shards_heads(): lax.all_to_all(jnp.concatenate(pieces, axis=0).reshape(pages_count * slot...  5.79 us
    dot_general x2, matrix products, shards_heads(): jnp.einsum('pshd,khd->phks', query_chunk, key_heads, preferred_element_ty...  5.66 us
    all_to_all x1, starting transfers between devices, shards_heads(): lax.all_to_all(jnp.tile(queries, (lax.axis_size('pages'), 1)), 'pages', 0...  4.38 us
    convert_element_type x2, local copies, waits for them, and re-layouts, shards_heads(): cache_local.reshape(pages_here * page_len, local_width).astype(jnp.float32)  4.26 us
    all_to_all x1, starting transfers between devices, shards_heads(): lax.all_to_all(jnp.dot(hidden, w_down, preferred_element_type=jnp.float32...  4.16 us
  transfers between devices with their start and end apart: 3, of which 3 were waited for; matrix products, arithmetic and copies ran while one was open for 16% of the time, Pallas kernels for 0%

profile of v12, /device:TPU:2, one launch (start us, length us, event | category | flops | bytes accessed | tf_op | source)
XLA Modules:
  0.0 118.4 jit_solution(10245256144627387971)
XLA Ops:
  0.0 1.4 %fusion.22 = f32[256]{0:T(256)S(1)} fusion(bf16[256,1280]{1,0:T(8,128)(2,1)} %param.13), kind=kLoop, calls=%fused_computation.27 | loop fusion | flops 982784 | bytes 656384 | tf_op jit(solution)/shard_map/reduce_sum | solution.py:16
  1.5 0.7 reduce_window_sum.11
  2.2 0.7 sub.37
  2.9 0.8 select_reduce_fusion.2
  3.7 2.8 %fusion.35 = bf16[3,256,320]{1,2,0:T(8,128)(2,1)S(1)} fusion(bf16[3,1280,320]{1,2,0:T(8,128)(2,1)} %param.14, bf16[256,1280]{1,0:T(8,128)(2,1)} %param.13, f32[256]{0:T(256)S(1)} %add_rsqrt_fusion.5), kind=kOutput, calls=%fused_computation.43 | convolution fusion | flops 630374400 | bytes 3605504 | tf_op jit(solution)/shard_map/sd,jdc->jsc/dot_general | solution.py:255
  6.5 0.7 fusion.73
  7.3 0.2 multiply_cosine_fusion
  7.5 0.7 multiply_subtract_fusion
  8.3 0.8 fusion.55
  9.0 0.8 dynamic_slice.33
  9.8 1.1 fusion.52
  10.9 1.2 tile.2
  12.0 4.4 %all-to-all-start = ((bf16[8,256,320]{1,2,0:T(8,128)(2,1)}), bf16[8,256,320]{1,2,0:T(8,128)(2,1)}, u32[]{:S(2)}, u32[]{:S(2)}) async-start(bf16[8,256,320]{1,2,0:T(8,128)(2,1)} %tile.2), calls=%async_computation | async-start | bytes 2621440 | tf_op jit(solution)/shard_map/all_to_all | solution.py:265
  16.6 0.2 select_reduce_fusion.3
  16.8 2.4 %constant_dynamic-slice_fusion = (bf16[4,128,320]{2,1,0:T(8,128)(2,1)}, bf16[4,128,320]{2,1,0:T(8,128)(2,1)}) fusion(bf16[4,128,1280]{2,1,0:T(8,128)(2,1)} %param.21, s32[]{:T(128)S(6)} %select_n.61, bf16[4,128,1280]{2,1,0:T(8,128)(2,1)} %param.22), kind=kLoop, calls=%fused_computation.111 | loop fusion | bytes 1310724 | tf_op jit(solution)/shard_map/dynamic_slice | solution.py:297
  19.2 1.9 %copy.65 = bf16[4,128,320]{1,2,0:T(8,128)(2,1)} copy(bf16[4,128,320]{2,1,0:T(8,128)(2,1)} %get-tuple-element.39) | data formatting | bytes 655360
  21.1 2.1 %copy.55 = f32[4,128,320]{1,0,2:T(4,128)} copy(bf16[4,128,320]{1,2,0:T(8,128)(2,1)} %copy.65) | data formatting | bytes 983040 | tf_op jit(solution)/shard_map/convert_element_type | solution.py:299
  23.2 2.2 %reshape.352 = f32[512,5,64]{0,2,1:T(8,128)} reshape(f32[4,128,320]{1,0,2:T(4,128)} %copy.55) | data formatting | bytes 1310720 | tf_op jit(solution)/shard_map/convert_element_type | solution.py:299
  25.4 1.2 multiply_reduce_fusion.2
  26.5 1.9 %copy.53 = bf16[4,128,320]{1,0,2:T(4,128)(2,1)} copy(bf16[4,128,320]{2,1,0:T(8,128)(2,1)} %get-tuple-element.40) | data formatting | bytes 655360 | tf_op jit(solution)/shard_map/dynamic_slice | solution.py:303
  28.4 1.8 %reshape.355 = bf16[512,5,64,1]{0,2,1,3:T(8,128)(2,1)} reshape(bf16[4,128,320]{1,0,2:T(4,128)(2,1)} %copy.53) | data formatting | bytes 655360 | tf_op jit(solution)/shard_map/reshape;reshape | solution.py:308
  30.4 1.7 %broadcast_compare_fusion.1 = (pred[4,512,256]{2,1,0:T(8,128)(4,1)}, pred[4,512,256]{2,1,0:T(8,128)(4,1)}) fusion(s32[4,256]{1,0:T(4,128)S(1)} %get-tuple-element.23, s32[512]{0:T(512)S(1)} %broadcast_bitcast_fusion, s32[4,256]{1,0:T(4,128)S(1)} %get-tuple-element.24), kind=kLoop, calls=%fused_computation.49 | loop fusion | flops 1048576 | bytes 1058816 | tf_op jit(solution)/shard_map/eq | solution.py:326
  32.0 1.2 %all-to-all-done = bf16[8,256,320]{1,2,0:T(8,128)(2,1)} async-done(((bf16[8,256,320]{1,2,0:T(8,128)(2,1)}), bf16[8,256,320]{1,2,0:T(8,128)(2,1)}, u32[]{:S(2)}, u32[]{:S(2)}) %all-to-all-start) | async-done | bytes 1310752 | tf_op jit(solution)/shard_map/all_to_all | solution.py:265
  33.2 1.5 %fusion.72 = (bf16[4,256,320]{1,2,0:T(8,128)(2,1)S(1)}, bf16[4,256,320]{1,2,0:T(8,128)(2,1)S(1)}) fusion(bf16[8,256,320]{1,2,0:T(8,128)(2,1)} %all-to-all-done), kind=kLoop, calls=%fused_computation.137 | loop fusion | bytes 2621440 | tf_op jit(solution)/shard_map/slice | solution.py:314
  34.9 2.8 %fusion.2 = (bf16[4,5,256]{2,0,1:T(4,128)(2,1)S(1)}, f32[5,512,4,256]{3,1,2,0:T(8,128)S(1)}) fusion(pred[4,512,256]{2,1,0:T(8,128)(4,1)S(1)} %copy-done.6, bf16[4,256,5,64]{1,3,2,0:T(8,128)(2,1)S(1)} %bitcast.121, f32[512,5,64]{0,2,1:T(8,128)S(1)} %copy-done.4, f32[5,64]{1,0:T(8,128)S(1)} %mul.324, f32[512,5]{0,1:T(8,128)S(1)} %add_rsqrt_fusion), kind=kOutput, calls=%fused_computation.4 | convolution fusion | flops 343895040 | bytes 12342528 | tf_op jit(solution)/shard_map/pshd,khd->phks/dot_general | solution.py:321
  37.7 2.0 %fusion.29 = bf16[4,256,5,64]{1,3,0,2:T(8,128)(2,1)S(1)} fusion(f32[5,512,4,256]{3,1,2,0:T(8,128)S(1)} %get-tuple-element.30, pred[4,512,256]{2,1,0:T(8,128)(4,1)S(1)} %copy-done.6, bf16[512,5,64,1]{0,2,1,3:T(8,128)(2,1)S(1)} %copy-done.7), kind=kOutput, calls=%fused_computation.41 | convolution fusion | flops 343736320 | bytes 11993088 | tf_op jit(solution)/shard_map/phks,khd->pshd/dot_general | solution.py:329
  39.8 2.8 %fusion = (bf16[4,5,256]{2,0,1:T(4,128)(2,1)S(1)}, f32[5,512,4,256]{3,1,2,0:T(8,128)S(1)}) fusion(pred[4,512,256]{2,1,0:T(8,128)(4,1)S(1)} %copy-done.5, bf16[4,256,5,64]{1,3,2,0:T(8,128)(2,1)S(1)} %bitcast.120, f32[512,5,64]{0,2,1:T(8,128)S(1)} %copy-done.4, f32[5,64]{1,0:T(8,128)S(1)} %mul.324, f32[512,5]{0,1:T(8,128)S(1)} %add_rsqrt_fusion), kind=kOutput, calls=%fused_computation.2 | convolution fusion | flops 343895040 | bytes 12342528 | tf_op jit(solution)/shard_map/pshd,khd->phks/dot_general | solution.py:321
  42.7 2.0 %fusion.32 = bf16[4,256,5,64]{1,3,0,2:T(8,128)(2,1)S(1)} fusion(f32[5,512,4,256]{3,1,2,0:T(8,128)S(1)} %get-tuple-element.32, pred[4,512,256]{2,1,0:T(8,128)(4,1)S(1)} %copy-done.5, bf16[512,5,64,1]{0,2,1,3:T(8,128)(2,1)S(1)} %copy-done.7), kind=kOutput, calls=%fused_computation.42 | convolution fusion | flops 343736320 | bytes 11993088 | tf_op jit(solution)/shard_map/phks,khd->pshd/dot_general | solution.py:329
  44.7 1.2 maximum_maximum_fusion
  45.9 5.8 %all-to-all-start.1 = ((bf16[8,256,325]{1,2,0:T(8,128)(2,1)}), bf16[8,256,325]{1,2,0:T(8,128)(2,1)}, u32[]{:S(2)}, u32[]{:S(2)}) async-start(bf16[8,256,325]{1,2,0:T(8,128)(2,1)} %maximum_maximum_fusion), calls=%async_computation.1 | async-start | bytes 2686976 | tf_op jit(solution)/shard_map/all_to_all | solution.py:344
  51.7 1.0 multiply_reduce_fusion.5
  52.8 0.2 and_and_fusion
  53.0 2.5 %fusion.75 = (f32[5,256]{1,0:T(8,128)S(1)}, bf16[5,256,256]{1,2,0:T(8,128)(2,1)}) fusion(f32[256,5,32]{0,2,1:T(8,128)} %get-tuple-element.18, f32[256,5,32]{0,2,1:T(8,128)S(1)} %get-tuple-element.17, f32[256,5]{0,1:T(8,128)S(1)} %add_rsqrt_fusion.1, f32[5,64]{1,0:T(8,128)S(1)} %mul.324, f32[256,5,64]{0,2,1:T(8,128)} %fusion.55, ...), kind=kOutput, calls=%fused_computation.140 | convolution fusion | flops 43744000 | bytes 1387776 | tf_op jit(solution)/shard_map/qhd,khd->hqk/dot_general | solution.py:269
  55.4 13.4 %all-to-all-done.1 = bf16[8,256,325]{1,2,0:T(8,128)(2,1)} async-done(((bf16[8,256,325]{1,2,0:T(8,128)(2,1)}), bf16[8,256,325]{1,2,0:T(8,128)(2,1)}, u32[]{:S(2)}, u32[]{:S(2)}) %all-to-all-start.1) | async-done | bytes 1331232 | tf_op jit(solution)/shard_map/all_to_all | solution.py:344
  68.9 1.6 %convert_reduce_fusion = f32[256,325]{0,1:T(8,128)S(1)} fusion(bf16[8,256,325]{1,2,0:T(8,128)(2,1)} %all-to-all-done.1), kind=kLoop, calls=%fused_computation.15 | loop fusion | flops 1248000 | bytes 1664000 | tf_op jit(solution)/shard_map/reduce_sum | solution.py:351
  70.6 0.2 fusion.38
  70.8 19.0 %all_gather.3 = bf16[256,1280]{0,1:T(8,128)(2,1)S(1)} all-gather(bf16[256,320]{0,1:T(8,128)(2,1)S(1)} %bitcast.126), channel_id=1, replica_groups=mesh['pages'=8,'mp'=4] {'mp'}, dimensions={1}, use_global_device_ids=true | all-gather | bytes 819200 | tf_op jit(solution)/shard_map/all_gather | solution.py:362
  89.8 1.1 multiply_reduce_fusion.1
  91.0 0.5 multiply_reduce_fusion
  91.5 0.4 multiply_convert_fusion
  91.9 1.9 %convolution_bitcast_fusion = f32[2,256,1280]{2,1,0:T(8,128)S(1)} fusion(bf16[2,1280,1280]{2,1,0:T(8,128)(2,1)S(1)} %bitcast.117, bf16[256,1280]{1,0:T(8,128)(2,1)S(1)} %multiply_convert_fusion), kind=kOutput, calls=%fused_computation.14 | convolution fusion | flops 1677721600 | bytes 9830400 | tf_op jit(solution)/shard_map/sd,jdf->jsf/dot_general | solution.py:369
  93.8 0.3 copy-done.11
  94.1 2.1 %convolution_convert_fusion = bf16[256,1280]{1,0:T(8,128)(2,1)} fusion(bf16[1280,1280]{1,0:T(8,128)(2,1)S(1)} %copy-done.11, f32[2,256,1280]{2,1,0:T(8,128)S(1)} %convolution_bitcast_fusion, f32[1280]{0:T(1024)S(1)} %get-tuple-element.8, f32[1280]{0:T(1024)S(1)} %get-tuple-element.7), kind=kOutput, calls=%fused_computation.16 | convolution fusion | flops 841809920 | bytes 6563840 | tf_op jit(solution)/shard_map/dot_general | solution.py:375
  96.2 4.2 %all-to-all-start.2 = ((bf16[4,64,1280]{2,1,0:T(8,128)(2,1)}), bf16[4,64,1280]{2,1,0:T(8,128)(2,1)}, u32[]{:S(2)}, u32[]{:S(2)}) async-start(bf16[4,64,1280]{2,1,0:T(8,128)(2,1)} %bitcast.122), calls=%async_computation.2 | async-start | bytes 1310720 | tf_op jit(solution)/shard_map/all_to_all | solution.py:374
  100.4 15.4 %all-to-all-done.2 = bf16[4,64,1280]{2,1,0:T(8,128)(2,1)} async-done(((bf16[4,64,1280]{2,1,0:T(8,128)(2,1)}), bf16[4,64,1280]{2,1,0:T(8,128)(2,1)}, u32[]{:S(2)}, u32[]{:S(2)}) %all-to-all-start.2) | async-done | bytes 655392 | tf_op jit(solution)/shard_map/all_to_all | solution.py:374
  115.8 1.3 %convert_reduce_fusion.1 = f32[64,1280]{1,0:T(8,128)S(1)} fusion(bf16[4,64,1280]{2,1,0:T(8,128)(2,1)} %all-to-all-done.2), kind=kLoop, calls=%fused_computation.36 | loop fusion | flops 573440 | bytes 983040 | tf_op jit(solution)/shard_map/reduce_sum | solution.py:381
  117.2 0.3 multiply_reduce_fusion.3
  117.5 0.9 multiply_convert_fusion.2
  (65 shorter events, 1.1 us)
Async XLA Ops:
  0.0 89.8 %copy-start = (bf16[1280,1280]{1,0:T(8,128)(2,1)S(1)}, bf16[1280,1280]{1,0:T(8,128)(2,1)}, u32[]{:S(2)}) copy-start(bf16[1280,1280]{1,0:T(8,128)(2,1)} %param.15) | copy-start | bytes 9830404
  12.0 4.6 %copy-start.12 = (s32[32]{0:T(128)S(1)}, s32[32]{0:T(128)}, u32[]{:S(2)}) copy-start(s32[32]{0:T(128)} %param.23) | copy-start | bytes 388
  12.0 21.2 %all-to-all-start = ((bf16[8,256,320]{1,2,0:T(8,128)(2,1)}), bf16[8,256,320]{1,2,0:T(8,128)(2,1)}, u32[]{:S(2)}, u32[]{:S(2)}) async-start(bf16[8,256,320]{1,2,0:T(8,128)(2,1)} %tile.2), calls=%async_computation | async-start | bytes 2621440 | tf_op jit(solution)/shard_map/all_to_all | solution.py:265
  33.2 1.5 %copy-start.4 = (f32[512,5,64]{0,2,1:T(8,128)S(1)}, f32[512,5,64]{0,2,1:T(8,128)}, u32[]{:S(2)}) copy-start(f32[512,5,64]{0,2,1:T(8,128)} %reshape.352) | copy-start | bytes 1966084
  33.2 1.6 %copy-start.6 = (pred[4,512,256]{2,1,0:T(8,128)(4,1)S(1)}, pred[4,512,256]{2,1,0:T(8,128)(4,1)}, u32[]{:S(2)}) copy-start(pred[4,512,256]{2,1,0:T(8,128)(4,1)} %get-tuple-element.26) | copy-start | bytes 1572868
  34.9 2.8 %copy-start.7 = (bf16[512,5,64,1]{0,2,1,3:T(8,128)(2,1)S(1)}, bf16[512,5,64,1]{0,2,1,3:T(8,128)(2,1)}, u32[]{:S(2)}) copy-start(bf16[512,5,64,1]{0,2,1,3:T(8,128)(2,1)} %reshape.355) | copy-start | bytes 983044
  37.7 2.1 %copy-start.5 = (pred[4,512,256]{2,1,0:T(8,128)(4,1)S(1)}, pred[4,512,256]{2,1,0:T(8,128)(4,1)}, u32[]{:S(2)}) copy-start(pred[4,512,256]{2,1,0:T(8,128)(4,1)} %get-tuple-element.25) | copy-start | bytes 1572868
  45.9 6.8 %copy-start.9 = (f32[2,1280]{1,0:T(2,128)S(1)}, f32[2,1280]{1,0:T(2,128)}, u32[]{:S(2)}) copy-start(f32[2,1280]{1,0:T(2,128)} %param.19) | copy-start | bytes 30724
  45.9 6.8 %copy-start.10 = (f32[2,1280]{1,0:T(2,128)S(1)}, f32[2,1280]{1,0:T(2,128)}, u32[]{:S(2)}) copy-start(f32[2,1280]{1,0:T(2,128)} %param.20) | copy-start | bytes 30724
  45.9 23.0 %all-to-all-start.1 = ((bf16[8,256,325]{1,2,0:T(8,128)(2,1)}), bf16[8,256,325]{1,2,0:T(8,128)(2,1)}, u32[]{:S(2)}, u32[]{:S(2)}) async-start(bf16[8,256,325]{1,2,0:T(8,128)(2,1)} %maximum_maximum_fusion), calls=%async_computation.1 | async-start | bytes 2686976 | tf_op jit(solution)/shard_map/all_to_all | solution.py:344
  55.4 15.1 %copy-start.8 = (bf16[1,256,320]{1,2,0:T(8,128)(2,1)S(1)}, bf16[1,256,320]{1,2,0:T(8,128)(2,1)}, u32[]{:S(2)}) copy-start(bf16[1,256,320]{1,2,0:T(8,128)(2,1)} %get-tuple-element.16) | copy-start | bytes 491524
  68.9 1.7 %copy-start.13 = (bf16[5,256,256]{1,2,0:T(8,128)(2,1)S(1)}, bf16[5,256,256]{1,2,0:T(8,128)(2,1)}, u32[]{:S(2)}) copy-start(bf16[5,256,256]{1,2,0:T(8,128)(2,1)} %get-tuple-element.34) | copy-start | bytes 1966084
  70.6 21.3 %slice-start = ((s8[6553600]{0:T(1024)(128)(4,1)}), s8[4194304]{0:T(1024)(128)(4,1)S(1)}, s32[]{:S(2)}) async-start(s8[6553600]{0:T(1024)(128)(4,1)} %bitcast.116), calls=%async_computation.3 | async-start | bytes 8388608
  89.8 1.1 copy-start.1
  89.8 2.1 %slice-start.1 = ((s8[6553600]{0:T(1024)(128)(4,1)}), s8[2359296]{0:T(1024)(128)(4,1)S(1)}, s32[]{:S(2)}) async-start(s8[6553600]{0:T(1024)(128)(4,1)} %bitcast.116), calls=%async_computation.4 | async-start | bytes 4718592
  91.9 1.9 %copy-start.2 = (bf16[256,1280]{1,0:T(8,128)(2,1)}, bf16[256,1280]{1,0:T(8,128)(2,1)S(1)}, u32[]{:S(2)}) copy-start(bf16[256,1280]{1,0:T(8,128)(2,1)S(1)} %multiply_convert_fusion) | copy-start | bytes 1966084
  91.9 2.2 %copy-start.11 = (bf16[1280,1280]{1,0:T(8,128)(2,1)S(1)}, bf16[1280,1280]{1,0:T(8,128)(2,1)}, u32[]{:S(2)}) copy-start(bf16[1280,1280]{1,0:T(8,128)(2,1)} %param.17) | copy-start | bytes 9830404
  96.2 19.6 %all-to-all-start.2 = ((bf16[4,64,1280]{2,1,0:T(8,128)(2,1)}), bf16[4,64,1280]{2,1,0:T(8,128)(2,1)}, u32[]{:S(2)}, u32[]{:S(2)}) async-start(bf16[4,64,1280]{2,1,0:T(8,128)(2,1)} %bitcast.122), calls=%async_computation.2 | async-start | bytes 1310720 | tf_op jit(solution)/shard_map/all_to_all | solution.py:374
  115.8 1.4 %copy-start.3 = (bf16[256,1280]{1,0:T(8,128)(2,1)S(1)}, bf16[256,1280]{1,0:T(8,128)(2,1)}, u32[]{:S(2)}) copy-start(bf16[256,1280]{1,0:T(8,128)(2,1)} %copy-done.2) | copy-start | bytes 1966084

commit v13 on v12

--- a/solution.py
+++ b/solution.py
@@ -47,7 +47,10 @@
 
 
 def slot_tables(suffix_len, request_group, slot_count):
-    end_slots = jnp.cumsum(suffix_len, axis=1)
+    running = [suffix_len[:, 0]]
+    for column in range(1, suffix_len.shape[1]):
+        running.append(running[-1] + suffix_len[:, column])
+    end_slots = jnp.stack(running, axis=1)
     start_slots = end_slots - suffix_len
     slot_ids = jnp.arange(slot_count)
     inside = (slot_ids[None, None, :] >= start_slots[:, :, None]) & (
@@ -252,16 +255,21 @@
     live_own = lax.dynamic_slice_in_dim(live_shard, row_first, own_rows, 0)
     scale_local = lax.dynamic_slice_in_dim(scale_qk, mp_index * local_width, local_width, 0)
     state_in = rms_rows(hidden_in.astype(jnp.float32)).astype(jnp.bfloat16)
+    projected_query = jnp.dot(state_in, w_qkv[0], preferred_element_type=jnp.float32).astype(
+        jnp.bfloat16
+    )
+    queries = head_norm(
+        rotate(projected_query.astype(jnp.float32), position_shard, local_heads),
+        scale_local,
+        local_heads,
+    ).astype(jnp.bfloat16)
     projected = jnp.einsum(
-        "sd,jdc->jsc", state_in, w_qkv, preferred_element_type=jnp.float32
-    ).astype(jnp.bfloat16)
-    queries = head_norm(
+        "sd,jdc->jsc", state_in, w_qkv[1:], preferred_element_type=jnp.float32
+    ).astype(jnp.bfloat16)
+    keys_new = head_norm(
         rotate(projected[0].astype(jnp.float32), position_shard, local_heads), scale_local, local_heads
     ).astype(jnp.bfloat16)
-    keys_new = head_norm(
-        rotate(projected[1].astype(jnp.float32), position_shard, local_heads), scale_local, local_heads
-    ).astype(jnp.bfloat16)
-    value_rows = projected[2]
+    value_rows = projected[1]
     gathered = lax.all_to_all(
         jnp.tile(queries, (lax.axis_size("pages"), 1)), "pages", 0, 0, tiled=True
     )

time: 119 us -> 120 us (level)
  other arithmetic: 17.1 us -> 15 us
  matrix products: 20.3 us -> 22.1 us
    dot_general x1 -> x2, matrix products: 2.82 us -> 4.69 us  [the longest x1 2.86 us: shards_heads(): jnp.einsum('sd,jdc->jsc', state_in, w_qkv[1:], preferred_element_type=jnp...]
    unnamed x33 -> x39, local copies, waits for them, and re-layouts: 2.4 us -> 2.42 us
where the time goes in v13:
time: 120 us; the launch traced here: 119 us
  waiting for transfers between devices  30 us (25%)
  matrix products  22.1 us (18%)
  blocking collectives  19 us (16%)
  local copies, waits for them, and re-layouts  18.3 us (15%)
  other arithmetic  15 us (12%)
  starting transfers between devices  14.3 us (12%)
    all_gather x1, blocking collectives, shards_heads(): attention = lax.all_gather(attention_local, 'mp', axis=1, tiled=True)  19 us
    all_to_all x1, waiting for transfers between devices, shards_heads(): lax.all_to_all(jnp.dot(hidden, w_down, preferred_element_type=jnp.float32...  15.4 us
    all_to_all x1, waiting for transfers between devices, shards_heads(): lax.all_to_all(jnp.concatenate(pieces, axis=0).reshape(pages_count * slot...  13.4 us
    all_to_all x1, starting transfers between devices, shards_heads(): lax.all_to_all(jnp.concatenate(pieces, axis=0).reshape(pages_count * slot...  5.8 us
    dot_general x2, matrix products, shards_heads(): jnp.einsum('pshd,khd->phks', query_chunk, key_heads, preferred_element_ty...  5.66 us
    all_to_all x1, starting transfers between devices, shards_heads(): lax.all_to_all(jnp.tile(queries, (lax.axis_size('pages'), 1)), 'pages', 0...  4.38 us
    convert_element_type x2, local copies, waits for them, and re-layouts, shards_heads(): cache_local.reshape(pages_here * page_len, local_width).astype(jnp.float32)  4.26 us
    all_to_all x1, starting transfers between devices, shards_heads(): lax.all_to_all(jnp.dot(hidden, w_down, preferred_element_type=jnp.float32...  4.16 us
  transfers between devices with their start and end apart: 3, of which 3 were waited for; matrix products, arithmetic and copies ran while one was open for 16% of the time, Pallas kernels for 0%

profile of v13, /device:TPU:2, one launch (start us, length us, event | category | flops | bytes accessed | tf_op | source)
XLA Modules:
  0.0 119.2 jit_solution(8505331693129532365)
XLA Ops:
  0.0 1.5 %fusion.24 = f32[256]{0:T(256)S(1)} fusion(bf16[256,1280]{1,0:T(8,128)(2,1)} %param.13), kind=kLoop, calls=%fused_computation.29 | loop fusion | flops 982784 | bytes 656384 | tf_op jit(solution)/shard_map/reduce_sum | solution.py:16
  1.5 1.8 %convolution_convert_fusion.1 = bf16[256,320]{0,1:T(8,128)(2,1)S(1)} fusion(bf16[3,1280,320]{1,2,0:T(8,128)(2,1)} %param.14, bf16[256,1280]{1,0:T(8,128)(2,1)} %param.13, f32[256]{0:T(256)S(1)} %add_rsqrt_fusion.5), kind=kOutput, calls=%fused_computation.50 | convolution fusion | flops 210780160 | bytes 1639424 | tf_op jit(solution)/shard_map/dot_general | solution.py:258
  3.4 2.9 %fusion.41 = bf16[2,256,320]{1,2,0:T(8,128)(2,1)} fusion(bf16[3,1280,320]{1,2,0:T(8,128)(2,1)} %param.14, bf16[256,1280]{1,0:T(8,128)(2,1)S(1)} %copy-done.1, f32[256]{0:T(256)S(1)} %add_rsqrt_fusion.5), kind=kOutput, calls=%fused_computation.47 | convolution fusion | flops 420577280 | bytes 2622464 | tf_op jit(solution)/shard_map/sd,jdc->jsc/dot_general | solution.py:266
  6.4 1.7 %fusion.84 = (bf16[1,256,320]{1,2,0:T(8,128)(2,1)S(1)}, bf16[1,256,320]{1,2,0:T(8,128)(2,1)}) fusion(bf16[2,256,320]{1,2,0:T(8,128)(2,1)} %fusion.41), kind=kLoop, calls=%fused_computation.148 | loop fusion | bytes 655360 | tf_op jit(solution)/shard_map/slice | solution.py:270
  8.1 0.2 multiply_cosine_fusion
  8.3 0.7 multiply_subtract_fusion
  9.1 0.8 fusion.64
  9.9 0.8 dynamic_slice.33
  10.6 1.1 fusion.61
  11.7 1.2 tile.2
  12.9 4.4 %all-to-all-start = ((bf16[8,256,320]{1,2,0:T(8,128)(2,1)}), bf16[8,256,320]{1,2,0:T(8,128)(2,1)}, u32[]{:S(2)}, u32[]{:S(2)}) async-start(bf16[8,256,320]{1,2,0:T(8,128)(2,1)} %tile.2), calls=%async_computation | async-start | bytes 2621440 | tf_op jit(solution)/shard_map/all_to_all | solution.py:273
  17.4 0.2 select_reduce_fusion.3
  17.6 2.4 %constant_dynamic-slice_fusion = (bf16[4,128,320]{2,1,0:T(8,128)(2,1)}, bf16[4,128,320]{2,1,0:T(8,128)(2,1)}) fusion(bf16[4,128,1280]{2,1,0:T(8,128)(2,1)} %param.21, s32[]{:T(128)S(6)} %select_n.61, bf16[4,128,1280]{2,1,0:T(8,128)(2,1)} %param.22), kind=kLoop, calls=%fused_computation.117 | loop fusion | bytes 1310724 | tf_op jit(solution)/shard_map/dynamic_slice | solution.py:305
  20.1 1.9 %copy.65 = bf16[4,128,320]{1,2,0:T(8,128)(2,1)} copy(bf16[4,128,320]{2,1,0:T(8,128)(2,1)} %get-tuple-element.44) | data formatting | bytes 655360
  21.9 2.1 %copy.55 = f32[4,128,320]{1,0,2:T(4,128)} copy(bf16[4,128,320]{1,2,0:T(8,128)(2,1)} %copy.65) | data formatting | bytes 983040 | tf_op jit(solution)/shard_map/convert_element_type | solution.py:307
  24.0 2.2 %reshape.357 = f32[512,5,64]{0,2,1:T(8,128)} reshape(f32[4,128,320]{1,0,2:T(4,128)} %copy.55) | data formatting | bytes 1310720 | tf_op jit(solution)/shard_map/convert_element_type | solution.py:307
  26.2 1.2 multiply_reduce_fusion.2
  27.4 1.9 %copy.53 = bf16[4,128,320]{1,0,2:T(4,128)(2,1)} copy(bf16[4,128,320]{2,1,0:T(8,128)(2,1)} %get-tuple-element.45) | data formatting | bytes 655360 | tf_op jit(solution)/shard_map/dynamic_slice | solution.py:311
  29.3 1.8 %reshape.360 = bf16[512,5,64,1]{0,2,1,3:T(8,128)(2,1)} reshape(bf16[4,128,320]{1,0,2:T(4,128)(2,1)} %copy.53) | data formatting | bytes 655360 | tf_op jit(solution)/shard_map/reshape;reshape | solution.py:316
  31.2 1.7 %broadcast_compare_fusion.1 = (pred[4,512,256]{2,1,0:T(8,128)(4,1)}, pred[4,512,256]{2,1,0:T(8,128)(4,1)}) fusion(s32[4,256]{1,0:T(4,128)S(1)} %get-tuple-element.25, s32[512]{0:T(512)S(1)} %broadcast_bitcast_fusion, s32[4,256]{1,0:T(4,128)S(1)} %get-tuple-element.26), kind=kLoop, calls=%fused_computation.52 | loop fusion | flops 1048576 | bytes 1058816 | tf_op jit(solution)/shard_map/eq | solution.py:334
  32.9 1.2 %all-to-all-done = bf16[8,256,320]{1,2,0:T(8,128)(2,1)} async-done(((bf16[8,256,320]{1,2,0:T(8,128)(2,1)}), bf16[8,256,320]{1,2,0:T(8,128)(2,1)}, u32[]{:S(2)}, u32[]{:S(2)}) %all-to-all-start) | async-done | bytes 1310752 | tf_op jit(solution)/shard_map/all_to_all | solution.py:273
  34.1 1.5 %fusion.83 = (bf16[4,256,320]{1,2,0:T(8,128)(2,1)S(1)}, bf16[4,256,320]{1,2,0:T(8,128)(2,1)S(1)}) fusion(bf16[8,256,320]{1,2,0:T(8,128)(2,1)} %all-to-all-done), kind=kLoop, calls=%fused_computation.147 | loop fusion | bytes 2621440 | tf_op jit(solution)/shard_map/slice | solution.py:322
  35.6 0.1 copy-done.7
  35.7 2.8 %fusion.2 = (bf16[4,5,256]{2,0,1:T(4,128)(2,1)S(1)}, f32[5,512,4,256]{3,1,2,0:T(8,128)S(1)}) fusion(pred[4,512,256]{2,1,0:T(8,128)(4,1)S(1)} %copy-done.7, bf16[4,256,5,64]{1,3,2,0:T(8,128)(2,1)S(1)} %bitcast.123, f32[512,5,64]{0,2,1:T(8,128)S(1)} %copy-done.5, f32[5,64]{1,0:T(8,128)S(1)} %mul.324, f32[512,5]{0,1:T(8,128)S(1)} %add_rsqrt_fusion), kind=kOutput, calls=%fused_computation.4 | convolution fusion | flops 343895040 | bytes 12342528 | tf_op jit(solution)/shard_map/pshd,khd->phks/dot_general | solution.py:329
  38.6 2.0 %fusion.31 = bf16[4,256,5,64]{1,3,0,2:T(8,128)(2,1)S(1)} fusion(f32[5,512,4,256]{3,1,2,0:T(8,128)S(1)} %get-tuple-element.35, pred[4,512,256]{2,1,0:T(8,128)(4,1)S(1)} %copy-done.7, bf16[512,5,64,1]{0,2,1,3:T(8,128)(2,1)S(1)} %copy-done.8), kind=kOutput, calls=%fused_computation.42 | convolution fusion | flops 343736320 | bytes 11993088 | tf_op jit(solution)/shard_map/phks,khd->pshd/dot_general | solution.py:337
  40.7 2.8 %fusion = (bf16[4,5,256]{2,0,1:T(4,128)(2,1)S(1)}, f32[5,512,4,256]{3,1,2,0:T(8,128)S(1)}) fusion(pred[4,512,256]{2,1,0:T(8,128)(4,1)S(1)} %copy-done.6, bf16[4,256,5,64]{1,3,2,0:T(8,128)(2,1)S(1)} %bitcast.122, f32[512,5,64]{0,2,1:T(8,128)S(1)} %copy-done.5, f32[5,64]{1,0:T(8,128)S(1)} %mul.324, f32[512,5]{0,1:T(8,128)S(1)} %add_rsqrt_fusion), kind=kOutput, calls=%fused_computation.2 | convolution fusion | flops 343895040 | bytes 12342528 | tf_op jit(solution)/shard_map/pshd,khd->phks/dot_general | solution.py:329
  43.5 2.0 %fusion.34 = bf16[4,256,5,64]{1,3,0,2:T(8,128)(2,1)S(1)} fusion(f32[5,512,4,256]{3,1,2,0:T(8,128)S(1)} %get-tuple-element.37, pred[4,512,256]{2,1,0:T(8,128)(4,1)S(1)} %copy-done.6, bf16[512,5,64,1]{0,2,1,3:T(8,128)(2,1)S(1)} %copy-done.8), kind=kOutput, calls=%fused_computation.43 | convolution fusion | flops 343736320 | bytes 11993088 | tf_op jit(solution)/shard_map/phks,khd->pshd/dot_general | solution.py:337
  45.6 1.2 maximum_maximum_fusion
  46.8 5.8 %all-to-all-start.1 = ((bf16[8,256,325]{1,2,0:T(8,128)(2,1)}), bf16[8,256,325]{1,2,0:T(8,128)(2,1)}, u32[]{:S(2)}, u32[]{:S(2)}) async-start(bf16[8,256,325]{1,2,0:T(8,128)(2,1)} %maximum_maximum_fusion), calls=%async_computation.1 | async-start | bytes 2686976 | tf_op jit(solution)/shard_map/all_to_all | solution.py:352
  52.6 1.0 multiply_reduce_fusion.5
  53.7 0.2 and_and_fusion
  53.8 2.5 %fusion.86 = (f32[5,256]{1,0:T(8,128)S(1)}, bf16[5,256,256]{1,2,0:T(8,128)(2,1)}) fusion(f32[256,5,32]{0,2,1:T(8,128)} %get-tuple-element.18, f32[256,5,32]{0,2,1:T(8,128)S(1)} %get-tuple-element.17, f32[256,5]{0,1:T(8,128)S(1)} %add_rsqrt_fusion.1, f32[5,64]{1,0:T(8,128)S(1)} %mul.324, f32[256,5,64]{0,2,1:T(8,128)} %fusion.64, ...), kind=kOutput, calls=%fused_computation.150 | convolution fusion | flops 43744000 | bytes 1387776 | tf_op jit(solution)/shard_map/qhd,khd->hqk/dot_general | solution.py:277
  56.3 13.4 %all-to-all-done.1 = bf16[8,256,325]{1,2,0:T(8,128)(2,1)} async-done(((bf16[8,256,325]{1,2,0:T(8,128)(2,1)}), bf16[8,256,325]{1,2,0:T(8,128)(2,1)}, u32[]{:S(2)}, u32[]{:S(2)}) %all-to-all-start.1) | async-done | bytes 1331232 | tf_op jit(solution)/shard_map/all_to_all | solution.py:352
  69.8 1.6 %convert_reduce_fusion = f32[256,325]{0,1:T(8,128)S(1)} fusion(bf16[8,256,325]{1,2,0:T(8,128)(2,1)} %all-to-all-done.1), kind=kLoop, calls=%fused_computation.15 | loop fusion | flops 1248000 | bytes 1664000 | tf_op jit(solution)/shard_map/reduce_sum | solution.py:359
  71.4 0.2 fusion.45
  71.7 19.0 %all_gather.3 = bf16[256,1280]{0,1:T(8,128)(2,1)S(1)} all-gather(bf16[256,320]{0,1:T(8,128)(2,1)S(1)} %bitcast.129), channel_id=1, replica_groups=mesh['pages'=8,'mp'=4] {'mp'}, dimensions={1}, use_global_device_ids=true | all-gather | bytes 819200 | tf_op jit(solution)/shard_map/all_gather | solution.py:370
  90.7 1.1 multiply_reduce_fusion.1
  91.8 0.5 multiply_reduce_fusion
  92.3 0.4 multiply_convert_fusion
  92.8 1.9 %convolution_bitcast_fusion = f32[2,256,1280]{2,1,0:T(8,128)S(1)} fusion(bf16[2,1280,1280]{2,1,0:T(8,128)(2,1)S(1)} %bitcast.119, bf16[256,1280]{1,0:T(8,128)(2,1)S(1)} %multiply_convert_fusion), kind=kOutput, calls=%fused_computation.14 | convolution fusion | flops 1677721600 | bytes 9830400 | tf_op jit(solution)/shard_map/sd,jdf->jsf/dot_general | solution.py:377
  94.7 0.3 copy-done.14
  94.9 2.1 %convolution_convert_fusion = bf16[256,1280]{1,0:T(8,128)(2,1)} fusion(bf16[1280,1280]{1,0:T(8,128)(2,1)S(1)} %copy-done.14, f32[2,256,1280]{2,1,0:T(8,128)S(1)} %convolution_bitcast_fusion, f32[1280]{0:T(1024)S(1)} %get-tuple-element.8, f32[1280]{0:T(1024)S(1)} %get-tuple-element.7), kind=kOutput, calls=%fused_computation.16 | convolution fusion | flops 841809920 | bytes 6563840 | tf_op jit(solution)/shard_map/dot_general | solution.py:383
  97.0 4.2 %all-to-all-start.2 = ((bf16[4,64,1280]{2,1,0:T(8,128)(2,1)}), bf16[4,64,1280]{2,1,0:T(8,128)(2,1)}, u32[]{:S(2)}, u32[]{:S(2)}) async-start(bf16[4,64,1280]{2,1,0:T(8,128)(2,1)} %bitcast.124), calls=%async_computation.2 | async-start | bytes 1310720 | tf_op jit(solution)/shard_map/all_to_all | solution.py:382
  101.3 15.4 %all-to-all-done.2 = bf16[4,64,1280]{2,1,0:T(8,128)(2,1)} async-done(((bf16[4,64,1280]{2,1,0:T(8,128)(2,1)}), bf16[4,64,1280]{2,1,0:T(8,128)(2,1)}, u32[]{:S(2)}, u32[]{:S(2)}) %all-to-all-start.2) | async-done | bytes 655392 | tf_op jit(solution)/shard_map/all_to_all | solution.py:382
  116.7 1.3 %convert_reduce_fusion.1 = f32[64,1280]{1,0:T(8,128)S(1)} fusion(bf16[4,64,1280]{2,1,0:T(8,128)(2,1)} %all-to-all-done.2), kind=kLoop, calls=%fused_computation.38 | loop fusion | flops 573440 | bytes 983040 | tf_op jit(solution)/shard_map/reduce_sum | solution.py:389
  117.9 0.1 multiply_reduce_fusion.4
  118.1 0.3 multiply_reduce_fusion.3
  118.3 0.9 multiply_convert_fusion.2
  (72 shorter events, 0.9 us)
Async XLA Ops:
  0.0 90.7 %copy-start = (bf16[1280,1280]{1,0:T(8,128)(2,1)S(1)}, bf16[1280,1280]{1,0:T(8,128)(2,1)}, u32[]{:S(2)}) copy-start(bf16[1280,1280]{1,0:T(8,128)(2,1)} %param.15) | copy-start | bytes 9830404
  0.0 3.3 %copy-start.1 = (bf16[256,1280]{1,0:T(8,128)(2,1)S(1)}, bf16[256,1280]{1,0:T(8,128)(2,1)}, u32[]{:S(2)}) copy-start(bf16[256,1280]{1,0:T(8,128)(2,1)} %param.13) | copy-start | bytes 1966084
  3.3 2.9 %copy-start.12 = (s32[8,4]{0,1:T(4,128)S(1)}, s32[8,4]{0,1:T(4,128)}, u32[]{:S(2)}) copy-start(s32[8,4]{0,1:T(4,128)} %param.25) | copy-start | bytes 388
  3.3 2.9 %copy-start.13 = (s32[8,4]{0,1:T(4,128)S(1)}, s32[8,4]{0,1:T(4,128)}, u32[]{:S(2)}) copy-start(s32[8,4]{0,1:T(4,128)} %param.24) | copy-start | bytes 388
  12.9 4.6 %copy-start.15 = (s32[32]{0:T(128)S(1)}, s32[32]{0:T(128)}, u32[]{:S(2)}) copy-start(s32[32]{0:T(128)} %param.23) | copy-start | bytes 388
  12.9 21.2 %all-to-all-start = ((bf16[8,256,320]{1,2,0:T(8,128)(2,1)}), bf16[8,256,320]{1,2,0:T(8,128)(2,1)}, u32[]{:S(2)}, u32[]{:S(2)}) async-start(bf16[8,256,320]{1,2,0:T(8,128)(2,1)} %tile.2), calls=%async_computation | async-start | bytes 2621440 | tf_op jit(solution)/shard_map/all_to_all | solution.py:273
  34.1 1.5 %copy-start.5 = (f32[512,5,64]{0,2,1:T(8,128)S(1)}, f32[512,5,64]{0,2,1:T(8,128)}, u32[]{:S(2)}) copy-start(f32[512,5,64]{0,2,1:T(8,128)} %reshape.357) | copy-start | bytes 1966084
  34.1 1.6 %copy-start.7 = (pred[4,512,256]{2,1,0:T(8,128)(4,1)S(1)}, pred[4,512,256]{2,1,0:T(8,128)(4,1)}, u32[]{:S(2)}) copy-start(pred[4,512,256]{2,1,0:T(8,128)(4,1)} %get-tuple-element.28) | copy-start | bytes 1572868
  35.7 2.8 %copy-start.8 = (bf16[512,5,64,1]{0,2,1,3:T(8,128)(2,1)S(1)}, bf16[512,5,64,1]{0,2,1,3:T(8,128)(2,1)}, u32[]{:S(2)}) copy-start(bf16[512,5,64,1]{0,2,1,3:T(8,128)(2,1)} %reshape.360) | copy-start | bytes 983044
  38.6 2.1 %copy-start.6 = (pred[4,512,256]{2,1,0:T(8,128)(4,1)S(1)}, pred[4,512,256]{2,1,0:T(8,128)(4,1)}, u32[]{:S(2)}) copy-start(pred[4,512,256]{2,1,0:T(8,128)(4,1)} %get-tuple-element.27) | copy-start | bytes 1572868
  46.8 6.8 %copy-start.10 = (f32[2,1280]{1,0:T(2,128)S(1)}, f32[2,1280]{1,0:T(2,128)}, u32[]{:S(2)}) copy-start(f32[2,1280]{1,0:T(2,128)} %param.19) | copy-start | bytes 30724
  46.8 6.8 %copy-start.11 = (f32[2,1280]{1,0:T(2,128)S(1)}, f32[2,1280]{1,0:T(2,128)}, u32[]{:S(2)}) copy-start(f32[2,1280]{1,0:T(2,128)} %param.20) | copy-start | bytes 30724
  46.8 23.0 %all-to-all-start.1 = ((bf16[8,256,325]{1,2,0:T(8,128)(2,1)}), bf16[8,256,325]{1,2,0:T(8,128)(2,1)}, u32[]{:S(2)}, u32[]{:S(2)}) async-start(bf16[8,256,325]{1,2,0:T(8,128)(2,1)} %maximum_maximum_fusion), calls=%async_computation.1 | async-start | bytes 2686976 | tf_op jit(solution)/shard_map/all_to_all | solution.py:352
  56.3 15.1 %copy-start.9 = (bf16[1,256,320]{1,2,0:T(8,128)(2,1)S(1)}, bf16[1,256,320]{1,2,0:T(8,128)(2,1)}, u32[]{:S(2)}) copy-start(bf16[1,256,320]{1,2,0:T(8,128)(2,1)} %get-tuple-element.22) | copy-start | bytes 491524
  69.7 1.7 %copy-start.16 = (bf16[5,256,256]{1,2,0:T(8,128)(2,1)S(1)}, bf16[5,256,256]{1,2,0:T(8,128)(2,1)}, u32[]{:S(2)}) copy-start(bf16[5,256,256]{1,2,0:T(8,128)(2,1)} %get-tuple-element.39) | copy-start | bytes 1966084
  71.4 21.3 %slice-start = ((s8[6553600]{0:T(1024)(128)(4,1)}), s8[4194304]{0:T(1024)(128)(4,1)S(1)}, s32[]{:S(2)}) async-start(s8[6553600]{0:T(1024)(128)(4,1)} %bitcast.118), calls=%async_computation.3 | async-start | bytes 8388608
  90.7 1.1 copy-start.2
  90.7 2.1 %slice-start.1 = ((s8[6553600]{0:T(1024)(128)(4,1)}), s8[2359296]{0:T(1024)(128)(4,1)S(1)}, s32[]{:S(2)}) async-start(s8[6553600]{0:T(1024)(128)(4,1)} %bitcast.118), calls=%async_computation.4 | async-start | bytes 4718592
  92.8 1.9 %copy-start.3 = (bf16[256,1280]{1,0:T(8,128)(2,1)}, bf16[256,1280]{1,0:T(8,128)(2,1)S(1)}, u32[]{:S(2)}) copy-start(bf16[256,1280]{1,0:T(8,128)(2,1)S(1)} %multiply_convert_fusion) | copy-start | bytes 1966084
  92.8 2.2 %copy-start.14 = (bf16[1280,1280]{1,0:T(8,128)(2,1)S(1)}, bf16[1280,1280]{1,0:T(8,128)(2,1)}, u32[]{:S(2)}) copy-start(bf16[1280,1280]{1,0:T(8,128)(2,1)} %param.17) | copy-start | bytes 9830404
  97.0 19.6 %all-to-all-start.2 = ((bf16[4,64,1280]{2,1,0:T(8,128)(2,1)}), bf16[4,64,1280]{2,1,0:T(8,128)(2,1)}, u32[]{:S(2)}, u32[]{:S(2)}) async-start(bf16[4,64,1280]{2,1,0:T(8,128)(2,1)} %bitcast.124), calls=%async_computation.2 | async-start | bytes 1310720 | tf_op jit(solution)/shard_map/all_to_all | solution.py:382
  116.7 1.4 %copy-start.4 = (bf16[256,1280]{1,0:T(8,128)(2,1)S(1)}, bf16[256,1280]{1,0:T(8,128)(2,1)}, u32[]{:S(2)}) copy-start(bf16[256,1280]{1,0:T(8,128)(2,1)} %copy-done.3) | copy-start | bytes 1966084

commit v14 on v13

--- a/solution.py
+++ b/solution.py
@@ -263,16 +263,17 @@
         scale_local,
         local_heads,
     ).astype(jnp.bfloat16)
+    gathered = lax.all_to_all(
+        jnp.tile(queries, (lax.axis_size("pages"), 1)), "pages", 0, 0, tiled=True
+    )
+    state_kv, gathered = lax.optimization_barrier((state_in, gathered))
     projected = jnp.einsum(
-        "sd,jdc->jsc", state_in, w_qkv[1:], preferred_element_type=jnp.float32
+        "sd,jdc->jsc", state_kv, w_qkv[1:], preferred_element_type=jnp.float32
     ).astype(jnp.bfloat16)
     keys_new = head_norm(
         rotate(projected[0].astype(jnp.float32), position_shard, local_heads), scale_local, local_heads
     ).astype(jnp.bfloat16)
     value_rows = projected[1]
-    gathered = lax.all_to_all(
-        jnp.tile(queries, (lax.axis_size("pages"), 1)), "pages", 0, 0, tiled=True
-    )
     scores = (
         jnp.einsum(
             "qhd,khd->hqk",

time: 120 us -> 126 us (1.050)
  local copies, waits for them, and re-layouts: 18.3 us -> 23.4 us
  other arithmetic: 15 us -> 17.5 us
  waiting for transfers between devices: 30 us -> 28.1 us
    slice x1 -> x3, local copies, waits for them, and re-layouts: 1.47 us -> 6.09 us  [shards_heads(): lax.slice_in_dim(gathered_heads, chunk * chunk_pages, (chunk + 1) * chunk...]
    dot_general x2, matrix products: 5.66 us -> 7.49 us  [shards_heads(): jnp.einsum('pshd,khd->phks', query_chunk, key_heads, preferred_element_ty...]
    slice x1, local copies, waits for them, and re-layouts: 1.68 us -> 0.02 us  [shards_heads(): projected[0].astype(jnp.float32)]
    all_to_all x0 -> x1, local copies, waits for them, and re-layouts: none -> 1.47 us  [shards_heads(): lax.all_to_all(jnp.tile(queries, (lax.axis_size('pages'), 1)), 'pages', 0...]
    convert_element_type x0 -> x1, other arithmetic: none -> 1.27 us  [shards_heads(): state_in = rms_rows(hidden_in.astype(jnp.float32)).astype(jnp.bfloat16)]
where the time goes in v14:
time: 126 us; the launch traced here: 125 us
  waiting for transfers between devices  28.1 us (22%)
  local copies, waits for them, and re-layouts  23.4 us (19%)
  matrix products  22.3 us (18%)
  blocking collectives  19.2 us (15%)
  other arithmetic  17.5 us (14%)
  starting transfers between devices  14.2 us (11%)
    all_gather x1, blocking collectives, shards_heads(): attention = lax.all_gather(attention_local, 'mp', axis=1, tiled=True)  19.2 us
    all_to_all x1, waiting for transfers between devices, shards_heads(): lax.all_to_all(jnp.dot(hidden, w_down, preferred_element_type=jnp.float32...  15.4 us
    all_to_all x1, waiting for transfers between devices, shards_heads(): lax.all_to_all(jnp.concatenate(pieces, axis=0).reshape(pages_count * slot...  12.5 us
    dot_general x2, matrix products, shards_heads(): jnp.einsum('pshd,khd->phks', query_chunk, key_heads, preferred_element_ty...  7.49 us
    slice x3, local copies, waits for them, and re-layouts, shards_heads(): lax.slice_in_dim(gathered_heads, chunk * chunk_pages, (chunk + 1) * chunk...  6.09 us
    all_to_all x1, starting transfers between devices, shards_heads(): lax.all_to_all(jnp.concatenate(pieces, axis=0).reshape(pages_count * slot...  5.67 us
    all_to_all x1, starting transfers between devices, shards_heads(): lax.all_to_all(jnp.tile(queries, (lax.axis_size('pages'), 1)), 'pages', 0...  4.38 us
    convert_element_type x2, local copies, waits for them, and re-layouts, shards_heads(): cache_local.reshape(pages_here * page_len, local_width).astype(jnp.float32)  4.28 us
  transfers between devices with their start and end apart: 3, of which 3 were waited for; matrix products, arithmetic and copies ran while one was open for 16% of the time, Pallas kernels for 0%

profile of v14, /device:TPU:2, one launch (start us, length us, event | category | flops | bytes accessed | tf_op | source)
XLA Modules:
  0.0 125.3 jit_solution(2783817559240864375)
XLA Ops:
  0.0 1.4 %fusion.24 = f32[256]{0:T(256)S(1)} fusion(bf16[256,1280]{1,0:T(8,128)(2,1)} %param.13), kind=kLoop, calls=%fused_computation.29 | loop fusion | flops 982784 | bytes 656384 | tf_op jit(solution)/shard_map/reduce_sum | solution.py:16
  1.5 0.8 slice_add_fusion.1
  2.3 0.7 fusion.79
  3.0 0.8 select_reduce_fusion.1
  3.8 1.3 %fusion.25 = bf16[256,1280]{1,0:T(8,128)(2,1)S(1)} fusion(bf16[256,1280]{1,0:T(8,128)(2,1)} %param.13, f32[256]{0:T(256)S(1)} %add_rsqrt_fusion.5), kind=kLoop, calls=%fused_computation.30 | loop fusion | flops 983040 | bytes 1311744 | tf_op jit(solution)/shard_map/convert_element_type | solution.py:257
  5.1 1.8 %convolution_convert_fusion.1 = bf16[256,320]{0,1:T(8,128)(2,1)S(1)} fusion(bf16[256,1280]{1,0:T(8,128)(2,1)S(1)} %fusion.25, bf16[3,1280,320]{1,2,0:T(8,128)(2,1)} %param.14), kind=kOutput, calls=%fused_computation.50 | convolution fusion | flops 209797120 | bytes 1638400 | tf_op jit(solution)/shard_map/dot_general | solution.py:258
  7.2 0.8 fusion.64
  8.0 0.8 dynamic_slice.28
  8.8 1.1 fusion.63
  9.8 1.2 tile.2
  11.0 4.4 %all-to-all-start = ((bf16[8,256,320]{1,2,0:T(8,128)(2,1)}), bf16[8,256,320]{1,2,0:T(8,128)(2,1)}, u32[]{:S(2)}, u32[]{:S(2)}) async-start(bf16[8,256,320]{1,2,0:T(8,128)(2,1)} %tile.2), calls=%async_computation | async-start | bytes 2621440 | tf_op jit(solution)/shard_map/all_to_all | solution.py:266
  15.9 2.4 %constant_dynamic-slice_fusion = (bf16[4,128,320]{2,1,0:T(8,128)(2,1)}, bf16[4,128,320]{2,1,0:T(8,128)(2,1)}) fusion(bf16[4,128,1280]{2,1,0:T(8,128)(2,1)} %param.21, s32[]{:T(128)S(6)} %select_n.60, bf16[4,128,1280]{2,1,0:T(8,128)(2,1)} %param.22), kind=kLoop, calls=%fused_computation.117 | loop fusion | bytes 1310724 | tf_op jit(solution)/shard_map/dynamic_slice | solution.py:306
  18.4 1.9 %copy.80 = bf16[4,128,320]{1,2,0:T(8,128)(2,1)} copy(bf16[4,128,320]{2,1,0:T(8,128)(2,1)} %get-tuple-element.46) | data formatting | bytes 655360
  20.3 2.1 %copy.70 = f32[4,128,320]{1,0,2:T(4,128)} copy(bf16[4,128,320]{1,2,0:T(8,128)(2,1)} %copy.80) | data formatting | bytes 983040 | tf_op jit(solution)/shard_map/convert_element_type | solution.py:308
  22.4 2.2 %reshape.353 = f32[512,5,64]{0,2,1:T(8,128)} reshape(f32[4,128,320]{1,0,2:T(4,128)} %copy.70) | data formatting | bytes 1310720 | tf_op jit(solution)/shard_map/convert_element_type | solution.py:308
  24.6 1.2 multiply_reduce_fusion.2
  25.7 1.9 %copy.68 = bf16[4,128,320]{1,0,2:T(4,128)(2,1)} copy(bf16[4,128,320]{2,1,0:T(8,128)(2,1)} %get-tuple-element.47) | data formatting | bytes 655360 | tf_op jit(solution)/shard_map/dynamic_slice | solution.py:312
  27.6 1.8 %reshape.356 = bf16[512,5,64,1]{0,2,1,3:T(8,128)(2,1)} reshape(bf16[4,128,320]{1,0,2:T(4,128)(2,1)} %copy.68) | data formatting | bytes 655360 | tf_op jit(solution)/shard_map/reshape;reshape | solution.py:317
  29.5 0.8 and_and_fusion
  30.3 1.6 %broadcast_compare_fusion.1 = (pred[4,512,256]{2,1,0:T(8,128)(4,1)}, pred[4,512,256]{2,1,0:T(8,128)(4,1)}) fusion(s32[4,256]{1,0:T(4,128)S(1)} %get-tuple-element.27, s32[512]{0:T(512)S(1)} %broadcast_bitcast_fusion, s32[4,256]{1,0:T(4,128)S(1)} %get-tuple-element.28), kind=kLoop, calls=%fused_computation.52 | loop fusion | flops 1048576 | bytes 1058816 | tf_op jit(solution)/shard_map/eq | solution.py:335
  32.2 1.5 %copy.81 = bf16[8,40,8,256]{3,2,0,1:T(8,128)(2,1)S(1)} copy(bf16[8,40,8,256]{3,2,1,0:T(8,128)(2,1)} %bitcast.34) | data formatting | bytes 2621440 | tf_op jit(solution)/shard_map/all_to_all | solution.py:266
  33.7 1.2 fusion.81
  34.9 2.5 %slice.93 = bf16[4,256,5,64]{1,0,3,2:T(4,128)(2,1)} reshape(bf16[1024,320]{0,1:T(8,128)(2,1)} %get-tuple-element.19) | data formatting | bytes 1310720 | tf_op jit(solution)/shard_map/slice | solution.py:323
  37.3 2.5 %slice.96 = bf16[4,256,5,64]{1,0,3,2:T(4,128)(2,1)} reshape(bf16[1024,320]{0,1:T(8,128)(2,1)} %get-tuple-element.20) | data formatting | bytes 1310720 | tf_op jit(solution)/shard_map/slice | solution.py:323
  39.8 4.5 %fusion.2 = (bf16[4,5,256]{2,0,1:T(4,128)(2,1)S(1)}, f32[5,512,4,256]{3,1,2,0:T(8,128)S(1)}) fusion(pred[4,512,256]{2,1,0:T(8,128)(4,1)} %get-tuple-element.30, bf16[4,256,5,64]{1,0,3,2:T(4,128)(2,1)} %slice.96, f32[512,5,64]{0,2,1:T(8,128)} %reshape.353, f32[5,64]{1,0:T(8,128)S(1)} %mul.327, f32[512,5]{0,1:T(8,128)S(1)} %add_rsqrt_fusion), kind=kOutput, calls=%fused_computation.4 | convolution fusion | flops 343895040 | bytes 12342528 | tf_op jit(solution)/shard_map/pshd,khd->phks/dot_general | solution.py:330
  44.3 2.0 %fusion.31 = bf16[4,256,5,64]{1,3,0,2:T(8,128)(2,1)S(1)} fusion(f32[5,512,4,256]{3,1,2,0:T(8,128)S(1)} %get-tuple-element.37, pred[4,512,256]{2,1,0:T(8,128)(4,1)S(1)} %copy-done.9, bf16[512,5,64,1]{0,2,1,3:T(8,128)(2,1)S(1)} %copy-done.10), kind=kOutput, calls=%fused_computation.42 | convolution fusion | flops 343736320 | bytes 11993088 | tf_op jit(solution)/shard_map/phks,khd->pshd/dot_general | solution.py:338
  46.5 3.0 %fusion = (bf16[4,5,256]{2,0,1:T(4,128)(2,1)S(1)}, f32[5,512,4,256]{3,1,2,0:T(8,128)S(1)}) fusion(pred[4,512,256]{2,1,0:T(8,128)(4,1)S(1)} %copy-done.8, bf16[4,256,5,64]{1,0,3,2:T(4,128)(2,1)S(1)} %copy-done.6, f32[512,5,64]{0,2,1:T(8,128)S(1)} %copy-done.4, f32[5,64]{1,0:T(8,128)S(1)} %mul.327, f32[512,5]{0,1:T(8,128)S(1)} %add_rsqrt_fusion), kind=kOutput, calls=%fused_computation.2 | convolution fusion | flops 343895040 | bytes 12342528 | tf_op jit(solution)/shard_map/pshd,khd->phks/dot_general | solution.py:330
  49.4 2.0 %fusion.34 = bf16[4,256,5,64]{1,3,0,2:T(8,128)(2,1)S(1)} fusion(f32[5,512,4,256]{3,1,2,0:T(8,128)S(1)} %get-tuple-element.39, pred[4,512,256]{2,1,0:T(8,128)(4,1)S(1)} %copy-done.8, bf16[512,5,64,1]{0,2,1,3:T(8,128)(2,1)S(1)} %copy-done.10), kind=kOutput, calls=%fused_computation.43 | convolution fusion | flops 343736320 | bytes 11993088 | tf_op jit(solution)/shard_map/phks,khd->pshd/dot_general | solution.py:338
  51.5 1.2 maximum_maximum_fusion
  52.7 5.7 %all-to-all-start.1 = ((bf16[8,256,325]{1,2,0:T(8,128)(2,1)}), bf16[8,256,325]{1,2,0:T(8,128)(2,1)}, u32[]{:S(2)}, u32[]{:S(2)}) async-start(bf16[8,256,325]{1,2,0:T(8,128)(2,1)} %maximum_maximum_fusion), calls=%async_computation.1 | async-start | bytes 2686976 | tf_op jit(solution)/shard_map/all_to_all | solution.py:353
  58.4 2.3 %fusion.41 = bf16[2,256,320]{1,2,0:T(8,128)(2,1)S(1)} fusion(bf16[3,1280,320]{1,2,0:T(8,128)(2,1)} %param.14, bf16[256,1280]{1,0:T(8,128)(2,1)} %copy-done.7), kind=kOutput, calls=%fused_computation.47 | convolution fusion | flops 419594240 | bytes 2621440 | tf_op jit(solution)/shard_map/sd,jdc->jsc/dot_general | solution.py:270
  60.8 0.8 copy-done.5
  61.6 1.4 %fusion.84 = (f32[5,256]{1,0:T(8,128)S(1)}, bf16[5,256,256]{1,2,0:T(8,128)(2,1)}) fusion(f32[256,5,32]{0,2,1:T(8,128)S(1)} %get-tuple-element.22, f32[256,5,32]{0,2,1:T(8,128)S(1)} %get-tuple-element.21, f32[256,5]{0,1:T(8,128)S(1)} %add_rsqrt_fusion.1, f32[5,64]{1,0:T(8,128)S(1)} %mul.327, f32[256,5,64]{0,2,1:T(8,128)S(1)} %copy-done.5, ...), kind=kOutput, calls=%fused_computation.150 | convolution fusion | flops 43744000 | bytes 1387776 | tf_op jit(solution)/shard_map/qhd,khd->hqk/dot_general | solution.py:278
  63.0 12.5 %all-to-all-done.1 = bf16[8,256,325]{1,2,0:T(8,128)(2,1)} async-done(((bf16[8,256,325]{1,2,0:T(8,128)(2,1)}), bf16[8,256,325]{1,2,0:T(8,128)(2,1)}, u32[]{:S(2)}, u32[]{:S(2)}) %all-to-all-start.1) | async-done | bytes 1331232 | tf_op jit(solution)/shard_map/all_to_all | solution.py:353
  75.5 1.6 %convert_reduce_fusion = f32[256,325]{0,1:T(8,128)S(1)} fusion(bf16[8,256,325]{1,2,0:T(8,128)(2,1)} %all-to-all-done.1), kind=kLoop, calls=%fused_computation.15 | loop fusion | flops 1248000 | bytes 1664000 | tf_op jit(solution)/shard_map/reduce_sum | solution.py:360
  77.2 0.2 fusion.45
  77.5 19.2 %all_gather.3 = bf16[256,1280]{0,1:T(8,128)(2,1)S(1)} all-gather(bf16[256,320]{0,1:T(8,128)(2,1)S(1)} %bitcast.132), channel_id=1, replica_groups=mesh['pages'=8,'mp'=4] {'mp'}, dimensions={1}, use_global_device_ids=true | all-gather | bytes 819200 | tf_op jit(solution)/shard_map/all_gather | solution.py:371
  96.7 1.1 multiply_reduce_fusion.1
  97.8 0.5 multiply_reduce_fusion
  98.3 0.4 multiply_convert_fusion
  98.8 1.9 %convolution_bitcast_fusion = f32[2,256,1280]{2,1,0:T(8,128)S(1)} fusion(bf16[2,1280,1280]{2,1,0:T(8,128)(2,1)S(1)} %bitcast.124, bf16[256,1280]{1,0:T(8,128)(2,1)S(1)} %multiply_convert_fusion), kind=kOutput, calls=%fused_computation.14 | convolution fusion | flops 1677721600 | bytes 9830400 | tf_op jit(solution)/shard_map/sd,jdf->jsf/dot_general | solution.py:378
  100.7 0.3 copy-done.14
  101.0 2.1 %convolution_convert_fusion = bf16[256,1280]{1,0:T(8,128)(2,1)} fusion(bf16[1280,1280]{1,0:T(8,128)(2,1)S(1)} %copy-done.14, f32[2,256,1280]{2,1,0:T(8,128)S(1)} %convolution_bitcast_fusion, f32[1280]{0:T(1024)S(1)} %get-tuple-element.12, f32[1280]{0:T(1024)S(1)} %get-tuple-element.11), kind=kOutput, calls=%fused_computation.16 | convolution fusion | flops 841809920 | bytes 6563840 | tf_op jit(solution)/shard_map/dot_general | solution.py:384
  103.0 4.2 %all-to-all-start.2 = ((bf16[4,64,1280]{2,1,0:T(8,128)(2,1)}), bf16[4,64,1280]{2,1,0:T(8,128)(2,1)}, u32[]{:S(2)}, u32[]{:S(2)}) async-start(bf16[4,64,1280]{2,1,0:T(8,128)(2,1)} %bitcast.128), calls=%async_computation.2 | async-start | bytes 1310720 | tf_op jit(solution)/shard_map/all_to_all | solution.py:383
  107.3 15.4 %all-to-all-done.2 = bf16[4,64,1280]{2,1,0:T(8,128)(2,1)} async-done(((bf16[4,64,1280]{2,1,0:T(8,128)(2,1)}), bf16[4,64,1280]{2,1,0:T(8,128)(2,1)}, u32[]{:S(2)}, u32[]{:S(2)}) %all-to-all-start.2) | async-done | bytes 655392 | tf_op jit(solution)/shard_map/all_to_all | solution.py:383
  122.7 1.3 %convert_reduce_fusion.1 = f32[64,1280]{1,0:T(8,128)S(1)} fusion(bf16[4,64,1280]{2,1,0:T(8,128)(2,1)} %all-to-all-done.2), kind=kLoop, calls=%fused_computation.38 | loop fusion | flops 573440 | bytes 983040 | tf_op jit(solution)/shard_map/reduce_sum | solution.py:390
  124.1 0.3 multiply_reduce_fusion.3
  124.4 0.9 multiply_convert_fusion.2
  (77 shorter events, 1.7 us)
Async XLA Ops:
  0.0 96.7 %copy-start = (bf16[1280,1280]{1,0:T(8,128)(2,1)S(1)}, bf16[1280,1280]{1,0:T(8,128)(2,1)}, u32[]{:S(2)}) copy-start(bf16[1280,1280]{1,0:T(8,128)(2,1)} %param.15) | copy-start | bytes 9830404
  5.1 2.1 %copy-start.7 = (bf16[256,1280]{1,0:T(8,128)(2,1)}, bf16[256,1280]{1,0:T(8,128)(2,1)S(1)}, u32[]{:S(2)}) copy-start(bf16[256,1280]{1,0:T(8,128)(2,1)S(1)} %fusion.25) | copy-start | bytes 1966084
  11.0 4.5 %copy-start.15 = (s32[32]{0:T(128)S(1)}, s32[32]{0:T(128)}, u32[]{:S(2)}) copy-start(s32[32]{0:T(128)} %param.23) | copy-start | bytes 388
  11.0 4.8 %copy-start.12 = (f32[2,1280]{1,0:T(2,128)S(1)}, f32[2,1280]{1,0:T(2,128)}, u32[]{:S(2)}) copy-start(f32[2,1280]{1,0:T(2,128)} %param.19) | copy-start | bytes 30724
  11.0 4.9 %copy-start.13 = (f32[2,1280]{1,0:T(2,128)S(1)}, f32[2,1280]{1,0:T(2,128)}, u32[]{:S(2)}) copy-start(f32[2,1280]{1,0:T(2,128)} %param.20) | copy-start | bytes 30724
  11.0 21.2 %all-to-all-start = ((bf16[8,256,320]{1,2,0:T(8,128)(2,1)}), bf16[8,256,320]{1,2,0:T(8,128)(2,1)}, u32[]{:S(2)}, u32[]{:S(2)}) async-start(bf16[8,256,320]{1,2,0:T(8,128)(2,1)} %tile.2), calls=%async_computation | async-start | bytes 2621440 | tf_op jit(solution)/shard_map/all_to_all | solution.py:266
  39.8 4.5 %copy-start.9 = (pred[4,512,256]{2,1,0:T(8,128)(4,1)S(1)}, pred[4,512,256]{2,1,0:T(8,128)(4,1)}, u32[]{:S(2)}) copy-start(pred[4,512,256]{2,1,0:T(8,128)(4,1)} %get-tuple-element.30) | copy-start | bytes 1572868
  39.8 4.5 %copy-start.10 = (bf16[512,5,64,1]{0,2,1,3:T(8,128)(2,1)S(1)}, bf16[512,5,64,1]{0,2,1,3:T(8,128)(2,1)}, u32[]{:S(2)}) copy-start(bf16[512,5,64,1]{0,2,1,3:T(8,128)(2,1)} %reshape.356) | copy-start | bytes 983044
  44.3 2.1 %copy-start.4 = (f32[512,5,64]{0,2,1:T(8,128)S(1)}, f32[512,5,64]{0,2,1:T(8,128)}, u32[]{:S(2)}) copy-start(f32[512,5,64]{0,2,1:T(8,128)} %reshape.353) | copy-start | bytes 1966084
  44.3 2.1 %copy-start.6 = (bf16[4,256,5,64]{1,0,3,2:T(4,128)(2,1)S(1)}, bf16[4,256,5,64]{1,0,3,2:T(4,128)(2,1)}, u32[]{:S(2)}) copy-start(bf16[4,256,5,64]{1,0,3,2:T(4,128)(2,1)} %slice.93) | copy-start | bytes 1966084
  44.3 2.1 %copy-start.8 = (pred[4,512,256]{2,1,0:T(8,128)(4,1)S(1)}, pred[4,512,256]{2,1,0:T(8,128)(4,1)}, u32[]{:S(2)}) copy-start(pred[4,512,256]{2,1,0:T(8,128)(4,1)} %get-tuple-element.29) | copy-start | bytes 1572868
  52.7 22.9 %all-to-all-start.1 = ((bf16[8,256,325]{1,2,0:T(8,128)(2,1)}), bf16[8,256,325]{1,2,0:T(8,128)(2,1)}, u32[]{:S(2)}, u32[]{:S(2)}) async-start(bf16[8,256,325]{1,2,0:T(8,128)(2,1)} %maximum_maximum_fusion), calls=%async_computation.1 | async-start | bytes 2686976 | tf_op jit(solution)/shard_map/all_to_all | solution.py:353
  60.6 1.0 copy-start.5
  60.6 1.0 copy-start.11
  75.5 1.7 %copy-start.16 = (bf16[5,256,256]{1,2,0:T(8,128)(2,1)S(1)}, bf16[5,256,256]{1,2,0:T(8,128)(2,1)}, u32[]{:S(2)}) copy-start(bf16[5,256,256]{1,2,0:T(8,128)(2,1)} %get-tuple-element.41) | copy-start | bytes 1966084
  77.2 21.6 %slice-start = ((s8[6553600]{0:T(1024)(128)(4,1)}), s8[4194304]{0:T(1024)(128)(4,1)S(1)}, s32[]{:S(2)}) async-start(s8[6553600]{0:T(1024)(128)(4,1)} %bitcast.123), calls=%async_computation.3 | async-start | bytes 8388608
  96.7 1.1 copy-start.1
  96.7 2.1 %slice-start.1 = ((s8[6553600]{0:T(1024)(128)(4,1)}), s8[2359296]{0:T(1024)(128)(4,1)S(1)}, s32[]{:S(2)}) async-start(s8[6553600]{0:T(1024)(128)(4,1)} %bitcast.123), calls=%async_computation.4 | async-start | bytes 4718592
  98.8 1.9 %copy-start.2 = (bf16[256,1280]{1,0:T(8,128)(2,1)}, bf16[256,1280]{1,0:T(8,128)(2,1)S(1)}, u32[]{:S(2)}) copy-start(bf16[256,1280]{1,0:T(8,128)(2,1)S(1)} %multiply_convert_fusion) | copy-start | bytes 1966084
  98.8 2.2 %copy-start.14 = (bf16[1280,1280]{1,0:T(8,128)(2,1)S(1)}, bf16[1280,1280]{1,0:T(8,128)(2,1)}, u32[]{:S(2)}) copy-start(bf16[1280,1280]{1,0:T(8,128)(2,1)} %param.17) | copy-start | bytes 9830404
  103.0 19.6 %all-to-all-start.2 = ((bf16[4,64,1280]{2,1,0:T(8,128)(2,1)}), bf16[4,64,1280]{2,1,0:T(8,128)(2,1)}, u32[]{:S(2)}, u32[]{:S(2)}) async-start(bf16[4,64,1280]{2,1,0:T(8,128)(2,1)} %bitcast.128), calls=%async_computation.2 | async-start | bytes 1310720 | tf_op jit(solution)/shard_map/all_to_all | solution.py:383
  122.7 1.4 %copy-start.3 = (bf16[256,1280]{1,0:T(8,128)(2,1)S(1)}, bf16[256,1280]{1,0:T(8,128)(2,1)}, u32[]{:S(2)}) copy-start(bf16[256,1280]{1,0:T(8,128)(2,1)} %copy-done.2) | copy-start | bytes 1966084

commit v15 on v12

--- a/solution.py
+++ b/solution.py
@@ -307,7 +307,7 @@
     key_heads = prefix_keys.reshape(-1, local_heads, head_dim)
     value_heads = prefix_values.reshape(-1, local_heads, head_dim)
     gathered_heads = gathered.reshape(pages_count, slot_count, local_heads, head_dim)
-    chunk_count = 2 if pages_count % 2 == 0 else 1
+    chunk_count = 4 if pages_count % 4 == 0 else 1
     chunk_pages = pages_count // chunk_count
     pieces = []
     for chunk in range(chunk_count):

time: 119 us -> 123 us (1.034)
  other arithmetic: 17.1 us -> 20.7 us
  matrix products: 20.3 us -> 22.2 us
    convert_element_type x0 -> x1, other arithmetic: none -> 1.95 us  [shards_heads(): prefix_keys = head_norm(cache_local.reshape(pages_here * page_len, local_...]
    dot_general x1, matrix products: 0.25 us -> 1.56 us  [shards_heads(): jnp.einsum('hqk,khd->qhd', weights.astype(jnp.bfloat16), value_rows.resha...]
    dot_general x2 -> x4, matrix products: 5.66 us -> 6.24 us  [shards_heads(): jnp.einsum('pshd,khd->phks', query_chunk, key_heads, preferred_element_ty...]
    dot_general x2 -> x4, matrix products: 4 us -> 4.09 us  [shards_heads(): jnp.einsum('phks,khd->pshd', prefix_weights.astype(jnp.bfloat16), value_h...]
  transfers between devices with their start and end apart: 3 -> 3, of which waited for: 3 -> 2; matrix products, arithmetic and copies ran while one was open for 16% -> 18% of each run, Pallas kernels for 0% -> 0%
where the time goes in v15:
time: 123 us; the launch traced here: 122 us
  waiting for transfers between devices  28.8 us (23%)
  matrix products  22.2 us (18%)
  other arithmetic  20.7 us (17%)
  blocking collectives  18.9 us (15%)
  local copies, waits for them, and re-layouts  17.1 us (14%)
  starting transfers between devices  13.3 us (11%)
    all_gather x1, blocking collectives, shards_heads(): attention = lax.all_gather(attention_local, 'mp', axis=1, tiled=True)  18.9 us
    all_to_all x1, waiting for transfers between devices, shards_heads(): lax.all_to_all(jnp.dot(hidden, w_down, preferred_element_type=jnp.float32...  15.4 us
    all_to_all x1, waiting for transfers between devices, shards_heads(): lax.all_to_all(jnp.concatenate(pieces, axis=0).reshape(pages_count * slot...  13.5 us
    dot_general x4, matrix products, shards_heads(): jnp.einsum('pshd,khd->phks', query_chunk, key_heads, preferred_element_ty...  6.24 us
    all_to_all x1, starting transfers between devices, shards_heads(): lax.all_to_all(jnp.concatenate(pieces, axis=0).reshape(pages_count * slot...  4.87 us
    all_to_all x1, starting transfers between devices, shards_heads(): lax.all_to_all(jnp.tile(queries, (lax.axis_size('pages'), 1)), 'pages', 0...  4.25 us
    convert_element_type x2, local copies, waits for them, and re-layouts, shards_heads(): cache_local.reshape(pages_here * page_len, local_width).astype(jnp.float32)  4.25 us
    all_to_all x1, starting transfers between devices, shards_heads(): lax.all_to_all(jnp.dot(hidden, w_down, preferred_element_type=jnp.float32...  4.16 us
  transfers between devices with their start and end apart: 3, of which 2 were waited for; matrix products, arithmetic and copies ran while one was open for 18% of the time, Pallas kernels for 0%

profile of v15, /device:TPU:2, one launch (start us, length us, event | category | flops | bytes accessed | tf_op | source)
XLA Modules:
  0.0 121.6 jit_solution(2158489010428754060)
XLA Ops:
  0.0 1.4 %fusion.30 = f32[256]{0:T(256)S(1)} fusion(bf16[256,1280]{1,0:T(8,128)(2,1)} %param.13), kind=kLoop, calls=%fused_computation.39 | loop fusion | flops 982784 | bytes 656384 | tf_op jit(solution)/shard_map/reduce_sum | solution.py:16
  1.5 0.7 reduce_window_sum.11
  2.2 0.7 sub.37
  2.9 0.8 select_reduce_fusion.2
  3.7 2.8 %fusion.49 = bf16[3,256,320]{1,2,0:T(8,128)(2,1)S(1)} fusion(bf16[3,1280,320]{1,2,0:T(8,128)(2,1)} %param.14, bf16[256,1280]{1,0:T(8,128)(2,1)} %param.13, f32[256]{0:T(256)S(1)} %add_rsqrt_fusion.5), kind=kOutput, calls=%fused_computation.57 | convolution fusion | flops 630374400 | bytes 3605504 | tf_op jit(solution)/shard_map/sd,jdc->jsc/dot_general | solution.py:255
  6.5 0.7 fusion.107
  7.5 0.7 multiply_subtract_fusion
  8.3 0.7 fusion.87
  9.0 0.8 dynamic_slice.33
  9.8 1.1 fusion.74
  10.9 1.2 tile.2
  12.0 4.3 %all-to-all-start = ((bf16[8,256,320]{1,2,0:T(8,128)(2,1)}), bf16[8,256,320]{1,2,0:T(8,128)(2,1)}, u32[]{:S(2)}, u32[]{:S(2)}) async-start(bf16[8,256,320]{1,2,0:T(8,128)(2,1)} %tile.2), calls=%async_computation | async-start | bytes 2621440 | tf_op jit(solution)/shard_map/all_to_all | solution.py:265
  16.6 2.4 %constant_dynamic-slice_fusion = (bf16[4,128,320]{2,1,0:T(8,128)(2,1)}, bf16[4,128,320]{2,1,0:T(8,128)(2,1)}) fusion(bf16[4,128,1280]{2,1,0:T(8,128)(2,1)} %param.21, s32[]{:T(128)S(6)} %select_n.67, bf16[4,128,1280]{2,1,0:T(8,128)(2,1)} %param.22), kind=kLoop, calls=%fused_computation.139 | loop fusion | bytes 1310724 | tf_op jit(solution)/shard_map/dynamic_slice | solution.py:297
  19.2 1.9 %copy.87 = bf16[4,128,320]{1,2,0:T(8,128)(2,1)} copy(bf16[4,128,320]{2,1,0:T(8,128)(2,1)} %get-tuple-element.49) | data formatting | bytes 655360
  21.1 2.1 %copy.71 = f32[4,128,320]{1,0,2:T(4,128)} copy(bf16[4,128,320]{1,2,0:T(8,128)(2,1)} %copy.87) | data formatting | bytes 983040 | tf_op jit(solution)/shard_map/convert_element_type | solution.py:299
  23.1 2.2 %reshape.372 = f32[512,5,64]{0,2,1:T(8,128)} reshape(f32[4,128,320]{1,0,2:T(4,128)} %copy.71) | data formatting | bytes 1310720 | tf_op jit(solution)/shard_map/convert_element_type | solution.py:299
  25.3 1.9 %copy.69 = bf16[4,128,320]{1,0,2:T(4,128)(2,1)} copy(bf16[4,128,320]{2,1,0:T(8,128)(2,1)} %get-tuple-element.50) | data formatting | bytes 655360 | tf_op jit(solution)/shard_map/dynamic_slice | solution.py:303
  27.2 1.8 %reshape.375 = bf16[512,5,64,1]{0,2,1,3:T(8,128)(2,1)} reshape(bf16[4,128,320]{1,0,2:T(4,128)(2,1)} %copy.69) | data formatting | bytes 655360 | tf_op jit(solution)/shard_map/reshape;reshape | solution.py:308
  29.1 1.2 multiply_reduce_fusion.2
  30.3 1.9 %fusion.73 = bf16[512,5,64,1]{0,2,3,1:T(8,128)(2,1)} fusion(f32[512,5,64]{0,2,1:T(8,128)} %reshape.372, f32[5,64]{1,0:T(8,128)S(1)} %mul.332, f32[512,5]{0,1:T(8,128)S(1)} %add_rsqrt_fusion), kind=kLoop, calls=%fused_computation.81 | loop fusion | flops 491520 | bytes 994560 | tf_op jit(solution)/shard_map/convert_element_type | solution.py:302
  32.2 1.7 %broadcast_compare_fusion.3 = (pred[2,512,256]{2,1,0:T(8,128)(4,1)}, pred[2,512,256]{2,1,0:T(8,128)(4,1)}, pred[2,512,256]{2,1,0:T(8,128)(4,1)}, pred[2,512,256]{2,1,0:T(8,128)(4,1)}) fusion(s32[2,256]{1,0:T(2,128)S(1)} %get-tuple-element.25, s32[512]{0:T(512)S(1)} %broadcast_bitcast_fusion, s32[2,256]{1,0:T(2,128)S(1)} %get-tuple-element.28, ...), kind=kLoop, calls=%fused_computation.77 | loop fusion | flops 1048576 | bytes 1058816 | tf_op jit(solution)/shard_map/eq | solution.py:326
  33.9 1.4 %fusion.106 = (bf16[2,256,320]{1,2,0:T(8,128)(2,1)S(1)}, bf16[2,256,320]{1,2,0:T(8,128)(2,1)S(1)}, bf16[2,256,320]{1,2,0:T(8,128)(2,1)S(1)}, bf16[2,256,320]{1,2,0:T(8,128)(2,1)S(1)}) fusion(bf16[8,256,320]{1,2,0:T(8,128)(2,1)} %all-to-all-done), kind=kLoop, calls=%fused_computation.169 | loop fusion | bytes 2621440 | tf_op jit(solution)/shard_map/slice | solution.py:314
  35.3 1.5 %fusion.6 = (bf16[2,5,256]{2,0,1:T(2,128)(2,1)S(1)}, f32[5,512,2,256]{3,1,2,0:T(8,128)S(1)}) fusion(pred[2,512,256]{2,1,0:T(8,128)(4,1)S(1)} %copy-done.8, bf16[512,5,64,1]{0,2,3,1:T(8,128)(2,1)S(1)} %copy-done.4, bf16[2,256,5,64]{1,3,2,0:T(8,128)(2,1)S(1)} %bitcast.166), kind=kOutput, calls=%fused_computation.10 | convolution fusion | flops 171701760 | bytes 6165504 | tf_op jit(solution)/shard_map/pshd,khd->phks/dot_general | solution.py:321
  36.9 1.0 fusion.52
  38.0 1.6 %fusion.4 = (bf16[2,5,256]{2,0,1:T(2,128)(2,1)S(1)}, f32[5,512,2,256]{3,1,2,0:T(8,128)S(1)}) fusion(pred[2,512,256]{2,1,0:T(8,128)(4,1)S(1)} %copy-done.7, bf16[512,5,64,1]{0,2,3,1:T(8,128)(2,1)S(1)} %copy-done.4, bf16[2,256,5,64]{1,3,2,0:T(8,128)(2,1)S(1)} %bitcast.165), kind=kOutput, calls=%fused_computation.8 | convolution fusion | flops 171701760 | bytes 6165504 | tf_op jit(solution)/shard_map/pshd,khd->phks/dot_general | solution.py:321
  39.6 1.1 fusion.55
  40.7 1.6 %fusion.2 = (bf16[2,5,256]{2,0,1:T(2,128)(2,1)S(1)}, f32[5,512,2,256]{3,1,2,0:T(8,128)S(1)}) fusion(pred[2,512,256]{2,1,0:T(8,128)(4,1)S(1)} %copy-done.6, bf16[512,5,64,1]{0,2,3,1:T(8,128)(2,1)S(1)} %copy-done.4, bf16[2,256,5,64]{1,3,2,0:T(8,128)(2,1)S(1)} %bitcast.164), kind=kOutput, calls=%fused_computation.6 | convolution fusion | flops 171701760 | bytes 6165504 | tf_op jit(solution)/shard_map/pshd,khd->phks/dot_general | solution.py:321
  42.2 1.0 fusion.58
  43.3 1.6 %fusion = (bf16[2,5,256]{2,0,1:T(2,128)(2,1)S(1)}, f32[5,512,2,256]{3,1,2,0:T(8,128)S(1)}) fusion(pred[2,512,256]{2,1,0:T(8,128)(4,1)S(1)} %copy-done.5, bf16[512,5,64,1]{0,2,3,1:T(8,128)(2,1)S(1)} %copy-done.4, bf16[2,256,5,64]{1,3,2,0:T(8,128)(2,1)S(1)} %bitcast.163), kind=kOutput, calls=%fused_computation.4 | convolution fusion | flops 171701760 | bytes 6165504 | tf_op jit(solution)/shard_map/pshd,khd->phks/dot_general | solution.py:321
  44.9 1.0 fusion.61
  46.0 1.2 maximum_maximum_fusion
  47.1 4.9 %all-to-all-start.1 = ((bf16[8,256,325]{1,2,0:T(8,128)(2,1)}), bf16[8,256,325]{1,2,0:T(8,128)(2,1)}, u32[]{:S(2)}, u32[]{:S(2)}) async-start(bf16[8,256,325]{1,2,0:T(8,128)(2,1)} %maximum_maximum_fusion), calls=%async_computation.1 | async-start | bytes 2686976 | tf_op jit(solution)/shard_map/all_to_all | solution.py:344
  52.0 1.0 multiply_reduce_fusion.5
  53.3 2.4 %fusion.109 = (f32[5,256]{1,0:T(8,128)S(1)}, bf16[5,256,256]{1,2,0:T(8,128)(2,1)}) fusion(f32[256,5,32]{0,2,1:T(8,128)} %get-tuple-element.20, f32[256,5,32]{0,2,1:T(8,128)S(1)} %get-tuple-element.19, f32[256,5]{0,1:T(8,128)S(1)} %add_rsqrt_fusion.1, f32[5,64]{1,0:T(8,128)S(1)} %mul.332, f32[256,5,64]{0,2,1:T(8,128)} %fusion.87, ...), kind=kOutput, calls=%fused_computation.172 | convolution fusion | flops 43744000 | bytes 1387776 | tf_op jit(solution)/shard_map/qhd,khd->hqk/dot_general | solution.py:269
  55.7 13.5 %all-to-all-done.1 = bf16[8,256,325]{1,2,0:T(8,128)(2,1)} async-done(((bf16[8,256,325]{1,2,0:T(8,128)(2,1)}), bf16[8,256,325]{1,2,0:T(8,128)(2,1)}, u32[]{:S(2)}, u32[]{:S(2)}) %all-to-all-start.1) | async-done | bytes 1331232 | tf_op jit(solution)/shard_map/all_to_all | solution.py:344
  69.2 1.5 %convert_reduce_fusion = f32[256,325]{0,1:T(8,128)S(1)} fusion(bf16[8,256,325]{1,2,0:T(8,128)(2,1)} %all-to-all-done.1), kind=kLoop, calls=%fused_computation.13 | loop fusion | flops 1248000 | bytes 1664000 | tf_op jit(solution)/shard_map/reduce_sum | solution.py:351
  70.8 1.6 %fusion.64 = bf16[256,5,64]{0,2,1:T(8,128)(2,1)S(1)} fusion(f32[256,5,64]{0,2,1:T(8,128)S(1)} %bitcast.167, bf16[256,5,64]{0,2,1:T(8,128)(2,1)} %bitcast.169, bf16[5,256,256]{1,2,0:T(8,128)(2,1)} %get-tuple-element.44, f32[256,5]{0,1:T(8,128)S(1)} %fusion.91), kind=kOutput, calls=%fused_computation.65 | convolution fusion | flops 42188800 | bytes 1315840 | tf_op jit(solution)/shard_map/hqk,khd->qhd/dot_general | solution.py:285
  72.3 18.9 %all_gather.3 = bf16[256,1280]{0,1:T(8,128)(2,1)S(1)} all-gather(bf16[256,320]{0,1:T(8,128)(2,1)S(1)} %bitcast.168), channel_id=1, replica_groups=mesh['pages'=8,'mp'=4] {'mp'}, dimensions={1}, use_global_device_ids=true | all-gather | bytes 819200 | tf_op jit(solution)/shard_map/all_gather | solution.py:362
  91.2 1.1 multiply_reduce_fusion.1
  92.4 0.5 multiply_reduce_fusion
  92.9 0.4 multiply_convert_fusion
  93.3 1.9 %convolution_bitcast_fusion = f32[2,256,1280]{2,1,0:T(8,128)S(1)} fusion(bf16[2,1280,1280]{2,1,0:T(8,128)(2,1)S(1)} %bitcast.155, bf16[256,1280]{1,0:T(8,128)(2,1)S(1)} %multiply_convert_fusion), kind=kOutput, calls=%fused_computation.12 | convolution fusion | flops 1677721600 | bytes 9830400 | tf_op jit(solution)/shard_map/sd,jdf->jsf/dot_general | solution.py:369
  95.5 2.1 %convolution_convert_fusion = bf16[256,1280]{1,0:T(8,128)(2,1)} fusion(bf16[1280,1280]{1,0:T(8,128)(2,1)S(1)} %copy-done.11, f32[2,256,1280]{2,1,0:T(8,128)S(1)} %convolution_bitcast_fusion, f32[1280]{0:T(1024)S(1)} %get-tuple-element.8, f32[1280]{0:T(1024)S(1)} %get-tuple-element.7), kind=kOutput, calls=%fused_computation.30 | convolution fusion | flops 841809920 | bytes 6563840 | tf_op jit(solution)/shard_map/dot_general | solution.py:375
  97.6 4.2 %all-to-all-start.2 = ((bf16[4,64,1280]{2,1,0:T(8,128)(2,1)}), bf16[4,64,1280]{2,1,0:T(8,128)(2,1)}, u32[]{:S(2)}, u32[]{:S(2)}) async-start(bf16[4,64,1280]{2,1,0:T(8,128)(2,1)} %bitcast.160), calls=%async_computation.2 | async-start | bytes 1310720 | tf_op jit(solution)/shard_map/all_to_all | solution.py:374
  101.9 15.4 %all-to-all-done.2 = bf16[4,64,1280]{2,1,0:T(8,128)(2,1)} async-done(((bf16[4,64,1280]{2,1,0:T(8,128)(2,1)}), bf16[4,64,1280]{2,1,0:T(8,128)(2,1)}, u32[]{:S(2)}, u32[]{:S(2)}) %all-to-all-start.2) | async-done | bytes 655392 | tf_op jit(solution)/shard_map/all_to_all | solution.py:374
  117.2 1.2 convert_reduce_fusion.1
  118.6 1.2 multiply_reduce_fusion.3
  119.8 1.8 %multiply_convert_fusion.2 = bf16[64,1280]{1,0:T(8,128)(2,1)} fusion(f32[64,1280]{1,0:T(8,128)S(1)} %convert_reduce_fusion.1, f32[64]{0:T(128)S(1)} %add_rsqrt_fusion.6, f32[64]{0:T(128)S(1)} %add_rsqrt_fusion.7, f32[1280]{0:T(1024)S(1)} %get-tuple-element.5, f32[64]{0:T(128)S(1)} %fusion.93, bf16[256,1280]{1,0:T(8,128)(2,1)} %copy-done.2, s32[]{:T(128)S(6)} %select_n.63), kind=kLoop, calls=%fused_computation.98 | loop fusion | flops 655360 | bytes 661252 | tf_op jit(solution)/shard_map/convert_element_type | solution.py:386
  (72 shorter events, 1.8 us)
Async XLA Ops:
  0.0 91.2 %copy-start = (bf16[1280,1280]{1,0:T(8,128)(2,1)S(1)}, bf16[1280,1280]{1,0:T(8,128)(2,1)}, u32[]{:S(2)}) copy-start(bf16[1280,1280]{1,0:T(8,128)(2,1)} %param.15) | copy-start | bytes 9830404
  8.2 8.1 %copy-start.12 = (s32[32]{0:T(128)S(1)}, s32[32]{0:T(128)}, u32[]{:S(2)}) copy-start(s32[32]{0:T(128)} %param.23) | copy-start | bytes 388
  12.0 21.9 %all-to-all-start = ((bf16[8,256,320]{1,2,0:T(8,128)(2,1)}), bf16[8,256,320]{1,2,0:T(8,128)(2,1)}, u32[]{:S(2)}, u32[]{:S(2)}) async-start(bf16[8,256,320]{1,2,0:T(8,128)(2,1)} %tile.2), calls=%async_computation | async-start | bytes 2621440 | tf_op jit(solution)/shard_map/all_to_all | solution.py:265
  33.9 1.4 %copy-start.4 = (bf16[512,5,64,1]{0,2,3,1:T(8,128)(2,1)S(1)}, bf16[512,5,64,1]{0,2,3,1:T(8,128)(2,1)}, u32[]{:S(2)}) copy-start(bf16[512,5,64,1]{0,2,3,1:T(8,128)(2,1)} %fusion.73) | copy-start | bytes 983044
  33.9 1.4 %copy-start.8 = (pred[2,512,256]{2,1,0:T(8,128)(4,1)S(1)}, pred[2,512,256]{2,1,0:T(8,128)(4,1)}, u32[]{:S(2)}) copy-start(pred[2,512,256]{2,1,0:T(8,128)(4,1)} %get-tuple-element.32) | copy-start | bytes 786436
  35.3 1.6 %copy-start.3 = (bf16[512,5,64,1]{0,2,1,3:T(8,128)(2,1)S(1)}, bf16[512,5,64,1]{0,2,1,3:T(8,128)(2,1)}, u32[]{:S(2)}) copy-start(bf16[512,5,64,1]{0,2,1,3:T(8,128)(2,1)} %reshape.375) | copy-start | bytes 983044
  36.9 1.1 copy-start.7
  39.6 1.1 copy-start.6
  42.2 1.1 copy-start.5
  45.9 7.0 %copy-start.9 = (f32[2,1280]{1,0:T(2,128)S(1)}, f32[2,1280]{1,0:T(2,128)}, u32[]{:S(2)}) copy-start(f32[2,1280]{1,0:T(2,128)} %param.19) | copy-start | bytes 30724
  45.9 7.1 %copy-start.10 = (f32[2,1280]{1,0:T(2,128)S(1)}, f32[2,1280]{1,0:T(2,128)}, u32[]{:S(2)}) copy-start(f32[2,1280]{1,0:T(2,128)} %param.20) | copy-start | bytes 30724
  47.1 22.0 %all-to-all-start.1 = ((bf16[8,256,325]{1,2,0:T(8,128)(2,1)}), bf16[8,256,325]{1,2,0:T(8,128)(2,1)}, u32[]{:S(2)}, u32[]{:S(2)}) async-start(bf16[8,256,325]{1,2,0:T(8,128)(2,1)} %maximum_maximum_fusion), calls=%async_computation.1 | async-start | bytes 2686976 | tf_op jit(solution)/shard_map/all_to_all | solution.py:344
  70.8 22.5 %slice-start = ((s8[6553600]{0:T(1024)(128)(4,1)}), s8[4194304]{0:T(1024)(128)(4,1)S(1)}, s32[]{:S(2)}) async-start(s8[6553600]{0:T(1024)(128)(4,1)} %bitcast.154), calls=%async_computation.3 | async-start | bytes 8388608
  91.2 1.1 copy-start.1
  91.2 2.1 %slice-start.1 = ((s8[6553600]{0:T(1024)(128)(4,1)}), s8[2359296]{0:T(1024)(128)(4,1)S(1)}, s32[]{:S(2)}) async-start(s8[6553600]{0:T(1024)(128)(4,1)} %bitcast.154), calls=%async_computation.4 | async-start | bytes 4718592
  93.3 1.9 %copy-start.2 = (bf16[256,1280]{1,0:T(8,128)(2,1)}, bf16[256,1280]{1,0:T(8,128)(2,1)S(1)}, u32[]{:S(2)}) copy-start(bf16[256,1280]{1,0:T(8,128)(2,1)S(1)} %multiply_convert_fusion) | copy-start | bytes 1966084
  93.3 2.2 %copy-start.11 = (bf16[1280,1280]{1,0:T(8,128)(2,1)S(1)}, bf16[1280,1280]{1,0:T(8,128)(2,1)}, u32[]{:S(2)}) copy-start(bf16[1280,1280]{1,0:T(8,128)(2,1)} %param.17) | copy-start | bytes 9830404
  97.6 19.6 %all-to-all-start.2 = ((bf16[4,64,1280]{2,1,0:T(8,128)(2,1)}), bf16[4,64,1280]{2,1,0:T(8,128)(2,1)}, u32[]{:S(2)}, u32[]{:S(2)}) async-start(bf16[4,64,1280]{2,1,0:T(8,128)(2,1)} %bitcast.160), calls=%async_computation.2 | async-start | bytes 1310720 | tf_op jit(solution)/shard_map/all_to_all | solution.py:374

commit v16 on v14

--- a/solution.py
+++ b/solution.py
@@ -266,7 +266,7 @@
     gathered = lax.all_to_all(
         jnp.tile(queries, (lax.axis_size("pages"), 1)), "pages", 0, 0, tiled=True
     )
-    state_kv, gathered = lax.optimization_barrier((state_in, gathered))
+    state_kv, _ = lax.optimization_barrier((state_in, gathered[:1, :1]))
     projected = jnp.einsum(
         "sd,jdc->jsc", state_kv, w_qkv[1:], preferred_element_type=jnp.float32
     ).astype(jnp.bfloat16)

time: 126 us -> 120 us (0.952)
  local copies, waits for them, and re-layouts: 23.4 us -> 17.3 us
  matrix products: 22.3 us -> 19.6 us
  waiting for transfers between devices: 28.1 us -> 30 us
    slice x3 -> x1, local copies, waits for them, and re-layouts: 6.09 us -> 1.47 us  [shards_heads(): lax.slice_in_dim(gathered_heads, chunk * chunk_pages, (chunk + 1) * chunk...]
    dot_general x2, matrix products: 7.49 us -> 5.66 us  [shards_heads(): jnp.einsum('pshd,khd->phks', query_chunk, key_heads, preferred_element_ty...]
    dot_general x1, matrix products: 2.26 us -> 0.63 us  [shards_heads(): jnp.einsum('sd,jdc->jsc', state_kv, w_qkv[1:], preferred_element_type=jnp...]
    all_to_all x1 -> x0, local copies, waits for them, and re-layouts: 1.47 us -> none  [shards_heads(): lax.all_to_all(jnp.tile(queries, (lax.axis_size('pages'), 1)), 'pages', 0...]
    unnamed x39 -> x35, local copies, waits for them, and re-layouts: 3.03 us -> 2.4 us
where the time goes in v16:
time: 120 us; the launch traced here: 119 us
  waiting for transfers between devices  30 us (25%)
  matrix products  19.6 us (16%)
  blocking collectives  19 us (16%)
  other arithmetic  18.6 us (16%)
  local copies, waits for them, and re-layouts  17.3 us (14%)
  starting transfers between devices  14.3 us (12%)
    all_gather x1, blocking collectives, shards_heads(): attention = lax.all_gather(attention_local, 'mp', axis=1, tiled=True)  19 us
    all_to_all x1, waiting for transfers between devices, shards_heads(): lax.all_to_all(jnp.dot(hidden, w_down, preferred_element_type=jnp.float32...  15.4 us
    all_to_all x1, waiting for transfers between devices, shards_heads(): lax.all_to_all(jnp.concatenate(pieces, axis=0).reshape(pages_count * slot...  13.4 us
    all_to_all x1, starting transfers between devices, shards_heads(): lax.all_to_all(jnp.concatenate(pieces, axis=0).reshape(pages_count * slot...  5.79 us
    dot_general x2, matrix products, shards_heads(): jnp.einsum('pshd,khd->phks', query_chunk, key_heads, preferred_element_ty...  5.66 us
    all_to_all x1, starting transfers between devices, shards_heads(): lax.all_to_all(jnp.tile(queries, (lax.axis_size('pages'), 1)), 'pages', 0...  4.38 us
    convert_element_type x2, local copies, waits for them, and re-layouts, shards_heads(): cache_local.reshape(pages_here * page_len, local_width).astype(jnp.float32)  4.26 us
    all_to_all x1, starting transfers between devices, shards_heads(): lax.all_to_all(jnp.dot(hidden, w_down, preferred_element_type=jnp.float32...  4.16 us
  transfers between devices with their start and end apart: 3, of which 3 were waited for; matrix products, arithmetic and copies ran while one was open for 16% of the time, Pallas kernels for 0%

profile of v16, /device:TPU:2, one launch (start us, length us, event | category | flops | bytes accessed | tf_op | source)
XLA Modules:
  0.0 119.3 jit_solution(18253278061086998034)
XLA Ops:
  0.0 1.4 %fusion.24 = f32[256]{0:T(256)S(1)} fusion(bf16[256,1280]{1,0:T(8,128)(2,1)} %param.13), kind=kLoop, calls=%fused_computation.29 | loop fusion | flops 982784 | bytes 656384 | tf_op jit(solution)/shard_map/reduce_sum | solution.py:16
  1.5 0.8 slice_add_fusion.1
  2.3 0.7 fusion.79
  3.0 0.8 select_reduce_fusion.2
  3.8 1.4 %fusion.25 = bf16[256,1280]{1,0:T(8,128)(2,1)S(1)} fusion(bf16[256,1280]{1,0:T(8,128)(2,1)} %param.13, f32[256]{0:T(256)S(1)} %add_rsqrt_fusion.5), kind=kLoop, calls=%fused_computation.30 | loop fusion | flops 983040 | bytes 1311744 | tf_op jit(solution)/shard_map/convert_element_type | solution.py:257
  5.2 1.5 %convolution_convert_fusion.1 = bf16[256,320]{0,1:T(8,128)(2,1)S(1)} fusion(bf16[256,1280]{1,0:T(8,128)(2,1)S(1)} %fusion.25, bf16[3,1280,320]{1,2,0:T(8,128)(2,1)} %param.14), kind=kOutput, calls=%fused_computation.50 | convolution fusion | flops 209797120 | bytes 1638400 | tf_op jit(solution)/shard_map/dot_general | solution.py:258
  6.8 0.6 fusion.41
  7.4 0.7 fusion.82
  8.2 0.2 multiply_cosine_fusion
  8.4 0.7 multiply_subtract_fusion
  9.2 0.8 fusion.64
  9.9 0.8 dynamic_slice.33
  10.7 1.1 fusion.61
  11.8 1.2 tile.2
  13.0 4.4 %all-to-all-start = ((bf16[8,256,320]{1,2,0:T(8,128)(2,1)}), bf16[8,256,320]{1,2,0:T(8,128)(2,1)}, u32[]{:S(2)}, u32[]{:S(2)}) async-start(bf16[8,256,320]{1,2,0:T(8,128)(2,1)} %tile.2), calls=%async_computation | async-start | bytes 2621440 | tf_op jit(solution)/shard_map/all_to_all | solution.py:266
  17.7 2.4 %constant_dynamic-slice_fusion = (bf16[4,128,320]{2,1,0:T(8,128)(2,1)}, bf16[4,128,320]{2,1,0:T(8,128)(2,1)}) fusion(bf16[4,128,1280]{2,1,0:T(8,128)(2,1)} %param.21, s32[]{:T(128)S(6)} %select_n.61, bf16[4,128,1280]{2,1,0:T(8,128)(2,1)} %param.22), kind=kLoop, calls=%fused_computation.117 | loop fusion | bytes 1310724 | tf_op jit(solution)/shard_map/dynamic_slice | solution.py:306
  20.1 1.9 %copy.65 = bf16[4,128,320]{1,2,0:T(8,128)(2,1)} copy(bf16[4,128,320]{2,1,0:T(8,128)(2,1)} %get-tuple-element.44) | data formatting | bytes 655360
  22.0 2.1 %copy.55 = f32[4,128,320]{1,0,2:T(4,128)} copy(bf16[4,128,320]{1,2,0:T(8,128)(2,1)} %copy.65) | data formatting | bytes 983040 | tf_op jit(solution)/shard_map/convert_element_type | solution.py:308
  24.1 2.2 %reshape.357 = f32[512,5,64]{0,2,1:T(8,128)} reshape(f32[4,128,320]{1,0,2:T(4,128)} %copy.55) | data formatting | bytes 1310720 | tf_op jit(solution)/shard_map/convert_element_type | solution.py:308
  26.3 1.2 multiply_reduce_fusion.2
  27.4 1.9 %copy.53 = bf16[4,128,320]{1,0,2:T(4,128)(2,1)} copy(bf16[4,128,320]{2,1,0:T(8,128)(2,1)} %get-tuple-element.45) | data formatting | bytes 655360 | tf_op jit(solution)/shard_map/dynamic_slice | solution.py:312
  29.4 1.8 %reshape.360 = bf16[512,5,64,1]{0,2,1,3:T(8,128)(2,1)} reshape(bf16[4,128,320]{1,0,2:T(4,128)(2,1)} %copy.53) | data formatting | bytes 655360 | tf_op jit(solution)/shard_map/reshape;reshape | solution.py:317
  31.3 1.7 %broadcast_compare_fusion.1 = (pred[4,512,256]{2,1,0:T(8,128)(4,1)}, pred[4,512,256]{2,1,0:T(8,128)(4,1)}) fusion(s32[4,256]{1,0:T(4,128)S(1)} %get-tuple-element.25, s32[512]{0:T(512)S(1)} %broadcast_bitcast_fusion, s32[4,256]{1,0:T(4,128)S(1)} %get-tuple-element.26), kind=kLoop, calls=%fused_computation.52 | loop fusion | flops 1048576 | bytes 1058816 | tf_op jit(solution)/shard_map/eq | solution.py:335
  33.0 1.2 %all-to-all-done = bf16[8,256,320]{1,2,0:T(8,128)(2,1)} async-done(((bf16[8,256,320]{1,2,0:T(8,128)(2,1)}), bf16[8,256,320]{1,2,0:T(8,128)(2,1)}, u32[]{:S(2)}, u32[]{:S(2)}) %all-to-all-start) | async-done | bytes 1310752 | tf_op jit(solution)/shard_map/all_to_all | solution.py:266
  34.2 1.5 %fusion.81 = (bf16[4,256,320]{1,2,0:T(8,128)(2,1)S(1)}, bf16[4,256,320]{1,2,0:T(8,128)(2,1)S(1)}) fusion(bf16[8,256,320]{1,2,0:T(8,128)(2,1)} %all-to-all-done), kind=kLoop, calls=%fused_computation.147 | loop fusion | bytes 2621440 | tf_op jit(solution)/shard_map/slice | solution.py:323
  35.8 2.8 %fusion.2 = (bf16[4,5,256]{2,0,1:T(4,128)(2,1)S(1)}, f32[5,512,4,256]{3,1,2,0:T(8,128)S(1)}) fusion(pred[4,512,256]{2,1,0:T(8,128)(4,1)S(1)} %copy-done.6, bf16[4,256,5,64]{1,3,2,0:T(8,128)(2,1)S(1)} %bitcast.124, f32[512,5,64]{0,2,1:T(8,128)S(1)} %copy-done.4, f32[5,64]{1,0:T(8,128)S(1)} %mul.324, f32[512,5]{0,1:T(8,128)S(1)} %add_rsqrt_fusion), kind=kOutput, calls=%fused_computation.4 | convolution fusion | flops 343895040 | bytes 12342528 | tf_op jit(solution)/shard_map/pshd,khd->phks/dot_general | solution.py:330
  38.7 2.0 %fusion.31 = bf16[4,256,5,64]{1,3,0,2:T(8,128)(2,1)S(1)} fusion(f32[5,512,4,256]{3,1,2,0:T(8,128)S(1)} %get-tuple-element.35, pred[4,512,256]{2,1,0:T(8,128)(4,1)S(1)} %copy-done.6, bf16[512,5,64,1]{0,2,1,3:T(8,128)(2,1)S(1)} %copy-done.7), kind=kOutput, calls=%fused_computation.42 | convolution fusion | flops 343736320 | bytes 11993088 | tf_op jit(solution)/shard_map/phks,khd->pshd/dot_general | solution.py:338
  40.7 2.8 %fusion = (bf16[4,5,256]{2,0,1:T(4,128)(2,1)S(1)}, f32[5,512,4,256]{3,1,2,0:T(8,128)S(1)}) fusion(pred[4,512,256]{2,1,0:T(8,128)(4,1)S(1)} %copy-done.5, bf16[4,256,5,64]{1,3,2,0:T(8,128)(2,1)S(1)} %bitcast.123, f32[512,5,64]{0,2,1:T(8,128)S(1)} %copy-done.4, f32[5,64]{1,0:T(8,128)S(1)} %mul.324, f32[512,5]{0,1:T(8,128)S(1)} %add_rsqrt_fusion), kind=kOutput, calls=%fused_computation.2 | convolution fusion | flops 343895040 | bytes 12342528 | tf_op jit(solution)/shard_map/pshd,khd->phks/dot_general | solution.py:330
  43.6 2.0 %fusion.34 = bf16[4,256,5,64]{1,3,0,2:T(8,128)(2,1)S(1)} fusion(f32[5,512,4,256]{3,1,2,0:T(8,128)S(1)} %get-tuple-element.37, pred[4,512,256]{2,1,0:T(8,128)(4,1)S(1)} %copy-done.5, bf16[512,5,64,1]{0,2,1,3:T(8,128)(2,1)S(1)} %copy-done.7), kind=kOutput, calls=%fused_computation.43 | convolution fusion | flops 343736320 | bytes 11993088 | tf_op jit(solution)/shard_map/phks,khd->pshd/dot_general | solution.py:338
  45.7 1.2 maximum_maximum_fusion
  46.8 5.8 %all-to-all-start.1 = ((bf16[8,256,325]{1,2,0:T(8,128)(2,1)}), bf16[8,256,325]{1,2,0:T(8,128)(2,1)}, u32[]{:S(2)}, u32[]{:S(2)}) async-start(bf16[8,256,325]{1,2,0:T(8,128)(2,1)} %maximum_maximum_fusion), calls=%async_computation.1 | async-start | bytes 2686976 | tf_op jit(solution)/shard_map/all_to_all | solution.py:353
  52.7 1.0 multiply_reduce_fusion.5
  53.9 2.5 %fusion.84 = (f32[5,256]{1,0:T(8,128)S(1)}, bf16[5,256,256]{1,2,0:T(8,128)(2,1)}) fusion(f32[256,5,32]{0,2,1:T(8,128)} %get-tuple-element.18, f32[256,5,32]{0,2,1:T(8,128)S(1)} %get-tuple-element.17, f32[256,5]{0,1:T(8,128)S(1)} %add_rsqrt_fusion.1, f32[5,64]{1,0:T(8,128)S(1)} %mul.324, f32[256,5,64]{0,2,1:T(8,128)} %fusion.64, ...), kind=kOutput, calls=%fused_computation.150 | convolution fusion | flops 43744000 | bytes 1387776 | tf_op jit(solution)/shard_map/qhd,khd->hqk/dot_general | solution.py:278
  56.4 13.4 %all-to-all-done.1 = bf16[8,256,325]{1,2,0:T(8,128)(2,1)} async-done(((bf16[8,256,325]{1,2,0:T(8,128)(2,1)}), bf16[8,256,325]{1,2,0:T(8,128)(2,1)}, u32[]{:S(2)}, u32[]{:S(2)}) %all-to-all-start.1) | async-done | bytes 1331232 | tf_op jit(solution)/shard_map/all_to_all | solution.py:353
  69.8 1.6 %convert_reduce_fusion = f32[256,325]{0,1:T(8,128)S(1)} fusion(bf16[8,256,325]{1,2,0:T(8,128)(2,1)} %all-to-all-done.1), kind=kLoop, calls=%fused_computation.15 | loop fusion | flops 1248000 | bytes 1664000 | tf_op jit(solution)/shard_map/reduce_sum | solution.py:360
  71.5 0.2 fusion.45
  71.8 19.0 %all_gather.3 = bf16[256,1280]{0,1:T(8,128)(2,1)S(1)} all-gather(bf16[256,320]{0,1:T(8,128)(2,1)S(1)} %bitcast.130), channel_id=1, replica_groups=mesh['pages'=8,'mp'=4] {'mp'}, dimensions={1}, use_global_device_ids=true | all-gather | bytes 819200 | tf_op jit(solution)/shard_map/all_gather | solution.py:371
  90.7 1.1 multiply_reduce_fusion.1
  91.9 0.5 multiply_reduce_fusion
  92.4 0.4 multiply_convert_fusion
  92.9 1.9 %convolution_bitcast_fusion = f32[2,256,1280]{2,1,0:T(8,128)S(1)} fusion(bf16[2,1280,1280]{2,1,0:T(8,128)(2,1)S(1)} %bitcast.120, bf16[256,1280]{1,0:T(8,128)(2,1)S(1)} %multiply_convert_fusion), kind=kOutput, calls=%fused_computation.14 | convolution fusion | flops 1677721600 | bytes 9830400 | tf_op jit(solution)/shard_map/sd,jdf->jsf/dot_general | solution.py:378
  94.7 0.3 copy-done.11
  95.0 2.1 %convolution_convert_fusion = bf16[256,1280]{1,0:T(8,128)(2,1)} fusion(bf16[1280,1280]{1,0:T(8,128)(2,1)S(1)} %copy-done.11, f32[2,256,1280]{2,1,0:T(8,128)S(1)} %convolution_bitcast_fusion, f32[1280]{0:T(1024)S(1)} %get-tuple-element.8, f32[1280]{0:T(1024)S(1)} %get-tuple-element.7), kind=kOutput, calls=%fused_computation.16 | convolution fusion | flops 841809920 | bytes 6563840 | tf_op jit(solution)/shard_map/dot_general | solution.py:384
  97.1 4.2 %all-to-all-start.2 = ((bf16[4,64,1280]{2,1,0:T(8,128)(2,1)}), bf16[4,64,1280]{2,1,0:T(8,128)(2,1)}, u32[]{:S(2)}, u32[]{:S(2)}) async-start(bf16[4,64,1280]{2,1,0:T(8,128)(2,1)} %bitcast.125), calls=%async_computation.2 | async-start | bytes 1310720 | tf_op jit(solution)/shard_map/all_to_all | solution.py:383
  101.4 15.4 %all-to-all-done.2 = bf16[4,64,1280]{2,1,0:T(8,128)(2,1)} async-done(((bf16[4,64,1280]{2,1,0:T(8,128)(2,1)}), bf16[4,64,1280]{2,1,0:T(8,128)(2,1)}, u32[]{:S(2)}, u32[]{:S(2)}) %all-to-all-start.2) | async-done | bytes 655392 | tf_op jit(solution)/shard_map/all_to_all | solution.py:383
  116.7 1.3 %convert_reduce_fusion.1 = f32[64,1280]{1,0:T(8,128)S(1)} fusion(bf16[4,64,1280]{2,1,0:T(8,128)(2,1)} %all-to-all-done.2), kind=kLoop, calls=%fused_computation.38 | loop fusion | flops 573440 | bytes 983040 | tf_op jit(solution)/shard_map/reduce_sum | solution.py:390
  118.2 0.3 multiply_reduce_fusion.3
  118.4 0.9 multiply_convert_fusion.2
  (69 shorter events, 1.5 us)
Async XLA Ops:
  0.0 90.7 %copy-start = (bf16[1280,1280]{1,0:T(8,128)(2,1)S(1)}, bf16[1280,1280]{1,0:T(8,128)(2,1)}, u32[]{:S(2)}) copy-start(bf16[1280,1280]{1,0:T(8,128)(2,1)} %param.15) | copy-start | bytes 9830404
  3.8 3.0 %copy-start.12 = (bf16[3,1280,320]{1,2,0:T(8,128)(2,1)S(1)}, bf16[3,1280,320]{1,2,0:T(8,128)(2,1)}, u32[]{:S(2)}) copy-start(bf16[3,1280,320]{1,2,0:T(8,128)(2,1)} %param.14) | copy-start | bytes 7372804
  13.0 4.6 %copy-start.13 = (s32[32]{0:T(128)S(1)}, s32[32]{0:T(128)}, u32[]{:S(2)}) copy-start(s32[32]{0:T(128)} %param.23) | copy-start | bytes 388
  13.0 21.2 %all-to-all-start = ((bf16[8,256,320]{1,2,0:T(8,128)(2,1)}), bf16[8,256,320]{1,2,0:T(8,128)(2,1)}, u32[]{:S(2)}, u32[]{:S(2)}) async-start(bf16[8,256,320]{1,2,0:T(8,128)(2,1)} %tile.2), calls=%async_computation | async-start | bytes 2621440 | tf_op jit(solution)/shard_map/all_to_all | solution.py:266
  34.2 1.5 %copy-start.4 = (f32[512,5,64]{0,2,1:T(8,128)S(1)}, f32[512,5,64]{0,2,1:T(8,128)}, u32[]{:S(2)}) copy-start(f32[512,5,64]{0,2,1:T(8,128)} %reshape.357) | copy-start | bytes 1966084
  34.2 1.6 %copy-start.6 = (pred[4,512,256]{2,1,0:T(8,128)(4,1)S(1)}, pred[4,512,256]{2,1,0:T(8,128)(4,1)}, u32[]{:S(2)}) copy-start(pred[4,512,256]{2,1,0:T(8,128)(4,1)} %get-tuple-element.28) | copy-start | bytes 1572868
  35.8 2.9 %copy-start.7 = (bf16[512,5,64,1]{0,2,1,3:T(8,128)(2,1)S(1)}, bf16[512,5,64,1]{0,2,1,3:T(8,128)(2,1)}, u32[]{:S(2)}) copy-start(bf16[512,5,64,1]{0,2,1,3:T(8,128)(2,1)} %reshape.360) | copy-start | bytes 983044
  38.7 2.1 %copy-start.5 = (pred[4,512,256]{2,1,0:T(8,128)(4,1)S(1)}, pred[4,512,256]{2,1,0:T(8,128)(4,1)}, u32[]{:S(2)}) copy-start(pred[4,512,256]{2,1,0:T(8,128)(4,1)} %get-tuple-element.27) | copy-start | bytes 1572868
  46.8 6.8 %copy-start.9 = (f32[2,1280]{1,0:T(2,128)S(1)}, f32[2,1280]{1,0:T(2,128)}, u32[]{:S(2)}) copy-start(f32[2,1280]{1,0:T(2,128)} %param.19) | copy-start | bytes 30724
  46.8 6.8 %copy-start.10 = (f32[2,1280]{1,0:T(2,128)S(1)}, f32[2,1280]{1,0:T(2,128)}, u32[]{:S(2)}) copy-start(f32[2,1280]{1,0:T(2,128)} %param.20) | copy-start | bytes 30724
  46.8 23.0 %all-to-all-start.1 = ((bf16[8,256,325]{1,2,0:T(8,128)(2,1)}), bf16[8,256,325]{1,2,0:T(8,128)(2,1)}, u32[]{:S(2)}, u32[]{:S(2)}) async-start(bf16[8,256,325]{1,2,0:T(8,128)(2,1)} %maximum_maximum_fusion), calls=%async_computation.1 | async-start | bytes 2686976 | tf_op jit(solution)/shard_map/all_to_all | solution.py:353
  56.4 15.1 %copy-start.8 = (bf16[1,256,320]{1,2,0:T(8,128)(2,1)S(1)}, bf16[1,256,320]{1,2,0:T(8,128)(2,1)}, u32[]{:S(2)}) copy-start(bf16[1,256,320]{1,2,0:T(8,128)(2,1)} %get-tuple-element.22) | copy-start | bytes 491524
  69.8 1.7 %copy-start.14 = (bf16[5,256,256]{1,2,0:T(8,128)(2,1)S(1)}, bf16[5,256,256]{1,2,0:T(8,128)(2,1)}, u32[]{:S(2)}) copy-start(bf16[5,256,256]{1,2,0:T(8,128)(2,1)} %get-tuple-element.39) | copy-start | bytes 1966084
  71.5 21.3 %slice-start = ((s8[6553600]{0:T(1024)(128)(4,1)}), s8[4194304]{0:T(1024)(128)(4,1)S(1)}, s32[]{:S(2)}) async-start(s8[6553600]{0:T(1024)(128)(4,1)} %bitcast.119), calls=%async_computation.3 | async-start | bytes 8388608
  90.7 1.1 copy-start.1
  90.7 2.1 %slice-start.1 = ((s8[6553600]{0:T(1024)(128)(4,1)}), s8[2359296]{0:T(1024)(128)(4,1)S(1)}, s32[]{:S(2)}) async-start(s8[6553600]{0:T(1024)(128)(4,1)} %bitcast.119), calls=%async_computation.4 | async-start | bytes 4718592
  92.8 1.9 %copy-start.2 = (bf16[256,1280]{1,0:T(8,128)(2,1)}, bf16[256,1280]{1,0:T(8,128)(2,1)S(1)}, u32[]{:S(2)}) copy-start(bf16[256,1280]{1,0:T(8,128)(2,1)S(1)} %multiply_convert_fusion) | copy-start | bytes 1966084
  92.8 2.2 %copy-start.11 = (bf16[1280,1280]{1,0:T(8,128)(2,1)S(1)}, bf16[1280,1280]{1,0:T(8,128)(2,1)}, u32[]{:S(2)}) copy-start(bf16[1280,1280]{1,0:T(8,128)(2,1)} %param.17) | copy-start | bytes 9830404
  97.1 19.6 %all-to-all-start.2 = ((bf16[4,64,1280]{2,1,0:T(8,128)(2,1)}), bf16[4,64,1280]{2,1,0:T(8,128)(2,1)}, u32[]{:S(2)}, u32[]{:S(2)}) async-start(bf16[4,64,1280]{2,1,0:T(8,128)(2,1)} %bitcast.125), calls=%async_computation.2 | async-start | bytes 1310720 | tf_op jit(solution)/shard_map/all_to_all | solution.py:383
  116.7 1.4 %copy-start.3 = (bf16[256,1280]{1,0:T(8,128)(2,1)S(1)}, bf16[256,1280]{1,0:T(8,128)(2,1)}, u32[]{:S(2)}) copy-start(bf16[256,1280]{1,0:T(8,128)(2,1)} %copy-done.2) | copy-start | bytes 1966084

commit v17 on v12

--- a/solution.py
+++ b/solution.py
@@ -359,8 +359,23 @@
         :, :, None
     ]
     attention_local = mixed.reshape(slot_count, local_width).astype(jnp.bfloat16)
-    attention = lax.all_gather(attention_local, "mp", axis=1, tiled=True)
-    projected_out = jnp.dot(attention, w_out, preferred_element_type=jnp.float32)
+    projected_out = jnp.dot(
+        attention_local,
+        lax.dynamic_slice_in_dim(w_out, mp_index * local_width, local_width, 0),
+        preferred_element_type=jnp.float32,
+    )
+    for shift in range(1, mp_count):
+        arrived = lax.ppermute(
+            attention_local,
+            "mp",
+            [(source, (source + shift) % mp_count) for source in range(mp_count)],
+        )
+        origin = (mp_index + mp_count - shift) % mp_count
+        projected_out = projected_out + jnp.dot(
+            arrived,
+            lax.dynamic_slice_in_dim(w_out, origin * local_width, local_width, 0),
+            preferred_element_type=jnp.float32,
+        )
     residual_in = state_in.astype(jnp.float32)
     state_mid = rms_rows(
         residual_in + eigen_rates[0][None, :] * (rms_rows(projected_out) - residual_in)

time: 119 us -> 122 us (1.025)
  blocking collectives: 19 us -> 0 us
  waiting for transfers between devices: 30 us -> 43.4 us
  starting transfers between devices: 14.3 us -> 21.5 us
    all_gather x1 -> x0, blocking collectives: 19 us -> none  [shards_heads(): attention = lax.all_gather(attention_local, 'mp', axis=1, tiled=True)]
    ppermute x0 -> x3, waiting for transfers between devices: none -> 11.5 us  [shards_heads(): lax.ppermute(attention_local, 'mp', [(source, (source + shift) % mp_count...]
    ppermute x0 -> x3, starting transfers between devices: none -> 5.11 us  [shards_heads(): lax.ppermute(attention_local, 'mp', [(source, (source + shift) % mp_count...]
    all_to_all x1, starting transfers between devices: 4.16 us -> 6.21 us  [shards_heads(): lax.all_to_all(jnp.dot(hidden, w_down, preferred_element_type=jnp.float32...]
    all_to_all x1, waiting for transfers between devices: 15.4 us -> 17.3 us  [shards_heads(): lax.all_to_all(jnp.dot(hidden, w_down, preferred_element_type=jnp.float32...]
  transfers between devices with their start and end apart: 3 -> 6, of which waited for: 3 -> 5; matrix products, arithmetic and copies ran while one was open for 16% -> 17% of each run, Pallas kernels for 0% -> 0%
where the time goes in v17:
time: 122 us; the launch traced here: 121 us
  waiting for transfers between devices  43.4 us (36%)
  starting transfers between devices  21.5 us (18%)
  matrix products  21.4 us (18%)
  local copies, waits for them, and re-layouts  17.3 us (14%)
  other arithmetic  17.1 us (14%)
    all_to_all x1, waiting for transfers between devices, shards_heads(): lax.all_to_all(jnp.dot(hidden, w_down, preferred_element_type=jnp.float32...  17.3 us
    all_to_all x1, waiting for transfers between devices, shards_heads(): lax.all_to_all(jnp.concatenate(pieces, axis=0).reshape(pages_count * slot...  13.4 us
    ppermute x3, waiting for transfers between devices, shards_heads(): lax.ppermute(attention_local, 'mp', [(source, (source + shift) % mp_count...  11.5 us
    all_to_all x1, starting transfers between devices, shards_heads(): lax.all_to_all(jnp.dot(hidden, w_down, preferred_element_type=jnp.float32...  6.21 us
    all_to_all x1, starting transfers between devices, shards_heads(): lax.all_to_all(jnp.concatenate(pieces, axis=0).reshape(pages_count * slot...  5.79 us
    dot_general x2, matrix products, shards_heads(): jnp.einsum('pshd,khd->phks', query_chunk, key_heads, preferred_element_ty...  5.66 us
    ppermute x3, starting transfers between devices, shards_heads(): lax.ppermute(attention_local, 'mp', [(source, (source + shift) % mp_count...  5.11 us
    all_to_all x1, starting transfers between devices, shards_heads(): lax.all_to_all(jnp.tile(queries, (lax.axis_size('pages'), 1)), 'pages', 0...  4.39 us
  transfers between devices with their start and end apart: 6, of which 5 were waited for; matrix products, arithmetic and copies ran while one was open for 17% of the time, Pallas kernels for 0%

profile of v17, /device:TPU:2, one launch (start us, length us, event | category | flops | bytes accessed | tf_op | source)
XLA Modules:
  0.0 121.1 jit_solution(7477255779669055547)
XLA Ops:
  0.0 1.4 %fusion.23 = f32[256]{0:T(256)S(1)} fusion(bf16[256,1280]{1,0:T(8,128)(2,1)} %param.13), kind=kLoop, calls=%fused_computation.30 | loop fusion | flops 982784 | bytes 656384 | tf_op jit(solution)/shard_map/reduce_sum | solution.py:16
  1.5 0.7 reduce_window_sum.11
  2.2 0.7 sub.46
  2.9 0.8 select_reduce_fusion.2
  3.7 2.8 %fusion.36 = bf16[3,256,320]{1,2,0:T(8,128)(2,1)S(1)} fusion(bf16[3,1280,320]{1,2,0:T(8,128)(2,1)} %param.14, bf16[256,1280]{1,0:T(8,128)(2,1)} %param.13, f32[256]{0:T(256)S(1)} %add_rsqrt_fusion.5), kind=kOutput, calls=%fused_computation.46 | convolution fusion | flops 630374400 | bytes 3605504 | tf_op jit(solution)/shard_map/sd,jdc->jsc/dot_general | solution.py:255
  6.5 0.7 fusion.84
  7.5 0.7 multiply_subtract_fusion
  8.3 0.8 fusion.62
  9.0 0.8 dynamic_slice.45
  9.8 1.1 fusion.59
  10.9 1.2 tile.2
  12.0 4.4 %all-to-all-start = ((bf16[8,256,320]{1,2,0:T(8,128)(2,1)}), bf16[8,256,320]{1,2,0:T(8,128)(2,1)}, u32[]{:S(2)}, u32[]{:S(2)}) async-start(bf16[8,256,320]{1,2,0:T(8,128)(2,1)} %tile.2), calls=%async_computation | async-start | bytes 2621440 | tf_op jit(solution)/shard_map/all_to_all | solution.py:265
  16.8 2.4 %constant_dynamic-slice_fusion = (bf16[4,128,320]{2,1,0:T(8,128)(2,1)}, bf16[4,128,320]{2,1,0:T(8,128)(2,1)}) fusion(bf16[4,128,1280]{2,1,0:T(8,128)(2,1)} %param.21, s32[]{:T(128)S(6)} %select_n.86, bf16[4,128,1280]{2,1,0:T(8,128)(2,1)} %param.22), kind=kLoop, calls=%fused_computation.121 | loop fusion | bytes 1310724 | tf_op jit(solution)/shard_map/dynamic_slice | solution.py:297
  19.2 1.9 %copy.65 = bf16[4,128,320]{1,2,0:T(8,128)(2,1)} copy(bf16[4,128,320]{2,1,0:T(8,128)(2,1)} %get-tuple-element.39) | data formatting | bytes 655360
  21.1 2.1 %copy.55 = f32[4,128,320]{1,0,2:T(4,128)} copy(bf16[4,128,320]{1,2,0:T(8,128)(2,1)} %copy.65) | data formatting | bytes 983040 | tf_op jit(solution)/shard_map/convert_element_type | solution.py:299
  23.2 2.2 %reshape.352 = f32[512,5,64]{0,2,1:T(8,128)} reshape(f32[4,128,320]{1,0,2:T(4,128)} %copy.55) | data formatting | bytes 1310720 | tf_op jit(solution)/shard_map/convert_element_type | solution.py:299
  25.4 1.2 multiply_reduce_fusion.2
  26.5 1.9 %copy.53 = bf16[4,128,320]{1,0,2:T(4,128)(2,1)} copy(bf16[4,128,320]{2,1,0:T(8,128)(2,1)} %get-tuple-element.40) | data formatting | bytes 655360 | tf_op jit(solution)/shard_map/dynamic_slice | solution.py:303
  28.5 1.8 %reshape.355 = bf16[512,5,64,1]{0,2,1,3:T(8,128)(2,1)} reshape(bf16[4,128,320]{1,0,2:T(4,128)(2,1)} %copy.53) | data formatting | bytes 655360 | tf_op jit(solution)/shard_map/reshape;reshape | solution.py:308
  30.4 1.7 %broadcast_compare_fusion.1 = (pred[4,512,256]{2,1,0:T(8,128)(4,1)}, pred[4,512,256]{2,1,0:T(8,128)(4,1)}) fusion(s32[4,256]{1,0:T(4,128)S(1)} %get-tuple-element.23, s32[512]{0:T(512)S(1)} %broadcast_bitcast_fusion, s32[4,256]{1,0:T(4,128)S(1)} %get-tuple-element.24), kind=kLoop, calls=%fused_computation.52 | loop fusion | flops 1048576 | bytes 1058816 | tf_op jit(solution)/shard_map/eq | solution.py:326
  32.0 1.2 all-to-all-done
  33.2 1.5 %fusion.83 = (bf16[4,256,320]{1,2,0:T(8,128)(2,1)S(1)}, bf16[4,256,320]{1,2,0:T(8,128)(2,1)S(1)}) fusion(bf16[8,256,320]{1,2,0:T(8,128)(2,1)} %all-to-all-done), kind=kLoop, calls=%fused_computation.150 | loop fusion | bytes 2621440 | tf_op jit(solution)/shard_map/slice | solution.py:314
  34.9 2.8 %fusion.2 = (bf16[4,5,256]{2,0,1:T(4,128)(2,1)S(1)}, f32[5,512,4,256]{3,1,2,0:T(8,128)S(1)}) fusion(pred[4,512,256]{2,1,0:T(8,128)(4,1)S(1)} %copy-done.6, bf16[4,256,5,64]{1,3,2,0:T(8,128)(2,1)S(1)} %bitcast.123, f32[512,5,64]{0,2,1:T(8,128)S(1)} %copy-done.4, f32[5,64]{1,0:T(8,128)S(1)} %mul.334, f32[512,5]{0,1:T(8,128)S(1)} %add_rsqrt_fusion), kind=kOutput, calls=%fused_computation.4 | convolution fusion | flops 343895040 | bytes 12342528 | tf_op jit(solution)/shard_map/pshd,khd->phks/dot_general | solution.py:321
  37.7 2.0 %fusion.30 = bf16[4,256,5,64]{1,3,0,2:T(8,128)(2,1)S(1)} fusion(f32[5,512,4,256]{3,1,2,0:T(8,128)S(1)} %get-tuple-element.30, pred[4,512,256]{2,1,0:T(8,128)(4,1)S(1)} %copy-done.6, bf16[512,5,64,1]{0,2,1,3:T(8,128)(2,1)S(1)} %copy-done.7), kind=kOutput, calls=%fused_computation.44 | convolution fusion | flops 343736320 | bytes 11993088 | tf_op jit(solution)/shard_map/phks,khd->pshd/dot_general | solution.py:329
  39.8 2.8 %fusion = (bf16[4,5,256]{2,0,1:T(4,128)(2,1)S(1)}, f32[5,512,4,256]{3,1,2,0:T(8,128)S(1)}) fusion(pred[4,512,256]{2,1,0:T(8,128)(4,1)S(1)} %copy-done.5, bf16[4,256,5,64]{1,3,2,0:T(8,128)(2,1)S(1)} %bitcast.122, f32[512,5,64]{0,2,1:T(8,128)S(1)} %copy-done.4, f32[5,64]{1,0:T(8,128)S(1)} %mul.334, f32[512,5]{0,1:T(8,128)S(1)} %add_rsqrt_fusion), kind=kOutput, calls=%fused_computation.2 | convolution fusion | flops 343895040 | bytes 12342528 | tf_op jit(solution)/shard_map/pshd,khd->phks/dot_general | solution.py:321
  42.7 2.0 %fusion.33 = bf16[4,256,5,64]{1,3,0,2:T(8,128)(2,1)S(1)} fusion(f32[5,512,4,256]{3,1,2,0:T(8,128)S(1)} %get-tuple-element.32, pred[4,512,256]{2,1,0:T(8,128)(4,1)S(1)} %copy-done.5, bf16[512,5,64,1]{0,2,1,3:T(8,128)(2,1)S(1)} %copy-done.7), kind=kOutput, calls=%fused_computation.45 | convolution fusion | flops 343736320 | bytes 11993088 | tf_op jit(solution)/shard_map/phks,khd->pshd/dot_general | solution.py:329
  44.7 1.2 maximum_maximum_fusion
  45.9 5.8 %all-to-all-start.1 = ((bf16[8,256,325]{1,2,0:T(8,128)(2,1)}), bf16[8,256,325]{1,2,0:T(8,128)(2,1)}, u32[]{:S(2)}, u32[]{:S(2)}) async-start(bf16[8,256,325]{1,2,0:T(8,128)(2,1)} %maximum_maximum_fusion), calls=%async_computation.1 | async-start | bytes 2686976 | tf_op jit(solution)/shard_map/all_to_all | solution.py:344
  51.7 1.0 multiply_reduce_fusion.5
  53.0 2.4 %fusion.86 = (f32[5,256]{1,0:T(8,128)S(1)}, bf16[5,256,256]{1,2,0:T(8,128)(2,1)}) fusion(f32[256,5,32]{0,2,1:T(8,128)} %get-tuple-element.18, f32[256,5,32]{0,2,1:T(8,128)S(1)} %get-tuple-element.17, f32[256,5]{0,1:T(8,128)S(1)} %add_rsqrt_fusion.1, f32[5,64]{1,0:T(8,128)S(1)} %mul.334, f32[256,5,64]{0,2,1:T(8,128)} %fusion.62, ...), kind=kOutput, calls=%fused_computation.153 | convolution fusion | flops 43744000 | bytes 1387776 | tf_op jit(solution)/shard_map/qhd,khd->hqk/dot_general | solution.py:269
  55.4 13.4 %all-to-all-done.1 = bf16[8,256,325]{1,2,0:T(8,128)(2,1)} async-done(((bf16[8,256,325]{1,2,0:T(8,128)(2,1)}), bf16[8,256,325]{1,2,0:T(8,128)(2,1)}, u32[]{:S(2)}, u32[]{:S(2)}) %all-to-all-start.1) | async-done | bytes 1331232 | tf_op jit(solution)/shard_map/all_to_all | solution.py:344
  68.9 1.6 %convert_reduce_fusion = f32[256,325]{0,1:T(8,128)S(1)} fusion(bf16[8,256,325]{1,2,0:T(8,128)(2,1)} %all-to-all-done.1), kind=kLoop, calls=%fused_computation.18 | loop fusion | flops 1248000 | bytes 1664000 | tf_op jit(solution)/shard_map/reduce_sum | solution.py:351
  70.8 4.1 %collective-permute-start.2 = (bf16[256,320]{0,1:T(8,128)(2,1)S(1)}, bf16[256,320]{0,1:T(8,128)(2,1)S(1)}, u32[]{:S(2)}, u32[]{:S(2)}) collective-permute-start(bf16[256,320]{0,1:T(8,128)(2,1)S(1)} %bitcast.128), channel_id=1, source_target_pairs={{0,3},{1,0},{2,1},{3,2},{4,7},{5,4},{6,5},{7,6},{8,11},{9,8},{10,9... | collective-permute-start | bytes 491528 | tf_op jit(solution)/shard_map/ppermute | solution.py:368
  74.9 1.0 collective-permute-start
  75.9 0.5 fusion.44
  76.5 10.2 %collective-permute-done = bf16[256,320]{0,1:T(8,128)(2,1)S(1)} collective-permute-done((bf16[256,320]{0,1:T(8,128)(2,1)S(1)}, bf16[256,320]{0,1:T(8,128)(2,1)S(1)}, u32[]{:S(2)}, u32[]{:S(2)}) %collective-permute-start) | collective-permute-done | bytes 163872 | tf_op jit(solution)/shard_map/ppermute | solution.py:368
  86.6 0.5 convolution_add_fusion.1
  87.2 0.5 fusion.40
  87.7 1.3 %collective-permute-done.1 = bf16[256,320]{0,1:T(8,128)(2,1)S(1)} collective-permute-done((bf16[256,320]{0,1:T(8,128)(2,1)S(1)}, bf16[256,320]{0,1:T(8,128)(2,1)S(1)}, u32[]{:S(2)}, u32[]{:S(2)}) %collective-permute-start.1) | collective-permute-done | bytes 163872 | tf_op jit(solution)/shard_map/ppermute | solution.py:368
  89.0 0.7 multiply_reduce_fusion.1
  89.7 0.5 multiply_reduce_fusion
  90.2 0.4 multiply_convert_fusion
  90.7 1.9 %convolution_bitcast_fusion = f32[2,256,1280]{2,1,0:T(8,128)S(1)} fusion(bf16[2,1280,1280]{2,1,0:T(8,128)(2,1)S(1)} %bitcast.119, bf16[256,1280]{1,0:T(8,128)(2,1)S(1)} %multiply_convert_fusion), kind=kOutput, calls=%fused_computation.14 | convolution fusion | flops 1677721600 | bytes 9830400 | tf_op jit(solution)/shard_map/sd,jdf->jsf/dot_general | solution.py:384
  92.8 2.1 %convolution_convert_fusion = bf16[256,1280]{1,0:T(8,128)(2,1)} fusion(bf16[1280,1280]{1,0:T(8,128)(2,1)S(1)} %copy-done.11, f32[2,256,1280]{2,1,0:T(8,128)S(1)} %convolution_bitcast_fusion, f32[1280]{0:T(1024)S(1)} %get-tuple-element.8, f32[1280]{0:T(1024)S(1)} %get-tuple-element.7), kind=kOutput, calls=%fused_computation.19 | convolution fusion | flops 841809920 | bytes 6563840 | tf_op jit(solution)/shard_map/dot_general | solution.py:390
  94.9 6.2 %all-to-all-start.2 = ((bf16[4,64,1280]{2,1,0:T(8,128)(2,1)}), bf16[4,64,1280]{2,1,0:T(8,128)(2,1)}, u32[]{:S(2)}, u32[]{:S(2)}) async-start(bf16[4,64,1280]{2,1,0:T(8,128)(2,1)} %bitcast.124), calls=%async_computation.2 | async-start | bytes 1310720 | tf_op jit(solution)/shard_map/all_to_all | solution.py:389
  101.2 17.3 %all-to-all-done.2 = bf16[4,64,1280]{2,1,0:T(8,128)(2,1)} async-done(((bf16[4,64,1280]{2,1,0:T(8,128)(2,1)}), bf16[4,64,1280]{2,1,0:T(8,128)(2,1)}, u32[]{:S(2)}, u32[]{:S(2)}) %all-to-all-start.2) | async-done | bytes 655392 | tf_op jit(solution)/shard_map/all_to_all | solution.py:389
  118.5 1.3 %convert_reduce_fusion.1 = f32[64,1280]{1,0:T(8,128)S(1)} fusion(bf16[4,64,1280]{2,1,0:T(8,128)(2,1)} %all-to-all-done.2), kind=kLoop, calls=%fused_computation.39 | loop fusion | flops 573440 | bytes 983040 | tf_op jit(solution)/shard_map/reduce_sum | solution.py:396
  120.2 0.9 multiply_convert_fusion.2
  (73 shorter events, 2.4 us)
Async XLA Ops:
  0.0 75.9 %copy-start = (bf16[1280,1280]{1,0:T(8,128)(2,1)S(1)}, bf16[1280,1280]{1,0:T(8,128)(2,1)}, u32[]{:S(2)}) copy-start(bf16[1280,1280]{1,0:T(8,128)(2,1)} %param.15) | copy-start | bytes 9830404
  12.0 4.6 %copy-start.12 = (s32[32]{0:T(128)S(1)}, s32[32]{0:T(128)}, u32[]{:S(2)}) copy-start(s32[32]{0:T(128)} %param.23) | copy-start | bytes 388
  12.0 21.2 %all-to-all-start = ((bf16[8,256,320]{1,2,0:T(8,128)(2,1)}), bf16[8,256,320]{1,2,0:T(8,128)(2,1)}, u32[]{:S(2)}, u32[]{:S(2)}) async-start(bf16[8,256,320]{1,2,0:T(8,128)(2,1)} %tile.2), calls=%async_computation | async-start | bytes 2621440 | tf_op jit(solution)/shard_map/all_to_all | solution.py:265
  33.2 1.5 %copy-start.4 = (f32[512,5,64]{0,2,1:T(8,128)S(1)}, f32[512,5,64]{0,2,1:T(8,128)}, u32[]{:S(2)}) copy-start(f32[512,5,64]{0,2,1:T(8,128)} %reshape.352) | copy-start | bytes 1966084
  33.2 1.6 %copy-start.6 = (pred[4,512,256]{2,1,0:T(8,128)(4,1)S(1)}, pred[4,512,256]{2,1,0:T(8,128)(4,1)}, u32[]{:S(2)}) copy-start(pred[4,512,256]{2,1,0:T(8,128)(4,1)} %get-tuple-element.26) | copy-start | bytes 1572868
  34.9 2.8 %copy-start.7 = (bf16[512,5,64,1]{0,2,1,3:T(8,128)(2,1)S(1)}, bf16[512,5,64,1]{0,2,1,3:T(8,128)(2,1)}, u32[]{:S(2)}) copy-start(bf16[512,5,64,1]{0,2,1,3:T(8,128)(2,1)} %reshape.355) | copy-start | bytes 983044
  37.7 2.1 %copy-start.5 = (pred[4,512,256]{2,1,0:T(8,128)(4,1)S(1)}, pred[4,512,256]{2,1,0:T(8,128)(4,1)}, u32[]{:S(2)}) copy-start(pred[4,512,256]{2,1,0:T(8,128)(4,1)} %get-tuple-element.25) | copy-start | bytes 1572868
  45.9 6.8 %copy-start.9 = (f32[2,1280]{1,0:T(2,128)S(1)}, f32[2,1280]{1,0:T(2,128)}, u32[]{:S(2)}) copy-start(f32[2,1280]{1,0:T(2,128)} %param.19) | copy-start | bytes 30724
  45.9 6.8 %copy-start.10 = (f32[2,1280]{1,0:T(2,128)S(1)}, f32[2,1280]{1,0:T(2,128)}, u32[]{:S(2)}) copy-start(f32[2,1280]{1,0:T(2,128)} %param.20) | copy-start | bytes 30724
  45.9 23.0 %all-to-all-start.1 = ((bf16[8,256,325]{1,2,0:T(8,128)(2,1)}), bf16[8,256,325]{1,2,0:T(8,128)(2,1)}, u32[]{:S(2)}, u32[]{:S(2)}) async-start(bf16[8,256,325]{1,2,0:T(8,128)(2,1)} %maximum_maximum_fusion), calls=%async_computation.1 | async-start | bytes 2686976 | tf_op jit(solution)/shard_map/all_to_all | solution.py:344
  55.4 15.1 %copy-start.8 = (bf16[1,256,320]{1,2,0:T(8,128)(2,1)S(1)}, bf16[1,256,320]{1,2,0:T(8,128)(2,1)}, u32[]{:S(2)}) copy-start(bf16[1,256,320]{1,2,0:T(8,128)(2,1)} %get-tuple-element.16) | copy-start | bytes 491524
  68.9 1.7 %copy-start.13 = (bf16[5,256,256]{1,2,0:T(8,128)(2,1)S(1)}, bf16[5,256,256]{1,2,0:T(8,128)(2,1)}, u32[]{:S(2)}) copy-start(bf16[5,256,256]{1,2,0:T(8,128)(2,1)} %get-tuple-element.34) | copy-start | bytes 1966084
  70.8 16.4 %collective-permute-start.2 = (bf16[256,320]{0,1:T(8,128)(2,1)S(1)}, bf16[256,320]{0,1:T(8,128)(2,1)S(1)}, u32[]{:S(2)}, u32[]{:S(2)}) collective-permute-start(bf16[256,320]{0,1:T(8,128)(2,1)S(1)} %bitcast.128), channel_id=1, source_target_pairs={{0,3},{1,0},{2,1},{3,2},{4,7},{5,4},{6,5},{7,6},{8,11},{9,8},{10,9... | collective-permute-start | bytes 491528 | tf_op jit(solution)/shard_map/ppermute | solution.py:368
  74.9 14.1 %collective-permute-start.1 = (bf16[256,320]{0,1:T(8,128)(2,1)S(1)}, bf16[256,320]{0,1:T(8,128)(2,1)S(1)}, u32[]{:S(2)}, u32[]{:S(2)}) collective-permute-start(bf16[256,320]{0,1:T(8,128)(2,1)S(1)} %bitcast.129), channel_id=1, source_target_pairs={{0,2},{1,3},{2,0},{3,1},{4,6},{5,7},{6,4},{7,5},{8,10},{9,11},{10,... | collective-permute-start | bytes 491528 | tf_op jit(solution)/shard_map/ppermute | solution.py:368
  74.9 11.7 %collective-permute-start = (bf16[256,320]{0,1:T(8,128)(2,1)S(1)}, bf16[256,320]{0,1:T(8,128)(2,1)S(1)}, u32[]{:S(2)}, u32[]{:S(2)}) collective-permute-start(bf16[256,320]{0,1:T(8,128)(2,1)S(1)} %bitcast.130), channel_id=1, source_target_pairs={{0,1},{1,2},{2,3},{3,0},{4,5},{5,6},{6,7},{7,4},{8,9},{9,10},{10,1... | collective-permute-start | bytes 491528 | tf_op jit(solution)/shard_map/ppermute | solution.py:368
  87.2 3.5 %slice-start = ((s8[6553600]{0:T(1024)(128)(4,1)}), s8[4194304]{0:T(1024)(128)(4,1)S(1)}, s32[]{:S(2)}) async-start(s8[6553600]{0:T(1024)(128)(4,1)} %bitcast.118), calls=%async_computation.3 | async-start | bytes 8388608
  87.7 2.0 %copy-start.1 = (bf16[256,1280]{1,0:T(8,128)(2,1)S(1)}, bf16[256,1280]{1,0:T(8,128)(2,1)}, u32[]{:S(2)}) copy-start(bf16[256,1280]{1,0:T(8,128)(2,1)} %param.13) | copy-start | bytes 1966084
  87.7 2.9 %slice-start.1 = ((s8[6553600]{0:T(1024)(128)(4,1)}), s8[2359296]{0:T(1024)(128)(4,1)S(1)}, s32[]{:S(2)}) async-start(s8[6553600]{0:T(1024)(128)(4,1)} %bitcast.118), calls=%async_computation.4 | async-start | bytes 4718592
  90.6 1.9 %copy-start.2 = (bf16[256,1280]{1,0:T(8,128)(2,1)}, bf16[256,1280]{1,0:T(8,128)(2,1)S(1)}, u32[]{:S(2)}) copy-start(bf16[256,1280]{1,0:T(8,128)(2,1)S(1)} %multiply_convert_fusion) | copy-start | bytes 1966084
  90.7 2.2 %copy-start.11 = (bf16[1280,1280]{1,0:T(8,128)(2,1)S(1)}, bf16[1280,1280]{1,0:T(8,128)(2,1)}, u32[]{:S(2)}) copy-start(bf16[1280,1280]{1,0:T(8,128)(2,1)} %param.17) | copy-start | bytes 9830404
  94.9 23.6 %all-to-all-start.2 = ((bf16[4,64,1280]{2,1,0:T(8,128)(2,1)}), bf16[4,64,1280]{2,1,0:T(8,128)(2,1)}, u32[]{:S(2)}, u32[]{:S(2)}) async-start(bf16[4,64,1280]{2,1,0:T(8,128)(2,1)} %bitcast.124), calls=%async_computation.2 | async-start | bytes 1310720 | tf_op jit(solution)/shard_map/all_to_all | solution.py:389
  118.5 1.4 %copy-start.3 = (bf16[256,1280]{1,0:T(8,128)(2,1)S(1)}, bf16[256,1280]{1,0:T(8,128)(2,1)}, u32[]{:S(2)}) copy-start(bf16[256,1280]{1,0:T(8,128)(2,1)} %copy-done.2) | copy-start | bytes 1966084

commit v18 on v15

--- a/solution.py
+++ b/solution.py
@@ -307,7 +307,7 @@
     key_heads = prefix_keys.reshape(-1, local_heads, head_dim)
     value_heads = prefix_values.reshape(-1, local_heads, head_dim)
     gathered_heads = gathered.reshape(pages_count, slot_count, local_heads, head_dim)
-    chunk_count = 4 if pages_count % 4 == 0 else 1
+    chunk_count = 1
     chunk_pages = pages_count // chunk_count
     pieces = []
     for chunk in range(chunk_count):

time: 123 us -> 128 us (1.041)
  matrix products: 22.2 us -> 31 us
  other arithmetic: 20.7 us -> 17.1 us
  local copies, waits for them, and re-layouts: 17.1 us -> 15.8 us
    dot_general x4 -> x1, matrix products: 6.24 us -> 11.3 us  [shards_heads(): jnp.einsum('pshd,khd->phks', query_chunk, key_heads, preferred_element_ty...]
    dot_general x4 -> x1, matrix products: 4.09 us -> 9.12 us  [shards_heads(): jnp.einsum('phks,khd->pshd', prefix_weights.astype(jnp.bfloat16), value_h...]
    convert_element_type x1 -> x0, other arithmetic: 1.95 us -> none  [shards_heads(): prefix_keys = head_norm(cache_local.reshape(pages_here * page_len, local_...]
    slice x2 -> x0, local copies, waits for them, and re-layouts: 1.42 us -> none  [the longest x1 1.42 us: shards_heads(): lax.slice_in_dim(gathered_heads, chunk * chunk_pages, (chunk + 1) * chunk...]
    dot_general x1, matrix products: 1.56 us -> 0.25 us  [shards_heads(): jnp.einsum('hqk,khd->qhd', weights.astype(jnp.bfloat16), value_rows.resha...]
  transfers between devices with their start and end apart: 3 -> 3, of which waited for: 2 -> 3; matrix products, arithmetic and copies ran while one was open for 18% -> 15% of each run, Pallas kernels for 0% -> 0%
where the time goes in v18:
time: 128 us
  matrix products  31 us (24%)
  waiting for transfers between devices  29.9 us (23%)
  blocking collectives  19.2 us (15%)
  other arithmetic  17.1 us (13%)
  local copies, waits for them, and re-layouts  15.8 us (12%)
  starting transfers between devices  14.2 us (11%)
    all_gather x1, blocking collectives, shards_heads(): attention = lax.all_gather(attention_local, 'mp', axis=1, tiled=True)  19.2 us
    all_to_all x1, waiting for transfers between devices, shards_heads(): lax.all_to_all(jnp.dot(hidden, w_down, preferred_element_type=jnp.float32...  15.4 us
    all_to_all x1, waiting for transfers between devices, shards_heads(): lax.all_to_all(jnp.concatenate(pieces, axis=0).reshape(pages_count * slot...  13.4 us
    dot_general x1, matrix products, shards_heads(): jnp.einsum('pshd,khd->phks', query_chunk, key_heads, preferred_element_ty...  11.3 us
    dot_general x1, matrix products, shards_heads(): jnp.einsum('phks,khd->pshd', prefix_weights.astype(jnp.bfloat16), value_h...  9.12 us
    all_to_all x1, starting transfers between devices, shards_heads(): lax.all_to_all(jnp.concatenate(pieces, axis=0).reshape(pages_count * slot...  5.79 us
    convert_element_type x2, local copies, waits for them, and re-layouts, shards_heads(): cache_local.reshape(pages_here * page_len, local_width).astype(jnp.float32)  4.28 us
    all_to_all x1, starting transfers between devices, shards_heads(): lax.all_to_all(jnp.tile(queries, (lax.axis_size('pages'), 1)), 'pages', 0...  4.25 us
  transfers between devices with their start and end apart: 3, of which 3 were waited for; matrix products, arithmetic and copies ran while one was open for 15% of the time, Pallas kernels for 0%

profile of v18, /device:TPU:2, one launch (start us, length us, event | category | flops | bytes accessed | tf_op | source)
XLA Modules:
  0.0 127.5 jit_solution(14530594855124454503)
XLA Ops:
  0.0 1.4 %fusion.15 = f32[256]{0:T(256)S(1)} fusion(bf16[256,1280]{1,0:T(8,128)(2,1)} %param.13), kind=kLoop, calls=%fused_computation.21 | loop fusion | flops 982784 | bytes 656384 | tf_op jit(solution)/shard_map/reduce_sum | solution.py:16
  1.5 0.7 reduce_window_sum.11
  2.2 0.7 sub.37
  2.9 0.8 select_reduce_fusion.2
  3.7 2.8 %fusion.24 = bf16[3,256,320]{1,2,0:T(8,128)(2,1)S(1)} fusion(bf16[3,1280,320]{1,2,0:T(8,128)(2,1)} %param.14, bf16[256,1280]{1,0:T(8,128)(2,1)} %param.13, f32[256]{0:T(256)S(1)} %add_rsqrt_fusion.5), kind=kOutput, calls=%fused_computation.37 | convolution fusion | flops 630374400 | bytes 3605504 | tf_op jit(solution)/shard_map/sd,jdc->jsc/dot_general | solution.py:255
  6.5 0.7 fusion.55
  7.3 0.2 multiply_cosine_fusion
  7.5 0.7 multiply_subtract_fusion
  8.2 0.8 fusion.42
  9.0 0.8 dynamic_slice.33
  9.8 1.1 fusion.38
  10.9 1.1 tile.2
  12.0 4.3 %all-to-all-start = ((bf16[8,256,320]{1,2,0:T(8,128)(2,1)}), bf16[8,256,320]{1,2,0:T(8,128)(2,1)}, u32[]{:S(2)}, u32[]{:S(2)}) async-start(bf16[8,256,320]{1,2,0:T(8,128)(2,1)} %tile.2), calls=%async_computation | async-start | bytes 2621440 | tf_op jit(solution)/shard_map/all_to_all | solution.py:265
  16.4 2.4 %constant_dynamic-slice_fusion = (bf16[4,128,320]{2,1,0:T(8,128)(2,1)}, bf16[4,128,320]{2,1,0:T(8,128)(2,1)}) fusion(bf16[4,128,1280]{2,1,0:T(8,128)(2,1)} %param.21, s32[]{:T(128)S(6)} %select_n.62, bf16[4,128,1280]{2,1,0:T(8,128)(2,1)} %param.22), kind=kLoop, calls=%fused_computation.99 | loop fusion | bytes 1310724 | tf_op jit(solution)/shard_map/dynamic_slice | solution.py:297
  18.9 1.9 %copy.54 = bf16[4,128,320]{1,2,0:T(8,128)(2,1)} copy(bf16[4,128,320]{2,1,0:T(8,128)(2,1)} %get-tuple-element.31) | data formatting | bytes 655360
  20.8 2.1 %copy.47 = f32[4,128,320]{1,0,2:T(4,128)} copy(bf16[4,128,320]{1,2,0:T(8,128)(2,1)} %copy.54) | data formatting | bytes 983040 | tf_op jit(solution)/shard_map/convert_element_type | solution.py:299
  22.9 2.2 %reshape.350 = f32[512,5,64]{0,2,1:T(8,128)} reshape(f32[4,128,320]{1,0,2:T(4,128)} %copy.47) | data formatting | bytes 1310720 | tf_op jit(solution)/shard_map/convert_element_type | solution.py:299
  25.1 1.2 multiply_reduce_fusion.2
  26.2 2.0 %copy.45 = bf16[4,128,320]{1,0,2:T(4,128)(2,1)} copy(bf16[4,128,320]{2,1,0:T(8,128)(2,1)} %get-tuple-element.32) | data formatting | bytes 655360 | tf_op jit(solution)/shard_map/dynamic_slice | solution.py:303
  28.2 1.8 %reshape.353 = bf16[512,5,64,1]{0,2,1,3:T(8,128)(2,1)} reshape(bf16[4,128,320]{1,0,2:T(4,128)(2,1)} %copy.45) | data formatting | bytes 655360 | tf_op jit(solution)/shard_map/reshape;reshape | solution.py:308
  30.0 0.2 select_reduce_fusion.3
  30.3 1.7 %broadcast_compare_fusion = pred[8,512,256]{2,1,0:T(8,128)(4,1)} fusion(s32[8,256]{1,0:T(8,128)S(1)} %broadcast_select_fusion, s32[512]{0:T(512)S(1)} %broadcast_bitcast_fusion), kind=kLoop, calls=%fused_computation.10 | loop fusion | flops 1048576 | bytes 1058816 | tf_op jit(solution)/shard_map/eq | solution.py:326
  32.0 1.1 all-to-all-done
  33.1 11.3 %fusion = (bf16[8,5,256]{2,0,1:T(8,128)(2,1)S(1)}, f32[5,512,8,256]{3,1,2,0:T(8,128)}) fusion(pred[8,512,256]{2,1,0:T(8,128)(4,1)} %broadcast_compare_fusion, bf16[8,256,5,64]{1,3,2,0:T(8,128)(2,1)} %bitcast.16, f32[512,5,64]{0,2,1:T(8,128)} %reshape.350, f32[5,64]{1,0:T(8,128)S(1)} %mul.323, f32[512,5]{0,1:T(8,128)S(1)} %add_rsqrt_fusion), kind=kOutput, calls=%fused_computation.1 | convolution fusion | flops 687298560 | bytes 24018176 | tf_op jit(solution)/shard_map/pshd,khd->phks/dot_general | solution.py:321
  44.4 9.1 %fusion.12 = bf16[8,256,5,64]{1,3,0,2:T(8,128)(2,1)S(1)} fusion(f32[5,512,8,256]{3,1,2,0:T(8,128)} %get-tuple-element.24, pred[8,512,256]{2,1,0:T(8,128)(4,1)S(1)} %copy-done.4, bf16[512,5,64,1]{0,2,1,3:T(8,128)(2,1)S(1)} %copy-done.5), kind=kOutput, calls=%fused_computation.19 | convolution fusion | flops 687472640 | bytes 23658496 | tf_op jit(solution)/shard_map/phks,khd->pshd/dot_general | solution.py:329
  53.5 0.1 copy.49
  53.7 1.2 pad_maximum_fusion
  54.9 5.8 %all-to-all-start.1 = ((bf16[8,256,325]{1,2,0:T(8,128)(2,1)}), bf16[8,256,325]{1,2,0:T(8,128)(2,1)}, u32[]{:S(2)}, u32[]{:S(2)}) async-start(bf16[8,256,325]{1,2,0:T(8,128)(2,1)} %pad_maximum_fusion), calls=%async_computation.1 | async-start | bytes 2686976 | tf_op jit(solution)/shard_map/all_to_all | solution.py:344
  60.7 1.0 multiply_reduce_fusion.5
  61.8 0.2 and_and_fusion
  62.0 2.5 %fusion.56 = (f32[5,256]{1,0:T(8,128)S(1)}, bf16[5,256,256]{1,2,0:T(8,128)(2,1)}) fusion(f32[256,5,32]{0,2,1:T(8,128)} %get-tuple-element.16, f32[256,5,32]{0,2,1:T(8,128)S(1)} %get-tuple-element.15, f32[256,5]{0,1:T(8,128)S(1)} %add_rsqrt_fusion.1, f32[5,64]{1,0:T(8,128)S(1)} %mul.323, f32[256,5,64]{0,2,1:T(8,128)} %fusion.42, ...), kind=kOutput, calls=%fused_computation.124 | convolution fusion | flops 43744000 | bytes 1387776 | tf_op jit(solution)/shard_map/qhd,khd->hqk/dot_general | solution.py:269
  64.4 13.4 %all-to-all-done.1 = bf16[8,256,325]{1,2,0:T(8,128)(2,1)} async-done(((bf16[8,256,325]{1,2,0:T(8,128)(2,1)}), bf16[8,256,325]{1,2,0:T(8,128)(2,1)}, u32[]{:S(2)}, u32[]{:S(2)}) %all-to-all-start.1) | async-done | bytes 1331232 | tf_op jit(solution)/shard_map/all_to_all | solution.py:344
  77.9 1.6 %convert_reduce_fusion = f32[256,325]{0,1:T(8,128)S(1)} fusion(bf16[8,256,325]{1,2,0:T(8,128)(2,1)} %all-to-all-done.1), kind=kLoop, calls=%fused_computation.8 | loop fusion | flops 1248000 | bytes 1664000 | tf_op jit(solution)/shard_map/reduce_sum | solution.py:351
  79.5 0.2 fusion.27
  79.8 19.2 %all_gather.3 = bf16[256,1280]{0,1:T(8,128)(2,1)S(1)} all-gather(bf16[256,320]{0,1:T(8,128)(2,1)S(1)} %bitcast.100), channel_id=1, replica_groups=mesh['pages'=8,'mp'=4] {'mp'}, dimensions={1}, use_global_device_ids=true | all-gather | bytes 819200 | tf_op jit(solution)/shard_map/all_gather | solution.py:362
  99.0 1.1 multiply_reduce_fusion.1
  100.1 0.5 multiply_reduce_fusion
  100.6 0.4 multiply_convert_fusion
  101.1 1.9 %convolution_bitcast_fusion = f32[2,256,1280]{2,1,0:T(8,128)S(1)} fusion(bf16[2,1280,1280]{2,1,0:T(8,128)(2,1)S(1)} %bitcast.94, bf16[256,1280]{1,0:T(8,128)(2,1)S(1)} %multiply_convert_fusion), kind=kOutput, calls=%fused_computation.7 | convolution fusion | flops 1677721600 | bytes 9830400 | tf_op jit(solution)/shard_map/sd,jdf->jsf/dot_general | solution.py:369
  103.0 0.3 copy-done.9
  103.2 2.1 %convolution_convert_fusion = bf16[256,1280]{1,0:T(8,128)(2,1)} fusion(bf16[1280,1280]{1,0:T(8,128)(2,1)S(1)} %copy-done.9, f32[2,256,1280]{2,1,0:T(8,128)S(1)} %convolution_bitcast_fusion, f32[1280]{0:T(1024)S(1)} %get-tuple-element.8, f32[1280]{0:T(1024)S(1)} %get-tuple-element.7), kind=kOutput, calls=%fused_computation.9 | convolution fusion | flops 841809920 | bytes 6563840 | tf_op jit(solution)/shard_map/dot_general | solution.py:375
  105.3 4.2 %all-to-all-start.2 = ((bf16[4,64,1280]{2,1,0:T(8,128)(2,1)}), bf16[4,64,1280]{2,1,0:T(8,128)(2,1)}, u32[]{:S(2)}, u32[]{:S(2)}) async-start(bf16[4,64,1280]{2,1,0:T(8,128)(2,1)} %bitcast.96), calls=%async_computation.2 | async-start | bytes 1310720 | tf_op jit(solution)/shard_map/all_to_all | solution.py:374
  109.5 0.1 fusion.48
  109.6 15.4 %all-to-all-done.2 = bf16[4,64,1280]{2,1,0:T(8,128)(2,1)} async-done(((bf16[4,64,1280]{2,1,0:T(8,128)(2,1)}), bf16[4,64,1280]{2,1,0:T(8,128)(2,1)}, u32[]{:S(2)}, u32[]{:S(2)}) %all-to-all-start.2) | async-done | bytes 655392 | tf_op jit(solution)/shard_map/all_to_all | solution.py:374
  125.0 1.3 convert_reduce_fusion.1
  126.2 0.1 multiply_reduce_fusion.4
  126.4 0.3 multiply_reduce_fusion.3
  126.6 0.9 multiply_convert_fusion.2
  (55 shorter events, 0.6 us)
Async XLA Ops:
  0.0 99.0 %copy-start = (bf16[1280,1280]{1,0:T(8,128)(2,1)S(1)}, bf16[1280,1280]{1,0:T(8,128)(2,1)}, u32[]{:S(2)}) copy-start(bf16[1280,1280]{1,0:T(8,128)(2,1)} %param.15) | copy-start | bytes 9830404
  12.0 21.1 %all-to-all-start = ((bf16[8,256,320]{1,2,0:T(8,128)(2,1)}), bf16[8,256,320]{1,2,0:T(8,128)(2,1)}, u32[]{:S(2)}, u32[]{:S(2)}) async-start(bf16[8,256,320]{1,2,0:T(8,128)(2,1)} %tile.2), calls=%async_computation | async-start | bytes 2621440 | tf_op jit(solution)/shard_map/all_to_all | solution.py:265
  25.1 5.0 %copy-start.10 = (s32[32]{0:T(128)S(1)}, s32[32]{0:T(128)}, u32[]{:S(2)}) copy-start(s32[32]{0:T(128)} %param.23) | copy-start | bytes 388
  33.1 11.3 %copy-start.4 = (pred[8,512,256]{2,1,0:T(8,128)(4,1)S(1)}, pred[8,512,256]{2,1,0:T(8,128)(4,1)}, u32[]{:S(2)}) copy-start(pred[8,512,256]{2,1,0:T(8,128)(4,1)} %broadcast_compare_fusion) | copy-start | bytes 3145732
  33.1 11.3 %copy-start.5 = (bf16[512,5,64,1]{0,2,1,3:T(8,128)(2,1)S(1)}, bf16[512,5,64,1]{0,2,1,3:T(8,128)(2,1)}, u32[]{:S(2)}) copy-start(bf16[512,5,64,1]{0,2,1,3:T(8,128)(2,1)} %reshape.353) | copy-start | bytes 983044
  54.9 6.8 %copy-start.7 = (f32[2,1280]{1,0:T(2,128)S(1)}, f32[2,1280]{1,0:T(2,128)}, u32[]{:S(2)}) copy-start(f32[2,1280]{1,0:T(2,128)} %param.19) | copy-start | bytes 30724
  54.9 6.8 %copy-start.8 = (f32[2,1280]{1,0:T(2,128)S(1)}, f32[2,1280]{1,0:T(2,128)}, u32[]{:S(2)}) copy-start(f32[2,1280]{1,0:T(2,128)} %param.20) | copy-start | bytes 30724
  54.9 23.0 %all-to-all-start.1 = ((bf16[8,256,325]{1,2,0:T(8,128)(2,1)}), bf16[8,256,325]{1,2,0:T(8,128)(2,1)}, u32[]{:S(2)}, u32[]{:S(2)}) async-start(bf16[8,256,325]{1,2,0:T(8,128)(2,1)} %pad_maximum_fusion), calls=%async_computation.1 | async-start | bytes 2686976 | tf_op jit(solution)/shard_map/all_to_all | solution.py:344
  64.4 15.1 %copy-start.6 = (bf16[1,256,320]{1,2,0:T(8,128)(2,1)S(1)}, bf16[1,256,320]{1,2,0:T(8,128)(2,1)}, u32[]{:S(2)}) copy-start(bf16[1,256,320]{1,2,0:T(8,128)(2,1)} %get-tuple-element.14) | copy-start | bytes 491524
  77.9 1.7 %copy-start.11 = (bf16[5,256,256]{1,2,0:T(8,128)(2,1)S(1)}, bf16[5,256,256]{1,2,0:T(8,128)(2,1)}, u32[]{:S(2)}) copy-start(bf16[5,256,256]{1,2,0:T(8,128)(2,1)} %get-tuple-element.26) | copy-start | bytes 1966084
  79.5 21.5 %slice-start = ((s8[6553600]{0:T(1024)(128)(4,1)}), s8[4194304]{0:T(1024)(128)(4,1)S(1)}, s32[]{:S(2)}) async-start(s8[6553600]{0:T(1024)(128)(4,1)} %bitcast.93), calls=%async_computation.3 | async-start | bytes 8388608
  99.0 1.1 copy-start.1
  99.0 2.1 %slice-start.1 = ((s8[6553600]{0:T(1024)(128)(4,1)}), s8[2359296]{0:T(1024)(128)(4,1)S(1)}, s32[]{:S(2)}) async-start(s8[6553600]{0:T(1024)(128)(4,1)} %bitcast.93), calls=%async_computation.4 | async-start | bytes 4718592
  101.1 1.9 %copy-start.2 = (bf16[256,1280]{1,0:T(8,128)(2,1)}, bf16[256,1280]{1,0:T(8,128)(2,1)S(1)}, u32[]{:S(2)}) copy-start(bf16[256,1280]{1,0:T(8,128)(2,1)S(1)} %multiply_convert_fusion) | copy-start | bytes 1966084
  101.1 2.2 %copy-start.9 = (bf16[1280,1280]{1,0:T(8,128)(2,1)S(1)}, bf16[1280,1280]{1,0:T(8,128)(2,1)}, u32[]{:S(2)}) copy-start(bf16[1280,1280]{1,0:T(8,128)(2,1)} %param.17) | copy-start | bytes 9830404
  105.3 19.6 %all-to-all-start.2 = ((bf16[4,64,1280]{2,1,0:T(8,128)(2,1)}), bf16[4,64,1280]{2,1,0:T(8,128)(2,1)}, u32[]{:S(2)}, u32[]{:S(2)}) async-start(bf16[4,64,1280]{2,1,0:T(8,128)(2,1)} %bitcast.96), calls=%async_computation.2 | async-start | bytes 1310720 | tf_op jit(solution)/shard_map/all_to_all | solution.py:374
  125.0 1.4 %copy-start.3 = (bf16[256,1280]{1,0:T(8,128)(2,1)S(1)}, bf16[256,1280]{1,0:T(8,128)(2,1)}, u32[]{:S(2)}) copy-start(bf16[256,1280]{1,0:T(8,128)(2,1)} %copy-done.2) | copy-start | bytes 1966084

commit v19 on v16

--- a/solution.py
+++ b/solution.py
@@ -266,7 +266,7 @@
     gathered = lax.all_to_all(
         jnp.tile(queries, (lax.axis_size("pages"), 1)), "pages", 0, 0, tiled=True
     )
-    state_kv, _ = lax.optimization_barrier((state_in, gathered[:1, :1]))
+    state_kv = state_in + jnp.zeros_like(state_in) * gathered[0, 0]
     projected = jnp.einsum(
         "sd,jdc->jsc", state_kv, w_qkv[1:], preferred_element_type=jnp.float32
     ).astype(jnp.bfloat16)

time: 120 us -> 119 us (level)
  waiting for transfers between devices: 30 us -> 27.5 us
  other arithmetic: 18.6 us -> 16.3 us
  local copies, waits for them, and re-layouts: 17.3 us -> 19.1 us
    dot_general x1, matrix products: 0.63 us -> 2.35 us  [shards_heads(): jnp.einsum('sd,jdc->jsc', state_kv, w_qkv[1:], preferred_element_type=jnp...]
    all_to_all x1, waiting for transfers between devices: 13.4 us -> 11.9 us  [shards_heads(): lax.all_to_all(jnp.concatenate(pieces, axis=0).reshape(pages_count * slot...]
    all_to_all x0 -> x1, local copies, waits for them, and re-layouts: none -> 1.47 us  [shards_heads(): lax.all_to_all(jnp.tile(queries, (lax.axis_size('pages'), 1)), 'pages', 0...]
    convert_element_type x1 -> x0, other arithmetic: 1.42 us -> none  [shards_heads(): state_in = rms_rows(hidden_in.astype(jnp.float32)).astype(jnp.bfloat16)]
  transfers between devices with their start and end apart: 3 -> 3, of which waited for: 3 -> 3; matrix products, arithmetic and copies ran while one was open for 16% -> 17% of each run, Pallas kernels for 0% -> 0%
where the time goes in v19:
time: 119 us; the launch traced here: 118 us
  waiting for transfers between devices  27.5 us (23%)
  matrix products  20.6 us (17%)
  local copies, waits for them, and re-layouts  19.1 us (16%)
  blocking collectives  19 us (16%)
  other arithmetic  16.3 us (14%)
  starting transfers between devices  14.2 us (12%)
    all_gather x1, blocking collectives, shards_heads(): attention = lax.all_gather(attention_local, 'mp', axis=1, tiled=True)  19 us
    all_to_all x1, waiting for transfers between devices, shards_heads(): lax.all_to_all(jnp.dot(hidden, w_down, preferred_element_type=jnp.float32...  15.4 us
    all_to_all x1, waiting for transfers between devices, shards_heads(): lax.all_to_all(jnp.concatenate(pieces, axis=0).reshape(pages_count * slot...  11.9 us
    all_to_all x1, starting transfers between devices, shards_heads(): lax.all_to_all(jnp.concatenate(pieces, axis=0).reshape(pages_count * slot...  5.67 us
    dot_general x2, matrix products, shards_heads(): jnp.einsum('pshd,khd->phks', query_chunk, key_heads, preferred_element_ty...  5.66 us
    all_to_all x1, starting transfers between devices, shards_heads(): lax.all_to_all(jnp.tile(queries, (lax.axis_size('pages'), 1)), 'pages', 0...  4.39 us
    convert_element_type x2, local copies, waits for them, and re-layouts, shards_heads(): cache_local.reshape(pages_here * page_len, local_width).astype(jnp.float32)  4.24 us
    all_to_all x1, starting transfers between devices, shards_heads(): lax.all_to_all(jnp.dot(hidden, w_down, preferred_element_type=jnp.float32...  4.16 us
  transfers between devices with their start and end apart: 3, of which 3 were waited for; matrix products, arithmetic and copies ran while one was open for 17% of the time, Pallas kernels for 0%

profile of v19, /device:TPU:2, one launch (start us, length us, event | category | flops | bytes accessed | tf_op | source)
XLA Modules:
  0.0 117.7 jit_solution(4205468601108901267)
XLA Ops:
  0.0 1.4 %fusion.24 = f32[256]{0:T(256)S(1)} fusion(bf16[256,1280]{1,0:T(8,128)(2,1)} %param.13), kind=kLoop, calls=%fused_computation.29 | loop fusion | flops 982784 | bytes 656384 | tf_op jit(solution)/shard_map/reduce_sum | solution.py:16
  1.5 0.8 slice_add_fusion.1
  2.3 0.7 fusion.81
  3.0 0.8 select_reduce_fusion.1
  3.8 1.8 %convolution_convert_fusion.1 = bf16[256,320]{0,1:T(8,128)(2,1)S(1)} fusion(bf16[3,1280,320]{1,2,0:T(8,128)(2,1)} %param.14, bf16[256,1280]{1,0:T(8,128)(2,1)} %param.13, f32[256]{0:T(256)S(1)} %add_rsqrt_fusion.5), kind=kOutput, calls=%fused_computation.50 | convolution fusion | flops 210780160 | bytes 1639424 | tf_op jit(solution)/shard_map/dot_general | solution.py:258
  5.7 0.2 multiply_cosine_fusion
  6.0 0.7 fusion.66
  6.7 0.8 dynamic_slice.28
  7.5 1.1 fusion.64
  8.6 1.2 tile.2
  9.7 4.4 %all-to-all-start = ((bf16[8,256,320]{1,2,0:T(8,128)(2,1)}), bf16[8,256,320]{1,2,0:T(8,128)(2,1)}, u32[]{:S(2)}, u32[]{:S(2)}) async-start(bf16[8,256,320]{1,2,0:T(8,128)(2,1)} %tile.2), calls=%async_computation | async-start | bytes 2621440 | tf_op jit(solution)/shard_map/all_to_all | solution.py:266
  14.7 2.4 %constant_dynamic-slice_fusion = (bf16[4,128,320]{2,1,0:T(8,128)(2,1)}, bf16[4,128,320]{2,1,0:T(8,128)(2,1)}) fusion(bf16[4,128,1280]{2,1,0:T(8,128)(2,1)} %param.21, s32[]{:T(128)S(6)} %select_n.60, bf16[4,128,1280]{2,1,0:T(8,128)(2,1)} %param.22), kind=kLoop, calls=%fused_computation.119 | loop fusion | bytes 1310724 | tf_op jit(solution)/shard_map/dynamic_slice | solution.py:306
  17.1 1.9 %copy.79 = bf16[4,128,320]{1,2,0:T(8,128)(2,1)} copy(bf16[4,128,320]{2,1,0:T(8,128)(2,1)} %get-tuple-element.42) | data formatting | bytes 655360
  19.0 2.1 %copy.69 = f32[4,128,320]{1,0,2:T(4,128)} copy(bf16[4,128,320]{1,2,0:T(8,128)(2,1)} %copy.79) | data formatting | bytes 983040 | tf_op jit(solution)/shard_map/convert_element_type | solution.py:308
  21.1 2.2 %reshape.359 = f32[512,5,64]{0,2,1:T(8,128)} reshape(f32[4,128,320]{1,0,2:T(4,128)} %copy.69) | data formatting | bytes 1310720 | tf_op jit(solution)/shard_map/convert_element_type | solution.py:308
  23.3 1.2 multiply_reduce_fusion.2
  24.4 1.9 %copy.67 = bf16[4,128,320]{1,0,2:T(4,128)(2,1)} copy(bf16[4,128,320]{2,1,0:T(8,128)(2,1)} %get-tuple-element.43) | data formatting | bytes 655360 | tf_op jit(solution)/shard_map/dynamic_slice | solution.py:312
  26.4 1.8 %reshape.362 = bf16[512,5,64,1]{0,2,1,3:T(8,128)(2,1)} reshape(bf16[4,128,320]{1,0,2:T(4,128)(2,1)} %copy.67) | data formatting | bytes 655360 | tf_op jit(solution)/shard_map/reshape;reshape | solution.py:317
  28.2 0.8 and_and_fusion
  29.0 1.7 %broadcast_compare_fusion.1 = (pred[4,512,256]{2,1,0:T(8,128)(4,1)}, pred[4,512,256]{2,1,0:T(8,128)(4,1)}) fusion(s32[4,256]{1,0:T(4,128)S(1)} %get-tuple-element.23, s32[512]{0:T(512)S(1)} %broadcast_bitcast_fusion, s32[4,256]{1,0:T(4,128)S(1)} %get-tuple-element.24), kind=kLoop, calls=%fused_computation.52 | loop fusion | flops 1048576 | bytes 1058816 | tf_op jit(solution)/shard_map/eq | solution.py:335
  30.7 0.3 all-to-all-done
  30.9 1.5 %copy.80 = bf16[8,40,8,256]{3,2,0,1:T(8,128)(2,1)S(1)} copy(bf16[8,40,8,256]{3,2,1,0:T(8,128)(2,1)} %bitcast.37) | data formatting | bytes 2621440 | tf_op jit(solution)/shard_map/all_to_all | solution.py:266
  32.4 0.5 slice.112
  32.9 1.4 %fusion.85 = (bf16[4,256,320]{1,2,0:T(8,128)(2,1)S(1)}, bf16[4,256,320]{1,2,0:T(8,128)(2,1)S(1)}) fusion(bf16[8,256,320]{1,2,0:T(8,128)(2,1)} %all-to-all-done), kind=kLoop, calls=%fused_computation.149 | loop fusion | bytes 2621440 | tf_op jit(solution)/shard_map/slice | solution.py:323
  34.3 2.8 %fusion.2 = (bf16[4,5,256]{2,0,1:T(4,128)(2,1)S(1)}, f32[5,512,4,256]{3,1,2,0:T(8,128)S(1)}) fusion(pred[4,512,256]{2,1,0:T(8,128)(4,1)S(1)} %copy-done.7, bf16[4,256,5,64]{1,3,2,0:T(8,128)(2,1)S(1)} %bitcast.127, f32[512,5,64]{0,2,1:T(8,128)S(1)} %copy-done.4, f32[5,64]{1,0:T(8,128)S(1)} %mul.331, f32[512,5]{0,1:T(8,128)S(1)} %add_rsqrt_fusion), kind=kOutput, calls=%fused_computation.4 | convolution fusion | flops 343895040 | bytes 12342528 | tf_op jit(solution)/shard_map/pshd,khd->phks/dot_general | solution.py:330
  37.2 2.0 %fusion.31 = bf16[4,256,5,64]{1,3,0,2:T(8,128)(2,1)S(1)} fusion(f32[5,512,4,256]{3,1,2,0:T(8,128)S(1)} %get-tuple-element.33, pred[4,512,256]{2,1,0:T(8,128)(4,1)S(1)} %copy-done.7, bf16[512,5,64,1]{0,2,1,3:T(8,128)(2,1)S(1)} %copy-done.8), kind=kOutput, calls=%fused_computation.42 | convolution fusion | flops 343736320 | bytes 11993088 | tf_op jit(solution)/shard_map/phks,khd->pshd/dot_general | solution.py:338
  39.3 2.8 %fusion = (bf16[4,5,256]{2,0,1:T(4,128)(2,1)S(1)}, f32[5,512,4,256]{3,1,2,0:T(8,128)S(1)}) fusion(pred[4,512,256]{2,1,0:T(8,128)(4,1)S(1)} %copy-done.6, bf16[4,256,5,64]{1,3,2,0:T(8,128)(2,1)S(1)} %bitcast.126, f32[512,5,64]{0,2,1:T(8,128)S(1)} %copy-done.4, f32[5,64]{1,0:T(8,128)S(1)} %mul.331, f32[512,5]{0,1:T(8,128)S(1)} %add_rsqrt_fusion), kind=kOutput, calls=%fused_computation.2 | convolution fusion | flops 343895040 | bytes 12342528 | tf_op jit(solution)/shard_map/pshd,khd->phks/dot_general | solution.py:330
  42.1 2.0 %fusion.34 = bf16[4,256,5,64]{1,3,0,2:T(8,128)(2,1)S(1)} fusion(f32[5,512,4,256]{3,1,2,0:T(8,128)S(1)} %get-tuple-element.35, pred[4,512,256]{2,1,0:T(8,128)(4,1)S(1)} %copy-done.6, bf16[512,5,64,1]{0,2,1,3:T(8,128)(2,1)S(1)} %copy-done.8), kind=kOutput, calls=%fused_computation.43 | convolution fusion | flops 343736320 | bytes 11993088 | tf_op jit(solution)/shard_map/phks,khd->pshd/dot_general | solution.py:338
  44.2 1.2 maximum_maximum_fusion
  45.3 5.7 %all-to-all-start.1 = ((bf16[8,256,325]{1,2,0:T(8,128)(2,1)}), bf16[8,256,325]{1,2,0:T(8,128)(2,1)}, u32[]{:S(2)}, u32[]{:S(2)}) async-start(bf16[8,256,325]{1,2,0:T(8,128)(2,1)} %maximum_maximum_fusion), calls=%async_computation.1 | async-start | bytes 2686976 | tf_op jit(solution)/shard_map/all_to_all | solution.py:353
  51.6 2.3 %fusion.41 = bf16[2,256,320]{1,2,0:T(8,128)(2,1)S(1)} fusion(bf16[3,1280,320]{1,2,0:T(8,128)(2,1)} %param.14, bf16[]{:T(256)} %bitcast.6, bf16[256,1280]{1,0:T(8,128)(2,1)} %param.13, f32[256]{0:T(256)S(1)} %add_rsqrt_fusion.5), kind=kOutput, calls=%fused_computation.47 | convolution fusion | flops 421888000 | bytes 2622976 | tf_op jit(solution)/shard_map/sd,jdc->jsc/dot_general | solution.py:270
  54.1 0.8 copy-done.5
  54.9 1.4 %fusion.88 = (f32[5,256]{1,0:T(8,128)S(1)}, bf16[5,256,256]{1,2,0:T(8,128)(2,1)}) fusion(f32[256,5,32]{0,2,1:T(8,128)S(1)} %get-tuple-element.18, f32[256,5,32]{0,2,1:T(8,128)S(1)} %get-tuple-element.17, f32[256,5]{0,1:T(8,128)S(1)} %add_rsqrt_fusion.1, f32[5,64]{1,0:T(8,128)S(1)} %mul.331, f32[256,5,64]{0,2,1:T(8,128)S(1)} %copy-done.5, ...), kind=kOutput, calls=%fused_computation.152 | convolution fusion | flops 43744000 | bytes 1387776 | tf_op jit(solution)/shard_map/qhd,khd->hqk/dot_general | solution.py:278
  56.3 11.9 %all-to-all-done.1 = bf16[8,256,325]{1,2,0:T(8,128)(2,1)} async-done(((bf16[8,256,325]{1,2,0:T(8,128)(2,1)}), bf16[8,256,325]{1,2,0:T(8,128)(2,1)}, u32[]{:S(2)}, u32[]{:S(2)}) %all-to-all-start.1) | async-done | bytes 1331232 | tf_op jit(solution)/shard_map/all_to_all | solution.py:353
  68.2 1.6 %convert_reduce_fusion = f32[256,325]{0,1:T(8,128)S(1)} fusion(bf16[8,256,325]{1,2,0:T(8,128)(2,1)} %all-to-all-done.1), kind=kLoop, calls=%fused_computation.15 | loop fusion | flops 1248000 | bytes 1664000 | tf_op jit(solution)/shard_map/reduce_sum | solution.py:360
  69.9 0.2 fusion.45
  70.1 19.0 %all_gather.3 = bf16[256,1280]{0,1:T(8,128)(2,1)S(1)} all-gather(bf16[256,320]{0,1:T(8,128)(2,1)S(1)} %bitcast.132), channel_id=1, replica_groups=mesh['pages'=8,'mp'=4] {'mp'}, dimensions={1}, use_global_device_ids=true | all-gather | bytes 819200 | tf_op jit(solution)/shard_map/all_gather | solution.py:371
  89.1 1.1 multiply_reduce_fusion.1
  90.3 0.5 multiply_reduce_fusion
  90.8 0.4 multiply_convert_fusion
  91.2 1.9 %convolution_bitcast_fusion = f32[2,256,1280]{2,1,0:T(8,128)S(1)} fusion(bf16[2,1280,1280]{2,1,0:T(8,128)(2,1)S(1)} %bitcast.122, bf16[256,1280]{1,0:T(8,128)(2,1)S(1)} %multiply_convert_fusion), kind=kOutput, calls=%fused_computation.14 | convolution fusion | flops 1677721600 | bytes 9830400 | tf_op jit(solution)/shard_map/sd,jdf->jsf/dot_general | solution.py:378
  93.1 0.3 copy-done.12
  93.4 2.1 %convolution_convert_fusion = bf16[256,1280]{1,0:T(8,128)(2,1)} fusion(bf16[1280,1280]{1,0:T(8,128)(2,1)S(1)} %copy-done.12, f32[2,256,1280]{2,1,0:T(8,128)S(1)} %convolution_bitcast_fusion, f32[1280]{0:T(1024)S(1)} %get-tuple-element.8, f32[1280]{0:T(1024)S(1)} %get-tuple-element.7), kind=kOutput, calls=%fused_computation.16 | convolution fusion | flops 841809920 | bytes 6563840 | tf_op jit(solution)/shard_map/dot_general | solution.py:384
  95.5 4.2 %all-to-all-start.2 = ((bf16[4,64,1280]{2,1,0:T(8,128)(2,1)}), bf16[4,64,1280]{2,1,0:T(8,128)(2,1)}, u32[]{:S(2)}, u32[]{:S(2)}) async-start(bf16[4,64,1280]{2,1,0:T(8,128)(2,1)} %bitcast.128), calls=%async_computation.2 | async-start | bytes 1310720 | tf_op jit(solution)/shard_map/all_to_all | solution.py:383
  99.7 15.4 %all-to-all-done.2 = bf16[4,64,1280]{2,1,0:T(8,128)(2,1)} async-done(((bf16[4,64,1280]{2,1,0:T(8,128)(2,1)}), bf16[4,64,1280]{2,1,0:T(8,128)(2,1)}, u32[]{:S(2)}, u32[]{:S(2)}) %all-to-all-start.2) | async-done | bytes 655392 | tf_op jit(solution)/shard_map/all_to_all | solution.py:383
  115.1 1.3 %convert_reduce_fusion.1 = f32[64,1280]{1,0:T(8,128)S(1)} fusion(bf16[4,64,1280]{2,1,0:T(8,128)(2,1)} %all-to-all-done.2), kind=kLoop, calls=%fused_computation.38 | loop fusion | flops 573440 | bytes 983040 | tf_op jit(solution)/shard_map/reduce_sum | solution.py:390
  116.5 0.3 multiply_reduce_fusion.3
  116.8 0.9 multiply_convert_fusion.2
  (71 shorter events, 1.3 us)
Async XLA Ops:
  0.0 89.1 %copy-start = (bf16[1280,1280]{1,0:T(8,128)(2,1)S(1)}, bf16[1280,1280]{1,0:T(8,128)(2,1)}, u32[]{:S(2)}) copy-start(bf16[1280,1280]{1,0:T(8,128)(2,1)} %param.15) | copy-start | bytes 9830404
  9.7 4.6 %copy-start.13 = (s32[32]{0:T(128)S(1)}, s32[32]{0:T(128)}, u32[]{:S(2)}) copy-start(s32[32]{0:T(128)} %param.23) | copy-start | bytes 388
  9.7 4.9 %copy-start.10 = (f32[2,1280]{1,0:T(2,128)S(1)}, f32[2,1280]{1,0:T(2,128)}, u32[]{:S(2)}) copy-start(f32[2,1280]{1,0:T(2,128)} %param.19) | copy-start | bytes 30724
  9.7 4.9 %copy-start.11 = (f32[2,1280]{1,0:T(2,128)S(1)}, f32[2,1280]{1,0:T(2,128)}, u32[]{:S(2)}) copy-start(f32[2,1280]{1,0:T(2,128)} %param.20) | copy-start | bytes 30724
  9.7 21.2 %all-to-all-start = ((bf16[8,256,320]{1,2,0:T(8,128)(2,1)}), bf16[8,256,320]{1,2,0:T(8,128)(2,1)}, u32[]{:S(2)}, u32[]{:S(2)}) async-start(bf16[8,256,320]{1,2,0:T(8,128)(2,1)} %tile.2), calls=%async_computation | async-start | bytes 2621440 | tf_op jit(solution)/shard_map/all_to_all | solution.py:266
  32.4 1.9 %copy-start.4 = (f32[512,5,64]{0,2,1:T(8,128)S(1)}, f32[512,5,64]{0,2,1:T(8,128)}, u32[]{:S(2)}) copy-start(f32[512,5,64]{0,2,1:T(8,128)} %reshape.359) | copy-start | bytes 1966084
  32.4 1.9 %copy-start.7 = (pred[4,512,256]{2,1,0:T(8,128)(4,1)S(1)}, pred[4,512,256]{2,1,0:T(8,128)(4,1)}, u32[]{:S(2)}) copy-start(pred[4,512,256]{2,1,0:T(8,128)(4,1)} %get-tuple-element.26) | copy-start | bytes 1572868
  34.3 2.9 %copy-start.8 = (bf16[512,5,64,1]{0,2,1,3:T(8,128)(2,1)S(1)}, bf16[512,5,64,1]{0,2,1,3:T(8,128)(2,1)}, u32[]{:S(2)}) copy-start(bf16[512,5,64,1]{0,2,1,3:T(8,128)(2,1)} %reshape.362) | copy-start | bytes 983044
  37.2 2.1 %copy-start.6 = (pred[4,512,256]{2,1,0:T(8,128)(4,1)S(1)}, pred[4,512,256]{2,1,0:T(8,128)(4,1)}, u32[]{:S(2)}) copy-start(pred[4,512,256]{2,1,0:T(8,128)(4,1)} %get-tuple-element.25) | copy-start | bytes 1572868
  45.3 22.8 %all-to-all-start.1 = ((bf16[8,256,325]{1,2,0:T(8,128)(2,1)}), bf16[8,256,325]{1,2,0:T(8,128)(2,1)}, u32[]{:S(2)}, u32[]{:S(2)}) async-start(bf16[8,256,325]{1,2,0:T(8,128)(2,1)} %maximum_maximum_fusion), calls=%async_computation.1 | async-start | bytes 2686976 | tf_op jit(solution)/shard_map/all_to_all | solution.py:353
  53.9 1.0 copy-start.5
  53.9 1.0 copy-start.9
  68.2 1.7 %copy-start.14 = (bf16[5,256,256]{1,2,0:T(8,128)(2,1)S(1)}, bf16[5,256,256]{1,2,0:T(8,128)(2,1)}, u32[]{:S(2)}) copy-start(bf16[5,256,256]{1,2,0:T(8,128)(2,1)} %get-tuple-element.37) | copy-start | bytes 1966084
  69.9 21.3 %slice-start = ((s8[6553600]{0:T(1024)(128)(4,1)}), s8[4194304]{0:T(1024)(128)(4,1)S(1)}, s32[]{:S(2)}) async-start(s8[6553600]{0:T(1024)(128)(4,1)} %bitcast.121), calls=%async_computation.3 | async-start | bytes 8388608
  89.1 1.2 copy-start.1
  89.1 2.1 %slice-start.1 = ((s8[6553600]{0:T(1024)(128)(4,1)}), s8[2359296]{0:T(1024)(128)(4,1)S(1)}, s32[]{:S(2)}) async-start(s8[6553600]{0:T(1024)(128)(4,1)} %bitcast.121), calls=%async_computation.4 | async-start | bytes 4718592
  91.2 1.9 %copy-start.2 = (bf16[256,1280]{1,0:T(8,128)(2,1)}, bf16[256,1280]{1,0:T(8,128)(2,1)S(1)}, u32[]{:S(2)}) copy-start(bf16[256,1280]{1,0:T(8,128)(2,1)S(1)} %multiply_convert_fusion) | copy-start | bytes 1966084
  91.2 2.2 %copy-start.12 = (bf16[1280,1280]{1,0:T(8,128)(2,1)S(1)}, bf16[1280,1280]{1,0:T(8,128)(2,1)}, u32[]{:S(2)}) copy-start(bf16[1280,1280]{1,0:T(8,128)(2,1)} %param.17) | copy-start | bytes 9830404
  95.5 19.6 %all-to-all-start.2 = ((bf16[4,64,1280]{2,1,0:T(8,128)(2,1)}), bf16[4,64,1280]{2,1,0:T(8,128)(2,1)}, u32[]{:S(2)}, u32[]{:S(2)}) async-start(bf16[4,64,1280]{2,1,0:T(8,128)(2,1)} %bitcast.128), calls=%async_computation.2 | async-start | bytes 1310720 | tf_op jit(solution)/shard_map/all_to_all | solution.py:383
  115.1 1.4 %copy-start.3 = (bf16[256,1280]{1,0:T(8,128)(2,1)S(1)}, bf16[256,1280]{1,0:T(8,128)(2,1)}, u32[]{:S(2)}) copy-start(bf16[256,1280]{1,0:T(8,128)(2,1)} %copy-done.2) | copy-start | bytes 1966084

commit v20 on v13

--- a/solution.py
+++ b/solution.py
@@ -263,38 +263,8 @@
         scale_local,
         local_heads,
     ).astype(jnp.bfloat16)
-    projected = jnp.einsum(
-        "sd,jdc->jsc", state_in, w_qkv[1:], preferred_element_type=jnp.float32
-    ).astype(jnp.bfloat16)
-    keys_new = head_norm(
-        rotate(projected[0].astype(jnp.float32), position_shard, local_heads), scale_local, local_heads
-    ).astype(jnp.bfloat16)
-    value_rows = projected[1]
     gathered = lax.all_to_all(
         jnp.tile(queries, (lax.axis_size("pages"), 1)), "pages", 0, 0, tiled=True
-    )
-    scores = (
-        jnp.einsum(
-            "qhd,khd->hqk",
-            queries.reshape(slot_count, local_heads, head_dim),
-            keys_new.reshape(slot_count, local_heads, head_dim),
-            preferred_element_type=jnp.float32,
-        )
-        * score_scale
-    )
-    allowed = (
-        (request_shard[:, None] == request_shard[None, :])
-        & (offset_shard[None, :] <= offset_shard[:, None])
-        & live_shard[:, None]
-        & live_shard[None, :]
-    )
-    weights = jnp.where(allowed[None], jnp.exp(scores), 0.0)
-    suffix_total = jnp.sum(weights, axis=-1)
-    suffix_sum = jnp.einsum(
-        "hqk,khd->qhd",
-        weights.astype(jnp.bfloat16),
-        value_rows.reshape(slot_count, local_heads, head_dim),
-        preferred_element_type=jnp.float32,
     )
     physical = shard_index * pages_here + jnp.arange(pages_here, dtype=jnp.int32)
     matches = page_table[:, None] == physical[None, :]
@@ -349,6 +319,37 @@
                 axis=2,
             ).astype(jnp.bfloat16)
         )
+    state_kv = state_in + jnp.zeros_like(state_in) * pieces[0][0, 0, 0]
+    projected = jnp.einsum(
+        "sd,jdc->jsc", state_kv, w_qkv[1:], preferred_element_type=jnp.float32
+    ).astype(jnp.bfloat16)
+    keys_new = head_norm(
+        rotate(projected[0].astype(jnp.float32), position_shard, local_heads), scale_local, local_heads
+    ).astype(jnp.bfloat16)
+    value_rows = projected[1]
+    scores = (
+        jnp.einsum(
+            "qhd,khd->hqk",
+            queries.reshape(slot_count, local_heads, head_dim),
+            keys_new.reshape(slot_count, local_heads, head_dim),
+            preferred_element_type=jnp.float32,
+        )
+        * score_scale
+    )
+    allowed = (
+        (request_shard[:, None] == request_shard[None, :])
+        & (offset_shard[None, :] <= offset_shard[:, None])
+        & live_shard[:, None]
+        & live_shard[None, :]
+    )
+    weights = jnp.where(allowed[None], jnp.exp(scores), 0.0)
+    suffix_total = jnp.sum(weights, axis=-1)
+    suffix_sum = jnp.einsum(
+        "hqk,khd->qhd",
+        weights.astype(jnp.bfloat16),
+        value_rows.reshape(slot_count, local_heads, head_dim),
+        preferred_element_type=jnp.float32,
+    )
     prefix_parts = lax.all_to_all(
         jnp.concatenate(pieces, axis=0).reshape(pages_count * slot_count, local_width + local_heads),
         "pages",

time: 120 us -> 118 us (0.983)
  waiting for transfers between devices: 30 us -> 27.4 us
  matrix products: 22.1 us -> 20.6 us
  other arithmetic: 15 us -> 16.3 us
    all_to_all x1, waiting for transfers between devices: 13.4 us -> 11.8 us  [shards_heads(): lax.all_to_all(jnp.concatenate(pieces, axis=0).reshape(pages_count * slot...]
    slice x1, local copies, waits for them, and re-layouts: 1.68 us -> 0.02 us  [shards_heads(): projected[0].astype(jnp.float32)]
    unnamed x39 -> x35, local copies, waits for them, and re-layouts: 2.42 us -> 3.59 us
  transfers between devices with their start and end apart: 3 -> 3, of which waited for: 3 -> 3; matrix products, arithmetic and copies ran while one was open for 16% -> 18% of each run, Pallas kernels for 0% -> 0%
where the time goes in v20:
time: 118 us; the launch traced here: 117 us
  waiting for transfers between devices  27.4 us (23%)
  matrix products  20.6 us (17%)
  blocking collectives  19 us (16%)
  local copies, waits for them, and re-layouts  18.4 us (16%)
  other arithmetic  16.3 us (14%)
  starting transfers between devices  14.2 us (12%)
    all_gather x1, blocking collectives, shards_heads(): attention = lax.all_gather(attention_local, 'mp', axis=1, tiled=True)  19 us
    all_to_all x1, waiting for transfers between devices, shards_heads(): lax.all_to_all(jnp.dot(hidden, w_down, preferred_element_type=jnp.float32...  15.4 us
    all_to_all x1, waiting for transfers between devices, shards_heads(): lax.all_to_all(jnp.concatenate(pieces, axis=0).reshape(pages_count * slot...  11.8 us
    all_to_all x1, starting transfers between devices, shards_heads(): lax.all_to_all(jnp.concatenate(pieces, axis=0).reshape(pages_count * slot...  5.66 us
    dot_general x2, matrix products, shards_heads(): jnp.einsum('pshd,khd->phks', query_chunk, key_heads, preferred_element_ty...  5.66 us
    all_to_all x1, starting transfers between devices, shards_heads(): lax.all_to_all(jnp.tile(queries, (lax.axis_size('pages'), 1)), 'pages', 0...  4.38 us
    convert_element_type x2, local copies, waits for them, and re-layouts, shards_heads(): cache_local.reshape(pages_here * page_len, local_width).astype(jnp.float32)  4.26 us
    all_to_all x1, starting transfers between devices, shards_heads(): lax.all_to_all(jnp.dot(hidden, w_down, preferred_element_type=jnp.float32...  4.16 us
  transfers between devices with their start and end apart: 3, of which 3 were waited for; matrix products, arithmetic and copies ran while one was open for 18% of the time, Pallas kernels for 0%

profile of v20, /device:TPU:2, one launch (start us, length us, event | category | flops | bytes accessed | tf_op | source)
XLA Modules:
  0.0 117.0 jit_solution(4007124715361717318)
XLA Ops:
  0.0 0.9 slice_add_fusion.1
  0.9 0.8 fusion.81
  1.7 0.8 select_reduce_fusion
  2.5 1.3 %fusion.24 = f32[256]{0:T(256)S(1)} fusion(bf16[256,1280]{1,0:T(8,128)(2,1)} %param.13), kind=kLoop, calls=%fused_computation.29 | loop fusion | flops 982784 | bytes 656384 | tf_op jit(solution)/shard_map/reduce_sum | solution.py:16
  3.9 1.8 %convolution_convert_fusion.1 = bf16[256,320]{0,1:T(8,128)(2,1)S(1)} fusion(bf16[3,1280,320]{1,2,0:T(8,128)(2,1)} %param.14, bf16[256,1280]{1,0:T(8,128)(2,1)} %param.13, f32[256]{0:T(256)S(1)} %add_rsqrt_fusion.5), kind=kOutput, calls=%fused_computation.50 | convolution fusion | flops 210780160 | bytes 1639424 | tf_op jit(solution)/shard_map/dot_general | solution.py:258
  5.7 0.2 multiply_cosine_fusion
  6.0 0.8 fusion.66
  6.8 0.8 dynamic_slice.29
  7.6 1.1 fusion.62
  8.6 1.2 tile.2
  9.8 4.4 %all-to-all-start = ((bf16[8,256,320]{1,2,0:T(8,128)(2,1)}), bf16[8,256,320]{1,2,0:T(8,128)(2,1)}, u32[]{:S(2)}, u32[]{:S(2)}) async-start(bf16[8,256,320]{1,2,0:T(8,128)(2,1)} %tile.2), calls=%async_computation | async-start | bytes 2621440 | tf_op jit(solution)/shard_map/all_to_all | solution.py:266
  14.7 2.4 %constant_dynamic-slice_fusion.2 = (bf16[4,128,320]{2,1,0:T(8,128)(2,1)}, bf16[4,128,320]{2,1,0:T(8,128)(2,1)}) fusion(bf16[4,128,1280]{2,1,0:T(8,128)(2,1)} %param.21, s32[]{:T(128)S(6)} %select_n.59, bf16[4,128,1280]{2,1,0:T(8,128)(2,1)} %param.22), kind=kLoop, calls=%fused_computation.121 | loop fusion | bytes 1310724 | tf_op jit(solution)/shard_map/dynamic_slice | solution.py:275
  17.1 1.9 %copy.65 = bf16[4,128,320]{1,2,0:T(8,128)(2,1)} copy(bf16[4,128,320]{2,1,0:T(8,128)(2,1)} %get-tuple-element.42) | data formatting | bytes 655360
  19.0 2.1 %copy.54 = f32[4,128,320]{1,0,2:T(4,128)} copy(bf16[4,128,320]{1,2,0:T(8,128)(2,1)} %copy.65) | data formatting | bytes 983040 | tf_op jit(solution)/shard_map/convert_element_type | solution.py:277
  21.0 2.2 %reshape.356 = f32[512,5,64]{0,2,1:T(8,128)} reshape(f32[4,128,320]{1,0,2:T(4,128)} %copy.54) | data formatting | bytes 1310720 | tf_op jit(solution)/shard_map/convert_element_type | solution.py:277
  23.2 1.2 %multiply_reduce_fusion.2 = f32[512,5]{0,1:T(8,128)S(1)} fusion(f32[512,5,64]{0,2,1:T(8,128)} %reshape.356), kind=kLoop, calls=%fused_computation.67 | loop fusion | flops 325120 | bytes 665600 | tf_op jit(solution)/shard_map/reduce_sum | solution.py:22
  24.4 1.9 %copy.52 = bf16[4,128,320]{1,0,2:T(4,128)(2,1)} copy(bf16[4,128,320]{2,1,0:T(8,128)(2,1)} %get-tuple-element.43) | data formatting | bytes 655360 | tf_op jit(solution)/shard_map/dynamic_slice | solution.py:281
  26.4 1.8 %reshape.361 = bf16[512,5,64,1]{0,2,1,3:T(8,128)(2,1)} reshape(bf16[4,128,320]{1,0,2:T(4,128)(2,1)} %copy.52) | data formatting | bytes 655360 | tf_op jit(solution)/shard_map/reshape;reshape | solution.py:286
  28.3 0.8 and_and_fusion
  29.1 1.6 %broadcast_compare_fusion.1 = (pred[4,512,256]{2,1,0:T(8,128)(4,1)}, pred[4,512,256]{2,1,0:T(8,128)(4,1)}) fusion(s32[4,256]{1,0:T(4,128)S(1)} %get-tuple-element.23, s32[512]{0:T(512)S(1)} %broadcast_bitcast_fusion, s32[4,256]{1,0:T(4,128)S(1)} %get-tuple-element.24), kind=kLoop, calls=%fused_computation.52 | loop fusion | flops 1048576 | bytes 1058816 | tf_op jit(solution)/shard_map/eq | solution.py:304
  30.8 0.2 all-to-all-done
  31.0 1.5 %fusion.85 = (bf16[4,256,320]{1,2,0:T(8,128)(2,1)S(1)}, bf16[4,256,320]{1,2,0:T(8,128)(2,1)S(1)}) fusion(bf16[8,256,320]{1,2,0:T(8,128)(2,1)} %all-to-all-done), kind=kLoop, calls=%fused_computation.149 | loop fusion | bytes 2621440 | tf_op jit(solution)/shard_map/slice | solution.py:292
  32.6 2.8 %fusion = (bf16[4,5,256]{2,0,1:T(4,128)(2,1)S(1)}, f32[5,512,4,256]{3,1,2,0:T(8,128)S(1)}) fusion(pred[4,512,256]{2,1,0:T(8,128)(4,1)S(1)} %copy-done.7, bf16[4,256,5,64]{1,3,2,0:T(8,128)(2,1)S(1)} %bitcast.125, f32[512,5,64]{0,2,1:T(8,128)S(1)} %copy-done.4, f32[5,64]{1,0:T(8,128)S(1)} %mul.318, f32[512,5]{0,1:T(8,128)S(1)} %add_rsqrt_fusion), kind=kOutput, calls=%fused_computation.2 | convolution fusion | flops 343895040 | bytes 12342528 | tf_op jit(solution)/shard_map/pshd,khd->phks/dot_general | solution.py:299
  35.5 2.0 %fusion.34 = bf16[4,256,5,64]{1,3,0,2:T(8,128)(2,1)S(1)} fusion(f32[5,512,4,256]{3,1,2,0:T(8,128)S(1)} %get-tuple-element.35, pred[4,512,256]{2,1,0:T(8,128)(4,1)S(1)} %copy-done.7, bf16[512,5,64,1]{0,2,1,3:T(8,128)(2,1)S(1)} %copy-done.8), kind=kOutput, calls=%fused_computation.43 | convolution fusion | flops 343736320 | bytes 11993088 | tf_op jit(solution)/shard_map/phks,khd->pshd/dot_general | solution.py:307
  37.6 0.6 slice.115
  38.1 0.4 copy-done.6
  38.5 2.8 %fusion.2 = (bf16[4,5,256]{2,0,1:T(4,128)(2,1)S(1)}, f32[5,512,4,256]{3,1,2,0:T(8,128)S(1)}) fusion(pred[4,512,256]{2,1,0:T(8,128)(4,1)S(1)} %copy-done.6, bf16[4,256,5,64]{1,3,2,0:T(8,128)(2,1)S(1)} %bitcast.124, f32[512,5,64]{0,2,1:T(8,128)S(1)} %copy-done.4, f32[5,64]{1,0:T(8,128)S(1)} %mul.318, f32[512,5]{0,1:T(8,128)S(1)} %add_rsqrt_fusion), kind=kOutput, calls=%fused_computation.4 | convolution fusion | flops 343895040 | bytes 12342528 | tf_op jit(solution)/shard_map/pshd,khd->phks/dot_general | solution.py:299
  41.4 2.0 %fusion.31 = bf16[4,256,5,64]{1,3,0,2:T(8,128)(2,1)S(1)} fusion(f32[5,512,4,256]{3,1,2,0:T(8,128)S(1)} %get-tuple-element.33, pred[4,512,256]{2,1,0:T(8,128)(4,1)S(1)} %copy-done.6, bf16[512,5,64,1]{0,2,1,3:T(8,128)(2,1)S(1)} %copy-done.8), kind=kOutput, calls=%fused_computation.42 | convolution fusion | flops 343736320 | bytes 11993088 | tf_op jit(solution)/shard_map/phks,khd->pshd/dot_general | solution.py:307
  43.4 1.2 %maximum_maximum_fusion = bf16[8,256,325]{1,2,0:T(8,128)(2,1)} fusion(bf16[4,256,5]{1,2,0:T(8,128)(2,1)S(1)} %copy.61, bf16[4,256,320]{1,2,0:T(8,128)(2,1)S(1)} %bitcast.123, bf16[4,256,5]{1,2,0:T(8,128)(2,1)S(1)} %copy.58, bf16[4,256,320]{1,2,0:T(8,128)(2,1)S(1)} %bitcast.122), kind=kLoop, calls=%fused_computation.28 | loop fusion | flops 5324800 | bytes 2662400 | tf_op jit(solution)/shard_map/concatenate | solution.py:354
  44.6 5.7 %all-to-all-start.1 = ((bf16[8,256,325]{1,2,0:T(8,128)(2,1)}), bf16[8,256,325]{1,2,0:T(8,128)(2,1)}, u32[]{:S(2)}, u32[]{:S(2)}) async-start(bf16[8,256,325]{1,2,0:T(8,128)(2,1)} %maximum_maximum_fusion), calls=%async_computation.1 | async-start | bytes 2686976 | tf_op jit(solution)/shard_map/all_to_all | solution.py:353
  50.9 2.3 %fusion.41 = bf16[2,256,320]{1,2,0:T(8,128)(2,1)S(1)} fusion(bf16[3,1280,320]{1,2,0:T(8,128)(2,1)} %param.14, bf16[]{:T(256)} %bitcast.14, bf16[256,1280]{1,0:T(8,128)(2,1)} %param.13, f32[256]{0:T(256)S(1)} %add_rsqrt_fusion.5), kind=kOutput, calls=%fused_computation.47 | convolution fusion | flops 421888000 | bytes 2622976 | tf_op jit(solution)/shard_map/sd,jdc->jsc/dot_general | solution.py:323
  53.5 0.8 copy-done.5
  54.3 1.4 %fusion.88 = (f32[5,256]{1,0:T(8,128)S(1)}, bf16[5,256,256]{1,2,0:T(8,128)(2,1)}) fusion(f32[256,5,32]{0,2,1:T(8,128)S(1)} %get-tuple-element.18, f32[256,5,32]{0,2,1:T(8,128)S(1)} %get-tuple-element.17, f32[256,5]{0,1:T(8,128)S(1)} %add_rsqrt_fusion.1, f32[5,64]{1,0:T(8,128)S(1)} %mul.318, f32[256,5,64]{0,2,1:T(8,128)S(1)} %copy-done.5, ...), kind=kOutput, calls=%fused_computation.152 | convolution fusion | flops 43744000 | bytes 1387776 | tf_op jit(solution)/shard_map/qhd,khd->hqk/dot_general | solution.py:331
  55.7 11.8 %all-to-all-done.1 = bf16[8,256,325]{1,2,0:T(8,128)(2,1)} async-done(((bf16[8,256,325]{1,2,0:T(8,128)(2,1)}), bf16[8,256,325]{1,2,0:T(8,128)(2,1)}, u32[]{:S(2)}, u32[]{:S(2)}) %all-to-all-start.1) | async-done | bytes 1331232 | tf_op jit(solution)/shard_map/all_to_all | solution.py:353
  67.5 1.6 %convert_reduce_fusion = f32[256,325]{0,1:T(8,128)S(1)} fusion(bf16[8,256,325]{1,2,0:T(8,128)(2,1)} %all-to-all-done.1), kind=kLoop, calls=%fused_computation.15 | loop fusion | flops 1248000 | bytes 1664000 | tf_op jit(solution)/shard_map/reduce_sum | solution.py:360
  69.1 0.2 fusion.45
  69.4 19.0 %all_gather.3 = bf16[256,1280]{0,1:T(8,128)(2,1)S(1)} all-gather(bf16[256,320]{0,1:T(8,128)(2,1)S(1)} %bitcast.130), channel_id=1, replica_groups=mesh['pages'=8,'mp'=4] {'mp'}, dimensions={1}, use_global_device_ids=true | all-gather | bytes 819200 | tf_op jit(solution)/shard_map/all_gather | solution.py:371
  88.4 1.1 multiply_reduce_fusion.1
  89.5 0.5 multiply_reduce_fusion
  90.0 0.4 multiply_convert_fusion
  90.5 1.9 %convolution_bitcast_fusion = f32[2,256,1280]{2,1,0:T(8,128)S(1)} fusion(bf16[2,1280,1280]{2,1,0:T(8,128)(2,1)S(1)} %bitcast.120, bf16[256,1280]{1,0:T(8,128)(2,1)S(1)} %multiply_convert_fusion), kind=kOutput, calls=%fused_computation.14 | convolution fusion | flops 1677721600 | bytes 9830400 | tf_op jit(solution)/shard_map/sd,jdf->jsf/dot_general | solution.py:378
  92.4 0.3 copy-done.12
  92.7 2.1 %convolution_convert_fusion = bf16[256,1280]{1,0:T(8,128)(2,1)} fusion(bf16[1280,1280]{1,0:T(8,128)(2,1)S(1)} %copy-done.12, f32[2,256,1280]{2,1,0:T(8,128)S(1)} %convolution_bitcast_fusion, f32[1280]{0:T(1024)S(1)} %get-tuple-element.8, f32[1280]{0:T(1024)S(1)} %get-tuple-element.7), kind=kOutput, calls=%fused_computation.16 | convolution fusion | flops 841809920 | bytes 6563840 | tf_op jit(solution)/shard_map/dot_general | solution.py:384
  94.7 4.2 %all-to-all-start.2 = ((bf16[4,64,1280]{2,1,0:T(8,128)(2,1)}), bf16[4,64,1280]{2,1,0:T(8,128)(2,1)}, u32[]{:S(2)}, u32[]{:S(2)}) async-start(bf16[4,64,1280]{2,1,0:T(8,128)(2,1)} %bitcast.126), calls=%async_computation.2 | async-start | bytes 1310720 | tf_op jit(solution)/shard_map/all_to_all | solution.py:383
  99.0 15.4 %all-to-all-done.2 = bf16[4,64,1280]{2,1,0:T(8,128)(2,1)} async-done(((bf16[4,64,1280]{2,1,0:T(8,128)(2,1)}), bf16[4,64,1280]{2,1,0:T(8,128)(2,1)}, u32[]{:S(2)}, u32[]{:S(2)}) %all-to-all-start.2) | async-done | bytes 655392 | tf_op jit(solution)/shard_map/all_to_all | solution.py:383
  114.4 1.3 %convert_reduce_fusion.1 = f32[64,1280]{1,0:T(8,128)S(1)} fusion(bf16[4,64,1280]{2,1,0:T(8,128)(2,1)} %all-to-all-done.2), kind=kLoop, calls=%fused_computation.38 | loop fusion | flops 573440 | bytes 983040 | tf_op jit(solution)/shard_map/reduce_sum | solution.py:390
  115.8 0.3 multiply_reduce_fusion.3
  116.1 0.9 multiply_convert_fusion.2
  (70 shorter events, 1.4 us)
Async XLA Ops:
  0.0 88.4 %copy-start = (bf16[1280,1280]{1,0:T(8,128)(2,1)S(1)}, bf16[1280,1280]{1,0:T(8,128)(2,1)}, u32[]{:S(2)}) copy-start(bf16[1280,1280]{1,0:T(8,128)(2,1)} %param.15) | copy-start | bytes 9830404
  9.8 4.6 %copy-start.13 = (s32[32]{0:T(128)S(1)}, s32[32]{0:T(128)}, u32[]{:S(2)}) copy-start(s32[32]{0:T(128)} %param.23) | copy-start | bytes 388
  9.8 21.2 %all-to-all-start = ((bf16[8,256,320]{1,2,0:T(8,128)(2,1)}), bf16[8,256,320]{1,2,0:T(8,128)(2,1)}, u32[]{:S(2)}, u32[]{:S(2)}) async-start(bf16[8,256,320]{1,2,0:T(8,128)(2,1)} %tile.2), calls=%async_computation | async-start | bytes 2621440 | tf_op jit(solution)/shard_map/all_to_all | solution.py:266
  23.2 5.0 %copy-start.10 = (f32[2,1280]{1,0:T(2,128)S(1)}, f32[2,1280]{1,0:T(2,128)}, u32[]{:S(2)}) copy-start(f32[2,1280]{1,0:T(2,128)} %param.20) | copy-start | bytes 30724
  23.2 5.0 %copy-start.11 = (f32[2,1280]{1,0:T(2,128)S(1)}, f32[2,1280]{1,0:T(2,128)}, u32[]{:S(2)}) copy-start(f32[2,1280]{1,0:T(2,128)} %param.19) | copy-start | bytes 30724
  31.0 1.5 %copy-start.4 = (f32[512,5,64]{0,2,1:T(8,128)S(1)}, f32[512,5,64]{0,2,1:T(8,128)}, u32[]{:S(2)}) copy-start(f32[512,5,64]{0,2,1:T(8,128)} %reshape.356) | copy-start | bytes 1966084
  31.0 1.6 %copy-start.7 = (pred[4,512,256]{2,1,0:T(8,128)(4,1)S(1)}, pred[4,512,256]{2,1,0:T(8,128)(4,1)}, u32[]{:S(2)}) copy-start(pred[4,512,256]{2,1,0:T(8,128)(4,1)} %get-tuple-element.25) | copy-start | bytes 1572868
  32.6 2.8 %copy-start.8 = (bf16[512,5,64,1]{0,2,1,3:T(8,128)(2,1)S(1)}, bf16[512,5,64,1]{0,2,1,3:T(8,128)(2,1)}, u32[]{:S(2)}) copy-start(bf16[512,5,64,1]{0,2,1,3:T(8,128)(2,1)} %reshape.361) | copy-start | bytes 983044
  37.5 1.1 copy-start.6
  44.6 22.8 %all-to-all-start.1 = ((bf16[8,256,325]{1,2,0:T(8,128)(2,1)}), bf16[8,256,325]{1,2,0:T(8,128)(2,1)}, u32[]{:S(2)}, u32[]{:S(2)}) async-start(bf16[8,256,325]{1,2,0:T(8,128)(2,1)} %maximum_maximum_fusion), calls=%async_computation.1 | async-start | bytes 2686976 | tf_op jit(solution)/shard_map/all_to_all | solution.py:353
  53.3 1.0 copy-start.5
  53.3 1.0 copy-start.9
  67.5 1.7 %copy-start.14 = (bf16[5,256,256]{1,2,0:T(8,128)(2,1)S(1)}, bf16[5,256,256]{1,2,0:T(8,128)(2,1)}, u32[]{:S(2)}) copy-start(bf16[5,256,256]{1,2,0:T(8,128)(2,1)} %get-tuple-element.37) | copy-start | bytes 1966084
  69.1 21.3 %slice-start = ((s8[6553600]{0:T(1024)(128)(4,1)}), s8[4194304]{0:T(1024)(128)(4,1)S(1)}, s32[]{:S(2)}) async-start(s8[6553600]{0:T(1024)(128)(4,1)} %bitcast.119), calls=%async_computation.3 | async-start | bytes 8388608
  88.4 1.1 copy-start.1
  88.4 2.1 %slice-start.1 = ((s8[6553600]{0:T(1024)(128)(4,1)}), s8[2359296]{0:T(1024)(128)(4,1)S(1)}, s32[]{:S(2)}) async-start(s8[6553600]{0:T(1024)(128)(4,1)} %bitcast.119), calls=%async_computation.4 | async-start | bytes 4718592
  90.5 1.9 %copy-start.2 = (bf16[256,1280]{1,0:T(8,128)(2,1)}, bf16[256,1280]{1,0:T(8,128)(2,1)S(1)}, u32[]{:S(2)}) copy-start(bf16[256,1280]{1,0:T(8,128)(2,1)S(1)} %multiply_convert_fusion) | copy-start | bytes 1966084
  90.5 2.2 %copy-start.12 = (bf16[1280,1280]{1,0:T(8,128)(2,1)S(1)}, bf16[1280,1280]{1,0:T(8,128)(2,1)}, u32[]{:S(2)}) copy-start(bf16[1280,1280]{1,0:T(8,128)(2,1)} %param.17) | copy-start | bytes 9830404
  94.7 19.6 %all-to-all-start.2 = ((bf16[4,64,1280]{2,1,0:T(8,128)(2,1)}), bf16[4,64,1280]{2,1,0:T(8,128)(2,1)}, u32[]{:S(2)}, u32[]{:S(2)}) async-start(bf16[4,64,1280]{2,1,0:T(8,128)(2,1)} %bitcast.126), calls=%async_computation.2 | async-start | bytes 1310720 | tf_op jit(solution)/shard_map/all_to_all | solution.py:383
  114.4 1.4 %copy-start.3 = (bf16[256,1280]{1,0:T(8,128)(2,1)S(1)}, bf16[256,1280]{1,0:T(8,128)(2,1)}, u32[]{:S(2)}) copy-start(bf16[256,1280]{1,0:T(8,128)(2,1)} %copy-done.2) | copy-start | bytes 1966084
